TPU v7x, 512 devices: a whole 4x4x16 slice. The times are simulated.
512 devices in a mesh: sub: 128 (over y, z, core), case: 4 (over x).
Axes of the slice: x: 4, y: 4, z: 16, core: 2. Of those that a mesh axis runs over, the one named last changes fastest.
Arguments:
- load_interior: float32 [128, 128, 4096], P('sub', None, 'case'), may hold values from -6 to 6
- load_boundary: float32 [128, 128, 1024], P('sub', None, 'case'), may hold values from -6 to 6
- cond_blocks: float32 [128, 128, 4096], P('sub', 'case'), may hold values from -0.25 to 0.25
- block_rows: int32 [128, 128], P('sub', 'case'), may hold values from 0 to 15
- block_cols: int32 [128, 128], P('sub', 'case'), may hold values from 0 to 63, as said below
- interface_maps: int32 [128, 7, 2, 1024], P('sub'), may hold values from 0 to 1023, as said below
- merge_maps: float32 [128, 7, 1024, 512], P('sub', None, 'case'), as said below
Outputs:
- leaf_loads: float32 [128, 1024, 128], P('sub', 'case')
- node_loads: float32 [128, 1024, 128], P('sub', 'case')
Inputs may be any that keep to these rules, and one draw needn't show every extreme that they name: `block_cols`: entry k of a substructure's row lies in [(k // 32) * 16, (k // 32 + 1) * 16); blocks may repeat. `interface_maps`: each row of 1024 entries is a permutation; at level index l, slots that agree in all but their lowest l + 1 bits hold equal entries. `merge_maps`: at level index l, slots that agree in all but their lowest l + 1 bits hold equal entries.
All inputs are finite; a program needn't handle non-finite values.
Results may differ from a plain program's by a relative error of at most 0.0003.
Values sent between devices are 32-bit elements; how exact they have to be, the bound alone decides.
No kernel may reach another device: no remote copies, remote signals or barrier semaphores. Data moves between devices by JAX's collectives and lax.ppermute only.
A program may use at most 64 MiB of HBM per device.

v0:
```python
import jax
import jax.numpy as jnp
from jax import lax
from jax.sharding import PartitionSpec as P

BLK = 64


def from_partner(value, axis, distance):
    mask = 2**distance
    pairs = [(source, source ^ mask) for source in range(lax.axis_size(axis))]
    return lax.ppermute(value, axis, pairs)


def on_device(
    load_interior, load_boundary, cond_blocks, block_rows, block_cols, interface_maps, merge_maps
):
    interior, boundary = (
        lax.all_to_all(load_interior, "sub", split_axis=1, concat_axis=0, tiled=True),
        lax.all_to_all(load_boundary, "sub", split_axis=1, concat_axis=0, tiled=True),
    )
    interior = jnp.transpose(interior[:, 0, :])
    boundary = jnp.transpose(boundary[:, 0, :])
    local_rows = interior.shape[0]
    num_cases = interior.shape[1]
    block_count = cond_blocks.shape[1]
    block_size = BLK
    blocks = cond_blocks[0].reshape(block_count, block_size, block_size)
    quarter = boundary.shape[0]
    groups = lax.axis_size("case")
    full_rows = quarter * groups
    position = lax.axis_index("case")
    local_cols = block_cols[0] - position * (local_rows // block_size)
    pieces = jnp.take(
        interior.reshape(local_rows // block_size, block_size, num_cases), local_cols, axis=0
    )
    products = jnp.einsum("krc,kcn->krn", blocks, pieces, precision=lax.Precision.HIGHEST)
    row_blocks = full_rows // block_size
    onehot = (block_rows[0][None, :] == jnp.arange(row_blocks, dtype=jnp.int32)[:, None]).astype(
        jnp.float32
    )
    partial_value = jnp.dot(
        onehot,
        products.reshape(block_count, block_size * num_cases),
        precision=lax.Precision.HIGHEST,
    )
    partial_value = partial_value.reshape(full_rows, num_cases)
    embedded = lax.dynamic_update_slice(
        jnp.zeros((full_rows, num_cases), jnp.float32), boundary, (position * quarter, 0)
    )
    contribution = embedded - partial_value
    current = lax.psum(contribution, "case")
    leaf_share = lax.dynamic_slice_in_dim(current, position * quarter, quarter, 0)
    slot = lax.axis_index("sub")
    levels = lax.axis_size("sub").bit_length() - 1
    nodes = jnp.zeros((quarter, num_cases), jnp.float32)
    for level in range(1, levels + 1):
        half = 1 << level - 1
        maps = interface_maps[0, level - 1]
        matrix = merge_maps[0, level - 1]
        shared_rows = matrix.shape[1]
        kept_index = jnp.concatenate([maps[0, shared_rows:], maps[1, shared_rows:] + full_rows])
        mine = lax.dynamic_slice_in_dim(kept_index, position * quarter, quarter)
        other = from_partner(current, "sub", level - 1)
        own_full, other_full = (current, other)
        upper = slot // half % 2 == 1
        left_full = jnp.where(upper, other_full, own_full)
        right_full = jnp.where(upper, own_full, other_full)
        stacked = jnp.concatenate([left_full, right_full], axis=0)
        shared = jnp.take(stacked, maps[0, :shared_rows], axis=0) + jnp.take(
            stacked, maps[1, :shared_rows] + full_rows, axis=0
        )
        parent = jnp.take(stacked, mine, axis=0) - jnp.dot(
            matrix, shared, precision=lax.Precision.HIGHEST
        )
        is_node = slot % (2 * half) == half
        if level == levels:
            is_node = jnp.logical_or(is_node, slot == 0)
        nodes = jnp.where(is_node, parent, nodes)
        if level < levels:
            current = lax.all_gather(parent, "case", axis=0, tiled=True)
    return (leaf_share[None], nodes[None])


def solution(mesh):
    placed = (
        P("sub", None, "case"),
        P("sub", None, "case"),
        P("sub", "case", None),
        P("sub", "case"),
        P("sub", "case"),
        P("sub", None, None, None),
        P("sub", None, "case", None),
    )
    return jax.shard_map(
        on_device,
        mesh=mesh,
        in_specs=placed,
        out_specs=(P("sub", "case", None), P("sub", "case", None)),
        check_vma=False,
    )
```

profile of v0, /device:TPU:1, one launch (start us, length us, event | category | flops | bytes accessed | tf_op | source)
XLA Modules:
  0.0 416.5 jit_solution(13161478264808261519)
XLA Ops:
  8.9 20.6 %all-to-all-start = ((f32[1,128,256]{2,0,1:T(1,128)}), f32[1,128,256]{2,0,1:T(1,128)S(1)}, u32[]{:S(2)}, u32[]{:S(2)}) async-start(f32[1,128,256]{2,0,1:T(1,128)} %copy.64), calls=%async_computation | async-start | bytes 262144 | tf_op jit(solution)/shard_map/all_to_all | solution.py:20
  29.5 2.4 copy.66
  33.8 13.1 %all-to-all-done = f32[1,128,256]{2,0,1:T(1,128)S(1)} async-done(((f32[1,128,256]{2,0,1:T(1,128)}), f32[1,128,256]{2,0,1:T(1,128)S(1)}, u32[]{:S(2)}, u32[]{:S(2)}) %all-to-all-start) | async-done | bytes 131104 | tf_op jit(solution)/shard_map/all_to_all | solution.py:20
  46.8 6.9 %all-to-all-start.1 = ((f32[1,128,1024]{2,0,1:T(1,128)}), f32[1,128,1024]{2,0,1:T(1,128)S(1)}, u32[]{:S(2)}, u32[]{:S(2)}) async-start(f32[1,128,1024]{2,0,1:T(1,128)} %copy.66), calls=%async_computation.1 | async-start | bytes 1048576 | tf_op jit(solution)/shard_map/all_to_all | solution.py:19
  56.0 31.1 %all-to-all-done.1 = f32[1,128,1024]{2,0,1:T(1,128)S(1)} async-done(((f32[1,128,1024]{2,0,1:T(1,128)}), f32[1,128,1024]{2,0,1:T(1,128)S(1)}, u32[]{:S(2)}, u32[]{:S(2)}) %all-to-all-start.1) | async-done | bytes 524320 | tf_op jit(solution)/shard_map/all_to_all | solution.py:19
  91.4 48.2 %all-reduce.2.cloned.1.call-done = f32[1024,128]{1,0:T(8,128)} async-done(((f32[1024,128]{1,0:T(8,128)}), f32[1024,128]{1,0:T(8,128)}) %all-reduce.2.cloned.1.call-update) | async-done | bytes 524304 | tf_op jit(solution)/shard_map/psum | solution.py:52
  139.6 4.7 %collective-permute-start = (f32[1024,128]{1,0:T(8,128)}, f32[1024,128]{1,0:T(8,128)S(1)}, u32[]{:S(2)}, u32[]{:S(2)}) collective-permute-start(f32[1024,128]{1,0:T(8,128)} %all-reduce.2.cloned.1.call-done), channel_id=1, source_target_pairs={{0,4},{4,0},{8,12},{12,8},{16,20},{20,16},{24,28},{28,24},{32,36},... | collective-permute-start | bytes 1572872 | tf_op jit(solution)/shard_map/ppermute | solution.py:12
  150.2 1.9 fusion.8
  152.1 9.9 %all_gather.18 = f32[1024,128]{0,1:T(8,128)S(1)} all-gather(f32[256,128]{0,1:T(8,128)S(1)} %fusion.8), channel_id=1, replica_groups=mesh['sub'=128,'case'=4] {'case'}, dimensions={0}, use_global_device_ids=true | all-gather | bytes 655360 | tf_op jit(solution)/shard_map/all_gather | solution.py:81
  162.0 3.4 collective-permute-start.1
  165.5 8.5 %collective-permute-done.1 = f32[1024,128]{0,1:T(8,128)S(1)} collective-permute-done((f32[1024,128]{0,1:T(8,128)S(1)}, f32[1024,128]{0,1:T(8,128)S(1)}, u32[]{:S(2)}, u32[]{:S(2)}) %collective-permute-start.1) | collective-permute-done | bytes 524320 | tf_op jit(solution)/shard_map/ppermute | solution.py:12
  177.4 1.9 fusion.7
  179.3 10.3 %all_gather.19 = f32[1024,128]{0,1:T(8,128)S(1)} all-gather(f32[256,128]{0,1:T(8,128)S(1)} %fusion.7), channel_id=1, replica_groups=mesh['sub'=128,'case'=4] {'case'}, dimensions={0}, use_global_device_ids=true | all-gather | bytes 655360 | tf_op jit(solution)/shard_map/all_gather | solution.py:81
  189.7 4.2 %collective-permute-start.2 = (f32[1024,128]{0,1:T(8,128)S(1)}, f32[1024,128]{0,1:T(8,128)S(1)}, u32[]{:S(2)}, u32[]{:S(2)}) collective-permute-start(f32[1024,128]{0,1:T(8,128)S(1)} %all_gather.19), channel_id=1, source_target_pairs={{0,16},{4,20},{8,24},{12,28},{16,0},{20,4},{24,8},{28,12},{32,48},... | collective-permute-start | bytes 1572872 | tf_op jit(solution)/shard_map/ppermute | solution.py:12
  193.9 21.7 %collective-permute-done.2 = f32[1024,128]{0,1:T(8,128)S(1)} collective-permute-done((f32[1024,128]{0,1:T(8,128)S(1)}, f32[1024,128]{0,1:T(8,128)S(1)}, u32[]{:S(2)}, u32[]{:S(2)}) %collective-permute-start.2) | collective-permute-done | bytes 524320 | tf_op jit(solution)/shard_map/ppermute | solution.py:12
  219.1 1.9 fusion.6
  221.0 10.4 %all_gather.20 = f32[1024,128]{0,1:T(8,128)S(1)} all-gather(f32[256,128]{0,1:T(8,128)S(1)} %fusion.6), channel_id=1, replica_groups=mesh['sub'=128,'case'=4] {'case'}, dimensions={0}, use_global_device_ids=true | all-gather | bytes 655360 | tf_op jit(solution)/shard_map/all_gather | solution.py:81
  231.4 7.4 %collective-permute-start.3 = (f32[1024,128]{0,1:T(8,128)S(1)}, f32[1024,128]{0,1:T(8,128)S(1)}, u32[]{:S(2)}, u32[]{:S(2)}) collective-permute-start(f32[1024,128]{0,1:T(8,128)S(1)} %all_gather.20), channel_id=1, source_target_pairs={{0,32},{4,36},{8,40},{12,44},{16,48},{20,52},{24,56},{28,60},{32,0... | collective-permute-start | bytes 1572872 | tf_op jit(solution)/shard_map/ppermute | solution.py:12
  238.9 45.0 %collective-permute-done.3 = f32[1024,128]{0,1:T(8,128)S(1)} collective-permute-done((f32[1024,128]{0,1:T(8,128)S(1)}, f32[1024,128]{0,1:T(8,128)S(1)}, u32[]{:S(2)}, u32[]{:S(2)}) %collective-permute-start.3) | collective-permute-done | bytes 524320 | tf_op jit(solution)/shard_map/ppermute | solution.py:12
  287.3 1.9 fusion.5
  289.2 11.2 %all_gather.21 = f32[1024,128]{0,1:T(8,128)S(1)} all-gather(f32[256,128]{0,1:T(8,128)S(1)} %fusion.5), channel_id=1, replica_groups=mesh['sub'=128,'case'=4] {'case'}, dimensions={0}, use_global_device_ids=true | all-gather | bytes 655360 | tf_op jit(solution)/shard_map/all_gather | solution.py:81
  300.4 10.5 %collective-permute-start.4 = (f32[1024,128]{0,1:T(8,128)S(1)}, f32[1024,128]{0,1:T(8,128)S(1)}, u32[]{:S(2)}, u32[]{:S(2)}) collective-permute-start(f32[1024,128]{0,1:T(8,128)S(1)} %all_gather.21), channel_id=1, source_target_pairs={{0,64},{4,68},{8,72},{12,76},{16,80},{20,84},{24,88},{28,92},{32,9... | collective-permute-start | bytes 1572872 | tf_op jit(solution)/shard_map/ppermute | solution.py:12
  311.0 38.4 %collective-permute-done.4 = f32[1024,128]{0,1:T(8,128)S(1)} collective-permute-done((f32[1024,128]{0,1:T(8,128)S(1)}, f32[1024,128]{0,1:T(8,128)S(1)}, u32[]{:S(2)}, u32[]{:S(2)}) %collective-permute-start.4) | collective-permute-done | bytes 524320 | tf_op jit(solution)/shard_map/ppermute | solution.py:12
  352.8 1.9 fusion.4
  354.7 9.9 %all_gather.22 = f32[1024,128]{0,1:T(8,128)S(1)} all-gather(f32[256,128]{0,1:T(8,128)S(1)} %fusion.4), channel_id=1, replica_groups=mesh['sub'=128,'case'=4] {'case'}, dimensions={0}, use_global_device_ids=true | all-gather | bytes 655360 | tf_op jit(solution)/shard_map/all_gather | solution.py:81
  364.6 3.1 collective-permute-start.5
  367.8 8.4 %collective-permute-done.5 = f32[1024,128]{0,1:T(8,128)S(1)} collective-permute-done((f32[1024,128]{0,1:T(8,128)S(1)}, f32[1024,128]{0,1:T(8,128)S(1)}, u32[]{:S(2)}, u32[]{:S(2)}) %collective-permute-start.5) | collective-permute-done | bytes 524320 | tf_op jit(solution)/shard_map/ppermute | solution.py:12
  379.6 1.9 fusion.3
  381.5 10.7 %all_gather.23 = f32[1024,128]{0,1:T(8,128)S(1)} all-gather(f32[256,128]{0,1:T(8,128)S(1)} %fusion.3), channel_id=1, replica_groups=mesh['sub'=128,'case'=4] {'case'}, dimensions={0}, use_global_device_ids=true | all-gather | bytes 655360 | tf_op jit(solution)/shard_map/all_gather | solution.py:81
  392.1 4.8 %collective-permute-start.6 = (f32[1024,128]{0,1:T(8,128)S(1)}, f32[1024,128]{0,1:T(8,128)S(1)}, u32[]{:S(2)}, u32[]{:S(2)}) collective-permute-start(f32[1024,128]{0,1:T(8,128)S(1)} %all_gather.23), channel_id=1, source_target_pairs={{0,256},{4,260},{8,264},{12,268},{16,272},{20,276},{24,280},{28,28... | collective-permute-start | bytes 1572872 | tf_op jit(solution)/shard_map/ppermute | solution.py:12
  398.6 4.9 %collective-permute-done.6 = f32[1024,128]{0,1:T(8,128)S(1)} collective-permute-done((f32[1024,128]{0,1:T(8,128)S(1)}, f32[1024,128]{0,1:T(8,128)S(1)}, u32[]{:S(2)}, u32[]{:S(2)}) %collective-permute-start.6) | collective-permute-done | bytes 524320 | tf_op jit(solution)/shard_map/ppermute | solution.py:12
  407.0 1.9 fusion.2
  (132 shorter events, 38.2 us)
Async XLA Ops:
  7.2 48.6 %copy-start.1 = (s32[1,32]{1,0:T(1,128)S(1)}, s32[1,32]{1,0:T(1,128)}, u32[]{:S(2)}) copy-start(s32[1,32]{1,0:T(1,128)} %param.15) | copy-start | bytes 388
  8.9 38.0 %all-to-all-start = ((f32[1,128,256]{2,0,1:T(1,128)}), f32[1,128,256]{2,0,1:T(1,128)S(1)}, u32[]{:S(2)}, u32[]{:S(2)}) async-start(f32[1,128,256]{2,0,1:T(1,128)} %copy.64), calls=%async_computation | async-start | bytes 262144 | tf_op jit(solution)/shard_map/all_to_all | solution.py:20
  46.8 40.2 %all-to-all-start.1 = ((f32[1,128,1024]{2,0,1:T(1,128)}), f32[1,128,1024]{2,0,1:T(1,128)S(1)}, u32[]{:S(2)}, u32[]{:S(2)}) async-start(f32[1,128,1024]{2,0,1:T(1,128)} %copy.66), calls=%async_computation.1 | async-start | bytes 1048576 | tf_op jit(solution)/shard_map/all_to_all | solution.py:19
  53.8 85.9 %all-reduce.2.cloned.1.call-start = ((), (), s32[]{:S(2)}) async-start(), calls=%async_computation.2 | async-start | bytes 1048576 | tf_op jit(solution)/shard_map/psum | solution.py:52
  55.8 33.5 %copy-start = (s32[1,32]{1,0:T(1,128)S(1)}, s32[1,32]{1,0:T(1,128)}, u32[]{:S(2)}) copy-start(s32[1,32]{1,0:T(1,128)} %param.14) | copy-start | bytes 388
  139.6 6.4 %collective-permute-start = (f32[1024,128]{1,0:T(8,128)}, f32[1024,128]{1,0:T(8,128)S(1)}, u32[]{:S(2)}, u32[]{:S(2)}) collective-permute-start(f32[1024,128]{1,0:T(8,128)} %all-reduce.2.cloned.1.call-done), channel_id=1, source_target_pairs={{0,4},{4,0},{8,12},{12,8},{16,20},{20,16},{24,28},{28,24},{32,36},... | collective-permute-start | bytes 1572872 | tf_op jit(solution)/shard_map/ppermute | solution.py:12
  162.0 12.0 %collective-permute-start.1 = (f32[1024,128]{0,1:T(8,128)S(1)}, f32[1024,128]{0,1:T(8,128)S(1)}, u32[]{:S(2)}, u32[]{:S(2)}) collective-permute-start(f32[1024,128]{0,1:T(8,128)S(1)} %all_gather.18), channel_id=1, source_target_pairs={{0,8},{4,12},{8,0},{12,4},{16,24},{20,28},{24,16},{28,20},{32,40},... | collective-permute-start | bytes 1572872 | tf_op jit(solution)/shard_map/ppermute | solution.py:12
  189.7 26.0 %collective-permute-start.2 = (f32[1024,128]{0,1:T(8,128)S(1)}, f32[1024,128]{0,1:T(8,128)S(1)}, u32[]{:S(2)}, u32[]{:S(2)}) collective-permute-start(f32[1024,128]{0,1:T(8,128)S(1)} %all_gather.19), channel_id=1, source_target_pairs={{0,16},{4,20},{8,24},{12,28},{16,0},{20,4},{24,8},{28,12},{32,48},... | collective-permute-start | bytes 1572872 | tf_op jit(solution)/shard_map/ppermute | solution.py:12
  231.4 52.5 %collective-permute-start.3 = (f32[1024,128]{0,1:T(8,128)S(1)}, f32[1024,128]{0,1:T(8,128)S(1)}, u32[]{:S(2)}, u32[]{:S(2)}) collective-permute-start(f32[1024,128]{0,1:T(8,128)S(1)} %all_gather.20), channel_id=1, source_target_pairs={{0,32},{4,36},{8,40},{12,44},{16,48},{20,52},{24,56},{28,60},{32,0... | collective-permute-start | bytes 1572872 | tf_op jit(solution)/shard_map/ppermute | solution.py:12
  300.4 49.0 %collective-permute-start.4 = (f32[1024,128]{0,1:T(8,128)S(1)}, f32[1024,128]{0,1:T(8,128)S(1)}, u32[]{:S(2)}, u32[]{:S(2)}) collective-permute-start(f32[1024,128]{0,1:T(8,128)S(1)} %all_gather.21), channel_id=1, source_target_pairs={{0,64},{4,68},{8,72},{12,76},{16,80},{20,84},{24,88},{28,92},{32,9... | collective-permute-start | bytes 1572872 | tf_op jit(solution)/shard_map/ppermute | solution.py:12
  364.6 11.5 %collective-permute-start.5 = (f32[1024,128]{0,1:T(8,128)S(1)}, f32[1024,128]{0,1:T(8,128)S(1)}, u32[]{:S(2)}, u32[]{:S(2)}) collective-permute-start(f32[1024,128]{0,1:T(8,128)S(1)} %all_gather.22), channel_id=1, source_target_pairs={{0,128},{4,132},{8,136},{12,140},{16,144},{20,148},{24,152},{28,15... | collective-permute-start | bytes 1572872 | tf_op jit(solution)/shard_map/ppermute | solution.py:12
  392.1 11.4 %collective-permute-start.6 = (f32[1024,128]{0,1:T(8,128)S(1)}, f32[1024,128]{0,1:T(8,128)S(1)}, u32[]{:S(2)}, u32[]{:S(2)}) collective-permute-start(f32[1024,128]{0,1:T(8,128)S(1)} %all_gather.23), channel_id=1, source_target_pairs={{0,256},{4,260},{8,264},{12,268},{16,272},{20,276},{24,280},{28,28... | collective-permute-start | bytes 1572872 | tf_op jit(solution)/shard_map/ppermute | solution.py:12
Sparse Core Ops, SparseCore 0:
  91.5 48.1 all-reduce.1
where the time goes:
time: 424 us; the launch traced here: 416 us
  waiting for transfers between devices  221 us (52%)
  starting transfers between devices  65.8 us (16%)
  blocking collectives  62.4 us (15%)
  local copies, waits for them, and re-layouts  32.1 us (8%)
  matrix products  15.4 us (4%)
  between operations  15.3 us (4%)
  other arithmetic  4.42 us (1%)
    ppermute x7, waiting for transfers between devices, from_partner(): return lax.ppermute(value, axis, pairs)  129 us
    all_gather x6, blocking collectives, on_device(): current = lax.all_gather(parent, 'case', axis=0, tiled=True)  62.4 us
    psum x1, waiting for transfers between devices, on_device(): current = lax.psum(contribution, 'case')  48.2 us
    ppermute x7, starting transfers between devices, from_partner(): return lax.ppermute(value, axis, pairs)  38.2 us
    all_to_all x1, waiting for transfers between devices, on_device(): lax.all_to_all(load_interior, 'sub', split_axis=1, concat_axis=0, tiled=T...  31.1 us
    all_to_all x1, starting transfers between devices, on_device(): lax.all_to_all(load_boundary, 'sub', split_axis=1, concat_axis=0, tiled=T...  20.6 us
    dot_general x7, matrix products, on_device(): jnp.dot(matrix, shared, precision=lax.Precision.HIGHEST)  13.2 us
    all_to_all x1, waiting for transfers between devices, on_device(): lax.all_to_all(load_boundary, 'sub', split_axis=1, concat_axis=0, tiled=T...  13.1 us
  transfers between devices with their start and end apart: 10, of which 10 were waited for; matrix products, arithmetic and copies ran while one was open for 2% of the time, Pallas kernels for 0%

commit v1 on v0

v1 whole, which is shorter than its diff:
```python
import jax
import jax.numpy as jnp
from jax import lax
from jax.sharding import PartitionSpec as P

BLK = 64


def from_partner(value, axis, distance):
    mask = 2**distance
    pairs = [(source, source ^ mask) for source in range(lax.axis_size(axis))]
    return lax.ppermute(value, axis, pairs)


def shifted(value, axis, shift):
    size = lax.axis_size(axis)
    pairs = [(source, (source + shift) % size) for source in range(size)]
    return lax.ppermute(value, axis, pairs)


def case_allreduce(value, position):
    groups = lax.axis_size("case")
    quarter = value.shape[0] // groups
    chunks = value.reshape(groups, quarter, value.shape[1])
    mine = chunks[position]
    for shift in range(1, groups):
        outgoing = chunks[(position + shift) % groups]
        mine = mine + shifted(outgoing, "case", shift)
    pieces = [mine] + [shifted(mine, "case", shift) for shift in range(1, groups)]
    stacked = jnp.stack(pieces)
    order = (position - jnp.arange(groups)) % groups
    full = jnp.take(stacked, order, axis=0).reshape(value.shape)
    return mine, full


def on_device(
    load_interior, load_boundary, cond_blocks, block_rows, block_cols, interface_maps, merge_maps
):
    local_rows = load_interior.shape[2]
    quarter = load_boundary.shape[2]
    joined = jnp.concatenate([load_interior, load_boundary], axis=2)
    joined = lax.all_to_all(joined, "sub", split_axis=1, concat_axis=0, tiled=True)
    interior = jnp.transpose(joined[:, 0, :local_rows])
    boundary = jnp.transpose(joined[:, 0, local_rows:])
    num_cases = interior.shape[1]
    block_count = cond_blocks.shape[1]
    block_size = BLK
    blocks = cond_blocks[0].reshape(block_count, block_size, block_size)
    groups = lax.axis_size("case")
    full_rows = quarter * groups
    position = lax.axis_index("case")
    local_cols = block_cols[0] - position * (local_rows // block_size)
    pieces = jnp.take(
        interior.reshape(local_rows // block_size, block_size, num_cases), local_cols, axis=0
    )
    products = jnp.einsum("krc,kcn->krn", blocks, pieces, precision=lax.Precision.HIGHEST)
    row_blocks = full_rows // block_size
    onehot = (block_rows[0][None, :] == jnp.arange(row_blocks, dtype=jnp.int32)[:, None]).astype(
        jnp.float32
    )
    partial_value = jnp.dot(
        onehot,
        products.reshape(block_count, block_size * num_cases),
        precision=lax.Precision.HIGHEST,
    )
    partial_value = partial_value.reshape(full_rows, num_cases)
    embedded = lax.dynamic_update_slice(
        jnp.zeros((full_rows, num_cases), jnp.float32), boundary, (position * quarter, 0)
    )
    contribution = embedded - partial_value
    leaf_share, current = case_allreduce(contribution, position)
    slot = lax.axis_index("sub")
    levels = lax.axis_size("sub").bit_length() - 1
    nodes = jnp.zeros((quarter, num_cases), jnp.float32)
    for level in range(1, levels + 1):
        half = 1 << level - 1
        maps = interface_maps[0, level - 1]
        last = level == levels
        if last:
            matrix = merge_maps[0, level - 1]
        else:
            matrix = lax.all_gather(merge_maps[0, level - 1], "case", axis=0, tiled=True)
        shared_rows = matrix.shape[1]
        other = from_partner(current, "sub", level - 1)
        upper = slot // half % 2 == 1
        left_base = jnp.where(upper, full_rows, 0)
        right_base = full_rows - left_base
        stacked = jnp.concatenate([current, other], axis=0)
        shared = jnp.take(stacked, maps[0, :shared_rows] + left_base, axis=0) + jnp.take(
            stacked, maps[1, :shared_rows] + right_base, axis=0
        )
        kept_index = jnp.concatenate(
            [maps[0, shared_rows:] + left_base, maps[1, shared_rows:] + right_base]
        )
        if last:
            kept_index = lax.dynamic_slice_in_dim(kept_index, position * quarter, quarter)
        parent = jnp.take(stacked, kept_index, axis=0) - jnp.dot(
            matrix, shared, precision=lax.Precision.HIGHEST
        )
        is_node = slot % (2 * half) == half
        if last:
            is_node = jnp.logical_or(is_node, slot == 0)
            own = parent
        else:
            own = lax.dynamic_slice_in_dim(parent, position * quarter, quarter, 0)
        nodes = jnp.where(is_node, own, nodes)
        current = parent
    return (leaf_share[None], nodes[None])


def solution(mesh):
    placed = (
        P("sub", None, "case"),
        P("sub", None, "case"),
        P("sub", "case", None),
        P("sub", "case"),
        P("sub", "case"),
        P("sub", None, None, None),
        P("sub", None, "case", None),
    )
    return jax.shard_map(
        on_device,
        mesh=mesh,
        in_specs=placed,
        out_specs=(P("sub", "case", None), P("sub", "case", None)),
        check_vma=False,
    )
```

time: 424 us -> 362 us (0.85); the launches traced: 416 us -> 359 us
  blocking collectives: 62.4 us -> 0 us
  waiting for transfers between devices: 221 us -> 202 us
  matrix products: 15.4 us -> 29.2 us
  local copies, waits for them, and re-layouts: 32.1 us -> 42.8 us
    all_gather x6 -> x0, blocking collectives: 62.4 us -> none  [on_device(): current = lax.all_gather(parent, 'case', axis=0, tiled=True)]
    psum x1 -> x0, waiting for transfers between devices: 48.2 us -> none  [on_device(): current = lax.psum(contribution, 'case')]
    ppermute x7, waiting for transfers between devices: 129 us -> 152 us  [from_partner(): return lax.ppermute(value, axis, pairs)]
    ppermute x0 -> x6, starting transfers between devices: none -> 21.1 us  [shifted(): return lax.ppermute(value, axis, pairs)]
    ppermute x7, starting transfers between devices: 38.2 us -> 23.7 us  [from_partner(): return lax.ppermute(value, axis, pairs)]
    dot_general x7, matrix products: 13.2 us -> 26.9 us  [on_device(): jnp.dot(matrix, shared, precision=lax.Precision.HIGHEST)]
    gather x28 -> x29, local copies, waits for them, and re-layouts: 20.3 us -> 34 us  [the longest x14 18.9 us: on_device(): jnp.take(stacked, kept_index, axis=0)]
    ppermute x0 -> x6, waiting for transfers between devices: none -> 11.5 us  [shifted(): return lax.ppermute(value, axis, pairs)]
  transfers between devices with their start and end apart: 10 -> 20, of which waited for: 10 -> 12; matrix products, arithmetic and copies ran while one was open for 2% -> 17% of each run, Pallas kernels for 0% -> 0%
where the time goes in v1:
time: 362 us; the launch traced here: 359 us
  waiting for transfers between devices  202 us (56%)
  starting transfers between devices  65.6 us (18%)
  local copies, waits for them, and re-layouts  42.8 us (12%)
  matrix products  29.2 us (8%)
  between operations  15.6 us (4%)
  other arithmetic  3.9 us (1%)
    ppermute x7, waiting for transfers between devices, from_partner(): return lax.ppermute(value, axis, pairs)  152 us
    all_to_all x1, waiting for transfers between devices, on_device(): lax.all_to_all(joined, 'sub', split_axis=1, concat_axis=0, tiled=True)  35.6 us
    dot_general x7, matrix products, on_device(): jnp.dot(matrix, shared, precision=lax.Precision.HIGHEST)  26.9 us
    ppermute x7, starting transfers between devices, from_partner(): return lax.ppermute(value, axis, pairs)  23.7 us
    ppermute x6, starting transfers between devices, shifted(): return lax.ppermute(value, axis, pairs)  21.1 us
    all_to_all x1, starting transfers between devices, on_device(): lax.all_to_all(joined, 'sub', split_axis=1, concat_axis=0, tiled=True)  20.6 us
    gather x14, local copies, waits for them, and re-layouts, on_device(): jnp.take(stacked, kept_index, axis=0)  18.9 us
    ppermute x6, waiting for transfers between devices, shifted(): return lax.ppermute(value, axis, pairs)  11.5 us
  transfers between devices with their start and end apart: 20, of which 12 were waited for; matrix products, arithmetic and copies ran while one was open for 17% of the time, Pallas kernels for 0%

profile of v1, /device:TPU:1, one launch (start us, length us, event | category | flops | bytes accessed | tf_op | source)
XLA Modules:
  0.0 359.4 jit_solution(10980745271162367843)
XLA Ops:
  7.2 3.5 fusion.109
  15.6 20.6 %all-to-all-start = ((f32[1,128,1280]{2,0,1:T(1,128)}), f32[1,128,1280]{2,0,1:T(1,128)S(1)}, u32[]{:S(2)}, u32[]{:S(2)}) async-start(f32[1,128,1280]{2,0,1:T(1,128)} %pad_maximum_fusion.7), calls=%async_computation | async-start | bytes 1310720 | tf_op jit(solution)/shard_map/all_to_all | solution.py:42
  38.9 35.6 %all-to-all-done = f32[1,128,1280]{2,0,1:T(1,128)S(1)} async-done(((f32[1,128,1280]{2,0,1:T(1,128)}), f32[1,128,1280]{2,0,1:T(1,128)S(1)}, u32[]{:S(2)}, u32[]{:S(2)}) %all-to-all-start) | async-done | bytes 655392 | tf_op jit(solution)/shard_map/all_to_all | solution.py:42
  78.3 3.1 collective-permute-start
  81.4 4.4 %collective-permute-start.1 = (f32[256,128]{1,0:T(8,128)S(1)}, f32[256,128]{1,0:T(8,128)S(1)}, u32[]{:S(2)}, u32[]{:S(2)}) collective-permute-start(f32[256,128]{1,0:T(8,128)S(1)} %get-tuple-element.20), channel_id=1, source_target_pairs={{0,2},{1,3},{2,0},{3,1},{4,6},{5,7},{6,4},{7,5},{8,10},{9,11},{10,... | collective-permute-start | bytes 393224 | tf_op jit(solution)/shard_map/ppermute | solution.py:18
  85.8 3.1 collective-permute-start.2
  89.1 6.5 %collective-permute-done.1 = f32[256,128]{1,0:T(8,128)S(1)} collective-permute-done((f32[256,128]{1,0:T(8,128)S(1)}, f32[256,128]{1,0:T(8,128)S(1)}, u32[]{:S(2)}, u32[]{:S(2)}) %collective-permute-start.1) | collective-permute-done | bytes 131104 | tf_op jit(solution)/shard_map/ppermute | solution.py:18
  99.5 4.7 %collective-permute-start.4 = (f32[256,128]{1,0:T(8,128)S(1)}, f32[256,128]{1,0:T(8,128)S(1)}, u32[]{:S(2)}, u32[]{:S(2)}) collective-permute-start(f32[256,128]{1,0:T(8,128)S(1)} %fusion.68), channel_id=1, source_target_pairs={{0,2},{1,3},{2,0},{3,1},{4,6},{5,7},{6,4},{7,5},{8,10},{9,11},{10,... | collective-permute-start | bytes 393224 | tf_op jit(solution)/shard_map/ppermute | solution.py:18
  104.2 3.5 collective-permute-start.5
  108.1 3.2 collective-permute-done.5
  112.0 4.3 %collective-permute-start.6 = (f32[1024,128]{1,0:T(8,128)S(1)}, f32[1024,128]{1,0:T(8,128)S(1)}, u32[]{:S(2)}, u32[]{:S(2)}) collective-permute-start(f32[1024,128]{1,0:T(8,128)S(1)} %bitcast_select_fusion), channel_id=1, source_target_pairs={{0,4},{4,0},{8,12},{12,8},{16,20},{20,16},{24,28},{28,24},{32,36},... | collective-permute-start | bytes 1572872 | tf_op jit(solution)/shard_map/ppermute | solution.py:12
  117.9 2.8 gather_fusion.3
  123.1 4.2 %select_subtract_fusion = f32[1024,128]{0,1:T(8,128)S(1)} fusion(f32[1024,128]{0,1:T(8,128)S(1)} %copy.67, f32[1,1,1024,512]{3,2,1,0:T(8,128)} %all-gather.13.cloned.1.call-done, f32[512,128]{1,0:T(8,128)S(1)} %gather_fusion.5, f32[512,128]{1,0:T(8,128)S(1)} %gather_fusion.4, pred[1024]{0:T(1024)(128)(4,1)S(1)} %get-tuple-element.75, ...), kind=kOutput, calls=%fused_computation.66 | convolution fusion | flops 805765120 | bytes 3672064 | tf_op jit(solution)/shard_map/dot_general | solution.py:97
  127.3 3.6 %collective-permute-start.7 = (f32[1024,128]{0,1:T(8,128)S(1)}, f32[1024,128]{0,1:T(8,128)S(1)}, u32[]{:S(2)}, u32[]{:S(2)}) collective-permute-start(f32[1024,128]{0,1:T(8,128)S(1)} %select_subtract_fusion), channel_id=1, source_target_pairs={{0,8},{4,12},{8,0},{12,4},{16,24},{20,28},{24,16},{28,20},{32,40},... | collective-permute-start | bytes 1572872 | tf_op jit(solution)/shard_map/ppermute | solution.py:12
  131.0 11.8 %collective-permute-done.7 = f32[1024,128]{0,1:T(8,128)S(1)} collective-permute-done((f32[1024,128]{0,1:T(8,128)S(1)}, f32[1024,128]{0,1:T(8,128)S(1)}, u32[]{:S(2)}, u32[]{:S(2)}) %collective-permute-start.7) | collective-permute-done | bytes 524320 | tf_op jit(solution)/shard_map/ppermute | solution.py:12
  145.2 2.8 gather_fusion.6
  148.3 4.1 %fusion.42 = f32[1024,128]{0,1:T(8,128)S(1)} fusion(f32[1,1,1024,512]{3,2,1,0:T(8,128)} %all-gather.15.cloned.1.call-done, f32[1024,128]{0,1:T(8,128)S(1)} %copy.69, f32[512,128]{1,0:T(8,128)S(1)} %gather_fusion.8, f32[512,128]{1,0:T(8,128)S(1)} %gather_fusion.7, pred[1024]{0:T(1024)(128)(4,1)S(1)} %get-tuple-element.74, ...), kind=kOutput, calls=%fused_computation.45 | convolution fusion | flops 805765120 | bytes 3672064 | tf_op jit(solution)/shard_map/dot_general | solution.py:97
  154.6 24.7 %collective-permute-done.8 = f32[1024,128]{0,1:T(8,128)S(1)} collective-permute-done((f32[1024,128]{0,1:T(8,128)S(1)}, f32[1024,128]{0,1:T(8,128)S(1)}, u32[]{:S(2)}, u32[]{:S(2)}) %collective-permute-start.8) | collective-permute-done | bytes 524320 | tf_op jit(solution)/shard_map/ppermute | solution.py:12
  184.9 4.1 %fusion.39 = f32[1024,128]{0,1:T(8,128)S(1)} fusion(f32[1,1,1024,512]{3,2,1,0:T(8,128)} %all-gather.17.cloned.1.call-done, f32[1024,128]{0,1:T(8,128)S(1)} %copy.73, f32[512,128]{1,0:T(8,128)S(1)} %gather_fusion.11, f32[512,128]{1,0:T(8,128)S(1)} %gather_fusion.10, pred[1024]{0:T(1024)(128)(4,1)S(1)} %get-tuple-element.73, ...), kind=kOutput, calls=%fused_computation.44 | convolution fusion | flops 805765120 | bytes 3672064 | tf_op jit(solution)/shard_map/dot_general | solution.py:97
  189.0 2.9 collective-permute-start.9
  192.0 49.3 %collective-permute-done.9 = f32[1024,128]{0,1:T(8,128)S(1)} collective-permute-done((f32[1024,128]{0,1:T(8,128)S(1)}, f32[1024,128]{0,1:T(8,128)S(1)}, u32[]{:S(2)}, u32[]{:S(2)}) %collective-permute-start.9) | collective-permute-done | bytes 524320 | tf_op jit(solution)/shard_map/ppermute | solution.py:12
  243.8 2.8 gather_fusion.12
  246.8 4.2 %fusion.36 = f32[1024,128]{0,1:T(8,128)S(1)} fusion(f32[1,1,1024,512]{3,2,1,0:T(8,128)} %all-gather.19.cloned.1.call-done, f32[1024,128]{0,1:T(8,128)S(1)} %copy.77, f32[512,128]{1,0:T(8,128)S(1)} %gather_fusion.14, f32[512,128]{1,0:T(8,128)S(1)} %gather_fusion.13, pred[1024]{0:T(1024)(128)(4,1)S(1)} %get-tuple-element.72, ...), kind=kOutput, calls=%fused_computation.43 | convolution fusion | flops 805765120 | bytes 3672064 | tf_op jit(solution)/shard_map/dot_general | solution.py:97
  251.1 4.9 %collective-permute-start.10 = (f32[1024,128]{0,1:T(8,128)S(1)}, f32[1024,128]{0,1:T(8,128)S(1)}, u32[]{:S(2)}, u32[]{:S(2)}) collective-permute-start(f32[1024,128]{0,1:T(8,128)S(1)} %fusion.36), channel_id=1, source_target_pairs={{0,64},{4,68},{8,72},{12,76},{16,80},{20,84},{24,88},{28,92},{32,9... | collective-permute-start | bytes 1572872 | tf_op jit(solution)/shard_map/ppermute | solution.py:12
  256.0 40.4 %collective-permute-done.10 = f32[1024,128]{0,1:T(8,128)S(1)} collective-permute-done((f32[1024,128]{0,1:T(8,128)S(1)}, f32[1024,128]{0,1:T(8,128)S(1)}, u32[]{:S(2)}, u32[]{:S(2)}) %collective-permute-start.10) | collective-permute-done | bytes 524320 | tf_op jit(solution)/shard_map/ppermute | solution.py:12
  299.0 2.8 gather_fusion.15
  302.0 4.1 %fusion.33 = f32[1024,128]{0,1:T(8,128)S(1)} fusion(f32[1,1,1024,512]{3,2,1,0:T(8,128)} %all-gather.21.cloned.1.call-done, f32[1024,128]{0,1:T(8,128)S(1)} %copy.81, f32[512,128]{1,0:T(8,128)S(1)} %gather_fusion.17, f32[512,128]{1,0:T(8,128)S(1)} %gather_fusion.16, pred[1024]{0:T(1024)(128)(4,1)S(1)} %get-tuple-element.71, ...), kind=kOutput, calls=%fused_computation.42 | convolution fusion | flops 805765120 | bytes 3672064 | tf_op jit(solution)/shard_map/dot_general | solution.py:97
  306.1 3.4 collective-permute-start.11
  309.7 11.5 %collective-permute-done.11 = f32[1024,128]{0,1:T(8,128)S(1)} collective-permute-done((f32[1024,128]{0,1:T(8,128)S(1)}, f32[1024,128]{0,1:T(8,128)S(1)}, u32[]{:S(2)}, u32[]{:S(2)}) %collective-permute-start.11) | collective-permute-done | bytes 524320 | tf_op jit(solution)/shard_map/ppermute | solution.py:12
  323.7 2.8 gather_fusion.18
  326.7 4.1 %fusion.30 = f32[1024,128]{0,1:T(8,128)S(1)} fusion(f32[1,1,1024,512]{3,2,1,0:T(8,128)} %all-gather.23.cloned.1.call-done, f32[1024,128]{0,1:T(8,128)S(1)} %copy.85, f32[512,128]{1,0:T(8,128)S(1)} %gather_fusion.20, f32[512,128]{1,0:T(8,128)S(1)} %gather_fusion.19, pred[1024]{0:T(1024)(128)(4,1)S(1)} %get-tuple-element.70, ...), kind=kOutput, calls=%fused_computation.41 | convolution fusion | flops 805765120 | bytes 3672064 | tf_op jit(solution)/shard_map/dot_general | solution.py:97
  333.3 13.1 %collective-permute-done.12 = f32[1024,128]{0,1:T(8,128)S(1)} collective-permute-done((f32[1024,128]{0,1:T(8,128)S(1)}, f32[1024,128]{0,1:T(8,128)S(1)}, u32[]{:S(2)}, u32[]{:S(2)}) %collective-permute-start.12) | collective-permute-done | bytes 524320 | tf_op jit(solution)/shard_map/ppermute | solution.py:12
  (162 shorter events, 47.0 us)
Async XLA Ops:
  7.2 115.9 %all-gather.13.cloned.1.call-start = ((), (), s32[]{:S(2)}) async-start(), calls=%async_computation.1 | async-start | bytes 2621440 | tf_op jit(solution)/shard_map/all_gather | solution.py:82
  10.7 2.7 copy-start.5
  10.7 3.3 copy-start.7
  10.8 137.5 %all-gather.15.cloned.1.call-start = ((), (), s32[]{:S(2)}) async-start(), calls=%async_computation.2 | async-start | bytes 2621440 | tf_op jit(solution)/shard_map/all_gather | solution.py:82
  11.5 173.4 %all-gather.17.cloned.1.call-start = ((), (), s32[]{:S(2)}) async-start(), calls=%async_computation.3 | async-start | bytes 2621440 | tf_op jit(solution)/shard_map/all_gather | solution.py:82
  12.2 234.6 %all-gather.19.cloned.1.call-start = ((), (), s32[]{:S(2)}) async-start(), calls=%async_computation.4 | async-start | bytes 2621440 | tf_op jit(solution)/shard_map/all_gather | solution.py:82
  12.8 289.2 %all-gather.21.cloned.1.call-start = ((), (), s32[]{:S(2)}) async-start(), calls=%async_computation.5 | async-start | bytes 2621440 | tf_op jit(solution)/shard_map/all_gather | solution.py:82
  13.4 23.3 %copy-start.11 = (s32[1,32]{1,0:T(1,128)S(1)}, s32[1,32]{1,0:T(1,128)}, u32[]{:S(2)}) copy-start(s32[1,32]{1,0:T(1,128)} %param.15) | copy-start | bytes 388
  13.4 24.0 %copy-start.8 = (s32[1,7,2,1024]{3,2,1,0:T(2,128)S(1)}, s32[1,7,2,1024]{3,2,1,0:T(2,128)}, u32[]{:S(2)}) copy-start(s32[1,7,2,1024]{3,2,1,0:T(2,128)} %param.16) | copy-start | bytes 172036
  14.0 23.6 %copy-start.4 = (f32[1,32,4096]{2,1,0:T(8,128)S(1)}, f32[1,32,4096]{2,1,0:T(8,128)}, u32[]{:S(2)}) copy-start(f32[1,32,4096]{2,1,0:T(8,128)} %param.13) | copy-start | bytes 1572868
  15.6 58.9 %all-to-all-start = ((f32[1,128,1280]{2,0,1:T(1,128)}), f32[1,128,1280]{2,0,1:T(1,128)S(1)}, u32[]{:S(2)}, u32[]{:S(2)}) async-start(f32[1,128,1280]{2,0,1:T(1,128)} %pad_maximum_fusion.7), calls=%async_computation | async-start | bytes 1310720 | tf_op jit(solution)/shard_map/all_to_all | solution.py:42
  36.1 290.6 %all-gather.23.cloned.1.call-start = ((), (), s32[]{:S(2)}) async-start(), calls=%async_computation.6 | async-start | bytes 2621440 | tf_op jit(solution)/shard_map/all_gather | solution.py:82
  74.9 0.8 copy-start.10
  75.7 1.2 copy-start.9
  78.3 10.9 %collective-permute-start = (f32[256,128]{1,0:T(8,128)S(1)}, f32[256,128]{1,0:T(8,128)S(1)}, u32[]{:S(2)}, u32[]{:S(2)}) collective-permute-start(f32[256,128]{1,0:T(8,128)S(1)} %get-tuple-element.18), channel_id=1, source_target_pairs={{0,1},{1,2},{2,3},{3,0},{4,5},{5,6},{6,7},{7,4},{8,9},{9,10},{10,1... | collective-permute-start | bytes 393224 | tf_op jit(solution)/shard_map/ppermute | solution.py:18
  81.4 14.2 %collective-permute-start.1 = (f32[256,128]{1,0:T(8,128)S(1)}, f32[256,128]{1,0:T(8,128)S(1)}, u32[]{:S(2)}, u32[]{:S(2)}) collective-permute-start(f32[256,128]{1,0:T(8,128)S(1)} %get-tuple-element.20), channel_id=1, source_target_pairs={{0,2},{1,3},{2,0},{3,1},{4,6},{5,7},{6,4},{7,5},{8,10},{9,11},{10,... | collective-permute-start | bytes 393224 | tf_op jit(solution)/shard_map/ppermute | solution.py:18
  85.8 11.4 %collective-permute-start.2 = (f32[256,128]{1,0:T(8,128)S(1)}, f32[256,128]{1,0:T(8,128)S(1)}, u32[]{:S(2)}, u32[]{:S(2)}) collective-permute-start(f32[256,128]{1,0:T(8,128)S(1)} %get-tuple-element.19), channel_id=1, source_target_pairs={{0,3},{1,0},{2,1},{3,2},{4,7},{5,4},{6,5},{7,6},{8,11},{9,8},{10,9... | collective-permute-start | bytes 393224 | tf_op jit(solution)/shard_map/ppermute | solution.py:18
  97.2 20.7 %copy-start.6 = (f32[256,128]{1,0:T(8,128)}, f32[256,128]{1,0:T(8,128)S(1)}, u32[]{:S(2)}) copy-start(f32[256,128]{1,0:T(8,128)S(1)} %fusion.68) | copy-start | bytes 393220
  97.2 10.8 %collective-permute-start.3 = (f32[256,128]{1,0:T(8,128)S(1)}, f32[256,128]{1,0:T(8,128)S(1)}, u32[]{:S(2)}, u32[]{:S(2)}) collective-permute-start(f32[256,128]{1,0:T(8,128)S(1)} %fusion.68), channel_id=1, source_target_pairs={{0,1},{1,2},{2,3},{3,0},{4,5},{5,6},{6,7},{7,4},{8,9},{9,10},{10,1... | collective-permute-start | bytes 393224 | tf_op jit(solution)/shard_map/ppermute | solution.py:18
  99.5 8.5 %collective-permute-start.4 = (f32[256,128]{1,0:T(8,128)S(1)}, f32[256,128]{1,0:T(8,128)S(1)}, u32[]{:S(2)}, u32[]{:S(2)}) collective-permute-start(f32[256,128]{1,0:T(8,128)S(1)} %fusion.68), channel_id=1, source_target_pairs={{0,2},{1,3},{2,0},{3,1},{4,6},{5,7},{6,4},{7,5},{8,10},{9,11},{10,... | collective-permute-start | bytes 393224 | tf_op jit(solution)/shard_map/ppermute | solution.py:18
  104.2 7.0 %collective-permute-start.5 = (f32[256,128]{1,0:T(8,128)S(1)}, f32[256,128]{1,0:T(8,128)S(1)}, u32[]{:S(2)}, u32[]{:S(2)}) collective-permute-start(f32[256,128]{1,0:T(8,128)S(1)} %fusion.68), channel_id=1, source_target_pairs={{0,3},{1,0},{2,1},{3,2},{4,7},{5,4},{6,5},{7,6},{8,11},{9,8},{10,9... | collective-permute-start | bytes 393224 | tf_op jit(solution)/shard_map/ppermute | solution.py:18
  112.0 5.8 %collective-permute-start.6 = (f32[1024,128]{1,0:T(8,128)S(1)}, f32[1024,128]{1,0:T(8,128)S(1)}, u32[]{:S(2)}, u32[]{:S(2)}) collective-permute-start(f32[1024,128]{1,0:T(8,128)S(1)} %bitcast_select_fusion), channel_id=1, source_target_pairs={{0,4},{4,0},{8,12},{12,8},{16,20},{20,16},{24,28},{28,24},{32,36},... | collective-permute-start | bytes 1572872 | tf_op jit(solution)/shard_map/ppermute | solution.py:12
  127.3 15.4 %collective-permute-start.7 = (f32[1024,128]{0,1:T(8,128)S(1)}, f32[1024,128]{0,1:T(8,128)S(1)}, u32[]{:S(2)}, u32[]{:S(2)}) collective-permute-start(f32[1024,128]{0,1:T(8,128)S(1)} %select_subtract_fusion), channel_id=1, source_target_pairs={{0,8},{4,12},{8,0},{12,4},{16,24},{20,28},{24,16},{28,20},{32,40},... | collective-permute-start | bytes 1572872 | tf_op jit(solution)/shard_map/ppermute | solution.py:12
  152.4 27.0 %collective-permute-start.8 = (f32[1024,128]{0,1:T(8,128)S(1)}, f32[1024,128]{0,1:T(8,128)S(1)}, u32[]{:S(2)}, u32[]{:S(2)}) collective-permute-start(f32[1024,128]{0,1:T(8,128)S(1)} %fusion.42), channel_id=1, source_target_pairs={{0,16},{4,20},{8,24},{12,28},{16,0},{20,4},{24,8},{28,12},{32,48},... | collective-permute-start | bytes 1572872 | tf_op jit(solution)/shard_map/ppermute | solution.py:12
  189.0 52.2 %copy-start = (f32[1024,128]{0,1:T(8,128)}, f32[1024,128]{0,1:T(8,128)S(1)}, u32[]{:S(2)}) copy-start(f32[1024,128]{0,1:T(8,128)S(1)} %fusion.39) | copy-start | bytes 1572868
  189.0 52.2 %collective-permute-start.9 = (f32[1024,128]{0,1:T(8,128)S(1)}, f32[1024,128]{0,1:T(8,128)S(1)}, u32[]{:S(2)}, u32[]{:S(2)}) collective-permute-start(f32[1024,128]{0,1:T(8,128)S(1)} %fusion.39), channel_id=1, source_target_pairs={{0,32},{4,36},{8,40},{12,44},{16,48},{20,52},{24,56},{28,60},{32,0... | collective-permute-start | bytes 1572872 | tf_op jit(solution)/shard_map/ppermute | solution.py:12
  251.0 45.4 %copy-start.1 = (f32[1024,128]{0,1:T(8,128)}, f32[1024,128]{0,1:T(8,128)S(1)}, u32[]{:S(2)}) copy-start(f32[1024,128]{0,1:T(8,128)S(1)} %fusion.36) | copy-start | bytes 1572868
  251.1 45.4 %collective-permute-start.10 = (f32[1024,128]{0,1:T(8,128)S(1)}, f32[1024,128]{0,1:T(8,128)S(1)}, u32[]{:S(2)}, u32[]{:S(2)}) collective-permute-start(f32[1024,128]{0,1:T(8,128)S(1)} %fusion.36), channel_id=1, source_target_pairs={{0,64},{4,68},{8,72},{12,76},{16,80},{20,84},{24,88},{28,92},{32,9... | collective-permute-start | bytes 1572872 | tf_op jit(solution)/shard_map/ppermute | solution.py:12
  306.1 15.0 %copy-start.2 = (f32[1024,128]{0,1:T(8,128)}, f32[1024,128]{0,1:T(8,128)S(1)}, u32[]{:S(2)}) copy-start(f32[1024,128]{0,1:T(8,128)S(1)} %fusion.33) | copy-start | bytes 1572868
  306.1 15.0 %collective-permute-start.11 = (f32[1024,128]{0,1:T(8,128)S(1)}, f32[1024,128]{0,1:T(8,128)S(1)}, u32[]{:S(2)}, u32[]{:S(2)}) collective-permute-start(f32[1024,128]{0,1:T(8,128)S(1)} %fusion.33), channel_id=1, source_target_pairs={{0,128},{4,132},{8,136},{12,140},{16,144},{20,148},{24,152},{28,15... | collective-permute-start | bytes 1572872 | tf_op jit(solution)/shard_map/ppermute | solution.py:12
  330.8 15.6 %copy-start.3 = (f32[1024,128]{0,1:T(8,128)}, f32[1024,128]{0,1:T(8,128)S(1)}, u32[]{:S(2)}) copy-start(f32[1024,128]{0,1:T(8,128)S(1)} %fusion.30) | copy-start | bytes 1572868
  330.8 15.5 %collective-permute-start.12 = (f32[1024,128]{0,1:T(8,128)S(1)}, f32[1024,128]{0,1:T(8,128)S(1)}, u32[]{:S(2)}, u32[]{:S(2)}) collective-permute-start(f32[1024,128]{0,1:T(8,128)S(1)} %fusion.30), channel_id=1, source_target_pairs={{0,256},{4,260},{8,264},{12,268},{16,272},{20,276},{24,280},{28,28... | collective-permute-start | bytes 1572872 | tf_op jit(solution)/shard_map/ppermute | solution.py:12
Sparse Core Ops, SparseCore 0:
  10.9 43.7 all-gather.12
  56.8 44.1 all-gather.14
  103.1 42.9 all-gather.16
  148.0 38.5 all-gather.18
  188.6 38.5 all-gather.20
  229.2 38.5 all-gather.22

commit v2 on v1

--- a/solution.py
+++ b/solution.py
@@ -81,16 +81,37 @@
         else:
             matrix = lax.all_gather(merge_maps[0, level - 1], "case", axis=0, tiled=True)
         shared_rows = matrix.shape[1]
-        other = from_partner(current, "sub", level - 1)
         upper = slot // half % 2 == 1
-        left_base = jnp.where(upper, full_rows, 0)
-        right_base = full_rows - left_base
-        stacked = jnp.concatenate([current, other], axis=0)
-        shared = jnp.take(stacked, maps[0, :shared_rows] + left_base, axis=0) + jnp.take(
-            stacked, maps[1, :shared_rows] + right_base, axis=0
+        if level == 1:
+            other = from_partner(current, "sub", 0)
+            stacked = jnp.concatenate([current, other], axis=0)
+
+            def partner_index(index):
+                return index + full_rows
+
+        else:
+            core = slot % 2
+            rows_half = full_rows // 2
+            piece = lax.dynamic_slice_in_dim(current, core * rows_half, rows_half, 0)
+            got = from_partner(piece, "sub", level - 1)
+            swapped = from_partner(got, "sub", 0)
+            stacked = jnp.concatenate([current, got, swapped], axis=0)
+
+            def partner_index(index):
+                away = (index // rows_half != core).astype(index.dtype)
+                return full_rows + index % rows_half + rows_half * away
+
+        def left_index(index):
+            return jnp.where(upper, partner_index(index), index)
+
+        def right_index(index):
+            return jnp.where(upper, index, partner_index(index))
+
+        shared = jnp.take(stacked, left_index(maps[0, :shared_rows]), axis=0) + jnp.take(
+            stacked, right_index(maps[1, :shared_rows]), axis=0
         )
         kept_index = jnp.concatenate(
-            [maps[0, shared_rows:] + left_base, maps[1, shared_rows:] + right_base]
+            [left_index(maps[0, shared_rows:]), right_index(maps[1, shared_rows:])]
         )
         if last:
             kept_index = lax.dynamic_slice_in_dim(kept_index, position * quarter, quarter)

time: 362 us -> 319 us (0.88)
  waiting for transfers between devices: 202 us -> 145 us
  starting transfers between devices: 65.6 us -> 82 us
    ppermute x7 -> x13, waiting for transfers between devices: 152 us -> 94.2 us  [from_partner(): return lax.ppermute(value, axis, pairs)]
    ppermute x7 -> x13, starting transfers between devices: 23.7 us -> 40.1 us  [from_partner(): return lax.ppermute(value, axis, pairs)]
  transfers between devices with their start and end apart: 20 -> 26, of which waited for: 12 -> 19; matrix products, arithmetic and copies ran while one was open for 17% -> 19% of each run, Pallas kernels for 0% -> 0%
where the time goes in v2:
time: 319 us; the launch traced here: 318 us
  waiting for transfers between devices  145 us (45%)
  starting transfers between devices  82 us (26%)
  local copies, waits for them, and re-layouts  43 us (13%)
  matrix products  29.1 us (9%)
  between operations  15.8 us (5%)
    ppermute x13, waiting for transfers between devices, from_partner(): return lax.ppermute(value, axis, pairs)  94.2 us
    ppermute x13, starting transfers between devices, from_partner(): return lax.ppermute(value, axis, pairs)  40.1 us
    all_to_all x1, waiting for transfers between devices, on_device(): lax.all_to_all(joined, 'sub', split_axis=1, concat_axis=0, tiled=True)  36.7 us
    dot_general x7, matrix products, on_device(): jnp.dot(matrix, shared, precision=lax.Precision.HIGHEST)  26.9 us
    ppermute x6, starting transfers between devices, shifted(): return lax.ppermute(value, axis, pairs)  21.1 us
    all_to_all x1, starting transfers between devices, on_device(): lax.all_to_all(joined, 'sub', split_axis=1, concat_axis=0, tiled=True)  20.6 us
    gather x14, local copies, waits for them, and re-layouts, on_device(): jnp.take(stacked, kept_index, axis=0)  18.9 us
    ppermute x6, waiting for transfers between devices, shifted(): return lax.ppermute(value, axis, pairs)  11.3 us
  transfers between devices with their start and end apart: 26, of which 19 were waited for; matrix products, arithmetic and copies ran while one was open for 19% of the time, Pallas kernels for 0%

profile of v2, /device:TPU:1, one launch (start us, length us, event | category | flops | bytes accessed | tf_op | source)
XLA Modules:
  0.0 318.0 jit_solution(7380270549679842058)
XLA Ops:
  7.2 3.6 %fusion.253 = (f32[1,1,256,512]{3,2,1,0:T(8,128)}, f32[1,1,256,512]{3,2,1,0:T(8,128)}, f32[1,1,256,512]{3,2,1,0:T(8,128)}, f32[1,1,256,512]{3,2,1,0:T(8,128)}, f...) fusion(f32[1,7,256,512]{3,2,1,0:T(8,128)} %param.17), kind=kLoop, calls=%fused_computation.510 | loop fusion | bytes 6291456 | tf_op jit(solution)/shard_map/slice | solution.py:82
  15.6 20.6 %all-to-all-start = ((f32[1,128,1280]{2,0,1:T(1,128)}), f32[1,128,1280]{2,0,1:T(1,128)S(1)}, u32[]{:S(2)}, u32[]{:S(2)}) async-start(f32[1,128,1280]{2,0,1:T(1,128)} %pad_maximum_fusion.7), calls=%async_computation | async-start | bytes 1310720 | tf_op jit(solution)/shard_map/all_to_all | solution.py:42
  37.8 36.7 %all-to-all-done = f32[1,128,1280]{2,0,1:T(1,128)S(1)} async-done(((f32[1,128,1280]{2,0,1:T(1,128)}), f32[1,128,1280]{2,0,1:T(1,128)S(1)}, u32[]{:S(2)}, u32[]{:S(2)}) %all-to-all-start) | async-done | bytes 655392 | tf_op jit(solution)/shard_map/all_to_all | solution.py:42
  78.2 3.1 collective-permute-start
  81.3 4.4 %collective-permute-start.1 = (f32[256,128]{1,0:T(8,128)S(1)}, f32[256,128]{1,0:T(8,128)S(1)}, u32[]{:S(2)}, u32[]{:S(2)}) collective-permute-start(f32[256,128]{1,0:T(8,128)S(1)} %get-tuple-element.48), channel_id=1, source_target_pairs={{0,2},{1,3},{2,0},{3,1},{4,6},{5,7},{6,4},{7,5},{8,10},{9,11},{10,... | collective-permute-start | bytes 393224 | tf_op jit(solution)/shard_map/ppermute | solution.py:18
  85.7 3.1 collective-permute-start.2
  89.1 6.5 %collective-permute-done.1 = f32[256,128]{1,0:T(8,128)S(1)} collective-permute-done((f32[256,128]{1,0:T(8,128)S(1)}, f32[256,128]{1,0:T(8,128)S(1)}, u32[]{:S(2)}, u32[]{:S(2)}) %collective-permute-start.1) | collective-permute-done | bytes 131104 | tf_op jit(solution)/shard_map/ppermute | solution.py:18
  99.5 4.4 %collective-permute-start.4 = (f32[256,128]{1,0:T(8,128)S(1)}, f32[256,128]{1,0:T(8,128)S(1)}, u32[]{:S(2)}, u32[]{:S(2)}) collective-permute-start(f32[256,128]{1,0:T(8,128)S(1)} %fusion.68), channel_id=1, source_target_pairs={{0,2},{1,3},{2,0},{3,1},{4,6},{5,7},{6,4},{7,5},{8,10},{9,11},{10,... | collective-permute-start | bytes 393224 | tf_op jit(solution)/shard_map/ppermute | solution.py:18
  103.9 3.8 %collective-permute-start.5 = (f32[256,128]{1,0:T(8,128)S(1)}, f32[256,128]{1,0:T(8,128)S(1)}, u32[]{:S(2)}, u32[]{:S(2)}) collective-permute-start(f32[256,128]{1,0:T(8,128)S(1)} %fusion.68), channel_id=1, source_target_pairs={{0,3},{1,0},{2,1},{3,2},{4,7},{5,4},{6,5},{7,6},{8,11},{9,8},{10,9... | collective-permute-start | bytes 393224 | tf_op jit(solution)/shard_map/ppermute | solution.py:18
  108.0 2.9 collective-permute-done.5
  111.7 4.5 %collective-permute-start.6 = (f32[1024,128]{1,0:T(8,128)S(1)}, f32[1024,128]{1,0:T(8,128)S(1)}, u32[]{:S(2)}, u32[]{:S(2)}) collective-permute-start(f32[1024,128]{1,0:T(8,128)S(1)} %bitcast_select_fusion), channel_id=1, source_target_pairs={{0,4},{4,0},{8,12},{12,8},{16,20},{20,16},{24,28},{28,24},{32,36},... | collective-permute-start | bytes 1572872 | tf_op jit(solution)/shard_map/ppermute | solution.py:12
  117.8 2.8 gather_fusion.3
  123.0 4.2 %select_subtract_fusion = f32[1024,128]{0,1:T(8,128)S(1)} fusion(f32[1024,128]{0,1:T(8,128)S(1)} %copy.67, f32[1,1,1024,512]{3,2,1,0:T(8,128)} %all-gather.13.cloned.1.call-done, f32[512,128]{1,0:T(8,128)S(1)} %gather_fusion.5, f32[512,128]{1,0:T(8,128)S(1)} %gather_fusion.4, pred[1024]{0:T(1024)(128)(4,1)S(1)} %compare_and_fusion.5, ...), kind=kOutput, calls=%fused_computation.66 | convolution fusion | flops 805765120 | bytes 3672064 | tf_op jit(solution)/shard_map/dot_general | solution.py:118
  127.2 3.5 %collective-permute-start.7 = (f32[512,128]{0,1:T(8,128)S(1)}, f32[512,128]{0,1:T(8,128)S(1)}, u32[]{:S(2)}, u32[]{:S(2)}) collective-permute-start(f32[512,128]{0,1:T(8,128)S(1)} %constant_dynamic-slice_fusion.5), channel_id=1, source_target_pairs={{0,8},{4,12},{8,0},{12,4},{16,24},{20,28},{24,16},{28,20},{32,40},... | collective-permute-start | bytes 786440 | tf_op jit(solution)/shard_map/ppermute | solution.py:12
  130.7 6.3 %collective-permute-done.7 = f32[512,128]{0,1:T(8,128)S(1)} collective-permute-done((f32[512,128]{0,1:T(8,128)S(1)}, f32[512,128]{0,1:T(8,128)S(1)}, u32[]{:S(2)}, u32[]{:S(2)}) %collective-permute-start.7) | collective-permute-done | bytes 262176 | tf_op jit(solution)/shard_map/ppermute | solution.py:12
  137.0 2.9 collective-permute-start.8
  143.5 2.8 gather_fusion.6
  146.5 4.1 %fusion.42 = f32[1024,128]{0,1:T(8,128)S(1)} fusion(f32[1,1,1024,512]{3,2,1,0:T(8,128)} %all-gather.15.cloned.1.call-done, f32[1024,128]{0,1:T(8,128)S(1)} %copy.69, f32[512,128]{1,0:T(8,128)S(1)} %gather_fusion.8, f32[512,128]{1,0:T(8,128)S(1)} %gather_fusion.7, pred[1024]{0:T(1024)(128)(4,1)S(1)} %compare_and_fusion.4, ...), kind=kOutput, calls=%fused_computation.45 | convolution fusion | flops 805765120 | bytes 3672064 | tf_op jit(solution)/shard_map/dot_general | solution.py:118
  152.9 13.7 %collective-permute-done.9 = f32[512,128]{0,1:T(8,128)S(1)} collective-permute-done((f32[512,128]{0,1:T(8,128)S(1)}, f32[512,128]{0,1:T(8,128)S(1)}, u32[]{:S(2)}, u32[]{:S(2)}) %collective-permute-start.9) | collective-permute-done | bytes 262176 | tf_op jit(solution)/shard_map/ppermute | solution.py:12
  166.6 3.1 collective-permute-start.10
  176.4 4.1 %fusion.39 = f32[1024,128]{0,1:T(8,128)S(1)} fusion(f32[1,1,1024,512]{3,2,1,0:T(8,128)} %all-gather.17.cloned.1.call-done, f32[1024,128]{0,1:T(8,128)S(1)} %copy.73, f32[512,128]{1,0:T(8,128)S(1)} %gather_fusion.11, f32[512,128]{1,0:T(8,128)S(1)} %gather_fusion.10, pred[1024]{0:T(1024)(128)(4,1)S(1)} %compare_and_fusion.3, ...), kind=kOutput, calls=%fused_computation.44 | convolution fusion | flops 805765120 | bytes 3672064 | tf_op jit(solution)/shard_map/dot_general | solution.py:118
  180.6 3.0 collective-permute-start.11
  183.6 25.9 %collective-permute-done.11 = f32[512,128]{0,1:T(8,128)S(1)} collective-permute-done((f32[512,128]{0,1:T(8,128)S(1)}, f32[512,128]{0,1:T(8,128)S(1)}, u32[]{:S(2)}, u32[]{:S(2)}) %collective-permute-start.11) | collective-permute-done | bytes 262176 | tf_op jit(solution)/shard_map/ppermute | solution.py:12
  218.6 4.1 %fusion.36 = f32[1024,128]{0,1:T(8,128)S(1)} fusion(f32[1,1,1024,512]{3,2,1,0:T(8,128)} %all-gather.19.cloned.1.call-done, f32[1024,128]{0,1:T(8,128)S(1)} %copy.77, f32[512,128]{1,0:T(8,128)S(1)} %gather_fusion.14, f32[512,128]{1,0:T(8,128)S(1)} %gather_fusion.13, pred[1024]{0:T(1024)(128)(4,1)S(1)} %compare_and_fusion.2, ...), kind=kOutput, calls=%fused_computation.43 | convolution fusion | flops 805765120 | bytes 3672064 | tf_op jit(solution)/shard_map/dot_general | solution.py:118
  222.8 5.8 %collective-permute-start.13 = (f32[512,128]{0,1:T(8,128)S(1)}, f32[512,128]{0,1:T(8,128)S(1)}, u32[]{:S(2)}, u32[]{:S(2)}) collective-permute-start(f32[512,128]{0,1:T(8,128)S(1)} %constant_dynamic-slice_fusion.2), channel_id=1, source_target_pairs={{0,64},{4,68},{8,72},{12,76},{16,80},{20,84},{24,88},{28,92},{32,9... | collective-permute-start | bytes 786440 | tf_op jit(solution)/shard_map/ppermute | solution.py:12
  228.7 24.5 %collective-permute-done.13 = f32[512,128]{0,1:T(8,128)S(1)} collective-permute-done((f32[512,128]{0,1:T(8,128)S(1)}, f32[512,128]{0,1:T(8,128)S(1)}, u32[]{:S(2)}, u32[]{:S(2)}) %collective-permute-start.13) | collective-permute-done | bytes 262176 | tf_op jit(solution)/shard_map/ppermute | solution.py:12
  262.2 4.1 %fusion.33 = f32[1024,128]{0,1:T(8,128)S(1)} fusion(f32[1,1,1024,512]{3,2,1,0:T(8,128)} %all-gather.21.cloned.1.call-done, f32[1024,128]{0,1:T(8,128)S(1)} %copy.81, f32[512,128]{1,0:T(8,128)S(1)} %gather_fusion.17, f32[512,128]{1,0:T(8,128)S(1)} %gather_fusion.16, pred[1024]{0:T(1024)(128)(4,1)S(1)} %compare_and_fusion.1, ...), kind=kOutput, calls=%fused_computation.42 | convolution fusion | flops 805765120 | bytes 3672064 | tf_op jit(solution)/shard_map/dot_general | solution.py:118
  268.4 7.4 %collective-permute-done.15 = f32[512,128]{0,1:T(8,128)S(1)} collective-permute-done((f32[512,128]{0,1:T(8,128)S(1)}, f32[512,128]{0,1:T(8,128)S(1)}, u32[]{:S(2)}, u32[]{:S(2)}) %collective-permute-start.15) | collective-permute-done | bytes 262176 | tf_op jit(solution)/shard_map/ppermute | solution.py:12
  275.8 3.1 collective-permute-start.16
  285.6 4.1 %fusion.30 = f32[1024,128]{0,1:T(8,128)S(1)} fusion(f32[1,1,1024,512]{3,2,1,0:T(8,128)} %all-gather.23.cloned.1.call-done, f32[1024,128]{0,1:T(8,128)S(1)} %copy.85, f32[512,128]{1,0:T(8,128)S(1)} %gather_fusion.20, f32[512,128]{1,0:T(8,128)S(1)} %gather_fusion.19, pred[1024]{0:T(1024)(128)(4,1)S(1)} %compare_and_fusion, ...), kind=kOutput, calls=%fused_computation.41 | convolution fusion | flops 805765120 | bytes 3672064 | tf_op jit(solution)/shard_map/dot_general | solution.py:118
  291.9 8.8 %collective-permute-done.17 = f32[512,128]{0,1:T(8,128)S(1)} collective-permute-done((f32[512,128]{0,1:T(8,128)S(1)}, f32[512,128]{0,1:T(8,128)S(1)}, u32[]{:S(2)}, u32[]{:S(2)}) %collective-permute-start.17) | collective-permute-done | bytes 262176 | tf_op jit(solution)/shard_map/ppermute | solution.py:12
  300.7 3.1 collective-permute-start.18
  (181 shorter events, 67.2 us)
Async XLA Ops:
  7.2 115.8 %all-gather.13.cloned.1.call-start = ((), (), s32[]{:S(2)}) async-start(), calls=%async_computation.1 | async-start | bytes 2621440 | tf_op jit(solution)/shard_map/all_gather | solution.py:82
  10.8 135.7 %all-gather.15.cloned.1.call-start = ((), (), s32[]{:S(2)}) async-start(), calls=%async_computation.2 | async-start | bytes 2621440 | tf_op jit(solution)/shard_map/all_gather | solution.py:82
  11.5 164.8 %all-gather.17.cloned.1.call-start = ((), (), s32[]{:S(2)}) async-start(), calls=%async_computation.3 | async-start | bytes 2621440 | tf_op jit(solution)/shard_map/all_gather | solution.py:82
  12.3 206.4 %all-gather.19.cloned.1.call-start = ((), (), s32[]{:S(2)}) async-start(), calls=%async_computation.4 | async-start | bytes 2621440 | tf_op jit(solution)/shard_map/all_gather | solution.py:82
  12.9 249.3 %all-gather.21.cloned.1.call-start = ((), (), s32[]{:S(2)}) async-start(), calls=%async_computation.5 | async-start | bytes 2621440 | tf_op jit(solution)/shard_map/all_gather | solution.py:82
  13.5 23.4 %copy-start.10 = (s32[1,32]{1,0:T(1,128)S(1)}, s32[1,32]{1,0:T(1,128)}, u32[]{:S(2)}) copy-start(s32[1,32]{1,0:T(1,128)} %param.15) | copy-start | bytes 388
  13.5 23.4 %copy-start.8 = (s32[1,7,2,1024]{3,2,1,0:T(2,128)S(1)}, s32[1,7,2,1024]{3,2,1,0:T(2,128)}, u32[]{:S(2)}) copy-start(s32[1,7,2,1024]{3,2,1,0:T(2,128)} %param.16) | copy-start | bytes 172036
  14.0 23.0 %copy-start.4 = (f32[1,32,4096]{2,1,0:T(8,128)S(1)}, f32[1,32,4096]{2,1,0:T(8,128)}, u32[]{:S(2)}) copy-start(f32[1,32,4096]{2,1,0:T(8,128)} %param.13) | copy-start | bytes 1572868
  15.6 58.9 %all-to-all-start = ((f32[1,128,1280]{2,0,1:T(1,128)}), f32[1,128,1280]{2,0,1:T(1,128)S(1)}, u32[]{:S(2)}, u32[]{:S(2)}) async-start(f32[1,128,1280]{2,0,1:T(1,128)} %pad_maximum_fusion.7), calls=%async_computation | async-start | bytes 1310720 | tf_op jit(solution)/shard_map/all_to_all | solution.py:42
  36.2 249.4 %all-gather.23.cloned.1.call-start = ((), (), s32[]{:S(2)}) async-start(), calls=%async_computation.6 | async-start | bytes 2621440 | tf_op jit(solution)/shard_map/all_gather | solution.py:82
  78.2 10.9 %collective-permute-start = (f32[256,128]{1,0:T(8,128)S(1)}, f32[256,128]{1,0:T(8,128)S(1)}, u32[]{:S(2)}, u32[]{:S(2)}) collective-permute-start(f32[256,128]{1,0:T(8,128)S(1)} %get-tuple-element.46), channel_id=1, source_target_pairs={{0,1},{1,2},{2,3},{3,0},{4,5},{5,6},{6,7},{7,4},{8,9},{9,10},{10,1... | collective-permute-start | bytes 393224 | tf_op jit(solution)/shard_map/ppermute | solution.py:18
  81.3 14.2 %collective-permute-start.1 = (f32[256,128]{1,0:T(8,128)S(1)}, f32[256,128]{1,0:T(8,128)S(1)}, u32[]{:S(2)}, u32[]{:S(2)}) collective-permute-start(f32[256,128]{1,0:T(8,128)S(1)} %get-tuple-element.48), channel_id=1, source_target_pairs={{0,2},{1,3},{2,0},{3,1},{4,6},{5,7},{6,4},{7,5},{8,10},{9,11},{10,... | collective-permute-start | bytes 393224 | tf_op jit(solution)/shard_map/ppermute | solution.py:18
  85.7 11.4 %collective-permute-start.2 = (f32[256,128]{1,0:T(8,128)S(1)}, f32[256,128]{1,0:T(8,128)S(1)}, u32[]{:S(2)}, u32[]{:S(2)}) collective-permute-start(f32[256,128]{1,0:T(8,128)S(1)} %get-tuple-element.47), channel_id=1, source_target_pairs={{0,3},{1,0},{2,1},{3,2},{4,7},{5,4},{6,5},{7,6},{8,11},{9,8},{10,9... | collective-permute-start | bytes 393224 | tf_op jit(solution)/shard_map/ppermute | solution.py:18
  97.1 20.7 %copy-start.6 = (f32[256,128]{1,0:T(8,128)}, f32[256,128]{1,0:T(8,128)S(1)}, u32[]{:S(2)}) copy-start(f32[256,128]{1,0:T(8,128)S(1)} %fusion.68) | copy-start | bytes 393220
  97.1 10.7 %collective-permute-start.3 = (f32[256,128]{1,0:T(8,128)S(1)}, f32[256,128]{1,0:T(8,128)S(1)}, u32[]{:S(2)}, u32[]{:S(2)}) collective-permute-start(f32[256,128]{1,0:T(8,128)S(1)} %fusion.68), channel_id=1, source_target_pairs={{0,1},{1,2},{2,3},{3,0},{4,5},{5,6},{6,7},{7,4},{8,9},{9,10},{10,1... | collective-permute-start | bytes 393224 | tf_op jit(solution)/shard_map/ppermute | solution.py:18
  99.5 8.5 %collective-permute-start.4 = (f32[256,128]{1,0:T(8,128)S(1)}, f32[256,128]{1,0:T(8,128)S(1)}, u32[]{:S(2)}, u32[]{:S(2)}) collective-permute-start(f32[256,128]{1,0:T(8,128)S(1)} %fusion.68), channel_id=1, source_target_pairs={{0,2},{1,3},{2,0},{3,1},{4,6},{5,7},{6,4},{7,5},{8,10},{9,11},{10,... | collective-permute-start | bytes 393224 | tf_op jit(solution)/shard_map/ppermute | solution.py:18
  103.9 7.0 %collective-permute-start.5 = (f32[256,128]{1,0:T(8,128)S(1)}, f32[256,128]{1,0:T(8,128)S(1)}, u32[]{:S(2)}, u32[]{:S(2)}) collective-permute-start(f32[256,128]{1,0:T(8,128)S(1)} %fusion.68), channel_id=1, source_target_pairs={{0,3},{1,0},{2,1},{3,2},{4,7},{5,4},{6,5},{7,6},{8,11},{9,8},{10,9... | collective-permute-start | bytes 393224 | tf_op jit(solution)/shard_map/ppermute | solution.py:18
  111.7 6.1 %collective-permute-start.6 = (f32[1024,128]{1,0:T(8,128)S(1)}, f32[1024,128]{1,0:T(8,128)S(1)}, u32[]{:S(2)}, u32[]{:S(2)}) collective-permute-start(f32[1024,128]{1,0:T(8,128)S(1)} %bitcast_select_fusion), channel_id=1, source_target_pairs={{0,4},{4,0},{8,12},{12,8},{16,20},{20,16},{24,28},{28,24},{32,36},... | collective-permute-start | bytes 1572872 | tf_op jit(solution)/shard_map/ppermute | solution.py:12
  127.2 9.8 %collective-permute-start.7 = (f32[512,128]{0,1:T(8,128)S(1)}, f32[512,128]{0,1:T(8,128)S(1)}, u32[]{:S(2)}, u32[]{:S(2)}) collective-permute-start(f32[512,128]{0,1:T(8,128)S(1)} %constant_dynamic-slice_fusion.5), channel_id=1, source_target_pairs={{0,8},{4,12},{8,0},{12,4},{16,24},{20,28},{24,16},{28,20},{32,40},... | collective-permute-start | bytes 786440 | tf_op jit(solution)/shard_map/ppermute | solution.py:12
  137.0 3.9 %collective-permute-start.8 = (f32[512,128]{0,1:T(8,128)S(1)}, f32[512,128]{0,1:T(8,128)S(1)}, u32[]{:S(2)}, u32[]{:S(2)}) collective-permute-start(f32[512,128]{0,1:T(8,128)S(1)} %collective-permute-done.7), channel_id=1, source_target_pairs={{0,4},{4,0},{8,12},{12,8},{16,20},{20,16},{24,28},{28,24},{32,36},... | collective-permute-start | bytes 786440 | tf_op jit(solution)/shard_map/ppermute | solution.py:12
  150.7 15.9 %collective-permute-start.9 = (f32[512,128]{0,1:T(8,128)S(1)}, f32[512,128]{0,1:T(8,128)S(1)}, u32[]{:S(2)}, u32[]{:S(2)}) collective-permute-start(f32[512,128]{0,1:T(8,128)S(1)} %constant_dynamic-slice_fusion.4), channel_id=1, source_target_pairs={{0,16},{4,20},{8,24},{12,28},{16,0},{20,4},{24,8},{28,12},{32,48},... | collective-permute-start | bytes 786440 | tf_op jit(solution)/shard_map/ppermute | solution.py:12
  166.6 4.2 %collective-permute-start.10 = (f32[512,128]{0,1:T(8,128)S(1)}, f32[512,128]{0,1:T(8,128)S(1)}, u32[]{:S(2)}, u32[]{:S(2)}) collective-permute-start(f32[512,128]{0,1:T(8,128)S(1)} %collective-permute-done.9), channel_id=1, source_target_pairs={{0,4},{4,0},{8,12},{12,8},{16,20},{20,16},{24,28},{28,24},{32,36},... | collective-permute-start | bytes 786440 | tf_op jit(solution)/shard_map/ppermute | solution.py:12
  180.5 32.6 %copy-start = (f32[1024,128]{0,1:T(8,128)}, f32[1024,128]{0,1:T(8,128)S(1)}, u32[]{:S(2)}) copy-start(f32[1024,128]{0,1:T(8,128)S(1)} %fusion.39) | copy-start | bytes 1572868
  180.6 29.0 %collective-permute-start.11 = (f32[512,128]{0,1:T(8,128)S(1)}, f32[512,128]{0,1:T(8,128)S(1)}, u32[]{:S(2)}, u32[]{:S(2)}) collective-permute-start(f32[512,128]{0,1:T(8,128)S(1)} %constant_dynamic-slice_fusion.3), channel_id=1, source_target_pairs={{0,32},{4,36},{8,40},{12,44},{16,48},{20,52},{24,56},{28,60},{32,0... | collective-permute-start | bytes 786440 | tf_op jit(solution)/shard_map/ppermute | solution.py:12
  209.6 3.5 %collective-permute-start.12 = (f32[512,128]{0,1:T(8,128)S(1)}, f32[512,128]{0,1:T(8,128)S(1)}, u32[]{:S(2)}, u32[]{:S(2)}) collective-permute-start(f32[512,128]{0,1:T(8,128)S(1)} %collective-permute-done.11), channel_id=1, source_target_pairs={{0,4},{4,0},{8,12},{12,8},{16,20},{20,16},{24,28},{28,24},{32,36},... | collective-permute-start | bytes 786440 | tf_op jit(solution)/shard_map/ppermute | solution.py:12
  222.8 33.9 %copy-start.1 = (f32[1024,128]{0,1:T(8,128)}, f32[1024,128]{0,1:T(8,128)S(1)}, u32[]{:S(2)}) copy-start(f32[1024,128]{0,1:T(8,128)S(1)} %fusion.36) | copy-start | bytes 1572868
  222.8 30.3 %collective-permute-start.13 = (f32[512,128]{0,1:T(8,128)S(1)}, f32[512,128]{0,1:T(8,128)S(1)}, u32[]{:S(2)}, u32[]{:S(2)}) collective-permute-start(f32[512,128]{0,1:T(8,128)S(1)} %constant_dynamic-slice_fusion.2), channel_id=1, source_target_pairs={{0,64},{4,68},{8,72},{12,76},{16,80},{20,84},{24,88},{28,92},{32,9... | collective-permute-start | bytes 786440 | tf_op jit(solution)/shard_map/ppermute | solution.py:12
  253.1 3.5 %collective-permute-start.14 = (f32[512,128]{0,1:T(8,128)S(1)}, f32[512,128]{0,1:T(8,128)S(1)}, u32[]{:S(2)}, u32[]{:S(2)}) collective-permute-start(f32[512,128]{0,1:T(8,128)S(1)} %collective-permute-done.13), channel_id=1, source_target_pairs={{0,4},{4,0},{8,12},{12,8},{16,20},{20,16},{24,28},{28,24},{32,36},... | collective-permute-start | bytes 786440 | tf_op jit(solution)/shard_map/ppermute | solution.py:12
  266.4 9.4 %collective-permute-start.15 = (f32[512,128]{0,1:T(8,128)S(1)}, f32[512,128]{0,1:T(8,128)S(1)}, u32[]{:S(2)}, u32[]{:S(2)}) collective-permute-start(f32[512,128]{0,1:T(8,128)S(1)} %constant_dynamic-slice_fusion.1), channel_id=1, source_target_pairs={{0,128},{4,132},{8,136},{12,140},{16,144},{20,148},{24,152},{28,15... | collective-permute-start | bytes 786440 | tf_op jit(solution)/shard_map/ppermute | solution.py:12
  275.8 4.2 %collective-permute-start.16 = (f32[512,128]{0,1:T(8,128)S(1)}, f32[512,128]{0,1:T(8,128)S(1)}, u32[]{:S(2)}, u32[]{:S(2)}) collective-permute-start(f32[512,128]{0,1:T(8,128)S(1)} %collective-permute-done.15), channel_id=1, source_target_pairs={{0,4},{4,0},{8,12},{12,8},{16,20},{20,16},{24,28},{28,24},{32,36},... | collective-permute-start | bytes 786440 | tf_op jit(solution)/shard_map/ppermute | solution.py:12
  289.8 10.9 %collective-permute-start.17 = (f32[512,128]{0,1:T(8,128)S(1)}, f32[512,128]{0,1:T(8,128)S(1)}, u32[]{:S(2)}, u32[]{:S(2)}) collective-permute-start(f32[512,128]{0,1:T(8,128)S(1)} %constant_dynamic-slice_fusion), channel_id=1, source_target_pairs={{0,256},{4,260},{8,264},{12,268},{16,272},{20,276},{24,280},{28,28... | collective-permute-start | bytes 786440 | tf_op jit(solution)/shard_map/ppermute | solution.py:12
  300.7 4.2 %collective-permute-start.18 = (f32[512,128]{0,1:T(8,128)S(1)}, f32[512,128]{0,1:T(8,128)S(1)}, u32[]{:S(2)}, u32[]{:S(2)}) collective-permute-start(f32[512,128]{0,1:T(8,128)S(1)} %collective-permute-done.17), channel_id=1, source_target_pairs={{0,4},{4,0},{8,12},{12,8},{16,20},{20,16},{24,28},{28,24},{32,36},... | collective-permute-start | bytes 786440 | tf_op jit(solution)/shard_map/ppermute | solution.py:12
  (5 other events, 36.1 us)
Sparse Core Ops, SparseCore 0:
  10.9 43.7 all-gather.12
  56.8 44.1 all-gather.14
  103.2 42.8 all-gather.16
  148.0 38.5 all-gather.18
  188.6 38.5 all-gather.20
  229.2 38.5 all-gather.22

commit v3 on v2

--- a/solution.py
+++ b/solution.py
@@ -72,6 +72,10 @@
     slot = lax.axis_index("sub")
     levels = lax.axis_size("sub").bit_length() - 1
     nodes = jnp.zeros((quarter, num_cases), jnp.float32)
+    core = slot % 2
+    rows_half = full_rows // 2
+    turn = core * rows_half
+    rest = None
     for level in range(1, levels + 1):
         half = 1 << level - 1
         maps = interface_maps[0, level - 1]
@@ -86,26 +90,23 @@
             other = from_partner(current, "sub", 0)
             stacked = jnp.concatenate([current, other], axis=0)
 
-            def partner_index(index):
-                return index + full_rows
+            def own_index(index):
+                return index
 
         else:
-            core = slot % 2
-            rows_half = full_rows // 2
-            piece = lax.dynamic_slice_in_dim(current, core * rows_half, rows_half, 0)
-            got = from_partner(piece, "sub", level - 1)
+            got = from_partner(current[:rows_half], "sub", level - 1)
+            got, rest = lax.optimization_barrier((got, rest))
             swapped = from_partner(got, "sub", 0)
             stacked = jnp.concatenate([current, got, swapped], axis=0)
 
-            def partner_index(index):
-                away = (index // rows_half != core).astype(index.dtype)
-                return full_rows + index % rows_half + rows_half * away
+            def own_index(index):
+                return jnp.bitwise_xor(index, turn)
 
         def left_index(index):
-            return jnp.where(upper, partner_index(index), index)
+            return jnp.where(upper, own_index(index) + full_rows, own_index(index))
 
         def right_index(index):
-            return jnp.where(upper, index, partner_index(index))
+            return jnp.where(upper, own_index(index), own_index(index) + full_rows)
 
         shared = jnp.take(stacked, left_index(maps[0, :shared_rows]), axis=0) + jnp.take(
             stacked, right_index(maps[1, :shared_rows]), axis=0
@@ -113,19 +114,30 @@
         kept_index = jnp.concatenate(
             [left_index(maps[0, shared_rows:]), right_index(maps[1, shared_rows:])]
         )
-        if last:
-            kept_index = lax.dynamic_slice_in_dim(kept_index, position * quarter, quarter)
-        parent = jnp.take(stacked, kept_index, axis=0) - jnp.dot(
-            matrix, shared, precision=lax.Precision.HIGHEST
-        )
+
+        def rows_of(begin, count):
+            index = lax.dynamic_slice_in_dim(kept_index, begin, count)
+            if last:
+                part = lax.dynamic_slice_in_dim(matrix, 0, count, 0)
+            else:
+                part = lax.dynamic_slice_in_dim(matrix, begin, count, 0)
+            return jnp.take(stacked, index, axis=0) - jnp.dot(
+                part, shared, precision=lax.Precision.HIGHEST
+            )
+
         is_node = slot % (2 * half) == half
         if last:
             is_node = jnp.logical_or(is_node, slot == 0)
-            own = parent
+            own = rows_of(position * quarter, quarter)
         else:
-            own = lax.dynamic_slice_in_dim(parent, position * quarter, quarter, 0)
+            first = rows_of(turn, rows_half)
+            second = rows_of(rows_half - turn, rows_half)
+            current = jnp.concatenate([first, second], axis=0)
+            rest = second
+            own = lax.dynamic_slice_in_dim(
+                current, jnp.bitwise_xor(position * quarter, turn), quarter, 0
+            )
         nodes = jnp.where(is_node, own, nodes)
-        current = parent
     return (leaf_share[None], nodes[None])
 
 

time: 319 us -> 307 us (0.962)
  waiting for transfers between devices: 145 us -> 123 us
  other arithmetic: 2.89 us -> 10.8 us
  matrix products: 29.1 us -> 36 us
    ppermute x13, waiting for transfers between devices: 94.2 us -> 70.5 us  [from_partner(): return lax.ppermute(value, axis, pairs)]
    dot_general x7 -> x13, matrix products: 26.9 us -> 33.1 us  [rows_of(): jnp.dot(part, shared, precision=lax.Precision.HIGHEST)]
    ppermute x6, starting transfers between devices: 21.1 us -> 17 us  [shifted(): return lax.ppermute(value, axis, pairs)]
    ppermute x6, waiting for transfers between devices: 11.3 us -> 15.2 us  [shifted(): return lax.ppermute(value, axis, pairs)]
    and x7, other arithmetic: 0.16 us -> 3.97 us  [rows_of(): jnp.take(stacked, index, axis=0)]
    gather x14 -> x13, local copies, waits for them, and re-layouts: 18.9 us -> 16.8 us  [rows_of(): jnp.take(stacked, index, axis=0)]
  transfers between devices with their start and end apart: 26 -> 26, of which waited for: 19 -> 18; matrix products, arithmetic and copies ran while one was open for 19% -> 24% of each run, Pallas kernels for 0% -> 0%
where the time goes in v3:
time: 307 us; the launch traced here: 306 us
  waiting for transfers between devices  123 us (40%)
  starting transfers between devices  79.3 us (26%)
  local copies, waits for them, and re-layouts  41.6 us (14%)
  matrix products  36 us (12%)
  between operations  15.6 us (5%)
  other arithmetic  10.8 us (4%)
    ppermute x13, waiting for transfers between devices, from_partner(): return lax.ppermute(value, axis, pairs)  70.5 us
    ppermute x13, starting transfers between devices, from_partner(): return lax.ppermute(value, axis, pairs)  41.5 us
    all_to_all x1, waiting for transfers between devices, on_device(): lax.all_to_all(joined, 'sub', split_axis=1, concat_axis=0, tiled=True)  34 us
    dot_general x13, matrix products, rows_of(): jnp.dot(part, shared, precision=lax.Precision.HIGHEST)  33.1 us
    all_to_all x1, starting transfers between devices, on_device(): lax.all_to_all(joined, 'sub', split_axis=1, concat_axis=0, tiled=True)  20.6 us
    ppermute x6, starting transfers between devices, shifted(): return lax.ppermute(value, axis, pairs)  17 us
    gather x13, local copies, waits for them, and re-layouts, rows_of(): jnp.take(stacked, index, axis=0)  16.8 us
    ppermute x6, waiting for transfers between devices, shifted(): return lax.ppermute(value, axis, pairs)  15.2 us
  transfers between devices with their start and end apart: 26, of which 18 were waited for; matrix products, arithmetic and copies ran while one was open for 24% of the time, Pallas kernels for 0%

profile of v3, /device:TPU:1, one launch (start us, length us, event | category | flops | bytes accessed | tf_op | source)
XLA Modules:
  0.0 305.9 jit_solution(1681413815785157125)
XLA Ops:
  7.2 3.5 %fusion.111 = (f32[1,1,256,512]{3,2,1,0:T(8,128)}, f32[1,1,256,512]{3,2,1,0:T(8,128)}, f32[1,1,256,512]{3,2,1,0:T(8,128)}, f32[1,1,256,512]{3,2,1,0:T(8,128)}, f...) fusion(f32[1,7,256,512]{3,2,1,0:T(8,128)} %param.15), kind=kLoop, calls=%fused_computation.323 | loop fusion | bytes 6291456 | tf_op jit(solution)/shard_map/slice | solution.py:86
  15.6 20.6 %all-to-all-start = ((f32[1,128,1280]{2,0,1:T(1,128)}), f32[1,128,1280]{2,0,1:T(1,128)S(1)}, u32[]{:S(2)}, u32[]{:S(2)}) async-start(f32[1,128,1280]{2,0,1:T(1,128)} %pad_maximum_fusion.7), calls=%async_computation | async-start | bytes 1310720 | tf_op jit(solution)/shard_map/all_to_all | solution.py:42
  40.5 34.0 %all-to-all-done = f32[1,128,1280]{2,0,1:T(1,128)S(1)} async-done(((f32[1,128,1280]{2,0,1:T(1,128)}), f32[1,128,1280]{2,0,1:T(1,128)S(1)}, u32[]{:S(2)}, u32[]{:S(2)}) %all-to-all-start) | async-done | bytes 655392 | tf_op jit(solution)/shard_map/all_to_all | solution.py:42
  78.8 4.4 %collective-permute-start.2 = (f32[256,128]{1,0:T(8,128)S(1)}, f32[256,128]{1,0:T(8,128)S(1)}, u32[]{:S(2)}, u32[]{:S(2)}) collective-permute-start(f32[256,128]{1,0:T(8,128)S(1)} %get-tuple-element.76), channel_id=1, source_target_pairs={{0,3},{1,0},{2,1},{3,2},{4,7},{5,4},{6,5},{7,6},{8,11},{9,8},{10,9... | collective-permute-start | bytes 393224 | tf_op jit(solution)/shard_map/ppermute | solution.py:18
  83.2 2.4 collective-permute-start.1
  85.6 2.5 collective-permute-start
  88.8 5.3 %collective-permute-done.1 = f32[256,128]{1,0:T(8,128)S(1)} collective-permute-done((f32[256,128]{1,0:T(8,128)S(1)}, f32[256,128]{1,0:T(8,128)S(1)}, u32[]{:S(2)}, u32[]{:S(2)}) %collective-permute-start.1) | collective-permute-done | bytes 131104 | tf_op jit(solution)/shard_map/ppermute | solution.py:18
  94.1 4.7 %collective-permute-done = f32[256,128]{1,0:T(8,128)S(1)} collective-permute-done((f32[256,128]{1,0:T(8,128)S(1)}, f32[256,128]{1,0:T(8,128)S(1)}, u32[]{:S(2)}, u32[]{:S(2)}) %collective-permute-start) | collective-permute-done | bytes 131104 | tf_op jit(solution)/shard_map/ppermute | solution.py:18
  98.8 3.3 %collective-permute-start.5 = (f32[256,128]{1,0:T(8,128)S(1)}, f32[256,128]{1,0:T(8,128)S(1)}, u32[]{:S(2)}, u32[]{:S(2)}) collective-permute-start(f32[256,128]{1,0:T(8,128)S(1)} %fusion.62), channel_id=1, source_target_pairs={{0,3},{1,0},{2,1},{3,2},{4,7},{5,4},{6,5},{7,6},{8,11},{9,8},{10,9... | collective-permute-start | bytes 393224 | tf_op jit(solution)/shard_map/ppermute | solution.py:18
  109.3 3.2 %collective-permute-done.3 = f32[256,128]{1,0:T(8,128)S(1)} collective-permute-done((f32[256,128]{1,0:T(8,128)S(1)}, f32[256,128]{1,0:T(8,128)S(1)}, u32[]{:S(2)}, u32[]{:S(2)}) %collective-permute-start.3) | collective-permute-done | bytes 131104 | tf_op jit(solution)/shard_map/ppermute | solution.py:18
  113.3 4.3 %collective-permute-start.6 = (f32[1024,128]{1,0:T(8,128)S(1)}, f32[1024,128]{1,0:T(8,128)S(1)}, u32[]{:S(2)}, u32[]{:S(2)}) collective-permute-start(f32[1024,128]{1,0:T(8,128)S(1)} %bitcast_select_fusion), channel_id=1, source_target_pairs={{0,4},{4,0},{8,12},{12,8},{16,20},{20,16},{24,28},{28,24},{32,36},... | collective-permute-start | bytes 1572872 | tf_op jit(solution)/shard_map/ppermute | solution.py:12
  124.7 3.5 %collective-permute-start.7 = (f32[512,128]{1,0:T(8,128)S(1)}, f32[512,128]{1,0:T(8,128)S(1)}, u32[]{:S(2)}, u32[]{:S(2)}) collective-permute-start(f32[512,128]{1,0:T(8,128)S(1)} %select_subtract_fusion.11), channel_id=1, source_target_pairs={{0,8},{4,12},{8,0},{12,4},{16,24},{20,28},{24,16},{28,20},{32,40},... | collective-permute-start | bytes 786440 | tf_op jit(solution)/shard_map/ppermute | solution.py:12
  131.6 2.6 collective-permute-done.7
  134.3 3.0 collective-permute-start.8
  144.0 3.2 %collective-permute-start.9 = (f32[512,128]{1,0:T(8,128)S(1)}, f32[512,128]{1,0:T(8,128)S(1)}, u32[]{:S(2)}, u32[]{:S(2)}) collective-permute-start(f32[512,128]{1,0:T(8,128)S(1)} %select_subtract_fusion.9), channel_id=1, source_target_pairs={{0,16},{4,20},{8,24},{12,28},{16,0},{20,4},{24,8},{28,12},{32,48},... | collective-permute-start | bytes 786440 | tf_op jit(solution)/shard_map/ppermute | solution.py:12
  150.6 9.4 %collective-permute-done.9 = f32[512,128]{1,0:T(8,128)S(1)} collective-permute-done((f32[512,128]{1,0:T(8,128)S(1)}, f32[512,128]{1,0:T(8,128)S(1)}, u32[]{:S(2)}, u32[]{:S(2)}) %collective-permute-start.9) | collective-permute-done | bytes 262176 | tf_op jit(solution)/shard_map/ppermute | solution.py:12
  159.9 3.1 %collective-permute-start.10 = (f32[512,128]{1,0:T(8,128)S(1)}, f32[512,128]{1,0:T(8,128)S(1)}, u32[]{:S(2)}, u32[]{:S(2)}) collective-permute-start(f32[512,128]{1,0:T(8,128)S(1)} %collective-permute-done.9), channel_id=1, source_target_pairs={{0,4},{4,0},{8,12},{12,8},{16,20},{20,16},{24,28},{28,24},{32,36},... | collective-permute-start | bytes 786440 | tf_op jit(solution)/shard_map/ppermute | solution.py:12
  169.8 4.0 %collective-permute-start.11 = (f32[512,128]{1,0:T(8,128)S(1)}, f32[512,128]{1,0:T(8,128)S(1)}, u32[]{:S(2)}, u32[]{:S(2)}) collective-permute-start(f32[512,128]{1,0:T(8,128)S(1)} %select_subtract_fusion.7), channel_id=1, source_target_pairs={{0,32},{4,36},{8,40},{12,44},{16,48},{20,52},{24,56},{28,60},{32,0... | collective-permute-start | bytes 786440 | tf_op jit(solution)/shard_map/ppermute | solution.py:12
  177.2 22.5 %collective-permute-done.11 = f32[512,128]{1,0:T(8,128)S(1)} collective-permute-done((f32[512,128]{1,0:T(8,128)S(1)}, f32[512,128]{1,0:T(8,128)S(1)}, u32[]{:S(2)}, u32[]{:S(2)}) %collective-permute-start.11) | collective-permute-done | bytes 262176 | tf_op jit(solution)/shard_map/ppermute | solution.py:12
  207.1 2.5 select_subtract_fusion.5
  209.5 5.2 %collective-permute-start.13 = (f32[512,128]{1,0:T(8,128)S(1)}, f32[512,128]{1,0:T(8,128)}, u32[]{:S(2)}, u32[]{:S(2)}) collective-permute-start(f32[512,128]{1,0:T(8,128)S(1)} %select_subtract_fusion.5), channel_id=1, source_target_pairs={{0,64},{4,68},{8,72},{12,76},{16,80},{20,84},{24,88},{28,92},{32,9... | collective-permute-start | bytes 786440 | tf_op jit(solution)/shard_map/ppermute | solution.py:12
  218.7 21.2 %collective-permute-done.13 = f32[512,128]{1,0:T(8,128)} collective-permute-done((f32[512,128]{1,0:T(8,128)S(1)}, f32[512,128]{1,0:T(8,128)}, u32[]{:S(2)}, u32[]{:S(2)}) %collective-permute-start.13) | collective-permute-done | bytes 262176 | tf_op jit(solution)/shard_map/ppermute | solution.py:12
  239.9 2.6 collective-permute-start.14
  249.6 2.5 select_subtract_fusion.3
  255.7 2.5 select_subtract_fusion.2
  258.2 3.4 %collective-permute-done.15 = f32[512,128]{1,0:T(8,128)} collective-permute-done((f32[512,128]{1,0:T(8,128)S(1)}, f32[512,128]{1,0:T(8,128)}, u32[]{:S(2)}, u32[]{:S(2)}) %collective-permute-start.15) | collective-permute-done | bytes 262176 | tf_op jit(solution)/shard_map/ppermute | solution.py:12
  261.6 3.1 %collective-permute-start.16 = (f32[512,128]{1,0:T(8,128)}, f32[512,128]{1,0:T(8,128)S(1)}, u32[]{:S(2)}, u32[]{:S(2)}) collective-permute-start(f32[512,128]{1,0:T(8,128)} %collective-permute-done.15), channel_id=1, source_target_pairs={{0,4},{4,0},{8,12},{12,8},{16,20},{20,16},{24,28},{28,24},{32,36},... | collective-permute-start | bytes 786440 | tf_op jit(solution)/shard_map/ppermute | solution.py:12
  272.0 3.2 %select_subtract_fusion.1 = f32[512,128]{1,0:T(8,128)} fusion(f32[512,128]{1,0:T(8,128)} %gather_fusion.23, pred[512]{0:T(512)(128)(4,1)S(1)} %get-tuple-element.113, f32[1,1,1024,512]{3,2,1,0:T(8,128)} %all-gather.23.cloned.1.call-done, s32[]{:T(128)S(6)} %select_n.417, f32[512,128]{1,0:T(8,128)} %gather_fusion.25, f32[512,128]{1,0:T(8,128)} %gather_fusion.24, ...), kind=kOutput, calls=%fused_computation.101 | convolution fusion | flops 402980864 | bytes 2098692 | tf_op jit(solution)/shard_map/dot_general | solution.py:124
  279.8 3.2 %select_subtract_fusion = f32[512,128]{1,0:T(8,128)} fusion(f32[512,128]{1,0:T(8,128)} %gather_fusion.26, pred[512]{0:T(512)(128)(4,1)S(1)} %get-tuple-element.21, f32[1,1,1024,512]{3,2,1,0:T(8,128)} %all-gather.23.cloned.1.call-done, s32[]{:T(128)S(6)} %select_n.420, f32[512,128]{1,0:T(8,128)} %gather_fusion.25, f32[512,128]{1,0:T(8,128)} %gather_fusion.24, ...), kind=kOutput, calls=%fused_computation.99 | convolution fusion | flops 402980864 | bytes 2098692 | tf_op jit(solution)/shard_map/dot_general | solution.py:124
  283.0 3.5 %collective-permute-done.17 = f32[512,128]{1,0:T(8,128)} collective-permute-done((f32[512,128]{1,0:T(8,128)}, f32[512,128]{1,0:T(8,128)}, u32[]{:S(2)}, u32[]{:S(2)}) %collective-permute-start.17) | collective-permute-done | bytes 262176 | tf_op jit(solution)/shard_map/ppermute | solution.py:12
  286.5 3.1 %collective-permute-start.18 = (f32[512,128]{1,0:T(8,128)}, f32[512,128]{1,0:T(8,128)}, u32[]{:S(2)}, u32[]{:S(2)}) collective-permute-start(f32[512,128]{1,0:T(8,128)} %collective-permute-done.17), channel_id=1, source_target_pairs={{0,4},{4,0},{8,12},{12,8},{16,20},{20,16},{24,28},{28,24},{32,36},... | collective-permute-start | bytes 786440 | tf_op jit(solution)/shard_map/ppermute | solution.py:12
  296.4 2.8 fusion.54
  (204 shorter events, 92.3 us)
Async XLA Ops:
  7.2 115.2 %all-gather.13.cloned.1.call-start = ((), (), s32[]{:S(2)}) async-start(), calls=%async_computation.1 | async-start | bytes 2621440 | tf_op jit(solution)/shard_map/all_gather | solution.py:86
  10.8 130.9 %all-gather.15.cloned.1.call-start = ((), (), s32[]{:S(2)}) async-start(), calls=%async_computation.2 | async-start | bytes 2621440 | tf_op jit(solution)/shard_map/all_gather | solution.py:86
  11.5 155.9 %all-gather.17.cloned.1.call-start = ((), (), s32[]{:S(2)}) async-start(), calls=%async_computation.3 | async-start | bytes 2621440 | tf_op jit(solution)/shard_map/all_gather | solution.py:86
  12.2 194.8 %all-gather.19.cloned.1.call-start = ((), (), s32[]{:S(2)}) async-start(), calls=%async_computation.4 | async-start | bytes 2621440 | tf_op jit(solution)/shard_map/all_gather | solution.py:86
  12.8 236.7 %all-gather.21.cloned.1.call-start = ((), (), s32[]{:S(2)}) async-start(), calls=%async_computation.5 | async-start | bytes 2621440 | tf_op jit(solution)/shard_map/all_gather | solution.py:86
  13.6 23.2 %copy-start.18 = (s32[1,32]{1,0:T(1,128)S(1)}, s32[1,32]{1,0:T(1,128)}, u32[]{:S(2)}) copy-start(s32[1,32]{1,0:T(1,128)} %param.13) | copy-start | bytes 388
  13.6 23.3 %copy-start.5 = (s32[1,7,2,1024]{3,2,1,0:T(2,128)S(1)}, s32[1,7,2,1024]{3,2,1,0:T(2,128)}, u32[]{:S(2)}) copy-start(s32[1,7,2,1024]{3,2,1,0:T(2,128)} %param.14) | copy-start | bytes 172036
  14.1 25.2 %copy-start.1 = (f32[1,32,4096]{2,1,0:T(8,128)S(1)}, f32[1,32,4096]{2,1,0:T(8,128)}, u32[]{:S(2)}) copy-start(f32[1,32,4096]{2,1,0:T(8,128)} %param.11) | copy-start | bytes 1572868
  15.6 58.9 %all-to-all-start = ((f32[1,128,1280]{2,0,1:T(1,128)}), f32[1,128,1280]{2,0,1:T(1,128)S(1)}, u32[]{:S(2)}, u32[]{:S(2)}) async-start(f32[1,128,1280]{2,0,1:T(1,128)} %pad_maximum_fusion.7), calls=%async_computation | async-start | bytes 1310720 | tf_op jit(solution)/shard_map/all_to_all | solution.py:42
  36.1 235.9 %all-gather.23.cloned.1.call-start = ((), (), s32[]{:S(2)}) async-start(), calls=%async_computation.6 | async-start | bytes 2621440 | tf_op jit(solution)/shard_map/all_gather | solution.py:86
  78.8 10.0 %collective-permute-start.2 = (f32[256,128]{1,0:T(8,128)S(1)}, f32[256,128]{1,0:T(8,128)S(1)}, u32[]{:S(2)}, u32[]{:S(2)}) collective-permute-start(f32[256,128]{1,0:T(8,128)S(1)} %get-tuple-element.76), channel_id=1, source_target_pairs={{0,3},{1,0},{2,1},{3,2},{4,7},{5,4},{6,5},{7,6},{8,11},{9,8},{10,9... | collective-permute-start | bytes 393224 | tf_op jit(solution)/shard_map/ppermute | solution.py:18
  83.2 11.0 %collective-permute-start.1 = (f32[256,128]{1,0:T(8,128)S(1)}, f32[256,128]{1,0:T(8,128)S(1)}, u32[]{:S(2)}, u32[]{:S(2)}) collective-permute-start(f32[256,128]{1,0:T(8,128)S(1)} %get-tuple-element.77), channel_id=1, source_target_pairs={{0,2},{1,3},{2,0},{3,1},{4,6},{5,7},{6,4},{7,5},{8,10},{9,11},{10,... | collective-permute-start | bytes 393224 | tf_op jit(solution)/shard_map/ppermute | solution.py:18
  85.6 13.2 %collective-permute-start = (f32[256,128]{1,0:T(8,128)S(1)}, f32[256,128]{1,0:T(8,128)S(1)}, u32[]{:S(2)}, u32[]{:S(2)}) collective-permute-start(f32[256,128]{1,0:T(8,128)S(1)} %get-tuple-element.75), channel_id=1, source_target_pairs={{0,1},{1,2},{2,3},{3,0},{4,5},{5,6},{6,7},{7,4},{8,9},{9,10},{10,1... | collective-permute-start | bytes 393224 | tf_op jit(solution)/shard_map/ppermute | solution.py:18
  98.8 13.7 %copy-start.3 = (f32[256,128]{1,0:T(8,128)}, f32[256,128]{1,0:T(8,128)S(1)}, u32[]{:S(2)}) copy-start(f32[256,128]{1,0:T(8,128)S(1)} %fusion.62) | copy-start | bytes 393220
  98.8 8.5 %collective-permute-start.5 = (f32[256,128]{1,0:T(8,128)S(1)}, f32[256,128]{1,0:T(8,128)S(1)}, u32[]{:S(2)}, u32[]{:S(2)}) collective-permute-start(f32[256,128]{1,0:T(8,128)S(1)} %fusion.62), channel_id=1, source_target_pairs={{0,3},{1,0},{2,1},{3,2},{4,7},{5,4},{6,5},{7,6},{8,11},{9,8},{10,9... | collective-permute-start | bytes 393224 | tf_op jit(solution)/shard_map/ppermute | solution.py:18
  102.1 7.2 %collective-permute-start.4 = (f32[256,128]{1,0:T(8,128)S(1)}, f32[256,128]{1,0:T(8,128)S(1)}, u32[]{:S(2)}, u32[]{:S(2)}) collective-permute-start(f32[256,128]{1,0:T(8,128)S(1)} %fusion.62), channel_id=1, source_target_pairs={{0,2},{1,3},{2,0},{3,1},{4,6},{5,7},{6,4},{7,5},{8,10},{9,11},{10,... | collective-permute-start | bytes 393224 | tf_op jit(solution)/shard_map/ppermute | solution.py:18
  104.3 8.2 %collective-permute-start.3 = (f32[256,128]{1,0:T(8,128)S(1)}, f32[256,128]{1,0:T(8,128)S(1)}, u32[]{:S(2)}, u32[]{:S(2)}) collective-permute-start(f32[256,128]{1,0:T(8,128)S(1)} %fusion.62), channel_id=1, source_target_pairs={{0,1},{1,2},{2,3},{3,0},{4,5},{5,6},{6,7},{7,4},{8,9},{9,10},{10,1... | collective-permute-start | bytes 393224 | tf_op jit(solution)/shard_map/ppermute | solution.py:18
  113.3 5.8 %collective-permute-start.6 = (f32[1024,128]{1,0:T(8,128)S(1)}, f32[1024,128]{1,0:T(8,128)S(1)}, u32[]{:S(2)}, u32[]{:S(2)}) collective-permute-start(f32[1024,128]{1,0:T(8,128)S(1)} %bitcast_select_fusion), channel_id=1, source_target_pairs={{0,4},{4,0},{8,12},{12,8},{16,20},{20,16},{24,28},{28,24},{32,36},... | collective-permute-start | bytes 1572872 | tf_op jit(solution)/shard_map/ppermute | solution.py:12
  124.7 9.5 %collective-permute-start.7 = (f32[512,128]{1,0:T(8,128)S(1)}, f32[512,128]{1,0:T(8,128)S(1)}, u32[]{:S(2)}, u32[]{:S(2)}) collective-permute-start(f32[512,128]{1,0:T(8,128)S(1)} %select_subtract_fusion.11), channel_id=1, source_target_pairs={{0,8},{4,12},{8,0},{12,4},{16,24},{20,28},{24,16},{28,20},{32,40},... | collective-permute-start | bytes 786440 | tf_op jit(solution)/shard_map/ppermute | solution.py:12
  134.3 4.1 %collective-permute-start.8 = (f32[512,128]{1,0:T(8,128)S(1)}, f32[512,128]{1,0:T(8,128)S(1)}, u32[]{:S(2)}, u32[]{:S(2)}) collective-permute-start(f32[512,128]{1,0:T(8,128)S(1)} %collective-permute-done.7), channel_id=1, source_target_pairs={{0,4},{4,0},{8,12},{12,8},{16,20},{20,16},{24,28},{28,24},{32,36},... | collective-permute-start | bytes 786440 | tf_op jit(solution)/shard_map/ppermute | solution.py:12
  144.0 15.9 %collective-permute-start.9 = (f32[512,128]{1,0:T(8,128)S(1)}, f32[512,128]{1,0:T(8,128)S(1)}, u32[]{:S(2)}, u32[]{:S(2)}) collective-permute-start(f32[512,128]{1,0:T(8,128)S(1)} %select_subtract_fusion.9), channel_id=1, source_target_pairs={{0,16},{4,20},{8,24},{12,28},{16,0},{20,4},{24,8},{28,12},{32,48},... | collective-permute-start | bytes 786440 | tf_op jit(solution)/shard_map/ppermute | solution.py:12
  159.9 4.2 %collective-permute-start.10 = (f32[512,128]{1,0:T(8,128)S(1)}, f32[512,128]{1,0:T(8,128)S(1)}, u32[]{:S(2)}, u32[]{:S(2)}) collective-permute-start(f32[512,128]{1,0:T(8,128)S(1)} %collective-permute-done.9), channel_id=1, source_target_pairs={{0,4},{4,0},{8,12},{12,8},{16,20},{20,16},{24,28},{28,24},{32,36},... | collective-permute-start | bytes 786440 | tf_op jit(solution)/shard_map/ppermute | solution.py:12
  169.8 29.9 %collective-permute-start.11 = (f32[512,128]{1,0:T(8,128)S(1)}, f32[512,128]{1,0:T(8,128)S(1)}, u32[]{:S(2)}, u32[]{:S(2)}) collective-permute-start(f32[512,128]{1,0:T(8,128)S(1)} %select_subtract_fusion.7), channel_id=1, source_target_pairs={{0,32},{4,36},{8,40},{12,44},{16,48},{20,52},{24,56},{28,60},{32,0... | collective-permute-start | bytes 786440 | tf_op jit(solution)/shard_map/ppermute | solution.py:12
  199.7 3.5 %collective-permute-start.12 = (f32[512,128]{1,0:T(8,128)S(1)}, f32[512,128]{1,0:T(8,128)S(1)}, u32[]{:S(2)}, u32[]{:S(2)}) collective-permute-start(f32[512,128]{1,0:T(8,128)S(1)} %collective-permute-done.11), channel_id=1, source_target_pairs={{0,4},{4,0},{8,12},{12,8},{16,20},{20,16},{24,28},{28,24},{32,36},... | collective-permute-start | bytes 786440 | tf_op jit(solution)/shard_map/ppermute | solution.py:12
  207.0 9.3 %copy-start.12 = (pred[512]{0:T(512)(128)(4,1)S(1)}, pred[512]{0:T(512)(128)(4,1)}, u32[]{:S(2)}) copy-start(pred[512]{0:T(512)(128)(4,1)} %get-tuple-element.37) | copy-start | bytes 1540
  209.5 30.4 %collective-permute-start.13 = (f32[512,128]{1,0:T(8,128)S(1)}, f32[512,128]{1,0:T(8,128)}, u32[]{:S(2)}, u32[]{:S(2)}) collective-permute-start(f32[512,128]{1,0:T(8,128)S(1)} %select_subtract_fusion.5), channel_id=1, source_target_pairs={{0,64},{4,68},{8,72},{12,76},{16,80},{20,84},{24,88},{28,92},{32,9... | collective-permute-start | bytes 786440 | tf_op jit(solution)/shard_map/ppermute | solution.py:12
  239.9 3.7 %collective-permute-start.14 = (f32[512,128]{1,0:T(8,128)}, f32[512,128]{1,0:T(8,128)S(1)}, u32[]{:S(2)}, u32[]{:S(2)}) collective-permute-start(f32[512,128]{1,0:T(8,128)} %collective-permute-done.13), channel_id=1, source_target_pairs={{0,4},{4,0},{8,12},{12,8},{16,20},{20,16},{24,28},{28,24},{32,36},... | collective-permute-start | bytes 786440 | tf_op jit(solution)/shard_map/ppermute | solution.py:12
  252.1 9.5 %collective-permute-start.15 = (f32[512,128]{1,0:T(8,128)S(1)}, f32[512,128]{1,0:T(8,128)}, u32[]{:S(2)}, u32[]{:S(2)}) collective-permute-start(f32[512,128]{1,0:T(8,128)S(1)} %select_subtract_fusion.3), channel_id=1, source_target_pairs={{0,128},{4,132},{8,136},{12,140},{16,144},{20,148},{24,152},{28,15... | collective-permute-start | bytes 786440 | tf_op jit(solution)/shard_map/ppermute | solution.py:12
  258.2 7.9 %copy-start = (f32[512,128]{1,0:T(8,128)}, f32[512,128]{1,0:T(8,128)S(1)}, u32[]{:S(2)}) copy-start(f32[512,128]{1,0:T(8,128)S(1)} %select_subtract_fusion.2) | copy-start | bytes 786436
  261.6 4.5 %collective-permute-start.16 = (f32[512,128]{1,0:T(8,128)}, f32[512,128]{1,0:T(8,128)S(1)}, u32[]{:S(2)}, u32[]{:S(2)}) collective-permute-start(f32[512,128]{1,0:T(8,128)} %collective-permute-done.15), channel_id=1, source_target_pairs={{0,4},{4,0},{8,12},{12,8},{16,20},{20,16},{24,28},{28,24},{32,36},... | collective-permute-start | bytes 786440 | tf_op jit(solution)/shard_map/ppermute | solution.py:12
  275.3 11.2 %collective-permute-start.17 = (f32[512,128]{1,0:T(8,128)}, f32[512,128]{1,0:T(8,128)}, u32[]{:S(2)}, u32[]{:S(2)}) collective-permute-start(f32[512,128]{1,0:T(8,128)} %select_subtract_fusion.1), channel_id=1, source_target_pairs={{0,256},{4,260},{8,264},{12,268},{16,272},{20,276},{24,280},{28,28... | collective-permute-start | bytes 786440 | tf_op jit(solution)/shard_map/ppermute | solution.py:12
  286.5 4.6 %collective-permute-start.18 = (f32[512,128]{1,0:T(8,128)}, f32[512,128]{1,0:T(8,128)}, u32[]{:S(2)}, u32[]{:S(2)}) collective-permute-start(f32[512,128]{1,0:T(8,128)} %collective-permute-done.17), channel_id=1, source_target_pairs={{0,4},{4,0},{8,12},{12,8},{16,20},{20,16},{24,28},{28,24},{32,36},... | collective-permute-start | bytes 786440 | tf_op jit(solution)/shard_map/ppermute | solution.py:12
  (13 other events, 43.7 us)
Sparse Core Ops, SparseCore 0:
  10.9 43.7 all-gather.12
  56.8 44.2 all-gather.14
  103.2 42.8 all-gather.16
  148.0 38.5 all-gather.18
  188.6 38.5 all-gather.20
  229.2 38.5 all-gather.22

commit v4 on v3

--- a/solution.py
+++ b/solution.py
@@ -53,7 +53,7 @@
     pieces = jnp.take(
         interior.reshape(local_rows // block_size, block_size, num_cases), local_cols, axis=0
     )
-    products = jnp.einsum("krc,kcn->krn", blocks, pieces, precision=lax.Precision.HIGHEST)
+    products = jnp.einsum("krc,kcn->krn", blocks, pieces, precision=lax.Precision.HIGH)
     row_blocks = full_rows // block_size
     onehot = (block_rows[0][None, :] == jnp.arange(row_blocks, dtype=jnp.int32)[:, None]).astype(
         jnp.float32
@@ -61,7 +61,7 @@
     partial_value = jnp.dot(
         onehot,
         products.reshape(block_count, block_size * num_cases),
-        precision=lax.Precision.HIGHEST,
+        precision=lax.Precision.HIGH,
     )
     partial_value = partial_value.reshape(full_rows, num_cases)
     embedded = lax.dynamic_update_slice(
@@ -122,7 +122,7 @@
             else:
                 part = lax.dynamic_slice_in_dim(matrix, begin, count, 0)
             return jnp.take(stacked, index, axis=0) - jnp.dot(
-                part, shared, precision=lax.Precision.HIGHEST
+                part, shared, precision=lax.Precision.HIGH
             )
 
         is_node = slot % (2 * half) == half

time: 307 us -> 304 us (level)
  matrix products: 36 us -> 30.9 us
    dot_general x14, matrix products: 34.9 us -> 30.1 us  [the longest x13 28.7 us: rows_of(): jnp.dot(part, shared, precision=lax.Precision.HIGH)]
  transfers between devices with their start and end apart: 26 -> 26, of which waited for: 18 -> 18; matrix products, arithmetic and copies ran while one was open for 24% -> 23% of each run, Pallas kernels for 0% -> 0%
where the time goes in v4:
time: 304 us; the launch traced here: 303 us
  waiting for transfers between devices  124 us (41%)
  starting transfers between devices  79.9 us (26%)
  local copies, waits for them, and re-layouts  41.6 us (14%)
  matrix products  30.9 us (10%)
  between operations  15.6 us (5%)
  other arithmetic  10.8 us (4%)
    ppermute x13, waiting for transfers between devices, from_partner(): return lax.ppermute(value, axis, pairs)  72.8 us
    ppermute x13, starting transfers between devices, from_partner(): return lax.ppermute(value, axis, pairs)  42.1 us
    all_to_all x1, waiting for transfers between devices, on_device(): lax.all_to_all(joined, 'sub', split_axis=1, concat_axis=0, tiled=True)  34 us
    dot_general x13, matrix products, rows_of(): jnp.dot(part, shared, precision=lax.Precision.HIGH)  28.7 us
    all_to_all x1, starting transfers between devices, on_device(): lax.all_to_all(joined, 'sub', split_axis=1, concat_axis=0, tiled=True)  20.6 us
    ppermute x6, starting transfers between devices, shifted(): return lax.ppermute(value, axis, pairs)  17 us
    gather x13, local copies, waits for them, and re-layouts, rows_of(): jnp.take(stacked, index, axis=0)  16.8 us
    ppermute x6, waiting for transfers between devices, shifted(): return lax.ppermute(value, axis, pairs)  14.5 us
  transfers between devices with their start and end apart: 26, of which 18 were waited for; matrix products, arithmetic and copies ran while one was open for 23% of the time, Pallas kernels for 0%

profile of v4, /device:TPU:1, one launch (start us, length us, event | category | flops | bytes accessed | tf_op | source)
XLA Modules:
  0.0 303.0 jit_solution(15492360071754767232)
XLA Ops:
  7.2 3.5 %fusion.111 = (f32[1,1,256,512]{3,2,1,0:T(8,128)}, f32[1,1,256,512]{3,2,1,0:T(8,128)}, f32[1,1,256,512]{3,2,1,0:T(8,128)}, f32[1,1,256,512]{3,2,1,0:T(8,128)}, f...) fusion(f32[1,7,256,512]{3,2,1,0:T(8,128)} %param.15), kind=kLoop, calls=%fused_computation.323 | loop fusion | bytes 6291456 | tf_op jit(solution)/shard_map/slice | solution.py:86
  15.6 20.6 %all-to-all-start = ((f32[1,128,1280]{2,0,1:T(1,128)}), f32[1,128,1280]{2,0,1:T(1,128)S(1)}, u32[]{:S(2)}, u32[]{:S(2)}) async-start(f32[1,128,1280]{2,0,1:T(1,128)} %pad_maximum_fusion.7), calls=%async_computation | async-start | bytes 1310720 | tf_op jit(solution)/shard_map/all_to_all | solution.py:42
  40.5 34.0 %all-to-all-done = f32[1,128,1280]{2,0,1:T(1,128)S(1)} async-done(((f32[1,128,1280]{2,0,1:T(1,128)}), f32[1,128,1280]{2,0,1:T(1,128)S(1)}, u32[]{:S(2)}, u32[]{:S(2)}) %all-to-all-start) | async-done | bytes 655392 | tf_op jit(solution)/shard_map/all_to_all | solution.py:42
  78.1 4.4 %collective-permute-start.2 = (f32[256,128]{1,0:T(8,128)S(1)}, f32[256,128]{1,0:T(8,128)S(1)}, u32[]{:S(2)}, u32[]{:S(2)}) collective-permute-start(f32[256,128]{1,0:T(8,128)S(1)} %get-tuple-element.76), channel_id=1, source_target_pairs={{0,3},{1,0},{2,1},{3,2},{4,7},{5,4},{6,5},{7,6},{8,11},{9,8},{10,9... | collective-permute-start | bytes 393224 | tf_op jit(solution)/shard_map/ppermute | solution.py:18
  82.5 2.4 collective-permute-start.1
  84.9 2.5 collective-permute-start
  88.1 5.3 %collective-permute-done.1 = f32[256,128]{1,0:T(8,128)S(1)} collective-permute-done((f32[256,128]{1,0:T(8,128)S(1)}, f32[256,128]{1,0:T(8,128)S(1)}, u32[]{:S(2)}, u32[]{:S(2)}) %collective-permute-start.1) | collective-permute-done | bytes 131104 | tf_op jit(solution)/shard_map/ppermute | solution.py:18
  93.4 4.7 %collective-permute-done = f32[256,128]{1,0:T(8,128)S(1)} collective-permute-done((f32[256,128]{1,0:T(8,128)S(1)}, f32[256,128]{1,0:T(8,128)S(1)}, u32[]{:S(2)}, u32[]{:S(2)}) %collective-permute-start) | collective-permute-done | bytes 131104 | tf_op jit(solution)/shard_map/ppermute | solution.py:18
  98.1 3.3 %collective-permute-start.5 = (f32[256,128]{1,0:T(8,128)S(1)}, f32[256,128]{1,0:T(8,128)S(1)}, u32[]{:S(2)}, u32[]{:S(2)}) collective-permute-start(f32[256,128]{1,0:T(8,128)S(1)} %fusion.62), channel_id=1, source_target_pairs={{0,3},{1,0},{2,1},{3,2},{4,7},{5,4},{6,5},{7,6},{8,11},{9,8},{10,9... | collective-permute-start | bytes 393224 | tf_op jit(solution)/shard_map/ppermute | solution.py:18
  108.6 2.5 collective-permute-done.3
  111.9 5.6 %collective-permute-start.6 = (f32[1024,128]{1,0:T(8,128)S(1)}, f32[1024,128]{1,0:T(8,128)S(1)}, u32[]{:S(2)}, u32[]{:S(2)}) collective-permute-start(f32[1024,128]{1,0:T(8,128)S(1)} %bitcast_select_fusion), channel_id=1, source_target_pairs={{0,4},{4,0},{8,12},{12,8},{16,20},{20,16},{24,28},{28,24},{32,36},... | collective-permute-start | bytes 1572872 | tf_op jit(solution)/shard_map/ppermute | solution.py:12
  124.2 3.0 collective-permute-start.7
  130.3 3.5 %collective-permute-done.7 = f32[512,128]{1,0:T(8,128)S(1)} collective-permute-done((f32[512,128]{1,0:T(8,128)S(1)}, f32[512,128]{1,0:T(8,128)S(1)}, u32[]{:S(2)}, u32[]{:S(2)}) %collective-permute-start.7) | collective-permute-done | bytes 262176 | tf_op jit(solution)/shard_map/ppermute | solution.py:12
  133.8 3.2 %collective-permute-start.8 = (f32[512,128]{1,0:T(8,128)S(1)}, f32[512,128]{1,0:T(8,128)S(1)}, u32[]{:S(2)}, u32[]{:S(2)}) collective-permute-start(f32[512,128]{1,0:T(8,128)S(1)} %collective-permute-done.7), channel_id=1, source_target_pairs={{0,4},{4,0},{8,12},{12,8},{16,20},{20,16},{24,28},{28,24},{32,36},... | collective-permute-start | bytes 786440 | tf_op jit(solution)/shard_map/ppermute | solution.py:12
  143.1 2.7 collective-permute-start.9
  148.9 10.1 %collective-permute-done.9 = f32[512,128]{1,0:T(8,128)S(1)} collective-permute-done((f32[512,128]{1,0:T(8,128)S(1)}, f32[512,128]{1,0:T(8,128)S(1)}, u32[]{:S(2)}, u32[]{:S(2)}) %collective-permute-start.9) | collective-permute-done | bytes 262176 | tf_op jit(solution)/shard_map/ppermute | solution.py:12
  159.0 3.1 %collective-permute-start.10 = (f32[512,128]{1,0:T(8,128)S(1)}, f32[512,128]{1,0:T(8,128)S(1)}, u32[]{:S(2)}, u32[]{:S(2)}) collective-permute-start(f32[512,128]{1,0:T(8,128)S(1)} %collective-permute-done.9), channel_id=1, source_target_pairs={{0,4},{4,0},{8,12},{12,8},{16,20},{20,16},{24,28},{28,24},{32,36},... | collective-permute-start | bytes 786440 | tf_op jit(solution)/shard_map/ppermute | solution.py:12
  168.6 3.3 %collective-permute-start.11 = (f32[512,128]{1,0:T(8,128)S(1)}, f32[512,128]{1,0:T(8,128)S(1)}, u32[]{:S(2)}, u32[]{:S(2)}) collective-permute-start(f32[512,128]{1,0:T(8,128)S(1)} %select_subtract_fusion.7), channel_id=1, source_target_pairs={{0,32},{4,36},{8,40},{12,44},{16,48},{20,52},{24,56},{28,60},{32,0... | collective-permute-start | bytes 786440 | tf_op jit(solution)/shard_map/ppermute | solution.py:12
  175.0 23.1 %collective-permute-done.11 = f32[512,128]{1,0:T(8,128)S(1)} collective-permute-done((f32[512,128]{1,0:T(8,128)S(1)}, f32[512,128]{1,0:T(8,128)S(1)}, u32[]{:S(2)}, u32[]{:S(2)}) %collective-permute-start.11) | collective-permute-done | bytes 262176 | tf_op jit(solution)/shard_map/ppermute | solution.py:12
  198.1 2.4 collective-permute-start.12
  207.6 5.3 %collective-permute-start.13 = (f32[512,128]{1,0:T(8,128)S(1)}, f32[512,128]{1,0:T(8,128)}, u32[]{:S(2)}, u32[]{:S(2)}) collective-permute-start(f32[512,128]{1,0:T(8,128)S(1)} %select_subtract_fusion.5), channel_id=1, source_target_pairs={{0,64},{4,68},{8,72},{12,76},{16,80},{20,84},{24,88},{28,92},{32,9... | collective-permute-start | bytes 786440 | tf_op jit(solution)/shard_map/ppermute | solution.py:12
  216.5 21.2 %collective-permute-done.13 = f32[512,128]{1,0:T(8,128)} collective-permute-done((f32[512,128]{1,0:T(8,128)S(1)}, f32[512,128]{1,0:T(8,128)}, u32[]{:S(2)}, u32[]{:S(2)}) %collective-permute-start.13) | collective-permute-done | bytes 262176 | tf_op jit(solution)/shard_map/ppermute | solution.py:12
  237.8 2.4 collective-permute-start.14
  247.4 2.3 select_subtract_fusion.3
  255.5 3.7 %collective-permute-done.15 = f32[512,128]{1,0:T(8,128)} collective-permute-done((f32[512,128]{1,0:T(8,128)S(1)}, f32[512,128]{1,0:T(8,128)}, u32[]{:S(2)}, u32[]{:S(2)}) %collective-permute-start.15) | collective-permute-done | bytes 262176 | tf_op jit(solution)/shard_map/ppermute | solution.py:12
  259.2 3.1 %collective-permute-start.16 = (f32[512,128]{1,0:T(8,128)}, f32[512,128]{1,0:T(8,128)S(1)}, u32[]{:S(2)}, u32[]{:S(2)}) collective-permute-start(f32[512,128]{1,0:T(8,128)} %collective-permute-done.15), channel_id=1, source_target_pairs={{0,4},{4,0},{8,12},{12,8},{16,20},{20,16},{24,28},{28,24},{32,36},... | collective-permute-start | bytes 786440 | tf_op jit(solution)/shard_map/ppermute | solution.py:12
  269.6 2.9 select_subtract_fusion.1
  272.5 3.0 collective-permute-start.17
  277.7 2.9 select_subtract_fusion
  280.6 3.1 %collective-permute-done.17 = f32[512,128]{1,0:T(8,128)} collective-permute-done((f32[512,128]{1,0:T(8,128)}, f32[512,128]{1,0:T(8,128)}, u32[]{:S(2)}, u32[]{:S(2)}) %collective-permute-start.17) | collective-permute-done | bytes 262176 | tf_op jit(solution)/shard_map/ppermute | solution.py:12
  283.7 3.1 %collective-permute-start.18 = (f32[512,128]{1,0:T(8,128)}, f32[512,128]{1,0:T(8,128)}, u32[]{:S(2)}, u32[]{:S(2)}) collective-permute-start(f32[512,128]{1,0:T(8,128)} %collective-permute-done.17), channel_id=1, source_target_pairs={{0,4},{4,0},{8,12},{12,8},{16,20},{20,16},{24,28},{28,24},{32,36},... | collective-permute-start | bytes 786440 | tf_op jit(solution)/shard_map/ppermute | solution.py:12
  293.6 2.6 fusion.54
  (204 shorter events, 88.8 us)
Async XLA Ops:
  7.2 115.1 %all-gather.13.cloned.1.call-start = ((), (), s32[]{:S(2)}) async-start(), calls=%async_computation.1 | async-start | bytes 2621440 | tf_op jit(solution)/shard_map/all_gather | solution.py:86
  10.8 130.4 %all-gather.15.cloned.1.call-start = ((), (), s32[]{:S(2)}) async-start(), calls=%async_computation.2 | async-start | bytes 2621440 | tf_op jit(solution)/shard_map/all_gather | solution.py:86
  11.5 155.0 %all-gather.17.cloned.1.call-start = ((), (), s32[]{:S(2)}) async-start(), calls=%async_computation.3 | async-start | bytes 2621440 | tf_op jit(solution)/shard_map/all_gather | solution.py:86
  12.2 193.2 %all-gather.19.cloned.1.call-start = ((), (), s32[]{:S(2)}) async-start(), calls=%async_computation.4 | async-start | bytes 2621440 | tf_op jit(solution)/shard_map/all_gather | solution.py:86
  12.8 234.6 %all-gather.21.cloned.1.call-start = ((), (), s32[]{:S(2)}) async-start(), calls=%async_computation.5 | async-start | bytes 2621440 | tf_op jit(solution)/shard_map/all_gather | solution.py:86
  13.6 23.2 %copy-start.18 = (s32[1,32]{1,0:T(1,128)S(1)}, s32[1,32]{1,0:T(1,128)}, u32[]{:S(2)}) copy-start(s32[1,32]{1,0:T(1,128)} %param.13) | copy-start | bytes 388
  13.6 23.3 %copy-start.5 = (s32[1,7,2,1024]{3,2,1,0:T(2,128)S(1)}, s32[1,7,2,1024]{3,2,1,0:T(2,128)}, u32[]{:S(2)}) copy-start(s32[1,7,2,1024]{3,2,1,0:T(2,128)} %param.14) | copy-start | bytes 172036
  14.1 25.2 %copy-start.1 = (f32[1,32,4096]{2,1,0:T(8,128)S(1)}, f32[1,32,4096]{2,1,0:T(8,128)}, u32[]{:S(2)}) copy-start(f32[1,32,4096]{2,1,0:T(8,128)} %param.11) | copy-start | bytes 1572868
  15.6 58.9 %all-to-all-start = ((f32[1,128,1280]{2,0,1:T(1,128)}), f32[1,128,1280]{2,0,1:T(1,128)S(1)}, u32[]{:S(2)}, u32[]{:S(2)}) async-start(f32[1,128,1280]{2,0,1:T(1,128)} %pad_maximum_fusion.7), calls=%async_computation | async-start | bytes 1310720 | tf_op jit(solution)/shard_map/all_to_all | solution.py:42
  36.1 233.5 %all-gather.23.cloned.1.call-start = ((), (), s32[]{:S(2)}) async-start(), calls=%async_computation.6 | async-start | bytes 2621440 | tf_op jit(solution)/shard_map/all_gather | solution.py:86
  78.1 10.0 %collective-permute-start.2 = (f32[256,128]{1,0:T(8,128)S(1)}, f32[256,128]{1,0:T(8,128)S(1)}, u32[]{:S(2)}, u32[]{:S(2)}) collective-permute-start(f32[256,128]{1,0:T(8,128)S(1)} %get-tuple-element.76), channel_id=1, source_target_pairs={{0,3},{1,0},{2,1},{3,2},{4,7},{5,4},{6,5},{7,6},{8,11},{9,8},{10,9... | collective-permute-start | bytes 393224 | tf_op jit(solution)/shard_map/ppermute | solution.py:18
  82.5 11.0 %collective-permute-start.1 = (f32[256,128]{1,0:T(8,128)S(1)}, f32[256,128]{1,0:T(8,128)S(1)}, u32[]{:S(2)}, u32[]{:S(2)}) collective-permute-start(f32[256,128]{1,0:T(8,128)S(1)} %get-tuple-element.77), channel_id=1, source_target_pairs={{0,2},{1,3},{2,0},{3,1},{4,6},{5,7},{6,4},{7,5},{8,10},{9,11},{10,... | collective-permute-start | bytes 393224 | tf_op jit(solution)/shard_map/ppermute | solution.py:18
  84.9 13.2 %collective-permute-start = (f32[256,128]{1,0:T(8,128)S(1)}, f32[256,128]{1,0:T(8,128)S(1)}, u32[]{:S(2)}, u32[]{:S(2)}) collective-permute-start(f32[256,128]{1,0:T(8,128)S(1)} %get-tuple-element.75), channel_id=1, source_target_pairs={{0,1},{1,2},{2,3},{3,0},{4,5},{5,6},{6,7},{7,4},{8,9},{9,10},{10,1... | collective-permute-start | bytes 393224 | tf_op jit(solution)/shard_map/ppermute | solution.py:18
  98.1 13.0 %copy-start.3 = (f32[256,128]{1,0:T(8,128)}, f32[256,128]{1,0:T(8,128)S(1)}, u32[]{:S(2)}) copy-start(f32[256,128]{1,0:T(8,128)S(1)} %fusion.62) | copy-start | bytes 393220
  98.1 8.5 %collective-permute-start.5 = (f32[256,128]{1,0:T(8,128)S(1)}, f32[256,128]{1,0:T(8,128)S(1)}, u32[]{:S(2)}, u32[]{:S(2)}) collective-permute-start(f32[256,128]{1,0:T(8,128)S(1)} %fusion.62), channel_id=1, source_target_pairs={{0,3},{1,0},{2,1},{3,2},{4,7},{5,4},{6,5},{7,6},{8,11},{9,8},{10,9... | collective-permute-start | bytes 393224 | tf_op jit(solution)/shard_map/ppermute | solution.py:18
  101.4 7.2 %collective-permute-start.4 = (f32[256,128]{1,0:T(8,128)S(1)}, f32[256,128]{1,0:T(8,128)S(1)}, u32[]{:S(2)}, u32[]{:S(2)}) collective-permute-start(f32[256,128]{1,0:T(8,128)S(1)} %fusion.62), channel_id=1, source_target_pairs={{0,2},{1,3},{2,0},{3,1},{4,6},{5,7},{6,4},{7,5},{8,10},{9,11},{10,... | collective-permute-start | bytes 393224 | tf_op jit(solution)/shard_map/ppermute | solution.py:18
  103.6 7.5 %collective-permute-start.3 = (f32[256,128]{1,0:T(8,128)S(1)}, f32[256,128]{1,0:T(8,128)S(1)}, u32[]{:S(2)}, u32[]{:S(2)}) collective-permute-start(f32[256,128]{1,0:T(8,128)S(1)} %fusion.62), channel_id=1, source_target_pairs={{0,1},{1,2},{2,3},{3,0},{4,5},{5,6},{6,7},{7,4},{8,9},{9,10},{10,1... | collective-permute-start | bytes 393224 | tf_op jit(solution)/shard_map/ppermute | solution.py:18
  111.9 7.1 %collective-permute-start.6 = (f32[1024,128]{1,0:T(8,128)S(1)}, f32[1024,128]{1,0:T(8,128)S(1)}, u32[]{:S(2)}, u32[]{:S(2)}) collective-permute-start(f32[1024,128]{1,0:T(8,128)S(1)} %bitcast_select_fusion), channel_id=1, source_target_pairs={{0,4},{4,0},{8,12},{12,8},{16,20},{20,16},{24,28},{28,24},{32,36},... | collective-permute-start | bytes 1572872 | tf_op jit(solution)/shard_map/ppermute | solution.py:12
  124.2 9.5 %collective-permute-start.7 = (f32[512,128]{1,0:T(8,128)S(1)}, f32[512,128]{1,0:T(8,128)S(1)}, u32[]{:S(2)}, u32[]{:S(2)}) collective-permute-start(f32[512,128]{1,0:T(8,128)S(1)} %select_subtract_fusion.11), channel_id=1, source_target_pairs={{0,8},{4,12},{8,0},{12,4},{16,24},{20,28},{24,16},{28,20},{32,40},... | collective-permute-start | bytes 786440 | tf_op jit(solution)/shard_map/ppermute | solution.py:12
  133.8 4.1 %collective-permute-start.8 = (f32[512,128]{1,0:T(8,128)S(1)}, f32[512,128]{1,0:T(8,128)S(1)}, u32[]{:S(2)}, u32[]{:S(2)}) collective-permute-start(f32[512,128]{1,0:T(8,128)S(1)} %collective-permute-done.7), channel_id=1, source_target_pairs={{0,4},{4,0},{8,12},{12,8},{16,20},{20,16},{24,28},{28,24},{32,36},... | collective-permute-start | bytes 786440 | tf_op jit(solution)/shard_map/ppermute | solution.py:12
  143.1 15.9 %collective-permute-start.9 = (f32[512,128]{1,0:T(8,128)S(1)}, f32[512,128]{1,0:T(8,128)S(1)}, u32[]{:S(2)}, u32[]{:S(2)}) collective-permute-start(f32[512,128]{1,0:T(8,128)S(1)} %select_subtract_fusion.9), channel_id=1, source_target_pairs={{0,16},{4,20},{8,24},{12,28},{16,0},{20,4},{24,8},{28,12},{32,48},... | collective-permute-start | bytes 786440 | tf_op jit(solution)/shard_map/ppermute | solution.py:12
  159.0 4.3 %collective-permute-start.10 = (f32[512,128]{1,0:T(8,128)S(1)}, f32[512,128]{1,0:T(8,128)S(1)}, u32[]{:S(2)}, u32[]{:S(2)}) collective-permute-start(f32[512,128]{1,0:T(8,128)S(1)} %collective-permute-done.9), channel_id=1, source_target_pairs={{0,4},{4,0},{8,12},{12,8},{16,20},{20,16},{24,28},{28,24},{32,36},... | collective-permute-start | bytes 786440 | tf_op jit(solution)/shard_map/ppermute | solution.py:12
  168.6 29.5 %collective-permute-start.11 = (f32[512,128]{1,0:T(8,128)S(1)}, f32[512,128]{1,0:T(8,128)S(1)}, u32[]{:S(2)}, u32[]{:S(2)}) collective-permute-start(f32[512,128]{1,0:T(8,128)S(1)} %select_subtract_fusion.7), channel_id=1, source_target_pairs={{0,32},{4,36},{8,40},{12,44},{16,48},{20,52},{24,56},{28,60},{32,0... | collective-permute-start | bytes 786440 | tf_op jit(solution)/shard_map/ppermute | solution.py:12
  198.1 3.5 %collective-permute-start.12 = (f32[512,128]{1,0:T(8,128)S(1)}, f32[512,128]{1,0:T(8,128)S(1)}, u32[]{:S(2)}, u32[]{:S(2)}) collective-permute-start(f32[512,128]{1,0:T(8,128)S(1)} %collective-permute-done.11), channel_id=1, source_target_pairs={{0,4},{4,0},{8,12},{12,8},{16,20},{20,16},{24,28},{28,24},{32,36},... | collective-permute-start | bytes 786440 | tf_op jit(solution)/shard_map/ppermute | solution.py:12
  205.5 9.1 %copy-start.12 = (pred[512]{0:T(512)(128)(4,1)S(1)}, pred[512]{0:T(512)(128)(4,1)}, u32[]{:S(2)}) copy-start(pred[512]{0:T(512)(128)(4,1)} %get-tuple-element.37) | copy-start | bytes 1540
  207.6 30.2 %collective-permute-start.13 = (f32[512,128]{1,0:T(8,128)S(1)}, f32[512,128]{1,0:T(8,128)}, u32[]{:S(2)}, u32[]{:S(2)}) collective-permute-start(f32[512,128]{1,0:T(8,128)S(1)} %select_subtract_fusion.5), channel_id=1, source_target_pairs={{0,64},{4,68},{8,72},{12,76},{16,80},{20,84},{24,88},{28,92},{32,9... | collective-permute-start | bytes 786440 | tf_op jit(solution)/shard_map/ppermute | solution.py:12
  237.8 3.7 %collective-permute-start.14 = (f32[512,128]{1,0:T(8,128)}, f32[512,128]{1,0:T(8,128)S(1)}, u32[]{:S(2)}, u32[]{:S(2)}) collective-permute-start(f32[512,128]{1,0:T(8,128)} %collective-permute-done.13), channel_id=1, source_target_pairs={{0,4},{4,0},{8,12},{12,8},{16,20},{20,16},{24,28},{28,24},{32,36},... | collective-permute-start | bytes 786440 | tf_op jit(solution)/shard_map/ppermute | solution.py:12
  249.7 9.5 %collective-permute-start.15 = (f32[512,128]{1,0:T(8,128)S(1)}, f32[512,128]{1,0:T(8,128)}, u32[]{:S(2)}, u32[]{:S(2)}) collective-permute-start(f32[512,128]{1,0:T(8,128)S(1)} %select_subtract_fusion.3), channel_id=1, source_target_pairs={{0,128},{4,132},{8,136},{12,140},{16,144},{20,148},{24,152},{28,15... | collective-permute-start | bytes 786440 | tf_op jit(solution)/shard_map/ppermute | solution.py:12
  255.5 8.2 %copy-start = (f32[512,128]{1,0:T(8,128)}, f32[512,128]{1,0:T(8,128)S(1)}, u32[]{:S(2)}) copy-start(f32[512,128]{1,0:T(8,128)S(1)} %select_subtract_fusion.2) | copy-start | bytes 786436
  259.2 4.4 %collective-permute-start.16 = (f32[512,128]{1,0:T(8,128)}, f32[512,128]{1,0:T(8,128)S(1)}, u32[]{:S(2)}, u32[]{:S(2)}) collective-permute-start(f32[512,128]{1,0:T(8,128)} %collective-permute-done.15), channel_id=1, source_target_pairs={{0,4},{4,0},{8,12},{12,8},{16,20},{20,16},{24,28},{28,24},{32,36},... | collective-permute-start | bytes 786440 | tf_op jit(solution)/shard_map/ppermute | solution.py:12
  272.5 11.2 %collective-permute-start.17 = (f32[512,128]{1,0:T(8,128)}, f32[512,128]{1,0:T(8,128)}, u32[]{:S(2)}, u32[]{:S(2)}) collective-permute-start(f32[512,128]{1,0:T(8,128)} %select_subtract_fusion.1), channel_id=1, source_target_pairs={{0,256},{4,260},{8,264},{12,268},{16,272},{20,276},{24,280},{28,28... | collective-permute-start | bytes 786440 | tf_op jit(solution)/shard_map/ppermute | solution.py:12
  283.7 4.6 %collective-permute-start.18 = (f32[512,128]{1,0:T(8,128)}, f32[512,128]{1,0:T(8,128)}, u32[]{:S(2)}, u32[]{:S(2)}) collective-permute-start(f32[512,128]{1,0:T(8,128)} %collective-permute-done.17), channel_id=1, source_target_pairs={{0,4},{4,0},{8,12},{12,8},{16,20},{20,16},{24,28},{28,24},{32,36},... | collective-permute-start | bytes 786440 | tf_op jit(solution)/shard_map/ppermute | solution.py:12
  (13 other events, 41.3 us)
Sparse Core Ops, SparseCore 0:
  10.9 43.7 all-gather.12
  56.8 44.2 all-gather.14
  103.2 42.7 all-gather.16
  147.9 38.5 all-gather.18
  188.5 38.5 all-gather.20
  229.1 38.5 all-gather.22

commit v5 on v0

v5 whole, which is shorter than its diff:
```python
import jax
import jax.numpy as jnp
from jax import lax
from jax.sharding import PartitionSpec as P

BLK = 64


def from_partner(value, axis, distance):
    mask = 2**distance
    pairs = [(source, source ^ mask) for source in range(lax.axis_size(axis))]
    return lax.ppermute(value, axis, pairs)


def to_row_quarters(value):
    return lax.all_to_all(value, "case", split_axis=0, concat_axis=1, tiled=True)


def on_device(
    load_interior, load_boundary, cond_blocks, block_rows, block_cols, interface_maps, merge_maps
):
    groups = lax.axis_size("case")
    local_rows = load_interior.shape[2]
    quarter = load_boundary.shape[2]
    full_rows = quarter * groups
    interior_rows = local_rows * groups
    block_size = BLK
    blocks = lax.all_gather(cond_blocks[0], "case", axis=0, tiled=True)
    rows_of_blocks = lax.all_gather(block_rows[0], "case", axis=0, tiled=True)
    cols_of_blocks = lax.all_gather(block_cols[0], "case", axis=0, tiled=True)
    block_count = blocks.shape[0]
    blocks = blocks.reshape(block_count, block_size, block_size)

    joined = jnp.concatenate([load_interior, load_boundary], axis=2)
    joined = lax.all_to_all(joined, "sub", split_axis=1, concat_axis=0, tiled=True)[:, 0, :]
    joined = lax.all_to_all(joined, "case", split_axis=0, concat_axis=1, tiled=True)
    num_cases = joined.shape[0]
    parts = joined.reshape(num_cases, groups, local_rows + quarter)
    interior = jnp.transpose(parts[:, :, :local_rows].reshape(num_cases, interior_rows))
    boundary = jnp.transpose(parts[:, :, local_rows:].reshape(num_cases, full_rows))

    pieces = jnp.take(
        interior.reshape(interior_rows // block_size, block_size, num_cases),
        cols_of_blocks,
        axis=0,
    )
    products = jnp.einsum("krc,kcn->krn", blocks, pieces, precision=lax.Precision.HIGH)
    row_blocks = full_rows // block_size
    onehot = (rows_of_blocks[None, :] == jnp.arange(row_blocks, dtype=jnp.int32)[:, None]).astype(
        jnp.float32
    )
    summed = jnp.dot(
        onehot,
        products.reshape(block_count, block_size * num_cases),
        precision=lax.Precision.HIGH,
    )
    leaf = boundary - summed.reshape(full_rows, num_cases)
    leaf_share = to_row_quarters(leaf)

    slot = lax.axis_index("sub")
    levels = lax.axis_size("sub").bit_length() - 1
    current = leaf
    nodes = jnp.zeros_like(leaf)
    for level in range(1, levels + 1):
        half = 1 << level - 1
        maps = interface_maps[0, level - 1]
        matrix = lax.all_gather(merge_maps[0, level - 1], "case", axis=0, tiled=True)
        shared_rows = matrix.shape[1]
        upper = slot // half % 2 == 1
        other = from_partner(current, "sub", level - 1)
        stacked = jnp.concatenate([current, other], axis=0)

        def left_index(index):
            return jnp.where(upper, index + full_rows, index)

        def right_index(index):
            return jnp.where(upper, index, index + full_rows)

        shared = jnp.take(stacked, left_index(maps[0, :shared_rows]), axis=0) + jnp.take(
            stacked, right_index(maps[1, :shared_rows]), axis=0
        )
        kept_index = jnp.concatenate(
            [left_index(maps[0, shared_rows:]), right_index(maps[1, shared_rows:])]
        )
        parent = jnp.take(stacked, kept_index, axis=0) - jnp.dot(
            matrix, shared, precision=lax.Precision.HIGH
        )
        is_node = slot % (2 * half) == half
        if level == levels:
            is_node = jnp.logical_or(is_node, slot == 0)
        nodes = jnp.where(is_node, parent, nodes)
        current = parent
    return (leaf_share[None], to_row_quarters(nodes)[None])


def solution(mesh):
    placed = (
        P("sub", None, "case"),
        P("sub", None, "case"),
        P("sub", "case", None),
        P("sub", "case"),
        P("sub", "case"),
        P("sub", None, None, None),
        P("sub", None, "case", None),
    )
    return jax.shard_map(
        on_device,
        mesh=mesh,
        in_specs=placed,
        out_specs=(P("sub", "case", None), P("sub", "case", None)),
        check_vma=False,
    )
```

time: 424 us -> 365 us (0.86); the launches traced: 416 us -> 364 us
  blocking collectives: 62.4 us -> 7.67 us
  waiting for transfers between devices: 221 us -> 174 us
  local copies, waits for them, and re-layouts: 32.1 us -> 68.1 us
  matrix products: 15.4 us -> 27.6 us
    ppermute x7, waiting for transfers between devices: 129 us -> 29.2 us  [from_partner(): return lax.ppermute(value, axis, pairs)]
    all_gather x0 -> x8, waiting for transfers between devices: none -> 92.3 us  [the longest x7 92.3 us: on_device(): lax.all_gather(merge_maps[0, level - 1], 'case', axis=0, tiled=True)]
    all_gather x6 -> x1, blocking collectives: 62.4 us -> 7.67 us  [on_device(): cols_of_blocks = lax.all_gather(block_cols[0], 'case', axis=0, tiled=True)]
    psum x1 -> x0, waiting for transfers between devices: 48.2 us -> none  [on_device(): current = lax.psum(contribution, 'case')]
    gather x29, local copies, waits for them, and re-layouts: 20.9 us -> 36.2 us  [the longest x14 20.9 us: on_device(): jnp.take(stacked, kept_index, axis=0)]
    dot_general x8, matrix products: 14.4 us -> 27.2 us  [the longest x7 20.2 us: on_device(): jnp.dot(matrix, shared, precision=lax.Precision.HIGH)]
    reshape x1 -> x5, local copies, waits for them, and re-layouts: 0.08 us -> 6.86 us  [the longest x1 5.62 us: on_device(): blocks = blocks.reshape(block_count, block_size, block_size)]
    all_gather x0 -> x1, local copies, waits for them, and re-layouts: none -> 5.64 us  [on_device(): blocks = lax.all_gather(cond_blocks[0], 'case', axis=0, tiled=True)]
  transfers between devices with their start and end apart: 10 -> 19, of which waited for: 10 -> 14; matrix products, arithmetic and copies ran while one was open for 2% -> 26% of each run, Pallas kernels for 0% -> 0%
where the time goes in v5:
time: 365 us; the launch traced here: 364 us
  waiting for transfers between devices  174 us (48%)
  starting transfers between devices  69.8 us (19%)
  local copies, waits for them, and re-layouts  68.1 us (19%)
  matrix products  27.6 us (8%)
  between operations  16.1 us (4%)
  blocking collectives  7.67 us (2%)
    all_gather x7, waiting for transfers between devices, on_device(): lax.all_gather(merge_maps[0, level - 1], 'case', axis=0, tiled=True)  92.3 us
    ppermute x7, starting transfers between devices, from_partner(): return lax.ppermute(value, axis, pairs)  38.3 us
    ppermute x7, waiting for transfers between devices, from_partner(): return lax.ppermute(value, axis, pairs)  29.2 us
    all_to_all x1, waiting for transfers between devices, on_device(): lax.all_to_all(joined, 'sub', split_axis=1, concat_axis=0, tiled=True)  26.8 us
    gather x14, local copies, waits for them, and re-layouts, on_device(): jnp.take(stacked, kept_index, axis=0)  20.9 us
    all_to_all x1, starting transfers between devices, on_device(): lax.all_to_all(joined, 'sub', split_axis=1, concat_axis=0, tiled=True)  20.6 us
    dot_general x7, matrix products, on_device(): jnp.dot(matrix, shared, precision=lax.Precision.HIGH)  20.2 us
    all_to_all x1, waiting for transfers between devices, on_device(): lax.all_to_all(joined, 'case', split_axis=0, concat_axis=1, tiled=True)  17.7 us
  transfers between devices with their start and end apart: 19, of which 14 were waited for; matrix products, arithmetic and copies ran while one was open for 26% of the time, Pallas kernels for 0%

profile of v5, /device:TPU:1, one launch (start us, length us, event | category | flops | bytes accessed | tf_op | source)
XLA Modules:
  0.0 363.7 jit_solution(5309197116855584580)
XLA Ops:
  9.6 3.9 %fusion.110 = (f32[1,1,256,512]{3,2,1,0:T(8,128)}, f32[1,1,256,512]{3,2,1,0:T(8,128)}, f32[1,1,256,512]{3,2,1,0:T(8,128)}, f32[1,1,256,512]{3,2,1,0:T(8,128)}, f...) fusion(f32[1,7,256,512]{3,2,1,0:T(8,128)} %param.17), kind=kLoop, calls=%fused_computation.216 | loop fusion | bytes 7340032 | tf_op jit(solution)/shard_map/slice | solution.py:67
  18.4 20.6 %all-to-all-start = ((f32[1,128,1280]{2,0,1:T(1,128)}), f32[1,128,1280]{2,0,1:T(1,128)S(1)}, u32[]{:S(2)}, u32[]{:S(2)}) async-start(f32[1,128,1280]{2,0,1:T(1,128)} %copy.232), calls=%async_computation | async-start | bytes 1310720 | tf_op jit(solution)/shard_map/all_to_all | solution.py:35
  41.9 7.7 %all-reduce.2 = (s32[128]{0:T(128)S(1)}, s32[128]{0:T(128)S(1)}) all-reduce(s32[128]{0:T(128)S(1)} %bitcast_dynamic-update-slice_fusion, s32[128]{0:T(128)S(1)} %bitcast_dynamic-update-slice_fusion.1), channel_id=3, replica_groups=mesh['sub'=128,'case'=4] {'case'}, use_global_device_ids=true, to_apply=%add.1 | all-reduce | flops 256 | bytes 2048 | tf_op jit(solution)/shard_map/all_gather | solution.py:30
  50.4 26.8 %all-to-all-done = f32[1,128,1280]{2,0,1:T(1,128)S(1)} async-done(((f32[1,128,1280]{2,0,1:T(1,128)}), f32[1,128,1280]{2,0,1:T(1,128)S(1)}, u32[]{:S(2)}, u32[]{:S(2)}) %all-to-all-start) | async-done | bytes 655392 | tf_op jit(solution)/shard_map/all_to_all | solution.py:35
  78.1 4.0 %all-to-all-start.1 = ((f32[4,32,1280]{2,1,0:T(8,128)}), f32[4,32,1280]{2,1,0:T(8,128)S(1)}, u32[]{:S(2)}, u32[]{:S(2)}) async-start(f32[4,32,1280]{2,1,0:T(8,128)} %bitcast.67), calls=%async_computation.1 | async-start | bytes 1310720 | tf_op jit(solution)/shard_map/all_to_all | solution.py:36
  82.2 17.7 %all-to-all-done.1 = f32[4,32,1280]{2,1,0:T(8,128)S(1)} async-done(((f32[4,32,1280]{2,1,0:T(8,128)}), f32[4,32,1280]{2,1,0:T(8,128)S(1)}, u32[]{:S(2)}, u32[]{:S(2)}) %all-to-all-start.1) | async-done | bytes 655392 | tf_op jit(solution)/shard_map/all_to_all | solution.py:36
  102.9 5.6 %copy.237 = f32[1,128,4096]{1,2,0:T(8,128)} copy(f32[1,128,4096]{2,0,1:T(1,128)} %all-gather.19.cloned.1.call-done) | data formatting | bytes 4194304 | tf_op jit(solution)/shard_map/all_gather | solution.py:28
  108.6 5.6 %copy.238 = f32[128,64,64]{2,1,0:T(8,128)} copy(f32[128,64,64]{0,2,1:T(8,128)} %bitcast.158) | data formatting | bytes 4194304 | tf_op jit(solution)/shard_map/reshape | solution.py:32
  114.2 7.0 %fusion.16 = f32[128,64,32]{1,2,0:T(8,128)} fusion(f32[128,64,64]{2,1,0:T(8,128)} %copy.238, f32[128,64,32]{1,2,0:T(8,128)S(1)} %gather_fusion, pred[128]{0:T(512)(128)(4,1)S(1)} %compare_and_fusion.21), kind=kOutput, calls=%fused_computation.38 | convolution fusion | flops 100925440 | bytes 4194432 | tf_op jit(solution)/shard_map/krc,kcn->krn/dot_general | solution.py:47
  121.2 3.1 copy.239
  124.9 4.4 %collective-permute-start = (f32[1024,32]{1,0:T(8,128)S(1)}, f32[1024,32]{1,0:T(8,128)S(1)}, u32[]{:S(2)}, u32[]{:S(2)}) collective-permute-start(f32[1024,32]{1,0:T(8,128)S(1)} %bitcast_subtract_fusion), channel_id=1, source_target_pairs={{0,4},{4,0},{8,12},{12,8},{16,20},{20,16},{24,28},{28,24},{32,36},... | collective-permute-start | bytes 393224 | tf_op jit(solution)/shard_map/ppermute | solution.py:12
  135.9 2.9 select_subtract_fusion
  138.9 3.3 collective-permute-start.1
  142.2 3.2 collective-permute-done.1
  153.8 3.0 collective-permute-start.2
  156.8 6.8 %collective-permute-done.2 = f32[1024,32]{0,1:T(8,128)S(1)} collective-permute-done((f32[1024,32]{0,1:T(8,128)S(1)}, f32[1024,32]{0,1:T(8,128)S(1)}, u32[]{:S(2)}, u32[]{:S(2)}) %collective-permute-start.2) | collective-permute-done | bytes 131104 | tf_op jit(solution)/shard_map/ppermute | solution.py:12
  169.1 12.6 %all-gather.25.cloned.1.call-done = f32[1,1,1024,512]{3,2,1,0:T(8,128)} async-done(((f32[1,1,256,512]{3,2,1,0:T(8,128)}), f32[1,1,1024,512]{3,2,1,0:T(8,128)}) %all-gather.25.cloned.1.call-update) | async-done | bytes 2097168 | tf_op jit(solution)/shard_map/all_gather | solution.py:67
  184.5 7.4 %collective-permute-start.3 = (f32[1024,32]{0,1:T(8,128)S(1)}, f32[1024,32]{0,1:T(8,128)S(1)}, u32[]{:S(2)}, u32[]{:S(2)}) collective-permute-start(f32[1024,32]{0,1:T(8,128)S(1)} %fusion.31), channel_id=1, source_target_pairs={{0,32},{4,36},{8,40},{12,44},{16,48},{20,52},{24,56},{28,60},{32,0... | collective-permute-start | bytes 393224 | tf_op jit(solution)/shard_map/ppermute | solution.py:12
  191.9 11.4 %collective-permute-done.3 = f32[1024,32]{0,1:T(8,128)S(1)} collective-permute-done((f32[1024,32]{0,1:T(8,128)S(1)}, f32[1024,32]{0,1:T(8,128)S(1)}, u32[]{:S(2)}, u32[]{:S(2)}) %collective-permute-start.3) | collective-permute-done | bytes 131104 | tf_op jit(solution)/shard_map/ppermute | solution.py:12
  208.8 13.5 %all-gather.27.cloned.1.call-done = f32[1,1,1024,512]{3,2,1,0:T(8,128)} async-done(((f32[1,1,256,512]{3,2,1,0:T(8,128)}), f32[1,1,1024,512]{3,2,1,0:T(8,128)}) %all-gather.27.cloned.1.call-update) | async-done | bytes 2097168 | tf_op jit(solution)/shard_map/all_gather | solution.py:67
  225.1 12.5 %collective-permute-start.4 = (f32[1024,32]{0,1:T(8,128)S(1)}, f32[1024,32]{0,1:T(8,128)S(1)}, u32[]{:S(2)}, u32[]{:S(2)}) collective-permute-start(f32[1024,32]{0,1:T(8,128)S(1)} %fusion.37), channel_id=1, source_target_pairs={{0,64},{4,68},{8,72},{12,76},{16,80},{20,84},{24,88},{28,92},{32,9... | collective-permute-start | bytes 393224 | tf_op jit(solution)/shard_map/ppermute | solution.py:12
  237.7 3.2 collective-permute-done.4
  246.3 16.5 %all-gather.29.cloned.1.call-done = f32[1,1,1024,512]{3,2,1,0:T(8,128)} async-done(((f32[1,1,256,512]{3,2,1,0:T(8,128)}), f32[1,1,1024,512]{3,2,1,0:T(8,128)}) %all-gather.29.cloned.1.call-update) | async-done | bytes 2097168 | tf_op jit(solution)/shard_map/all_gather | solution.py:67
  265.7 3.1 collective-permute-start.5
  268.9 3.1 collective-permute-done.5
  277.4 26.2 %all-gather.31.cloned.1.call-done = f32[1,1,1024,512]{3,2,1,0:T(8,128)} async-done(((f32[1,1,256,512]{3,2,1,0:T(8,128)}), f32[1,1,1024,512]{3,2,1,0:T(8,128)}) %all-gather.31.cloned.1.call-update) | async-done | bytes 2097168 | tf_op jit(solution)/shard_map/all_gather | solution.py:67
  306.5 4.6 %collective-permute-start.6 = (f32[1024,32]{0,1:T(8,128)S(1)}, f32[1024,32]{0,1:T(8,128)S(1)}, u32[]{:S(2)}, u32[]{:S(2)}) collective-permute-start(f32[1024,32]{0,1:T(8,128)S(1)} %fusion.49), channel_id=1, source_target_pairs={{0,256},{4,260},{8,264},{12,268},{16,272},{20,276},{24,280},{28,28... | collective-permute-start | bytes 393224 | tf_op jit(solution)/shard_map/ppermute | solution.py:12
  312.1 3.3 all-to-all-start.2
  320.9 23.5 %all-gather.33.cloned.1.call-done = f32[1,1,1024,512]{3,2,1,0:T(8,128)} async-done(((f32[1,1,256,512]{3,2,1,0:T(8,128)}), f32[1,1,1024,512]{3,2,1,0:T(8,128)}) %all-gather.33.cloned.1.call-update) | async-done | bytes 2097168 | tf_op jit(solution)/shard_map/all_gather | solution.py:67
  344.4 2.9 fusion.58
  347.9 3.3 all-to-all-start.3
  352.0 4.0 %all-to-all-done.3 = f32[4,256,32]{1,2,0:T(8,128)S(1)} async-done(((f32[4,256,32]{1,2,0:T(8,128)}), f32[4,256,32]{1,2,0:T(8,128)S(1)}, u32[]{:S(2)}, u32[]{:S(2)}) %all-to-all-start.3) | async-done | bytes 131104 | tf_op jit(solution)/shard_map/all_to_all | solution.py:16
  (165 shorter events, 70.9 us)
Async XLA Ops:
  7.2 95.7 %all-gather.19.cloned.1.call-start = ((), (), s32[]{:S(2)}) async-start(), calls=%async_computation.4 | async-start | bytes 2621440 | tf_op jit(solution)/shard_map/all_gather | solution.py:28
  9.6 126.3 %all-gather.21.cloned.1.call-start = ((), (), s32[]{:S(2)}) async-start(), calls=%async_computation.5 | async-start | bytes 2621440 | tf_op jit(solution)/shard_map/all_gather | solution.py:67
  13.5 3.3 copy-start.1
  13.5 3.3 copy-start.2
  13.6 137.3 %all-gather.23.cloned.1.call-start = ((), (), s32[]{:S(2)}) async-start(), calls=%async_computation.6 | async-start | bytes 2621440 | tf_op jit(solution)/shard_map/all_gather | solution.py:67
  14.3 167.3 %all-gather.25.cloned.1.call-start = ((), (), s32[]{:S(2)}) async-start(), calls=%async_computation.7 | async-start | bytes 2621440 | tf_op jit(solution)/shard_map/all_gather | solution.py:67
  14.9 207.3 %all-gather.27.cloned.1.call-start = ((), (), s32[]{:S(2)}) async-start(), calls=%async_computation.8 | async-start | bytes 2621440 | tf_op jit(solution)/shard_map/all_gather | solution.py:67
  15.5 247.3 %all-gather.29.cloned.1.call-start = ((), (), s32[]{:S(2)}) async-start(), calls=%async_computation.9 | async-start | bytes 2621440 | tf_op jit(solution)/shard_map/all_gather | solution.py:67
  16.0 287.6 %all-gather.31.cloned.1.call-start = ((), (), s32[]{:S(2)}) async-start(), calls=%async_computation.10 | async-start | bytes 2621440 | tf_op jit(solution)/shard_map/all_gather | solution.py:67
  16.8 24.9 %copy-start.4 = (s32[1,32]{1,0:T(1,128)S(1)}, s32[1,32]{1,0:T(1,128)}, u32[]{:S(2)}) copy-start(s32[1,32]{1,0:T(1,128)} %param.15) | copy-start | bytes 388
  16.8 25.0 %copy-start.5 = (s32[1,32]{1,0:T(1,128)S(1)}, s32[1,32]{1,0:T(1,128)}, u32[]{:S(2)}) copy-start(s32[1,32]{1,0:T(1,128)} %param.14) | copy-start | bytes 388
  16.8 32.7 %copy-start.3 = (s32[1,7,2,1024]{3,2,1,0:T(2,128)S(1)}, s32[1,7,2,1024]{3,2,1,0:T(2,128)}, u32[]{:S(2)}) copy-start(s32[1,7,2,1024]{3,2,1,0:T(2,128)} %param.16) | copy-start | bytes 172036
  18.4 58.9 %all-to-all-start = ((f32[1,128,1280]{2,0,1:T(1,128)}), f32[1,128,1280]{2,0,1:T(1,128)S(1)}, u32[]{:S(2)}, u32[]{:S(2)}) async-start(f32[1,128,1280]{2,0,1:T(1,128)} %copy.232), calls=%async_computation | async-start | bytes 1310720 | tf_op jit(solution)/shard_map/all_to_all | solution.py:35
  39.0 305.4 %all-gather.33.cloned.1.call-start = ((), (), s32[]{:S(2)}) async-start(), calls=%async_computation.11 | async-start | bytes 2621440 | tf_op jit(solution)/shard_map/all_gather | solution.py:67
  78.1 21.7 %all-to-all-start.1 = ((f32[4,32,1280]{2,1,0:T(8,128)}), f32[4,32,1280]{2,1,0:T(8,128)S(1)}, u32[]{:S(2)}, u32[]{:S(2)}) async-start(f32[4,32,1280]{2,1,0:T(8,128)} %bitcast.67), calls=%async_computation.1 | async-start | bytes 1310720 | tf_op jit(solution)/shard_map/all_to_all | solution.py:36
  121.2 3.7 %copy-start = (f32[32,4,256]{0,2,1:T(8,128)S(1)}, f32[32,4,256]{0,2,1:T(8,128)}, u32[]{:S(2)}) copy-start(f32[32,4,256]{0,2,1:T(8,128)} %copy.233) | copy-start | bytes 393220
  124.9 5.9 %collective-permute-start = (f32[1024,32]{1,0:T(8,128)S(1)}, f32[1024,32]{1,0:T(8,128)S(1)}, u32[]{:S(2)}, u32[]{:S(2)}) collective-permute-start(f32[1024,32]{1,0:T(8,128)S(1)} %bitcast_subtract_fusion), channel_id=1, source_target_pairs={{0,4},{4,0},{8,12},{12,8},{16,20},{20,16},{24,28},{28,24},{32,36},... | collective-permute-start | bytes 393224 | tf_op jit(solution)/shard_map/ppermute | solution.py:12
  138.9 6.6 %collective-permute-start.1 = (f32[1024,32]{0,1:T(8,128)S(1)}, f32[1024,32]{0,1:T(8,128)S(1)}, u32[]{:S(2)}, u32[]{:S(2)}) collective-permute-start(f32[1024,32]{0,1:T(8,128)S(1)} %select_subtract_fusion), channel_id=1, source_target_pairs={{0,8},{4,12},{8,0},{12,4},{16,24},{20,28},{24,16},{28,20},{32,40},... | collective-permute-start | bytes 393224 | tf_op jit(solution)/shard_map/ppermute | solution.py:12
  153.8 9.9 %collective-permute-start.2 = (f32[1024,32]{0,1:T(8,128)S(1)}, f32[1024,32]{0,1:T(8,128)S(1)}, u32[]{:S(2)}, u32[]{:S(2)}) collective-permute-start(f32[1024,32]{0,1:T(8,128)S(1)} %fusion.25), channel_id=1, source_target_pairs={{0,16},{4,20},{8,24},{12,28},{16,0},{20,4},{24,8},{28,12},{32,48},... | collective-permute-start | bytes 393224 | tf_op jit(solution)/shard_map/ppermute | solution.py:12
  184.5 18.8 %collective-permute-start.3 = (f32[1024,32]{0,1:T(8,128)S(1)}, f32[1024,32]{0,1:T(8,128)S(1)}, u32[]{:S(2)}, u32[]{:S(2)}) collective-permute-start(f32[1024,32]{0,1:T(8,128)S(1)} %fusion.31), channel_id=1, source_target_pairs={{0,32},{4,36},{8,40},{12,44},{16,48},{20,52},{24,56},{28,60},{32,0... | collective-permute-start | bytes 393224 | tf_op jit(solution)/shard_map/ppermute | solution.py:12
  225.1 15.7 %collective-permute-start.4 = (f32[1024,32]{0,1:T(8,128)S(1)}, f32[1024,32]{0,1:T(8,128)S(1)}, u32[]{:S(2)}, u32[]{:S(2)}) collective-permute-start(f32[1024,32]{0,1:T(8,128)S(1)} %fusion.37), channel_id=1, source_target_pairs={{0,64},{4,68},{8,72},{12,76},{16,80},{20,84},{24,88},{28,92},{32,9... | collective-permute-start | bytes 393224 | tf_op jit(solution)/shard_map/ppermute | solution.py:12
  265.7 6.3 %collective-permute-start.5 = (f32[1024,32]{0,1:T(8,128)S(1)}, f32[1024,32]{0,1:T(8,128)S(1)}, u32[]{:S(2)}, u32[]{:S(2)}) collective-permute-start(f32[1024,32]{0,1:T(8,128)S(1)} %fusion.43), channel_id=1, source_target_pairs={{0,128},{4,132},{8,136},{12,140},{16,144},{20,148},{24,152},{28,15... | collective-permute-start | bytes 393224 | tf_op jit(solution)/shard_map/ppermute | solution.py:12
  306.5 8.9 %collective-permute-start.6 = (f32[1024,32]{0,1:T(8,128)S(1)}, f32[1024,32]{0,1:T(8,128)S(1)}, u32[]{:S(2)}, u32[]{:S(2)}) collective-permute-start(f32[1024,32]{0,1:T(8,128)S(1)} %fusion.49), channel_id=1, source_target_pairs={{0,256},{4,260},{8,264},{12,268},{16,272},{20,276},{24,280},{28,28... | collective-permute-start | bytes 393224 | tf_op jit(solution)/shard_map/ppermute | solution.py:12
  312.1 35.9 %all-to-all-start.2 = ((f32[4,256,32]{1,2,0:T(8,128)}), f32[4,256,32]{1,2,0:T(8,128)S(1)}, u32[]{:S(2)}, u32[]{:S(2)}) async-start(f32[4,256,32]{1,2,0:T(8,128)} %copy.240), calls=%async_computation.2 | async-start | bytes 262144 | tf_op jit(solution)/shard_map/all_to_all | solution.py:16
  347.9 8.1 %all-to-all-start.3 = ((f32[4,256,32]{1,2,0:T(8,128)}), f32[4,256,32]{1,2,0:T(8,128)S(1)}, u32[]{:S(2)}, u32[]{:S(2)}) async-start(f32[4,256,32]{1,2,0:T(8,128)} %bitcast.157), calls=%async_computation.3 | async-start | bytes 262144 | tf_op jit(solution)/shard_map/all_to_all | solution.py:16
Sparse Core Ops, SparseCore 0:
  10.1 43.8 all-gather.18
  56.1 45.4 all-gather.20
  103.7 37.3 all-gather.22
  143.0 38.5 all-gather.24
  183.6 38.5 all-gather.26
  224.2 38.5 all-gather.28
  264.9 38.6 all-gather.30
  305.7 38.6 all-gather.32

commit v6 on v5

--- a/solution.py
+++ b/solution.py
@@ -60,12 +60,17 @@
     slot = lax.axis_index("sub")
     levels = lax.axis_size("sub").bit_length() - 1
     current = leaf
+    core = slot % 2
     nodes = jnp.zeros_like(leaf)
     for level in range(1, levels + 1):
         half = 1 << level - 1
         maps = interface_maps[0, level - 1]
-        matrix = lax.all_gather(merge_maps[0, level - 1], "case", axis=0, tiled=True)
-        shared_rows = matrix.shape[1]
+        shared_rows = merge_maps.shape[3]
+        width = shared_rows // 2
+        begin = core * width
+        mine = lax.dynamic_slice_in_dim(merge_maps[0, level - 1], begin, width, 1)
+        mine = lax.all_gather(mine, "case", axis=0, tiled=True)
+        theirs = from_partner(mine, "sub", 0)
         upper = slot // half % 2 == 1
         other = from_partner(current, "sub", level - 1)
         stacked = jnp.concatenate([current, other], axis=0)
@@ -82,9 +87,16 @@
         kept_index = jnp.concatenate(
             [left_index(maps[0, shared_rows:]), right_index(maps[1, shared_rows:])]
         )
-        parent = jnp.take(stacked, kept_index, axis=0) - jnp.dot(
-            matrix, shared, precision=lax.Precision.HIGH
+        product = jnp.dot(
+            mine,
+            lax.dynamic_slice_in_dim(shared, begin, width, 0),
+            precision=lax.Precision.HIGH,
+        ) + jnp.dot(
+            theirs,
+            lax.dynamic_slice_in_dim(shared, width - begin, width, 0),
+            precision=lax.Precision.HIGH,
         )
+        parent = jnp.take(stacked, kept_index, axis=0) - product
         is_node = slot % (2 * half) == half
         if level == levels:
             is_node = jnp.logical_or(is_node, slot == 0)

time: 365 us -> 350 us (0.959)
  waiting for transfers between devices: 174 us -> 104 us
  starting transfers between devices: 69.8 us -> 95.9 us
  other arithmetic: 0.76 us -> 19.8 us
  local copies, waits for them, and re-layouts: 68.1 us -> 79.8 us
    ppermute x7 -> x14, waiting for transfers between devices: 29.2 us -> 0.13 us  [from_partner(): return lax.ppermute(value, axis, pairs)]
    ppermute x7 -> x14, starting transfers between devices: 38.3 us -> 63.4 us  [from_partner(): return lax.ppermute(value, axis, pairs)]
    all_gather x7, waiting for transfers between devices: 92.3 us -> 74 us  [on_device(): mine = lax.all_gather(mine, 'case', axis=0, tiled=True)]
    all_to_all x1, waiting for transfers between devices: 17.7 us -> 7.11 us  [on_device(): lax.all_to_all(joined, 'case', split_axis=0, concat_axis=1, tiled=True)]
    all_to_all x1, waiting for transfers between devices: 26.8 us -> 18.6 us  [on_device(): lax.all_to_all(joined, 'sub', split_axis=1, concat_axis=0, tiled=True)]
    gather x21, other arithmetic: 0.16 us -> 7.82 us
    dynamic_slice x0 -> x7, local copies, waits for them, and re-layouts: none -> 6.09 us  [on_device(): mine = lax.dynamic_slice_in_dim(merge_maps[0, level - 1], begin, width, 1)]
    add x0 -> x7, other arithmetic: none -> 4.45 us  [on_device(): jnp.take(stacked, left_index(maps[0, :shared_rows]), axis=0)]
  transfers between devices with their start and end apart: 19 -> 26, of which waited for: 14 -> 9; matrix products, arithmetic and copies ran while one was open for 26% -> 34% of each run, Pallas kernels for 0% -> 0%
where the time goes in v6:
time: 350 us; the launch traced here: 348 us
  waiting for transfers between devices  104 us (30%)
  starting transfers between devices  95.9 us (27%)
  local copies, waits for them, and re-layouts  79.8 us (23%)
  matrix products  25.1 us (7%)
  other arithmetic  19.8 us (6%)
  between operations  16.4 us (5%)
  blocking collectives  7.51 us (2%)
    all_gather x7, waiting for transfers between devices, on_device(): mine = lax.all_gather(mine, 'case', axis=0, tiled=True)  74 us
    ppermute x14, starting transfers between devices, from_partner(): return lax.ppermute(value, axis, pairs)  63.4 us
    gather x14, local copies, waits for them, and re-layouts, on_device(): parent = jnp.take(stacked, kept_index, axis=0) - product  22.1 us
    all_to_all x1, starting transfers between devices, on_device(): lax.all_to_all(joined, 'sub', split_axis=1, concat_axis=0, tiled=True)  20.6 us
    all_to_all x1, waiting for transfers between devices, on_device(): lax.all_to_all(joined, 'sub', split_axis=1, concat_axis=0, tiled=True)  18.6 us
    dot_general x7, matrix products, on_device(): jnp.dot(theirs, lax.dynamic_slice_in_dim(shared, width - begin, width, 0)...  12.6 us
    gather x7, local copies, waits for them, and re-layouts, on_device(): jnp.take(stacked, left_index(maps[0, :shared_rows]), axis=0)  9.06 us
    gather x7, local copies, waits for them, and re-layouts, on_device(): jnp.take(stacked, right_index(maps[1, :shared_rows]), axis=0)  8.48 us
  transfers between devices with their start and end apart: 26, of which 9 were waited for; matrix products, arithmetic and copies ran while one was open for 34% of the time, Pallas kernels for 0%

profile of v6, /device:TPU:1, one launch (start us, length us, event | category | flops | bytes accessed | tf_op | source)
XLA Modules:
  0.0 348.5 jit_solution(5071647686694839932)
XLA Ops:
  7.2 3.5 fusion.68
  20.6 20.6 %all-to-all-start = ((f32[1,128,1280]{2,0,1:T(1,128)}), f32[1,128,1280]{2,0,1:T(1,128)S(1)}, u32[]{:S(2)}, u32[]{:S(2)}) async-start(f32[1,128,1280]{2,0,1:T(1,128)} %copy.232), calls=%async_computation | async-start | bytes 1310720 | tf_op jit(solution)/shard_map/all_to_all | solution.py:35
  44.1 7.5 %all-reduce.2 = (s32[128]{0:T(128)S(1)}, s32[128]{0:T(128)S(1)}) all-reduce(s32[128]{0:T(128)S(1)} %bitcast_dynamic-update-slice_fusion, s32[128]{0:T(128)S(1)} %bitcast_dynamic-update-slice_fusion.1), channel_id=3, replica_groups=mesh['sub'=128,'case'=4] {'case'}, use_global_device_ids=true, to_apply=%add.1 | all-reduce | flops 256 | bytes 2048 | tf_op jit(solution)/shard_map/all_gather | solution.py:30
  60.8 18.6 %all-to-all-done = f32[1,128,1280]{2,0,1:T(1,128)S(1)} async-done(((f32[1,128,1280]{2,0,1:T(1,128)}), f32[1,128,1280]{2,0,1:T(1,128)S(1)}, u32[]{:S(2)}, u32[]{:S(2)}) %all-to-all-start) | async-done | bytes 655392 | tf_op jit(solution)/shard_map/all_to_all | solution.py:35
  80.3 4.0 %all-to-all-start.1 = ((f32[4,32,1280]{2,1,0:T(8,128)}), f32[4,32,1280]{2,1,0:T(8,128)S(1)}, u32[]{:S(2)}, u32[]{:S(2)}) async-start(f32[4,32,1280]{2,1,0:T(8,128)} %bitcast.60), calls=%async_computation.1 | async-start | bytes 1310720 | tf_op jit(solution)/shard_map/all_to_all | solution.py:36
  86.1 3.8 %collective-permute-start.1 = (f32[1024,256]{1,0:T(8,128)}, f32[1024,256]{1,0:T(8,128)}, u32[]{:S(2)}, u32[]{:S(2)}) collective-permute-start(f32[1024,256]{1,0:T(8,128)} %bitcast.117), channel_id=1, source_target_pairs={{0,4},{4,0},{8,12},{12,8},{16,20},{20,16},{24,28},{28,24},{32,36},... | collective-permute-start | bytes 3145736 | tf_op jit(solution)/shard_map/ppermute | solution.py:12
  89.9 7.1 %all-to-all-done.1 = f32[4,32,1280]{2,1,0:T(8,128)S(1)} async-done(((f32[4,32,1280]{2,1,0:T(8,128)}), f32[4,32,1280]{2,1,0:T(8,128)S(1)}, u32[]{:S(2)}, u32[]{:S(2)}) %all-to-all-start.1) | async-done | bytes 655392 | tf_op jit(solution)/shard_map/all_to_all | solution.py:36
  100.0 5.6 %copy.237 = f32[1,128,4096]{1,2,0:T(8,128)} copy(f32[1,128,4096]{2,0,1:T(1,128)} %all-gather.19.cloned.1.call-done) | data formatting | bytes 4194304 | tf_op jit(solution)/shard_map/all_gather | solution.py:28
  105.7 5.6 %copy.238 = f32[128,64,64]{2,1,0:T(8,128)} copy(f32[128,64,64]{0,2,1:T(8,128)} %bitcast.105) | data formatting | bytes 4194304 | tf_op jit(solution)/shard_map/reshape | solution.py:32
  111.3 6.9 %fusion.2 = f32[128,64,32]{1,2,0:T(8,128)} fusion(f32[128,64,64]{2,1,0:T(8,128)} %copy.238, f32[128,64,32]{1,2,0:T(8,128)S(1)} %gather_fusion, pred[128]{0:T(512)(128)(4,1)S(1)} %compare_and_fusion.21), kind=kOutput, calls=%fused_computation.24 | convolution fusion | flops 100925440 | bytes 4194432 | tf_op jit(solution)/shard_map/krc,kcn->krn/dot_general | solution.py:47
  125.6 4.9 %all-gather.23.cloned.1.call-done = f32[1,1,1024,256]{3,2,1,0:T(8,128)} async-done(((f32[1,1,256,256]{3,2,1,0:T(8,128)}), f32[1,1,1024,256]{3,2,1,0:T(8,128)}) %all-gather.23.cloned.1.call-update) | async-done | bytes 1048592 | tf_op jit(solution)/shard_map/all_gather | solution.py:72
  130.5 3.5 collective-permute-start.3
  141.8 3.2 collective-permute-start.2
  146.2 18.3 %all-gather.25.cloned.1.call-done = f32[1,1,1024,256]{3,2,1,0:T(8,128)} async-done(((f32[1,1,256,256]{3,2,1,0:T(8,128)}), f32[1,1,1024,256]{3,2,1,0:T(8,128)}) %all-gather.25.cloned.1.call-update) | async-done | bytes 1048592 | tf_op jit(solution)/shard_map/all_gather | solution.py:72
  164.6 3.8 %collective-permute-start.5 = (f32[1024,256]{1,0:T(8,128)}, f32[1024,256]{1,0:T(8,128)}, u32[]{:S(2)}, u32[]{:S(2)}) collective-permute-start(f32[1024,256]{1,0:T(8,128)} %bitcast.115), channel_id=1, source_target_pairs={{0,4},{4,0},{8,12},{12,8},{16,20},{20,16},{24,28},{28,24},{32,36},... | collective-permute-start | bytes 3145736 | tf_op jit(solution)/shard_map/ppermute | solution.py:12
  171.5 3.4 gather_fusion.4
  178.7 4.2 %collective-permute-start.4 = (f32[1024,32]{0,1:T(8,128)S(1)}, f32[1024,32]{0,1:T(8,128)S(1)}, u32[]{:S(2)}, u32[]{:S(2)}) collective-permute-start(f32[1024,32]{0,1:T(8,128)S(1)} %fusion.5), channel_id=1, source_target_pairs={{0,16},{4,20},{8,24},{12,28},{16,0},{20,4},{24,8},{28,12},{32,48},... | collective-permute-start | bytes 393224 | tf_op jit(solution)/shard_map/ppermute | solution.py:12
  184.1 14.4 %all-gather.27.cloned.1.call-done = f32[1,1,1024,256]{3,2,1,0:T(8,128)} async-done(((f32[1,1,256,256]{3,2,1,0:T(8,128)}), f32[1,1,1024,256]{3,2,1,0:T(8,128)}) %all-gather.27.cloned.1.call-update) | async-done | bytes 1048592 | tf_op jit(solution)/shard_map/all_gather | solution.py:72
  198.6 3.6 %collective-permute-start.7 = (f32[1024,256]{1,0:T(8,128)}, f32[1024,256]{1,0:T(8,128)}, u32[]{:S(2)}, u32[]{:S(2)}) collective-permute-start(f32[1024,256]{1,0:T(8,128)} %bitcast.114), channel_id=1, source_target_pairs={{0,4},{4,0},{8,12},{12,8},{16,20},{20,16},{24,28},{28,24},{32,36},... | collective-permute-start | bytes 3145736 | tf_op jit(solution)/shard_map/ppermute | solution.py:12
  212.6 7.4 %collective-permute-start.6 = (f32[1024,32]{0,1:T(8,128)S(1)}, f32[1024,32]{0,1:T(8,128)S(1)}, u32[]{:S(2)}, u32[]{:S(2)}) collective-permute-start(f32[1024,32]{0,1:T(8,128)S(1)} %fusion.6), channel_id=1, source_target_pairs={{0,32},{4,36},{8,40},{12,44},{16,48},{20,52},{24,56},{28,60},{32,0... | collective-permute-start | bytes 393224 | tf_op jit(solution)/shard_map/ppermute | solution.py:12
  221.2 11.4 %all-gather.29.cloned.1.call-done = f32[1,1,1024,256]{3,2,1,0:T(8,128)} async-done(((f32[1,1,256,256]{3,2,1,0:T(8,128)}), f32[1,1,1024,256]{3,2,1,0:T(8,128)}) %all-gather.29.cloned.1.call-update) | async-done | bytes 1048592 | tf_op jit(solution)/shard_map/all_gather | solution.py:72
  232.6 3.6 %collective-permute-start.9 = (f32[1024,256]{1,0:T(8,128)}, f32[1024,256]{1,0:T(8,128)}, u32[]{:S(2)}, u32[]{:S(2)}) collective-permute-start(f32[1024,256]{1,0:T(8,128)} %bitcast.113), channel_id=1, source_target_pairs={{0,4},{4,0},{8,12},{12,8},{16,20},{20,16},{24,28},{28,24},{32,36},... | collective-permute-start | bytes 3145736 | tf_op jit(solution)/shard_map/ppermute | solution.py:12
  239.9 3.4 gather_fusion.10
  247.2 12.5 %collective-permute-start.8 = (f32[1024,32]{0,1:T(8,128)S(1)}, f32[1024,32]{0,1:T(8,128)S(1)}, u32[]{:S(2)}, u32[]{:S(2)}) collective-permute-start(f32[1024,32]{0,1:T(8,128)S(1)} %fusion.7), channel_id=1, source_target_pairs={{0,64},{4,68},{8,72},{12,76},{16,80},{20,84},{24,88},{28,92},{32,9... | collective-permute-start | bytes 393224 | tf_op jit(solution)/shard_map/ppermute | solution.py:12
  259.7 7.0 %all-gather.31.cloned.1.call-done = f32[1,1,1024,256]{3,2,1,0:T(8,128)} async-done(((f32[1,1,256,256]{3,2,1,0:T(8,128)}), f32[1,1,1024,256]{3,2,1,0:T(8,128)}) %all-gather.31.cloned.1.call-update) | async-done | bytes 1048592 | tf_op jit(solution)/shard_map/all_gather | solution.py:72
  266.7 3.6 %collective-permute-start.11 = (f32[1024,256]{1,0:T(8,128)}, f32[1024,256]{1,0:T(8,128)}, u32[]{:S(2)}, u32[]{:S(2)}) collective-permute-start(f32[1024,256]{1,0:T(8,128)} %bitcast.112), channel_id=1, source_target_pairs={{0,4},{4,0},{8,12},{12,8},{16,20},{20,16},{24,28},{28,24},{32,36},... | collective-permute-start | bytes 3145736 | tf_op jit(solution)/shard_map/ppermute | solution.py:12
  282.9 18.0 %all-gather.33.cloned.1.call-done = f32[1,1,1024,256]{3,2,1,0:T(8,128)} async-done(((f32[1,1,256,256]{3,2,1,0:T(8,128)}), f32[1,1,1024,256]{3,2,1,0:T(8,128)}) %all-gather.33.cloned.1.call-update) | async-done | bytes 1048592 | tf_op jit(solution)/shard_map/all_gather | solution.py:72
  300.9 3.5 collective-permute-start.13
  313.3 4.6 %collective-permute-start.12 = (f32[1024,32]{0,1:T(8,128)S(1)}, f32[1024,32]{0,1:T(8,128)S(1)}, u32[]{:S(2)}, u32[]{:S(2)}) collective-permute-start(f32[1024,32]{0,1:T(8,128)S(1)} %fusion.9), channel_id=1, source_target_pairs={{0,256},{4,260},{8,264},{12,268},{16,272},{20,276},{24,280},{28,28... | collective-permute-start | bytes 393224 | tf_op jit(solution)/shard_map/ppermute | solution.py:12
  318.9 3.3 all-to-all-start.2
  331.9 4.2 %all-to-all-start.3 = ((f32[4,256,32]{1,2,0:T(8,128)}), f32[4,256,32]{1,2,0:T(8,128)S(1)}, u32[]{:S(2)}, u32[]{:S(2)}) async-start(f32[4,256,32]{1,2,0:T(8,128)} %bitcast.104), calls=%async_computation.3 | async-start | bytes 262144 | tf_op jit(solution)/shard_map/all_to_all | solution.py:16
  336.8 4.1 %all-to-all-done.3 = f32[4,256,32]{1,2,0:T(8,128)S(1)} async-done(((f32[4,256,32]{1,2,0:T(8,128)}), f32[4,256,32]{1,2,0:T(8,128)S(1)}, u32[]{:S(2)}, u32[]{:S(2)}) %all-to-all-start.3) | async-done | bytes 131104 | tf_op jit(solution)/shard_map/all_to_all | solution.py:16
  (276 shorter events, 102.8 us)
Async XLA Ops:
  7.2 78.9 %all-gather.21.cloned.1.call-start = ((), (), s32[]{:S(2)}) async-start(), calls=%async_computation.5 | async-start | bytes 1310720 | tf_op jit(solution)/shard_map/all_gather | solution.py:72
  12.4 87.6 %all-gather.19.cloned.1.call-start = ((), (), s32[]{:S(2)}) async-start(), calls=%async_computation.4 | async-start | bytes 2621440 | tf_op jit(solution)/shard_map/all_gather | solution.py:28
  14.9 115.7 %all-gather.23.cloned.1.call-start = ((), (), s32[]{:S(2)}) async-start(), calls=%async_computation.6 | async-start | bytes 1310720 | tf_op jit(solution)/shard_map/all_gather | solution.py:72
  15.7 148.9 %all-gather.25.cloned.1.call-start = ((), (), s32[]{:S(2)}) async-start(), calls=%async_computation.7 | async-start | bytes 1310720 | tf_op jit(solution)/shard_map/all_gather | solution.py:72
  16.5 182.1 %all-gather.27.cloned.1.call-start = ((), (), s32[]{:S(2)}) async-start(), calls=%async_computation.8 | async-start | bytes 1310720 | tf_op jit(solution)/shard_map/all_gather | solution.py:72
  17.3 215.2 %all-gather.29.cloned.1.call-start = ((), (), s32[]{:S(2)}) async-start(), calls=%async_computation.9 | async-start | bytes 1310720 | tf_op jit(solution)/shard_map/all_gather | solution.py:72
  18.1 248.6 %all-gather.31.cloned.1.call-start = ((), (), s32[]{:S(2)}) async-start(), calls=%async_computation.10 | async-start | bytes 1310720 | tf_op jit(solution)/shard_map/all_gather | solution.py:72
  19.0 32.6 %copy-start.9 = (s32[1,7,2,1024]{3,2,1,0:T(2,128)S(1)}, s32[1,7,2,1024]{3,2,1,0:T(2,128)}, u32[]{:S(2)}) copy-start(s32[1,7,2,1024]{3,2,1,0:T(2,128)} %param.16) | copy-start | bytes 172036
  20.6 58.9 %all-to-all-start = ((f32[1,128,1280]{2,0,1:T(1,128)}), f32[1,128,1280]{2,0,1:T(1,128)S(1)}, u32[]{:S(2)}, u32[]{:S(2)}) async-start(f32[1,128,1280]{2,0,1:T(1,128)} %copy.232), calls=%async_computation | async-start | bytes 1310720 | tf_op jit(solution)/shard_map/all_to_all | solution.py:35
  41.1 259.8 %all-gather.33.cloned.1.call-start = ((), (), s32[]{:S(2)}) async-start(), calls=%async_computation.11 | async-start | bytes 1310720 | tf_op jit(solution)/shard_map/all_gather | solution.py:72
  80.3 16.7 %all-to-all-start.1 = ((f32[4,32,1280]{2,1,0:T(8,128)}), f32[4,32,1280]{2,1,0:T(8,128)S(1)}, u32[]{:S(2)}, u32[]{:S(2)}) async-start(f32[4,32,1280]{2,1,0:T(8,128)} %bitcast.60), calls=%async_computation.1 | async-start | bytes 1310720 | tf_op jit(solution)/shard_map/all_to_all | solution.py:36
  86.1 53.9 %collective-permute-start.1 = (f32[1024,256]{1,0:T(8,128)}, f32[1024,256]{1,0:T(8,128)}, u32[]{:S(2)}, u32[]{:S(2)}) collective-permute-start(f32[1024,256]{1,0:T(8,128)} %bitcast.117), channel_id=1, source_target_pairs={{0,4},{4,0},{8,12},{12,8},{16,20},{20,16},{24,28},{28,24},{32,36},... | collective-permute-start | bytes 3145736 | tf_op jit(solution)/shard_map/ppermute | solution.py:12
  122.0 12.1 %collective-permute-start = (f32[1024,32]{1,0:T(8,128)S(1)}, f32[1024,32]{1,0:T(8,128)S(1)}, u32[]{:S(2)}, u32[]{:S(2)}) collective-permute-start(f32[1024,32]{1,0:T(8,128)S(1)} %bitcast_subtract_fusion), channel_id=1, source_target_pairs={{0,4},{4,0},{8,12},{12,8},{16,20},{20,16},{24,28},{28,24},{32,36},... | collective-permute-start | bytes 393224 | tf_op jit(solution)/shard_map/ppermute | solution.py:12
  130.5 46.4 %collective-permute-start.3 = (f32[1024,256]{1,0:T(8,128)}, f32[1024,256]{1,0:T(8,128)}, u32[]{:S(2)}, u32[]{:S(2)}) collective-permute-start(f32[1024,256]{1,0:T(8,128)} %bitcast.116), channel_id=1, source_target_pairs={{0,4},{4,0},{8,12},{12,8},{16,20},{20,16},{24,28},{28,24},{32,36},... | collective-permute-start | bytes 3145736 | tf_op jit(solution)/shard_map/ppermute | solution.py:12
  139.4 29.3 %copy-start.20 = (s32[1024]{0:T(1024)S(1)}, s32[1024]{0:T(1024)}, u32[]{:S(2)}) copy-start(s32[1024]{0:T(1024)} %pad_clamp_fusion.10) | copy-start | bytes 12292
  141.8 26.6 %collective-permute-start.2 = (f32[1024,32]{0,1:T(8,128)S(1)}, f32[1024,32]{0,1:T(8,128)S(1)}, u32[]{:S(2)}, u32[]{:S(2)}) collective-permute-start(f32[1024,32]{0,1:T(8,128)S(1)} %select_subtract_fusion), channel_id=1, source_target_pairs={{0,8},{4,12},{8,0},{12,4},{16,24},{20,28},{24,16},{28,20},{32,40},... | collective-permute-start | bytes 393224 | tf_op jit(solution)/shard_map/ppermute | solution.py:12
  164.6 46.2 %collective-permute-start.5 = (f32[1024,256]{1,0:T(8,128)}, f32[1024,256]{1,0:T(8,128)}, u32[]{:S(2)}, u32[]{:S(2)}) collective-permute-start(f32[1024,256]{1,0:T(8,128)} %bitcast.115), channel_id=1, source_target_pairs={{0,4},{4,0},{8,12},{12,8},{16,20},{20,16},{24,28},{28,24},{32,36},... | collective-permute-start | bytes 3145736 | tf_op jit(solution)/shard_map/ppermute | solution.py:12
  176.3 26.2 %copy-start.22 = (s32[1024]{0:T(1024)S(1)}, s32[1024]{0:T(1024)}, u32[]{:S(2)}) copy-start(s32[1024]{0:T(1024)} %pad_clamp_fusion.8) | copy-start | bytes 12292
  178.7 23.4 %collective-permute-start.4 = (f32[1024,32]{0,1:T(8,128)S(1)}, f32[1024,32]{0,1:T(8,128)S(1)}, u32[]{:S(2)}, u32[]{:S(2)}) collective-permute-start(f32[1024,32]{0,1:T(8,128)S(1)} %fusion.5), channel_id=1, source_target_pairs={{0,16},{4,20},{8,24},{12,28},{16,0},{20,4},{24,8},{28,12},{32,48},... | collective-permute-start | bytes 393224 | tf_op jit(solution)/shard_map/ppermute | solution.py:12
  198.6 46.8 %collective-permute-start.7 = (f32[1024,256]{1,0:T(8,128)}, f32[1024,256]{1,0:T(8,128)}, u32[]{:S(2)}, u32[]{:S(2)}) collective-permute-start(f32[1024,256]{1,0:T(8,128)} %bitcast.114), channel_id=1, source_target_pairs={{0,4},{4,0},{8,12},{12,8},{16,20},{20,16},{24,28},{28,24},{32,36},... | collective-permute-start | bytes 3145736 | tf_op jit(solution)/shard_map/ppermute | solution.py:12
  210.2 26.4 %copy-start.24 = (s32[1024]{0:T(1024)S(1)}, s32[1024]{0:T(1024)}, u32[]{:S(2)}) copy-start(s32[1024]{0:T(1024)} %pad_clamp_fusion.6) | copy-start | bytes 12292
  212.6 23.6 %collective-permute-start.6 = (f32[1024,32]{0,1:T(8,128)S(1)}, f32[1024,32]{0,1:T(8,128)S(1)}, u32[]{:S(2)}, u32[]{:S(2)}) collective-permute-start(f32[1024,32]{0,1:T(8,128)S(1)} %fusion.6), channel_id=1, source_target_pairs={{0,32},{4,36},{8,40},{12,44},{16,48},{20,52},{24,56},{28,60},{32,0... | collective-permute-start | bytes 393224 | tf_op jit(solution)/shard_map/ppermute | solution.py:12
  232.6 45.4 %collective-permute-start.9 = (f32[1024,256]{1,0:T(8,128)}, f32[1024,256]{1,0:T(8,128)}, u32[]{:S(2)}, u32[]{:S(2)}) collective-permute-start(f32[1024,256]{1,0:T(8,128)} %bitcast.113), channel_id=1, source_target_pairs={{0,4},{4,0},{8,12},{12,8},{16,20},{20,16},{24,28},{28,24},{32,36},... | collective-permute-start | bytes 3145736 | tf_op jit(solution)/shard_map/ppermute | solution.py:12
  244.7 26.0 %copy-start.26 = (s32[1024]{0:T(1024)S(1)}, s32[1024]{0:T(1024)}, u32[]{:S(2)}) copy-start(s32[1024]{0:T(1024)} %pad_clamp_fusion.4) | copy-start | bytes 12292
  247.2 23.2 %collective-permute-start.8 = (f32[1024,32]{0,1:T(8,128)S(1)}, f32[1024,32]{0,1:T(8,128)S(1)}, u32[]{:S(2)}, u32[]{:S(2)}) collective-permute-start(f32[1024,32]{0,1:T(8,128)S(1)} %fusion.7), channel_id=1, source_target_pairs={{0,64},{4,68},{8,72},{12,76},{16,80},{20,84},{24,88},{28,92},{32,9... | collective-permute-start | bytes 393224 | tf_op jit(solution)/shard_map/ppermute | solution.py:12
  266.7 44.8 %collective-permute-start.11 = (f32[1024,256]{1,0:T(8,128)}, f32[1024,256]{1,0:T(8,128)}, u32[]{:S(2)}, u32[]{:S(2)}) collective-permute-start(f32[1024,256]{1,0:T(8,128)} %bitcast.112), channel_id=1, source_target_pairs={{0,4},{4,0},{8,12},{12,8},{16,20},{20,16},{24,28},{28,24},{32,36},... | collective-permute-start | bytes 3145736 | tf_op jit(solution)/shard_map/ppermute | solution.py:12
  276.1 28.6 %copy-start.28 = (s32[1024]{0:T(1024)S(1)}, s32[1024]{0:T(1024)}, u32[]{:S(2)}) copy-start(s32[1024]{0:T(1024)} %pad_clamp_fusion.2) | copy-start | bytes 12292
  279.8 24.6 %collective-permute-start.10 = (f32[1024,32]{0,1:T(8,128)S(1)}, f32[1024,32]{0,1:T(8,128)S(1)}, u32[]{:S(2)}, u32[]{:S(2)}) collective-permute-start(f32[1024,32]{0,1:T(8,128)S(1)} %fusion.8), channel_id=1, source_target_pairs={{0,128},{4,132},{8,136},{12,140},{16,144},{20,148},{24,152},{28,15... | collective-permute-start | bytes 393224 | tf_op jit(solution)/shard_map/ppermute | solution.py:12
  300.9 28.5 %collective-permute-start.13 = (f32[1024,256]{1,0:T(8,128)}, f32[1024,256]{1,0:T(8,128)}, u32[]{:S(2)}, u32[]{:S(2)}) collective-permute-start(f32[1024,256]{1,0:T(8,128)} %bitcast.111), channel_id=1, source_target_pairs={{0,4},{4,0},{8,12},{12,8},{16,20},{20,16},{24,28},{28,24},{32,36},... | collective-permute-start | bytes 3145736 | tf_op jit(solution)/shard_map/ppermute | solution.py:12
  313.3 8.9 %collective-permute-start.12 = (f32[1024,32]{0,1:T(8,128)S(1)}, f32[1024,32]{0,1:T(8,128)S(1)}, u32[]{:S(2)}, u32[]{:S(2)}) collective-permute-start(f32[1024,32]{0,1:T(8,128)S(1)} %fusion.9), channel_id=1, source_target_pairs={{0,256},{4,260},{8,264},{12,268},{16,272},{20,276},{24,280},{28,28... | collective-permute-start | bytes 393224 | tf_op jit(solution)/shard_map/ppermute | solution.py:12
  318.9 12.9 %all-to-all-start.2 = ((f32[4,256,32]{1,2,0:T(8,128)}), f32[4,256,32]{1,2,0:T(8,128)S(1)}, u32[]{:S(2)}, u32[]{:S(2)}) async-start(f32[4,256,32]{1,2,0:T(8,128)} %copy.240), calls=%async_computation.2 | async-start | bytes 262144 | tf_op jit(solution)/shard_map/all_to_all | solution.py:16
  331.9 9.0 %all-to-all-start.3 = ((f32[4,256,32]{1,2,0:T(8,128)}), f32[4,256,32]{1,2,0:T(8,128)S(1)}, u32[]{:S(2)}, u32[]{:S(2)}) async-start(f32[4,256,32]{1,2,0:T(8,128)} %bitcast.104), calls=%async_computation.3 | async-start | bytes 262144 | tf_op jit(solution)/shard_map/all_to_all | solution.py:16
  (41 other events, 252.4 us)
Sparse Core Ops, SparseCore 0:
  12.5 36.0 all-gather.20
  50.7 40.9 all-gather.18
  93.7 36.7 all-gather.22
  132.5 32.0 all-gather.24
  166.5 32.0 all-gather.26
  200.5 32.0 all-gather.28
  234.7 32.0 all-gather.30
  268.8 32.0 all-gather.32

commit v7 on v4

--- a/solution.py
+++ b/solution.py
@@ -22,14 +22,12 @@
     groups = lax.axis_size("case")
     quarter = value.shape[0] // groups
     chunks = value.reshape(groups, quarter, value.shape[1])
-    mine = chunks[position]
-    for shift in range(1, groups):
-        outgoing = chunks[(position + shift) % groups]
-        mine = mine + shifted(outgoing, "case", shift)
-    pieces = [mine] + [shifted(mine, "case", shift) for shift in range(1, groups)]
-    stacked = jnp.stack(pieces)
-    order = (position - jnp.arange(groups)) % groups
-    full = jnp.take(stacked, order, axis=0).reshape(value.shape)
+    received = lax.all_to_all(chunks, "case", split_axis=0, concat_axis=0)
+    mine = received[0]
+    for source in range(1, groups):
+        mine = mine + received[source]
+    copies = jnp.broadcast_to(mine[None], chunks.shape)
+    full = lax.all_to_all(copies, "case", split_axis=0, concat_axis=0).reshape(value.shape)
     return mine, full
 
 

time: 304 us -> 305 us (level)
  starting transfers between devices: 79.9 us -> 72.3 us
  waiting for transfers between devices: 124 us -> 128 us
    all_to_all x0 -> x2, waiting for transfers between devices: none -> 21.8 us  [the longest x1 14.9 us: case_allreduce(): received = lax.all_to_all(chunks, 'case', split_axis=0, concat_axis=0)]
    ppermute x6 -> x0, starting transfers between devices: 17 us -> none  [shifted(): return lax.ppermute(value, axis, pairs)]
    ppermute x6 -> x0, waiting for transfers between devices: 14.5 us -> none  [shifted(): return lax.ppermute(value, axis, pairs)]
    all_to_all x0 -> x2, starting transfers between devices: none -> 7.48 us  [the longest x1 4.01 us: case_allreduce(): received = lax.all_to_all(chunks, 'case', split_axis=0, concat_axis=0)]
  transfers between devices with their start and end apart: 26 -> 22, of which waited for: 18 -> 16; matrix products, arithmetic and copies ran while one was open for 23% -> 24% of each run, Pallas kernels for 0% -> 0%
where the time goes in v7:
time: 305 us; the launch traced here: 303 us
  waiting for transfers between devices  128 us (42%)
  starting transfers between devices  72.3 us (24%)
  local copies, waits for them, and re-layouts  44.2 us (14%)
  matrix products  31.2 us (10%)
  between operations  15.5 us (5%)
  other arithmetic  12.5 us (4%)
    ppermute x13, waiting for transfers between devices, from_partner(): return lax.ppermute(value, axis, pairs)  69.8 us
    ppermute x13, starting transfers between devices, from_partner(): return lax.ppermute(value, axis, pairs)  44 us
    all_to_all x1, waiting for transfers between devices, on_device(): lax.all_to_all(joined, 'sub', split_axis=1, concat_axis=0, tiled=True)  33.3 us
    dot_general x13, matrix products, rows_of(): jnp.dot(part, shared, precision=lax.Precision.HIGH)  29.6 us
    all_to_all x1, starting transfers between devices, on_device(): lax.all_to_all(joined, 'sub', split_axis=1, concat_axis=0, tiled=True)  20.6 us
    gather x13, local copies, waits for them, and re-layouts, rows_of(): jnp.take(stacked, index, axis=0)  18.1 us
    all_to_all x1, waiting for transfers between devices, case_allreduce(): received = lax.all_to_all(chunks, 'case', split_axis=0, concat_axis=0)  14.9 us
    gather x7, local copies, waits for them, and re-layouts, on_device(): jnp.take(stacked, left_index(maps[0, :shared_rows]), axis=0)  9.67 us
  transfers between devices with their start and end apart: 22, of which 16 were waited for; matrix products, arithmetic and copies ran while one was open for 24% of the time, Pallas kernels for 0%

profile of v7, /device:TPU:1, one launch (start us, length us, event | category | flops | bytes accessed | tf_op | source)
XLA Modules:
  0.0 303.5 jit_solution(5608718762518458902)
XLA Ops:
  7.2 3.5 %fusion.106 = (f32[1,1,256,512]{3,2,1,0:T(8,128)}, f32[1,1,256,512]{3,2,1,0:T(8,128)}, f32[1,1,256,512]{3,2,1,0:T(8,128)}, f32[1,1,256,512]{3,2,1,0:T(8,128)}, f...) fusion(f32[1,7,256,512]{3,2,1,0:T(8,128)} %param.15), kind=kLoop, calls=%fused_computation.304 | loop fusion | bytes 6291456 | tf_op jit(solution)/shard_map/slice | solution.py:84
  15.5 20.6 %all-to-all-start = ((f32[1,128,1280]{2,0,1:T(1,128)}), f32[1,128,1280]{2,0,1:T(1,128)S(1)}, u32[]{:S(2)}, u32[]{:S(2)}) async-start(f32[1,128,1280]{2,0,1:T(1,128)} %pad_maximum_fusion.7), calls=%async_computation | async-start | bytes 1310720 | tf_op jit(solution)/shard_map/all_to_all | solution.py:40
  41.1 33.3 %all-to-all-done = f32[1,128,1280]{2,0,1:T(1,128)S(1)} async-done(((f32[1,128,1280]{2,0,1:T(1,128)}), f32[1,128,1280]{2,0,1:T(1,128)S(1)}, u32[]{:S(2)}, u32[]{:S(2)}) %all-to-all-start) | async-done | bytes 655392 | tf_op jit(solution)/shard_map/all_to_all | solution.py:40
  78.1 4.0 %all-to-all-start.1 = ((f32[4,256,128]{2,1,0:T(8,128)}), f32[4,256,128]{2,1,0:T(8,128)S(1)}, u32[]{:S(2)}, u32[]{:S(2)}) async-start(f32[4,256,128]{2,1,0:T(8,128)} %bitcast.11), calls=%async_computation.1 | async-start | bytes 1048576 | tf_op jit(solution)/shard_map/all_to_all | solution.py:25
  82.2 14.9 %all-to-all-done.1 = f32[4,256,128]{2,1,0:T(8,128)S(1)} async-done(((f32[4,256,128]{2,1,0:T(8,128)}), f32[4,256,128]{2,1,0:T(8,128)S(1)}, u32[]{:S(2)}, u32[]{:S(2)}) %all-to-all-start.1) | async-done | bytes 524320 | tf_op jit(solution)/shard_map/all_to_all | solution.py:25
  97.9 3.5 %all-to-all-start.2 = ((f32[4,256,128]{2,1,0:T(8,128)}), f32[4,256,128]{2,1,0:T(8,128)S(1)}, u32[]{:S(2)}, u32[]{:S(2)}) async-start(f32[4,256,128]{2,1,0:T(8,128)} %broadcast_in_dim.55), calls=%async_computation.2 | async-start | bytes 1048576 | tf_op jit(solution)/shard_map/all_to_all | solution.py:30
  101.4 6.9 %all-to-all-done.2 = f32[4,256,128]{2,1,0:T(8,128)S(1)} async-done(((f32[4,256,128]{2,1,0:T(8,128)}), f32[4,256,128]{2,1,0:T(8,128)S(1)}, u32[]{:S(2)}, u32[]{:S(2)}) %all-to-all-start.2) | async-done | bytes 524320 | tf_op jit(solution)/shard_map/all_to_all | solution.py:30
  108.3 5.6 %collective-permute-start = (f32[1024,128]{1,0:T(8,128)S(1)}, f32[1024,128]{1,0:T(8,128)S(1)}, u32[]{:S(2)}, u32[]{:S(2)}) collective-permute-start(f32[1024,128]{1,0:T(8,128)S(1)} %bitcast.146), channel_id=1, source_target_pairs={{0,4},{4,0},{8,12},{12,8},{16,20},{20,16},{24,28},{28,24},{32,36},... | collective-permute-start | bytes 1572872 | tf_op jit(solution)/shard_map/ppermute | solution.py:12
  120.6 3.5 %collective-permute-start.1 = (f32[512,128]{1,0:T(8,128)S(1)}, f32[512,128]{1,0:T(8,128)S(1)}, u32[]{:S(2)}, u32[]{:S(2)}) collective-permute-start(f32[512,128]{1,0:T(8,128)S(1)} %select_subtract_fusion.11), channel_id=1, source_target_pairs={{0,8},{4,12},{8,0},{12,4},{16,24},{20,28},{24,16},{28,20},{32,40},... | collective-permute-start | bytes 786440 | tf_op jit(solution)/shard_map/ppermute | solution.py:12
  127.2 3.2 %collective-permute-done.1 = f32[512,128]{1,0:T(8,128)S(1)} collective-permute-done((f32[512,128]{1,0:T(8,128)S(1)}, f32[512,128]{1,0:T(8,128)S(1)}, u32[]{:S(2)}, u32[]{:S(2)}) %collective-permute-start.1) | collective-permute-done | bytes 262176 | tf_op jit(solution)/shard_map/ppermute | solution.py:12
  130.4 2.9 collective-permute-start.2
  139.7 3.2 %collective-permute-start.3 = (f32[512,128]{1,0:T(8,128)S(1)}, f32[512,128]{1,0:T(8,128)S(1)}, u32[]{:S(2)}, u32[]{:S(2)}) collective-permute-start(f32[512,128]{1,0:T(8,128)S(1)} %select_subtract_fusion.9), channel_id=1, source_target_pairs={{0,16},{4,20},{8,24},{12,28},{16,0},{20,4},{24,8},{28,12},{32,48},... | collective-permute-start | bytes 786440 | tf_op jit(solution)/shard_map/ppermute | solution.py:12
  145.9 9.8 %collective-permute-done.3 = f32[512,128]{1,0:T(8,128)S(1)} collective-permute-done((f32[512,128]{1,0:T(8,128)S(1)}, f32[512,128]{1,0:T(8,128)S(1)}, u32[]{:S(2)}, u32[]{:S(2)}) %collective-permute-start.3) | collective-permute-done | bytes 262176 | tf_op jit(solution)/shard_map/ppermute | solution.py:12
  155.6 3.1 %collective-permute-start.4 = (f32[512,128]{1,0:T(8,128)S(1)}, f32[512,128]{1,0:T(8,128)S(1)}, u32[]{:S(2)}, u32[]{:S(2)}) collective-permute-start(f32[512,128]{1,0:T(8,128)S(1)} %collective-permute-done.3), channel_id=1, source_target_pairs={{0,4},{4,0},{8,12},{12,8},{16,20},{20,16},{24,28},{28,24},{32,36},... | collective-permute-start | bytes 786440 | tf_op jit(solution)/shard_map/ppermute | solution.py:12
  165.8 3.0 collective-permute-start.5
  172.5 22.7 %collective-permute-done.5 = f32[512,128]{1,0:T(8,128)} collective-permute-done((f32[512,128]{1,0:T(8,128)S(1)}, f32[512,128]{1,0:T(8,128)}, u32[]{:S(2)}, u32[]{:S(2)}) %collective-permute-start.5) | collective-permute-done | bytes 262176 | tf_op jit(solution)/shard_map/ppermute | solution.py:12
  195.2 2.4 collective-permute-start.6
  204.9 2.2 select_subtract_fusion.5
  207.1 6.6 %collective-permute-start.7 = (f32[512,128]{1,0:T(8,128)S(1)}, f32[512,128]{1,0:T(8,128)}, u32[]{:S(2)}, u32[]{:S(2)}) collective-permute-start(f32[512,128]{1,0:T(8,128)S(1)} %select_subtract_fusion.5), channel_id=1, source_target_pairs={{0,64},{4,68},{8,72},{12,76},{16,80},{20,84},{24,88},{28,92},{32,9... | collective-permute-start | bytes 786440 | tf_op jit(solution)/shard_map/ppermute | solution.py:12
  215.3 2.2 select_subtract_fusion.4
  217.5 19.8 %collective-permute-done.7 = f32[512,128]{1,0:T(8,128)} collective-permute-done((f32[512,128]{1,0:T(8,128)S(1)}, f32[512,128]{1,0:T(8,128)}, u32[]{:S(2)}, u32[]{:S(2)}) %collective-permute-start.7) | collective-permute-done | bytes 262176 | tf_op jit(solution)/shard_map/ppermute | solution.py:12
  237.3 2.4 collective-permute-start.8
  247.0 2.9 select_subtract_fusion.3
  249.9 2.4 collective-permute-start.9
  256.7 2.7 collective-permute-done.9
  259.4 3.3 %collective-permute-start.10 = (f32[512,128]{1,0:T(8,128)}, f32[512,128]{1,0:T(8,128)S(1)}, u32[]{:S(2)}, u32[]{:S(2)}) collective-permute-start(f32[512,128]{1,0:T(8,128)} %collective-permute-done.9), channel_id=1, source_target_pairs={{0,4},{4,0},{8,12},{12,8},{16,20},{20,16},{24,28},{28,24},{32,36},... | collective-permute-start | bytes 786440 | tf_op jit(solution)/shard_map/ppermute | solution.py:12
  270.1 2.9 select_subtract_fusion.1
  272.9 2.7 collective-permute-start.11
  277.3 2.9 select_subtract_fusion
  280.2 4.0 %collective-permute-done.11 = f32[512,128]{1,0:T(8,128)} collective-permute-done((f32[512,128]{1,0:T(8,128)}, f32[512,128]{1,0:T(8,128)}, u32[]{:S(2)}, u32[]{:S(2)}) %collective-permute-start.11) | collective-permute-done | bytes 262176 | tf_op jit(solution)/shard_map/ppermute | solution.py:12
  284.1 3.1 %collective-permute-start.12 = (f32[512,128]{1,0:T(8,128)}, f32[512,128]{1,0:T(8,128)}, u32[]{:S(2)}, u32[]{:S(2)}) collective-permute-start(f32[512,128]{1,0:T(8,128)} %collective-permute-done.11), channel_id=1, source_target_pairs={{0,4},{4,0},{8,12},{12,8},{16,20},{20,16},{24,28},{28,24},{32,36},... | collective-permute-start | bytes 786440 | tf_op jit(solution)/shard_map/ppermute | solution.py:12
  294.1 2.6 fusion.54
  (196 shorter events, 79.7 us)
Async XLA Ops:
  7.2 111.5 %all-gather.13.cloned.1.call-start = ((), (), s32[]{:S(2)}) async-start(), calls=%async_computation.3 | async-start | bytes 2621440 | tf_op jit(solution)/shard_map/all_gather | solution.py:84
  10.7 126.9 %all-gather.15.cloned.1.call-start = ((), (), s32[]{:S(2)}) async-start(), calls=%async_computation.4 | async-start | bytes 2621440 | tf_op jit(solution)/shard_map/all_gather | solution.py:84
  11.5 152.2 %all-gather.17.cloned.1.call-start = ((), (), s32[]{:S(2)}) async-start(), calls=%async_computation.5 | async-start | bytes 2621440 | tf_op jit(solution)/shard_map/all_gather | solution.py:84
  12.2 192.6 %all-gather.19.cloned.1.call-start = ((), (), s32[]{:S(2)}) async-start(), calls=%async_computation.6 | async-start | bytes 2621440 | tf_op jit(solution)/shard_map/all_gather | solution.py:84
  12.8 234.2 %all-gather.21.cloned.1.call-start = ((), (), s32[]{:S(2)}) async-start(), calls=%async_computation.7 | async-start | bytes 2621440 | tf_op jit(solution)/shard_map/all_gather | solution.py:84
  13.6 23.2 %copy-start.21 = (s32[1,32]{1,0:T(1,128)S(1)}, s32[1,32]{1,0:T(1,128)}, u32[]{:S(2)}) copy-start(s32[1,32]{1,0:T(1,128)} %param.13) | copy-start | bytes 388
  13.6 23.2 %copy-start.7 = (s32[1,7,2,1024]{3,2,1,0:T(2,128)S(1)}, s32[1,7,2,1024]{3,2,1,0:T(2,128)}, u32[]{:S(2)}) copy-start(s32[1,7,2,1024]{3,2,1,0:T(2,128)} %param.14) | copy-start | bytes 172036
  14.1 25.1 %copy-start.4 = (f32[1,32,4096]{2,1,0:T(8,128)S(1)}, f32[1,32,4096]{2,1,0:T(8,128)}, u32[]{:S(2)}) copy-start(f32[1,32,4096]{2,1,0:T(8,128)} %param.11) | copy-start | bytes 1572868
  15.5 58.9 %all-to-all-start = ((f32[1,128,1280]{2,0,1:T(1,128)}), f32[1,128,1280]{2,0,1:T(1,128)S(1)}, u32[]{:S(2)}, u32[]{:S(2)}) async-start(f32[1,128,1280]{2,0,1:T(1,128)} %pad_maximum_fusion.7), calls=%async_computation | async-start | bytes 1310720 | tf_op jit(solution)/shard_map/all_to_all | solution.py:40
  36.1 233.9 %all-gather.23.cloned.1.call-start = ((), (), s32[]{:S(2)}) async-start(), calls=%async_computation.8 | async-start | bytes 2621440 | tf_op jit(solution)/shard_map/all_gather | solution.py:84
  78.1 18.9 %all-to-all-start.1 = ((f32[4,256,128]{2,1,0:T(8,128)}), f32[4,256,128]{2,1,0:T(8,128)S(1)}, u32[]{:S(2)}, u32[]{:S(2)}) async-start(f32[4,256,128]{2,1,0:T(8,128)} %bitcast.11), calls=%async_computation.1 | async-start | bytes 1048576 | tf_op jit(solution)/shard_map/all_to_all | solution.py:25
  97.9 10.4 %all-to-all-start.2 = ((f32[4,256,128]{2,1,0:T(8,128)}), f32[4,256,128]{2,1,0:T(8,128)S(1)}, u32[]{:S(2)}, u32[]{:S(2)}) async-start(f32[4,256,128]{2,1,0:T(8,128)} %broadcast_in_dim.55), calls=%async_computation.2 | async-start | bytes 1048576 | tf_op jit(solution)/shard_map/all_to_all | solution.py:30
  108.3 7.1 %collective-permute-start = (f32[1024,128]{1,0:T(8,128)S(1)}, f32[1024,128]{1,0:T(8,128)S(1)}, u32[]{:S(2)}, u32[]{:S(2)}) collective-permute-start(f32[1024,128]{1,0:T(8,128)S(1)} %bitcast.146), channel_id=1, source_target_pairs={{0,4},{4,0},{8,12},{12,8},{16,20},{20,16},{24,28},{28,24},{32,36},... | collective-permute-start | bytes 1572872 | tf_op jit(solution)/shard_map/ppermute | solution.py:12
  118.7 6.5 %copy-start.10 = (pred[512]{0:T(512)(128)(4,1)S(1)}, pred[512]{0:T(512)(128)(4,1)}, u32[]{:S(2)}) copy-start(pred[512]{0:T(512)(128)(4,1)} %get-tuple-element.61) | copy-start | bytes 1540
  120.6 9.7 %collective-permute-start.1 = (f32[512,128]{1,0:T(8,128)S(1)}, f32[512,128]{1,0:T(8,128)S(1)}, u32[]{:S(2)}, u32[]{:S(2)}) collective-permute-start(f32[512,128]{1,0:T(8,128)S(1)} %select_subtract_fusion.11), channel_id=1, source_target_pairs={{0,8},{4,12},{8,0},{12,4},{16,24},{20,28},{24,16},{28,20},{32,40},... | collective-permute-start | bytes 786440 | tf_op jit(solution)/shard_map/ppermute | solution.py:12
  130.4 4.0 %collective-permute-start.2 = (f32[512,128]{1,0:T(8,128)S(1)}, f32[512,128]{1,0:T(8,128)S(1)}, u32[]{:S(2)}, u32[]{:S(2)}) collective-permute-start(f32[512,128]{1,0:T(8,128)S(1)} %collective-permute-done.1), channel_id=1, source_target_pairs={{0,4},{4,0},{8,12},{12,8},{16,20},{20,16},{24,28},{28,24},{32,36},... | collective-permute-start | bytes 786440 | tf_op jit(solution)/shard_map/ppermute | solution.py:12
  137.7 6.2 %copy-start.11 = (pred[512]{0:T(512)(128)(4,1)S(1)}, pred[512]{0:T(512)(128)(4,1)}, u32[]{:S(2)}) copy-start(pred[512]{0:T(512)(128)(4,1)} %get-tuple-element.53) | copy-start | bytes 1540
  139.7 15.9 %collective-permute-start.3 = (f32[512,128]{1,0:T(8,128)S(1)}, f32[512,128]{1,0:T(8,128)S(1)}, u32[]{:S(2)}, u32[]{:S(2)}) collective-permute-start(f32[512,128]{1,0:T(8,128)S(1)} %select_subtract_fusion.9), channel_id=1, source_target_pairs={{0,16},{4,20},{8,24},{12,28},{16,0},{20,4},{24,8},{28,12},{32,48},... | collective-permute-start | bytes 786440 | tf_op jit(solution)/shard_map/ppermute | solution.py:12
  155.6 4.2 %collective-permute-start.4 = (f32[512,128]{1,0:T(8,128)S(1)}, f32[512,128]{1,0:T(8,128)S(1)}, u32[]{:S(2)}, u32[]{:S(2)}) collective-permute-start(f32[512,128]{1,0:T(8,128)S(1)} %collective-permute-done.3), channel_id=1, source_target_pairs={{0,4},{4,0},{8,12},{12,8},{16,20},{20,16},{24,28},{28,24},{32,36},... | collective-permute-start | bytes 786440 | tf_op jit(solution)/shard_map/ppermute | solution.py:12
  163.7 6.8 %copy-start.8 = (pred[512]{0:T(512)(128)(4,1)S(1)}, pred[512]{0:T(512)(128)(4,1)}, u32[]{:S(2)}) copy-start(pred[512]{0:T(512)(128)(4,1)} %get-tuple-element.45) | copy-start | bytes 1540
  165.8 29.4 %collective-permute-start.5 = (f32[512,128]{1,0:T(8,128)S(1)}, f32[512,128]{1,0:T(8,128)}, u32[]{:S(2)}, u32[]{:S(2)}) collective-permute-start(f32[512,128]{1,0:T(8,128)S(1)} %select_subtract_fusion.7), channel_id=1, source_target_pairs={{0,32},{4,36},{8,40},{12,44},{16,48},{20,52},{24,56},{28,60},{32,0... | collective-permute-start | bytes 786440 | tf_op jit(solution)/shard_map/ppermute | solution.py:12
  195.2 3.7 %collective-permute-start.6 = (f32[512,128]{1,0:T(8,128)}, f32[512,128]{1,0:T(8,128)S(1)}, u32[]{:S(2)}, u32[]{:S(2)}) collective-permute-start(f32[512,128]{1,0:T(8,128)} %collective-permute-done.5), channel_id=1, source_target_pairs={{0,4},{4,0},{8,12},{12,8},{16,20},{20,16},{24,28},{28,24},{32,36},... | collective-permute-start | bytes 786440 | tf_op jit(solution)/shard_map/ppermute | solution.py:12
  204.9 10.5 %copy-start.16 = (pred[512]{0:T(512)(128)(4,1)S(1)}, pred[512]{0:T(512)(128)(4,1)}, u32[]{:S(2)}) copy-start(pred[512]{0:T(512)(128)(4,1)} %get-tuple-element.37) | copy-start | bytes 1540
  207.1 30.2 %collective-permute-start.7 = (f32[512,128]{1,0:T(8,128)S(1)}, f32[512,128]{1,0:T(8,128)}, u32[]{:S(2)}, u32[]{:S(2)}) collective-permute-start(f32[512,128]{1,0:T(8,128)S(1)} %select_subtract_fusion.5), channel_id=1, source_target_pairs={{0,64},{4,68},{8,72},{12,76},{16,80},{20,84},{24,88},{28,92},{32,9... | collective-permute-start | bytes 786440 | tf_op jit(solution)/shard_map/ppermute | solution.py:12
  217.5 23.5 %copy-start = (f32[512,128]{1,0:T(8,128)}, f32[512,128]{1,0:T(8,128)S(1)}, u32[]{:S(2)}) copy-start(f32[512,128]{1,0:T(8,128)S(1)} %select_subtract_fusion.4) | copy-start | bytes 786436
  237.3 3.7 %collective-permute-start.8 = (f32[512,128]{1,0:T(8,128)}, f32[512,128]{1,0:T(8,128)S(1)}, u32[]{:S(2)}, u32[]{:S(2)}) collective-permute-start(f32[512,128]{1,0:T(8,128)} %collective-permute-done.7), channel_id=1, source_target_pairs={{0,4},{4,0},{8,12},{12,8},{16,20},{20,16},{24,28},{28,24},{32,36},... | collective-permute-start | bytes 786440 | tf_op jit(solution)/shard_map/ppermute | solution.py:12
  247.0 7.6 %copy-start.14 = (pred[512]{0:T(512)(128)(4,1)S(1)}, pred[512]{0:T(512)(128)(4,1)}, u32[]{:S(2)}) copy-start(pred[512]{0:T(512)(128)(4,1)} %get-tuple-element.29) | copy-start | bytes 1540
  249.9 9.6 %collective-permute-start.9 = (f32[512,128]{1,0:T(8,128)}, f32[512,128]{1,0:T(8,128)}, u32[]{:S(2)}, u32[]{:S(2)}) collective-permute-start(f32[512,128]{1,0:T(8,128)} %select_subtract_fusion.3), channel_id=1, source_target_pairs={{0,128},{4,132},{8,136},{12,140},{16,144},{20,148},{24,152},{28,15... | collective-permute-start | bytes 786440 | tf_op jit(solution)/shard_map/ppermute | solution.py:12
  256.7 7.3 %copy-start.2 = (f32[512,128]{1,0:T(8,128)}, f32[512,128]{1,0:T(8,128)S(1)}, u32[]{:S(2)}) copy-start(f32[512,128]{1,0:T(8,128)S(1)} %select_subtract_fusion.2) | copy-start | bytes 786436
  259.4 4.6 %collective-permute-start.10 = (f32[512,128]{1,0:T(8,128)}, f32[512,128]{1,0:T(8,128)S(1)}, u32[]{:S(2)}, u32[]{:S(2)}) collective-permute-start(f32[512,128]{1,0:T(8,128)} %collective-permute-done.9), channel_id=1, source_target_pairs={{0,4},{4,0},{8,12},{12,8},{16,20},{20,16},{24,28},{28,24},{32,36},... | collective-permute-start | bytes 786440 | tf_op jit(solution)/shard_map/ppermute | solution.py:12
  272.9 11.2 %collective-permute-start.11 = (f32[512,128]{1,0:T(8,128)}, f32[512,128]{1,0:T(8,128)}, u32[]{:S(2)}, u32[]{:S(2)}) collective-permute-start(f32[512,128]{1,0:T(8,128)} %select_subtract_fusion.1), channel_id=1, source_target_pairs={{0,256},{4,260},{8,264},{12,268},{16,272},{20,276},{24,280},{28,28... | collective-permute-start | bytes 786440 | tf_op jit(solution)/shard_map/ppermute | solution.py:12
  284.1 4.6 %collective-permute-start.12 = (f32[512,128]{1,0:T(8,128)}, f32[512,128]{1,0:T(8,128)}, u32[]{:S(2)}, u32[]{:S(2)}) collective-permute-start(f32[512,128]{1,0:T(8,128)} %collective-permute-done.11), channel_id=1, source_target_pairs={{0,4},{4,0},{8,12},{12,8},{16,20},{20,16},{24,28},{28,24},{32,36},... | collective-permute-start | bytes 786440 | tf_op jit(solution)/shard_map/ppermute | solution.py:12
  (12 other events, 30.7 us)
Sparse Core Ops, SparseCore 0:
  10.9 43.7 all-gather.12
  56.8 44.1 all-gather.14
  103.1 41.5 all-gather.16
  146.6 38.5 all-gather.18
  187.2 38.5 all-gather.20
  227.8 38.5 all-gather.22

commit v8 on v7

--- a/solution.py
+++ b/solution.py
@@ -106,29 +106,45 @@
         def right_index(index):
             return jnp.where(upper, own_index(index), own_index(index) + full_rows)
 
-        shared = jnp.take(stacked, left_index(maps[0, :shared_rows]), axis=0) + jnp.take(
-            stacked, right_index(maps[1, :shared_rows]), axis=0
-        )
         kept_index = jnp.concatenate(
             [left_index(maps[0, shared_rows:]), right_index(maps[1, shared_rows:])]
         )
+        if last:
+            first_begin, first_count = position * quarter, quarter
+        else:
+            first_begin, first_count = turn, rows_half
+        picked = jnp.take(
+            stacked,
+            jnp.concatenate(
+                [
+                    left_index(maps[0, :shared_rows]),
+                    right_index(maps[1, :shared_rows]),
+                    lax.dynamic_slice_in_dim(kept_index, first_begin, first_count),
+                ]
+            ),
+            axis=0,
+            mode="clip",
+        )
+        shared = picked[:shared_rows] + picked[shared_rows : 2 * shared_rows]
 
-        def rows_of(begin, count):
-            index = lax.dynamic_slice_in_dim(kept_index, begin, count)
+        def rows_of(begin, count, kept=None):
+            if kept is None:
+                index = lax.dynamic_slice_in_dim(kept_index, begin, count)
+                kept = jnp.take(stacked, index, axis=0, mode="clip")
             if last:
                 part = lax.dynamic_slice_in_dim(matrix, 0, count, 0)
             else:
                 part = lax.dynamic_slice_in_dim(matrix, begin, count, 0)
-            return jnp.take(stacked, index, axis=0) - jnp.dot(
-                part, shared, precision=lax.Precision.HIGH
-            )
+            return kept - jnp.dot(part, shared, precision=lax.Precision.HIGH)
+
+        first_kept = picked[2 * shared_rows :]
 
         is_node = slot % (2 * half) == half
         if last:
             is_node = jnp.logical_or(is_node, slot == 0)
-            own = rows_of(position * quarter, quarter)
+            own = rows_of(first_begin, first_count, first_kept)
         else:
-            first = rows_of(turn, rows_half)
+            first = rows_of(first_begin, first_count, first_kept)
             second = rows_of(rows_half - turn, rows_half)
             current = jnp.concatenate([first, second], axis=0)
             rest = second

time: 305 us -> 300 us (0.984)
  local copies, waits for them, and re-layouts: 44.2 us -> 39.5 us
    gather x27 -> x13, local copies, waits for them, and re-layouts: 37.4 us -> 32.3 us  [the longest x7 23 us: on_device(): jnp.take(stacked, jnp.concatenate([left_index(maps[0, :shared_rows]), rig...]
    sub x0 -> x6, other arithmetic: none -> 4.94 us  [rows_of(): return kept - jnp.dot(part, shared, precision=lax.Precision.HIGH)]
    ppermute x13, waiting for transfers between devices: 69.8 us -> 65.2 us  [from_partner(): return lax.ppermute(value, axis, pairs)]
    and x14 -> x0, other arithmetic: 4.55 us -> none  [the longest x7 3.9 us: rows_of(): jnp.take(stacked, index, axis=0)]
    all_to_all x1, waiting for transfers between devices: 33.3 us -> 36.3 us  [on_device(): lax.all_to_all(joined, 'sub', split_axis=1, concat_axis=0, tiled=True)]
  transfers between devices with their start and end apart: 22 -> 22, of which waited for: 16 -> 17; matrix products, arithmetic and copies ran while one was open for 24% -> 23% of each run, Pallas kernels for 0% -> 0%
where the time goes in v8:
time: 300 us; the launch traced here: 298 us
  waiting for transfers between devices  127 us (42%)
  starting transfers between devices  74 us (25%)
  local copies, waits for them, and re-layouts  39.5 us (13%)
  matrix products  28.8 us (10%)
  between operations  15.2 us (5%)
  other arithmetic  13.6 us (5%)
    ppermute x13, waiting for transfers between devices, from_partner(): return lax.ppermute(value, axis, pairs)  65.2 us
    ppermute x13, starting transfers between devices, from_partner(): return lax.ppermute(value, axis, pairs)  45.7 us
    all_to_all x1, waiting for transfers between devices, on_device(): lax.all_to_all(joined, 'sub', split_axis=1, concat_axis=0, tiled=True)  36.3 us
    dot_general x13, matrix products, rows_of(): return kept - jnp.dot(part, shared, precision=lax.Precision.HIGH)  27.3 us
    gather x7, local copies, waits for them, and re-layouts, on_device(): jnp.take(stacked, jnp.concatenate([left_index(maps[0, :shared_rows]), rig...  23 us
    all_to_all x1, starting transfers between devices, on_device(): lax.all_to_all(joined, 'sub', split_axis=1, concat_axis=0, tiled=True)  20.6 us
    all_to_all x1, waiting for transfers between devices, case_allreduce(): received = lax.all_to_all(chunks, 'case', split_axis=0, concat_axis=0)  14.9 us
    gather x6, local copies, waits for them, and re-layouts, rows_of(): kept = jnp.take(stacked, index, axis=0, mode='clip')  9.25 us
  transfers between devices with their start and end apart: 22, of which 17 were waited for; matrix products, arithmetic and copies ran while one was open for 23% of the time, Pallas kernels for 0%

profile of v8, /device:TPU:1, one launch (start us, length us, event | category | flops | bytes accessed | tf_op | source)
XLA Modules:
  0.0 298.3 jit_solution(3899373143181106477)
XLA Ops:
  7.2 3.5 %fusion.88 = (f32[1,1,256,512]{3,2,1,0:T(8,128)}, f32[1,1,256,512]{3,2,1,0:T(8,128)}, f32[1,1,256,512]{3,2,1,0:T(8,128)}, f32[1,1,256,512]{3,2,1,0:T(8,128)}, f3...) fusion(f32[1,7,256,512]{3,2,1,0:T(8,128)} %param.13), kind=kLoop, calls=%fused_computation.220 | loop fusion | bytes 6291456 | tf_op jit(solution)/shard_map/slice | solution.py:84
  15.6 20.6 %all-to-all-start = ((f32[1,128,1280]{2,0,1:T(1,128)}), f32[1,128,1280]{2,0,1:T(1,128)S(1)}, u32[]{:S(2)}, u32[]{:S(2)}) async-start(f32[1,128,1280]{2,0,1:T(1,128)} %pad_maximum_fusion.7), calls=%async_computation | async-start | bytes 1310720 | tf_op jit(solution)/shard_map/all_to_all | solution.py:40
  38.1 36.3 %all-to-all-done = f32[1,128,1280]{2,0,1:T(1,128)S(1)} async-done(((f32[1,128,1280]{2,0,1:T(1,128)}), f32[1,128,1280]{2,0,1:T(1,128)S(1)}, u32[]{:S(2)}, u32[]{:S(2)}) %all-to-all-start) | async-done | bytes 655392 | tf_op jit(solution)/shard_map/all_to_all | solution.py:40
  78.1 4.0 %all-to-all-start.1 = ((f32[4,256,128]{2,1,0:T(8,128)}), f32[4,256,128]{2,1,0:T(8,128)S(1)}, u32[]{:S(2)}, u32[]{:S(2)}) async-start(f32[4,256,128]{2,1,0:T(8,128)} %bitcast.11), calls=%async_computation.1 | async-start | bytes 1048576 | tf_op jit(solution)/shard_map/all_to_all | solution.py:25
  82.2 14.9 %all-to-all-done.1 = f32[4,256,128]{2,1,0:T(8,128)S(1)} async-done(((f32[4,256,128]{2,1,0:T(8,128)}), f32[4,256,128]{2,1,0:T(8,128)S(1)}, u32[]{:S(2)}, u32[]{:S(2)}) %all-to-all-start.1) | async-done | bytes 524320 | tf_op jit(solution)/shard_map/all_to_all | solution.py:25
  97.9 3.5 %all-to-all-start.2 = ((f32[4,256,128]{2,1,0:T(8,128)}), f32[4,256,128]{2,1,0:T(8,128)S(1)}, u32[]{:S(2)}, u32[]{:S(2)}) async-start(f32[4,256,128]{2,1,0:T(8,128)} %broadcast_in_dim.75), calls=%async_computation.2 | async-start | bytes 1048576 | tf_op jit(solution)/shard_map/all_to_all | solution.py:30
  101.4 6.9 %all-to-all-done.2 = f32[4,256,128]{2,1,0:T(8,128)S(1)} async-done(((f32[4,256,128]{2,1,0:T(8,128)}), f32[4,256,128]{2,1,0:T(8,128)S(1)}, u32[]{:S(2)}, u32[]{:S(2)}) %all-to-all-start.2) | async-done | bytes 524320 | tf_op jit(solution)/shard_map/all_to_all | solution.py:30
  108.3 5.6 %collective-permute-start = (f32[1024,128]{1,0:T(8,128)S(1)}, f32[1024,128]{1,0:T(8,128)S(1)}, u32[]{:S(2)}, u32[]{:S(2)}) collective-permute-start(f32[1024,128]{1,0:T(8,128)S(1)} %bitcast.134), channel_id=1, source_target_pairs={{0,4},{4,0},{8,12},{12,8},{16,20},{20,16},{24,28},{28,24},{32,36},... | collective-permute-start | bytes 1572872 | tf_op jit(solution)/shard_map/ppermute | solution.py:12
  115.5 2.6 gather_fusion.1
  119.9 3.4 %collective-permute-start.1 = (f32[512,128]{1,0:T(8,128)S(1)}, f32[512,128]{1,0:T(8,128)S(1)}, u32[]{:S(2)}, u32[]{:S(2)}) collective-permute-start(f32[512,128]{1,0:T(8,128)S(1)} %slice_subtract_fusion.5), channel_id=1, source_target_pairs={{0,8},{4,12},{8,0},{12,4},{16,24},{20,28},{24,16},{28,20},{32,40},... | collective-permute-start | bytes 786440 | tf_op jit(solution)/shard_map/ppermute | solution.py:12
  126.4 3.2 %collective-permute-done.1 = f32[512,128]{1,0:T(8,128)S(1)} collective-permute-done((f32[512,128]{1,0:T(8,128)S(1)}, f32[512,128]{1,0:T(8,128)S(1)}, u32[]{:S(2)}, u32[]{:S(2)}) %collective-permute-start.1) | collective-permute-done | bytes 262176 | tf_op jit(solution)/shard_map/ppermute | solution.py:12
  129.6 2.9 collective-permute-start.2
  133.7 2.6 gather_fusion.3
  138.2 3.0 %collective-permute-start.3 = (f32[512,128]{1,0:T(8,128)S(1)}, f32[512,128]{1,0:T(8,128)}, u32[]{:S(2)}, u32[]{:S(2)}) collective-permute-start(f32[512,128]{1,0:T(8,128)S(1)} %slice_subtract_fusion.4), channel_id=1, source_target_pairs={{0,16},{4,20},{8,24},{12,28},{16,0},{20,4},{24,8},{28,12},{32,48},... | collective-permute-start | bytes 786440 | tf_op jit(solution)/shard_map/ppermute | solution.py:12
  145.7 8.6 %collective-permute-done.3 = f32[512,128]{1,0:T(8,128)} collective-permute-done((f32[512,128]{1,0:T(8,128)S(1)}, f32[512,128]{1,0:T(8,128)}, u32[]{:S(2)}, u32[]{:S(2)}) %collective-permute-start.3) | collective-permute-done | bytes 262176 | tf_op jit(solution)/shard_map/ppermute | solution.py:12
  154.3 3.3 %collective-permute-start.4 = (f32[512,128]{1,0:T(8,128)}, f32[512,128]{1,0:T(8,128)S(1)}, u32[]{:S(2)}, u32[]{:S(2)}) collective-permute-start(f32[512,128]{1,0:T(8,128)} %collective-permute-done.3), channel_id=1, source_target_pairs={{0,4},{4,0},{8,12},{12,8},{16,20},{20,16},{24,28},{28,24},{32,36},... | collective-permute-start | bytes 786440 | tf_op jit(solution)/shard_map/ppermute | solution.py:12
  159.7 3.7 %gather_fusion.5 = f32[1536,128]{1,0:T(8,128)} fusion(f32[2048,128]{1,0:T(8,128)S(1)} %pad_maximum_fusion.2, s32[2048]{0:T(1024)S(1)} %pad_clamp_fusion.4), kind=kCustom, calls=%fused_computation.5 | custom fusion | bytes 1579008 | tf_op jit(solution)/shard_map/jit(_take)/gather | solution.py:116
  165.6 3.0 %collective-permute-start.5 = (f32[512,128]{1,0:T(8,128)S(1)}, f32[512,128]{1,0:T(8,128)}, u32[]{:S(2)}, u32[]{:S(2)}) collective-permute-start(f32[512,128]{1,0:T(8,128)S(1)} %slice_subtract_fusion.3), channel_id=1, source_target_pairs={{0,32},{4,36},{8,40},{12,44},{16,48},{20,52},{24,56},{28,60},{32,0... | collective-permute-start | bytes 786440 | tf_op jit(solution)/shard_map/ppermute | solution.py:12
  173.2 21.7 %collective-permute-done.5 = f32[512,128]{1,0:T(8,128)} collective-permute-done((f32[512,128]{1,0:T(8,128)S(1)}, f32[512,128]{1,0:T(8,128)}, u32[]{:S(2)}, u32[]{:S(2)}) %collective-permute-start.5) | collective-permute-done | bytes 262176 | tf_op jit(solution)/shard_map/ppermute | solution.py:12
  199.6 3.7 %gather_fusion.7 = f32[1536,128]{1,0:T(8,128)} fusion(f32[2048,128]{1,0:T(8,128)S(1)} %pad_maximum_fusion.3, s32[2048]{0:T(1024)S(1)} %pad_clamp_fusion.3), kind=kCustom, calls=%fused_computation.7 | custom fusion | bytes 1579008 | tf_op jit(solution)/shard_map/jit(_take)/gather | solution.py:116
  205.4 6.5 %collective-permute-start.7 = (f32[512,128]{1,0:T(8,128)S(1)}, f32[512,128]{1,0:T(8,128)}, u32[]{:S(2)}, u32[]{:S(2)}) collective-permute-start(f32[512,128]{1,0:T(8,128)S(1)} %slice_subtract_fusion.2), channel_id=1, source_target_pairs={{0,64},{4,68},{8,72},{12,76},{16,80},{20,84},{24,88},{28,92},{32,9... | collective-permute-start | bytes 786440 | tf_op jit(solution)/shard_map/ppermute | solution.py:12
  216.6 18.9 %collective-permute-done.7 = f32[512,128]{1,0:T(8,128)} collective-permute-done((f32[512,128]{1,0:T(8,128)S(1)}, f32[512,128]{1,0:T(8,128)}, u32[]{:S(2)}, u32[]{:S(2)}) %collective-permute-start.7) | collective-permute-done | bytes 262176 | tf_op jit(solution)/shard_map/ppermute | solution.py:12
  240.2 3.7 %gather_fusion.9 = f32[1536,128]{1,0:T(8,128)} fusion(f32[2048,128]{1,0:T(8,128)S(1)} %pad_maximum_fusion.4, s32[2048]{0:T(1024)S(1)} %pad_clamp_fusion.2), kind=kCustom, calls=%fused_computation.9 | custom fusion | bytes 1579008 | tf_op jit(solution)/shard_map/jit(_take)/gather | solution.py:116
  243.9 2.8 slice_subtract_fusion.1
  253.5 3.0 %collective-permute-done.9 = f32[512,128]{1,0:T(8,128)} collective-permute-done((f32[512,128]{1,0:T(8,128)}, f32[512,128]{1,0:T(8,128)}, u32[]{:S(2)}, u32[]{:S(2)}) %collective-permute-start.9) | collective-permute-done | bytes 262176 | tf_op jit(solution)/shard_map/ppermute | solution.py:12
  256.6 3.0 collective-permute-start.10
  262.0 3.7 %gather_fusion.11 = f32[1536,128]{1,0:T(8,128)} fusion(f32[2048,128]{1,0:T(8,128)S(1)} %pad_maximum_fusion.5, s32[2048]{0:T(1024)S(1)} %pad_clamp_fusion.1), kind=kCustom, calls=%fused_computation.11 | custom fusion | bytes 1579008 | tf_op jit(solution)/shard_map/jit(_take)/gather | solution.py:116
  266.4 2.7 slice_subtract_fusion
  269.1 4.6 %collective-permute-start.11 = (f32[512,128]{1,0:T(8,128)}, f32[512,128]{1,0:T(8,128)}, u32[]{:S(2)}, u32[]{:S(2)}) collective-permute-start(f32[512,128]{1,0:T(8,128)} %slice_subtract_fusion), channel_id=1, source_target_pairs={{0,256},{4,260},{8,264},{12,268},{16,272},{20,276},{24,280},{28,28... | collective-permute-start | bytes 786440 | tf_op jit(solution)/shard_map/ppermute | solution.py:12
  280.0 3.4 %collective-permute-start.12 = (f32[512,128]{1,0:T(8,128)}, f32[512,128]{1,0:T(8,128)S(1)}, u32[]{:S(2)}, u32[]{:S(2)}) collective-permute-start(f32[512,128]{1,0:T(8,128)} %collective-permute-done.11), channel_id=1, source_target_pairs={{0,4},{4,0},{8,12},{12,8},{16,20},{20,16},{24,28},{28,24},{32,36},... | collective-permute-start | bytes 786440 | tf_op jit(solution)/shard_map/ppermute | solution.py:12
  285.9 3.1 %gather_fusion.13 = f32[1280,128]{1,0:T(8,128)} fusion(f32[2048,128]{1,0:T(8,128)S(1)} %pad_maximum_fusion.6, s32[2048]{0:T(1024)S(1)} %pad_clamp_fusion), kind=kCustom, calls=%fused_computation.13 | custom fusion | bytes 1315840 | tf_op jit(solution)/shard_map/jit(_take)/gather | solution.py:116
  289.1 2.4 fusion.54
  (154 shorter events, 68.3 us)
Async XLA Ops:
  7.2 110.9 %all-gather.13.cloned.1.call-start = ((), (), s32[]{:S(2)}) async-start(), calls=%async_computation.3 | async-start | bytes 2621440 | tf_op jit(solution)/shard_map/all_gather | solution.py:84
  10.7 2.7 copy-start.5
  10.7 2.8 copy-start.4
  10.8 125.6 %all-gather.15.cloned.1.call-start = ((), (), s32[]{:S(2)}) async-start(), calls=%async_computation.4 | async-start | bytes 2621440 | tf_op jit(solution)/shard_map/all_gather | solution.py:84
  11.5 151.9 %all-gather.17.cloned.1.call-start = ((), (), s32[]{:S(2)}) async-start(), calls=%async_computation.5 | async-start | bytes 2621440 | tf_op jit(solution)/shard_map/all_gather | solution.py:84
  12.2 191.0 %all-gather.19.cloned.1.call-start = ((), (), s32[]{:S(2)}) async-start(), calls=%async_computation.6 | async-start | bytes 2621440 | tf_op jit(solution)/shard_map/all_gather | solution.py:84
  12.8 231.1 %all-gather.21.cloned.1.call-start = ((), (), s32[]{:S(2)}) async-start(), calls=%async_computation.7 | async-start | bytes 2621440 | tf_op jit(solution)/shard_map/all_gather | solution.py:84
  13.6 23.2 %copy-start.8 = (s32[1,32]{1,0:T(1,128)S(1)}, s32[1,32]{1,0:T(1,128)}, u32[]{:S(2)}) copy-start(s32[1,32]{1,0:T(1,128)} %param.11) | copy-start | bytes 388
  13.6 23.3 %copy-start.6 = (s32[1,7,2,1024]{3,2,1,0:T(2,128)S(1)}, s32[1,7,2,1024]{3,2,1,0:T(2,128)}, u32[]{:S(2)}) copy-start(s32[1,7,2,1024]{3,2,1,0:T(2,128)} %param.12) | copy-start | bytes 172036
  14.1 23.1 %copy-start.3 = (f32[1,32,4096]{2,1,0:T(8,128)S(1)}, f32[1,32,4096]{2,1,0:T(8,128)}, u32[]{:S(2)}) copy-start(f32[1,32,4096]{2,1,0:T(8,128)} %param.9) | copy-start | bytes 1572868
  15.6 58.9 %all-to-all-start = ((f32[1,128,1280]{2,0,1:T(1,128)}), f32[1,128,1280]{2,0,1:T(1,128)S(1)}, u32[]{:S(2)}, u32[]{:S(2)}) async-start(f32[1,128,1280]{2,0,1:T(1,128)} %pad_maximum_fusion.7), calls=%async_computation | async-start | bytes 1310720 | tf_op jit(solution)/shard_map/all_to_all | solution.py:40
  36.1 230.3 %all-gather.23.cloned.1.call-start = ((), (), s32[]{:S(2)}) async-start(), calls=%async_computation.8 | async-start | bytes 2621440 | tf_op jit(solution)/shard_map/all_gather | solution.py:84
  75.5 0.7 copy-start.7
  78.1 18.9 %all-to-all-start.1 = ((f32[4,256,128]{2,1,0:T(8,128)}), f32[4,256,128]{2,1,0:T(8,128)S(1)}, u32[]{:S(2)}, u32[]{:S(2)}) async-start(f32[4,256,128]{2,1,0:T(8,128)} %bitcast.11), calls=%async_computation.1 | async-start | bytes 1048576 | tf_op jit(solution)/shard_map/all_to_all | solution.py:25
  97.9 10.4 %all-to-all-start.2 = ((f32[4,256,128]{2,1,0:T(8,128)}), f32[4,256,128]{2,1,0:T(8,128)S(1)}, u32[]{:S(2)}, u32[]{:S(2)}) async-start(f32[4,256,128]{2,1,0:T(8,128)} %broadcast_in_dim.75), calls=%async_computation.2 | async-start | bytes 1048576 | tf_op jit(solution)/shard_map/all_to_all | solution.py:30
  108.3 7.1 %collective-permute-start = (f32[1024,128]{1,0:T(8,128)S(1)}, f32[1024,128]{1,0:T(8,128)S(1)}, u32[]{:S(2)}, u32[]{:S(2)}) collective-permute-start(f32[1024,128]{1,0:T(8,128)S(1)} %bitcast.134), channel_id=1, source_target_pairs={{0,4},{4,0},{8,12},{12,8},{16,20},{20,16},{24,28},{28,24},{32,36},... | collective-permute-start | bytes 1572872 | tf_op jit(solution)/shard_map/ppermute | solution.py:12
  119.9 9.7 %collective-permute-start.1 = (f32[512,128]{1,0:T(8,128)S(1)}, f32[512,128]{1,0:T(8,128)S(1)}, u32[]{:S(2)}, u32[]{:S(2)}) collective-permute-start(f32[512,128]{1,0:T(8,128)S(1)} %slice_subtract_fusion.5), channel_id=1, source_target_pairs={{0,8},{4,12},{8,0},{12,4},{16,24},{20,28},{24,16},{28,20},{32,40},... | collective-permute-start | bytes 786440 | tf_op jit(solution)/shard_map/ppermute | solution.py:12
  129.6 4.0 %collective-permute-start.2 = (f32[512,128]{1,0:T(8,128)S(1)}, f32[512,128]{1,0:T(8,128)S(1)}, u32[]{:S(2)}, u32[]{:S(2)}) collective-permute-start(f32[512,128]{1,0:T(8,128)S(1)} %collective-permute-done.1), channel_id=1, source_target_pairs={{0,4},{4,0},{8,12},{12,8},{16,20},{20,16},{24,28},{28,24},{32,36},... | collective-permute-start | bytes 786440 | tf_op jit(solution)/shard_map/ppermute | solution.py:12
  138.2 16.1 %collective-permute-start.3 = (f32[512,128]{1,0:T(8,128)S(1)}, f32[512,128]{1,0:T(8,128)}, u32[]{:S(2)}, u32[]{:S(2)}) collective-permute-start(f32[512,128]{1,0:T(8,128)S(1)} %slice_subtract_fusion.4), channel_id=1, source_target_pairs={{0,16},{4,20},{8,24},{12,28},{16,0},{20,4},{24,8},{28,12},{32,48},... | collective-permute-start | bytes 786440 | tf_op jit(solution)/shard_map/ppermute | solution.py:12
  154.3 4.4 %collective-permute-start.4 = (f32[512,128]{1,0:T(8,128)}, f32[512,128]{1,0:T(8,128)S(1)}, u32[]{:S(2)}, u32[]{:S(2)}) collective-permute-start(f32[512,128]{1,0:T(8,128)} %collective-permute-done.3), channel_id=1, source_target_pairs={{0,4},{4,0},{8,12},{12,8},{16,20},{20,16},{24,28},{28,24},{32,36},... | collective-permute-start | bytes 786440 | tf_op jit(solution)/shard_map/ppermute | solution.py:12
  165.6 33.0 %copy-start = (f32[512,128]{1,0:T(8,128)}, f32[512,128]{1,0:T(8,128)S(1)}, u32[]{:S(2)}) copy-start(f32[512,128]{1,0:T(8,128)S(1)} %slice_subtract_fusion.3) | copy-start | bytes 786436
  165.6 29.3 %collective-permute-start.5 = (f32[512,128]{1,0:T(8,128)S(1)}, f32[512,128]{1,0:T(8,128)}, u32[]{:S(2)}, u32[]{:S(2)}) collective-permute-start(f32[512,128]{1,0:T(8,128)S(1)} %slice_subtract_fusion.3), channel_id=1, source_target_pairs={{0,32},{4,36},{8,40},{12,44},{16,48},{20,52},{24,56},{28,60},{32,0... | collective-permute-start | bytes 786440 | tf_op jit(solution)/shard_map/ppermute | solution.py:12
  194.8 3.7 %collective-permute-start.6 = (f32[512,128]{1,0:T(8,128)}, f32[512,128]{1,0:T(8,128)S(1)}, u32[]{:S(2)}, u32[]{:S(2)}) collective-permute-start(f32[512,128]{1,0:T(8,128)} %collective-permute-done.5), channel_id=1, source_target_pairs={{0,4},{4,0},{8,12},{12,8},{16,20},{20,16},{24,28},{28,24},{32,36},... | collective-permute-start | bytes 786440 | tf_op jit(solution)/shard_map/ppermute | solution.py:12
  205.3 38.6 %copy-start.2 = (f32[512,128]{1,0:T(8,128)}, f32[512,128]{1,0:T(8,128)S(1)}, u32[]{:S(2)}) copy-start(f32[512,128]{1,0:T(8,128)S(1)} %slice_subtract_fusion.2) | copy-start | bytes 786436
  205.4 30.1 %collective-permute-start.7 = (f32[512,128]{1,0:T(8,128)S(1)}, f32[512,128]{1,0:T(8,128)}, u32[]{:S(2)}, u32[]{:S(2)}) collective-permute-start(f32[512,128]{1,0:T(8,128)S(1)} %slice_subtract_fusion.2), channel_id=1, source_target_pairs={{0,64},{4,68},{8,72},{12,76},{16,80},{20,84},{24,88},{28,92},{32,9... | collective-permute-start | bytes 786440 | tf_op jit(solution)/shard_map/ppermute | solution.py:12
  235.5 3.7 %collective-permute-start.8 = (f32[512,128]{1,0:T(8,128)}, f32[512,128]{1,0:T(8,128)S(1)}, u32[]{:S(2)}, u32[]{:S(2)}) collective-permute-start(f32[512,128]{1,0:T(8,128)} %collective-permute-done.7), channel_id=1, source_target_pairs={{0,4},{4,0},{8,12},{12,8},{16,20},{20,16},{24,28},{28,24},{32,36},... | collective-permute-start | bytes 786440 | tf_op jit(solution)/shard_map/ppermute | solution.py:12
  246.8 9.8 %collective-permute-start.9 = (f32[512,128]{1,0:T(8,128)}, f32[512,128]{1,0:T(8,128)}, u32[]{:S(2)}, u32[]{:S(2)}) collective-permute-start(f32[512,128]{1,0:T(8,128)} %slice_subtract_fusion.1), channel_id=1, source_target_pairs={{0,128},{4,132},{8,136},{12,140},{16,144},{20,148},{24,152},{28,15... | collective-permute-start | bytes 786440 | tf_op jit(solution)/shard_map/ppermute | solution.py:12
  256.6 4.3 %collective-permute-start.10 = (f32[512,128]{1,0:T(8,128)}, f32[512,128]{1,0:T(8,128)S(1)}, u32[]{:S(2)}, u32[]{:S(2)}) collective-permute-start(f32[512,128]{1,0:T(8,128)} %collective-permute-done.9), channel_id=1, source_target_pairs={{0,4},{4,0},{8,12},{12,8},{16,20},{20,16},{24,28},{28,24},{32,36},... | collective-permute-start | bytes 786440 | tf_op jit(solution)/shard_map/ppermute | solution.py:12
  269.1 10.9 %collective-permute-start.11 = (f32[512,128]{1,0:T(8,128)}, f32[512,128]{1,0:T(8,128)}, u32[]{:S(2)}, u32[]{:S(2)}) collective-permute-start(f32[512,128]{1,0:T(8,128)} %slice_subtract_fusion), channel_id=1, source_target_pairs={{0,256},{4,260},{8,264},{12,268},{16,272},{20,276},{24,280},{28,28... | collective-permute-start | bytes 786440 | tf_op jit(solution)/shard_map/ppermute | solution.py:12
  280.0 4.8 %collective-permute-start.12 = (f32[512,128]{1,0:T(8,128)}, f32[512,128]{1,0:T(8,128)S(1)}, u32[]{:S(2)}, u32[]{:S(2)}) collective-permute-start(f32[512,128]{1,0:T(8,128)} %collective-permute-done.11), channel_id=1, source_target_pairs={{0,4},{4,0},{8,12},{12,8},{16,20},{20,16},{24,28},{28,24},{32,36},... | collective-permute-start | bytes 786440 | tf_op jit(solution)/shard_map/ppermute | solution.py:12
  285.9 3.2 %copy-start.1 = (f32[512,128]{1,0:T(8,128)S(1)}, f32[512,128]{1,0:T(8,128)}, u32[]{:S(2)}) copy-start(f32[512,128]{1,0:T(8,128)} %copy-done) | copy-start | bytes 786436
Sparse Core Ops, SparseCore 0:
  10.9 43.7 all-gather.12
  56.8 44.1 all-gather.14
  103.1 41.5 all-gather.16
  146.6 38.5 all-gather.18
  187.2 38.5 all-gather.20
  227.8 38.5 all-gather.22

commit v9 on v8

--- a/solution.py
+++ b/solution.py
@@ -92,10 +92,18 @@
                 return index
 
         else:
-            got = from_partner(current[:rows_half], "sub", level - 1)
+            if half in (8, 16):
+                slice_rows = rows_half // groups
+                piece = lax.dynamic_slice_in_dim(first, position * slice_rows, slice_rows, 0)
+                piece = from_partner(piece, "sub", level - 1)
+                copies = jnp.broadcast_to(piece[None], (groups,) + piece.shape)
+                got = lax.all_to_all(copies, "case", split_axis=0, concat_axis=0)
+                got = got.reshape(rows_half, num_cases)
+            else:
+                got = from_partner(first, "sub", level - 1)
             got, rest = lax.optimization_barrier((got, rest))
             swapped = from_partner(got, "sub", 0)
-            stacked = jnp.concatenate([current, got, swapped], axis=0)
+            stacked = jnp.concatenate([first, rest, got, swapped], axis=0)
 
             def own_index(index):
                 return jnp.bitwise_xor(index, turn)

time: 300 us -> 305 us (1.017)
  starting transfers between devices: 74 us -> 90.5 us
  waiting for transfers between devices: 127 us -> 121 us
    ppermute x13, waiting for transfers between devices: 65.2 us -> 36.5 us  [from_partner(): return lax.ppermute(value, axis, pairs)]
    all_gather x6, waiting for transfers between devices: 0.78 us -> 13.2 us  [on_device(): lax.all_gather(merge_maps[0, level - 1], 'case', axis=0, tiled=True)]
    all_to_all x0 -> x2, waiting for transfers between devices: none -> 9.98 us  [on_device(): got = lax.all_to_all(copies, 'case', split_axis=0, concat_axis=0)]
    ppermute x13, starting transfers between devices: 45.7 us -> 54.8 us  [from_partner(): return lax.ppermute(value, axis, pairs)]
    all_to_all x0 -> x2, starting transfers between devices: none -> 7.44 us  [on_device(): got = lax.all_to_all(copies, 'case', split_axis=0, concat_axis=0)]
  transfers between devices with their start and end apart: 22 -> 24, of which waited for: 17 -> 19; matrix products, arithmetic and copies ran while one was open for 23% -> 21% of each run, Pallas kernels for 0% -> 0%
where the time goes in v9:
time: 305 us; the launch traced here: 304 us
  waiting for transfers between devices  121 us (40%)
  starting transfers between devices  90.5 us (30%)
  local copies, waits for them, and re-layouts  38.2 us (13%)
  matrix products  28.2 us (9%)
  between operations  15.3 us (5%)
  other arithmetic  10.8 us (4%)
    ppermute x13, starting transfers between devices, from_partner(): return lax.ppermute(value, axis, pairs)  54.8 us
    ppermute x13, waiting for transfers between devices, from_partner(): return lax.ppermute(value, axis, pairs)  36.5 us
    all_to_all x1, waiting for transfers between devices, on_device(): lax.all_to_all(joined, 'sub', split_axis=1, concat_axis=0, tiled=True)  36.3 us
    dot_general x13, matrix products, rows_of(): return kept - jnp.dot(part, shared, precision=lax.Precision.HIGH)  26.6 us
    gather x7, local copies, waits for them, and re-layouts, on_device(): jnp.take(stacked, jnp.concatenate([left_index(maps[0, :shared_rows]), rig...  22 us
    all_to_all x1, starting transfers between devices, on_device(): lax.all_to_all(joined, 'sub', split_axis=1, concat_axis=0, tiled=True)  20.6 us
    all_to_all x1, waiting for transfers between devices, case_allreduce(): received = lax.all_to_all(chunks, 'case', split_axis=0, concat_axis=0)  14.9 us
    all_gather x6, waiting for transfers between devices, on_device(): lax.all_gather(merge_maps[0, level - 1], 'case', axis=0, tiled=True)  13.2 us
  transfers between devices with their start and end apart: 24, of which 19 were waited for; matrix products, arithmetic and copies ran while one was open for 21% of the time, Pallas kernels for 0%

profile of v9, /device:TPU:1, one launch (start us, length us, event | category | flops | bytes accessed | tf_op | source)
XLA Modules:
  0.0 303.9 jit_solution(11481299058100480266)
XLA Ops:
  7.2 3.5 %fusion.88 = (f32[1,1,256,512]{3,2,1,0:T(8,128)}, f32[1,1,256,512]{3,2,1,0:T(8,128)}, f32[1,1,256,512]{3,2,1,0:T(8,128)}, f32[1,1,256,512]{3,2,1,0:T(8,128)}, f3...) fusion(f32[1,7,256,512]{3,2,1,0:T(8,128)} %param.13), kind=kLoop, calls=%fused_computation.222 | loop fusion | bytes 6291456 | tf_op jit(solution)/shard_map/slice | solution.py:84
  15.6 20.6 %all-to-all-start = ((f32[1,128,1280]{2,0,1:T(1,128)}), f32[1,128,1280]{2,0,1:T(1,128)S(1)}, u32[]{:S(2)}, u32[]{:S(2)}) async-start(f32[1,128,1280]{2,0,1:T(1,128)} %pad_maximum_fusion.7), calls=%async_computation | async-start | bytes 1310720 | tf_op jit(solution)/shard_map/all_to_all | solution.py:40
  38.1 36.3 %all-to-all-done = f32[1,128,1280]{2,0,1:T(1,128)S(1)} async-done(((f32[1,128,1280]{2,0,1:T(1,128)}), f32[1,128,1280]{2,0,1:T(1,128)S(1)}, u32[]{:S(2)}, u32[]{:S(2)}) %all-to-all-start) | async-done | bytes 655392 | tf_op jit(solution)/shard_map/all_to_all | solution.py:40
  78.1 4.0 %all-to-all-start.1 = ((f32[4,256,128]{2,1,0:T(8,128)}), f32[4,256,128]{2,1,0:T(8,128)S(1)}, u32[]{:S(2)}, u32[]{:S(2)}) async-start(f32[4,256,128]{2,1,0:T(8,128)} %bitcast.11), calls=%async_computation.1 | async-start | bytes 1048576 | tf_op jit(solution)/shard_map/all_to_all | solution.py:25
  82.2 14.9 %all-to-all-done.1 = f32[4,256,128]{2,1,0:T(8,128)S(1)} async-done(((f32[4,256,128]{2,1,0:T(8,128)}), f32[4,256,128]{2,1,0:T(8,128)S(1)}, u32[]{:S(2)}, u32[]{:S(2)}) %all-to-all-start.1) | async-done | bytes 524320 | tf_op jit(solution)/shard_map/all_to_all | solution.py:25
  97.9 3.5 %all-to-all-start.2 = ((f32[4,256,128]{2,1,0:T(8,128)}), f32[4,256,128]{2,1,0:T(8,128)S(1)}, u32[]{:S(2)}, u32[]{:S(2)}) async-start(f32[4,256,128]{2,1,0:T(8,128)} %broadcast_in_dim.87), calls=%async_computation.2 | async-start | bytes 1048576 | tf_op jit(solution)/shard_map/all_to_all | solution.py:30
  101.4 6.9 %all-to-all-done.2 = f32[4,256,128]{2,1,0:T(8,128)S(1)} async-done(((f32[4,256,128]{2,1,0:T(8,128)}), f32[4,256,128]{2,1,0:T(8,128)S(1)}, u32[]{:S(2)}, u32[]{:S(2)}) %all-to-all-start.2) | async-done | bytes 524320 | tf_op jit(solution)/shard_map/all_to_all | solution.py:30
  108.3 5.6 %collective-permute-start = (f32[1024,128]{1,0:T(8,128)S(1)}, f32[1024,128]{1,0:T(8,128)S(1)}, u32[]{:S(2)}, u32[]{:S(2)}) collective-permute-start(f32[1024,128]{1,0:T(8,128)S(1)} %bitcast.136), channel_id=1, source_target_pairs={{0,4},{4,0},{8,12},{12,8},{16,20},{20,16},{24,28},{28,24},{32,36},... | collective-permute-start | bytes 1572872 | tf_op jit(solution)/shard_map/ppermute | solution.py:12
  120.0 3.4 %collective-permute-start.1 = (f32[512,128]{1,0:T(8,128)S(1)}, f32[512,128]{1,0:T(8,128)S(1)}, u32[]{:S(2)}, u32[]{:S(2)}) collective-permute-start(f32[512,128]{1,0:T(8,128)S(1)} %slice_subtract_fusion.5), channel_id=1, source_target_pairs={{0,8},{4,12},{8,0},{12,4},{16,24},{20,28},{24,16},{28,20},{32,40},... | collective-permute-start | bytes 786440 | tf_op jit(solution)/shard_map/ppermute | solution.py:12
  126.5 3.2 %collective-permute-done.1 = f32[512,128]{1,0:T(8,128)S(1)} collective-permute-done((f32[512,128]{1,0:T(8,128)S(1)}, f32[512,128]{1,0:T(8,128)S(1)}, u32[]{:S(2)}, u32[]{:S(2)}) %collective-permute-start.1) | collective-permute-done | bytes 262176 | tf_op jit(solution)/shard_map/ppermute | solution.py:12
  129.7 2.9 collective-permute-start.2
  138.3 3.0 collective-permute-start.3
  144.2 10.1 %collective-permute-done.3 = f32[512,128]{1,0:T(8,128)} collective-permute-done((f32[512,128]{1,0:T(8,128)S(1)}, f32[512,128]{1,0:T(8,128)}, u32[]{:S(2)}, u32[]{:S(2)}) %collective-permute-start.3) | collective-permute-done | bytes 262176 | tf_op jit(solution)/shard_map/ppermute | solution.py:12
  154.3 3.3 %collective-permute-start.4 = (f32[512,128]{1,0:T(8,128)}, f32[512,128]{1,0:T(8,128)S(1)}, u32[]{:S(2)}, u32[]{:S(2)}) collective-permute-start(f32[512,128]{1,0:T(8,128)} %collective-permute-done.3), channel_id=1, source_target_pairs={{0,4},{4,0},{8,12},{12,8},{16,20},{20,16},{24,28},{28,24},{32,36},... | collective-permute-start | bytes 786440 | tf_op jit(solution)/shard_map/ppermute | solution.py:12
  164.3 3.1 %collective-permute-start.5 = (f32[128,128]{1,0:T(8,128)S(1)}, f32[128,128]{1,0:T(8,128)S(1)}, u32[]{:S(2)}, u32[]{:S(2)}) collective-permute-start(f32[128,128]{1,0:T(8,128)S(1)} %constant_dynamic-slice_fusion.1), channel_id=1, source_target_pairs={{0,32},{4,36},{8,40},{12,44},{16,48},{20,52},{24,56},{28,60},{32,0... | collective-permute-start | bytes 196616 | tf_op jit(solution)/shard_map/ppermute | solution.py:12
  167.4 9.3 %collective-permute-done.5 = f32[128,128]{1,0:T(8,128)S(1)} collective-permute-done((f32[128,128]{1,0:T(8,128)S(1)}, f32[128,128]{1,0:T(8,128)S(1)}, u32[]{:S(2)}, u32[]{:S(2)}) %collective-permute-start.5) | collective-permute-done | bytes 65568 | tf_op jit(solution)/shard_map/ppermute | solution.py:12
  177.4 4.0 %all-to-all-start.3 = ((f32[4,128,128]{2,1,0:T(8,128)}), f32[4,128,128]{2,1,0:T(8,128)}, u32[]{:S(2)}, u32[]{:S(2)}) async-start(f32[4,128,128]{2,1,0:T(8,128)} %broadcast_in_dim.93), calls=%async_computation.3 | async-start | bytes 524288 | tf_op jit(solution)/shard_map/all_to_all | solution.py:100
  184.4 3.2 %all-to-all-done.3 = f32[4,128,128]{2,1,0:T(8,128)} async-done(((f32[4,128,128]{2,1,0:T(8,128)}), f32[4,128,128]{2,1,0:T(8,128)}, u32[]{:S(2)}, u32[]{:S(2)}) %all-to-all-start.3) | async-done | bytes 262176 | tf_op jit(solution)/shard_map/all_to_all | solution.py:100
  187.6 3.5 %collective-permute-start.6 = (f32[512,128]{1,0:T(8,128)}, f32[512,128]{1,0:T(8,128)S(1)}, u32[]{:S(2)}, u32[]{:S(2)}) collective-permute-start(f32[512,128]{1,0:T(8,128)} %bitcast.34), channel_id=1, source_target_pairs={{0,4},{4,0},{8,12},{12,8},{16,20},{20,16},{24,28},{28,24},{32,36},... | collective-permute-start | bytes 786440 | tf_op jit(solution)/shard_map/ppermute | solution.py:12
  193.4 3.7 %gather_fusion.7 = f32[1536,128]{1,0:T(8,128)} fusion(f32[2048,128]{1,0:T(8,128)S(1)} %pad_maximum_fusion.3, s32[2048]{0:T(1024)S(1)} %pad_clamp_fusion.3), kind=kCustom, calls=%fused_computation.7 | custom fusion | bytes 1579008 | tf_op jit(solution)/shard_map/jit(_take)/gather | solution.py:124
  199.2 10.3 %collective-permute-start.7 = (f32[128,128]{1,0:T(8,128)S(1)}, f32[128,128]{1,0:T(8,128)S(1)}, u32[]{:S(2)}, u32[]{:S(2)}) collective-permute-start(f32[128,128]{1,0:T(8,128)S(1)} %constant_dynamic-slice_fusion), channel_id=1, source_target_pairs={{0,64},{4,68},{8,72},{12,76},{16,80},{20,84},{24,88},{28,92},{32,9... | collective-permute-start | bytes 196616 | tf_op jit(solution)/shard_map/ppermute | solution.py:12
  213.8 3.4 %all-to-all-start.4 = ((f32[4,128,128]{2,1,0:T(8,128)}), f32[4,128,128]{2,1,0:T(8,128)S(1)}, u32[]{:S(2)}, u32[]{:S(2)}) async-start(f32[4,128,128]{2,1,0:T(8,128)} %broadcast_in_dim.96), calls=%async_computation.4 | async-start | bytes 524288 | tf_op jit(solution)/shard_map/all_to_all | solution.py:100
  219.2 6.8 %all-to-all-done.4 = f32[4,128,128]{2,1,0:T(8,128)S(1)} async-done(((f32[4,128,128]{2,1,0:T(8,128)}), f32[4,128,128]{2,1,0:T(8,128)S(1)}, u32[]{:S(2)}, u32[]{:S(2)}) %all-to-all-start.4) | async-done | bytes 262176 | tf_op jit(solution)/shard_map/all_to_all | solution.py:100
  226.0 5.3 %collective-permute-start.8 = (f32[512,128]{1,0:T(8,128)S(1)}, f32[512,128]{1,0:T(8,128)S(1)}, u32[]{:S(2)}, u32[]{:S(2)}) collective-permute-start(f32[512,128]{1,0:T(8,128)S(1)} %bitcast.138), channel_id=1, source_target_pairs={{0,4},{4,0},{8,12},{12,8},{16,20},{20,16},{24,28},{28,24},{32,36},... | collective-permute-start | bytes 786440 | tf_op jit(solution)/shard_map/ppermute | solution.py:12
  233.4 3.7 %gather_fusion.9 = f32[1536,128]{1,0:T(8,128)} fusion(f32[2048,128]{1,0:T(8,128)S(1)} %pad_maximum_fusion.4, s32[2048]{0:T(1024)S(1)} %pad_clamp_fusion.2), kind=kCustom, calls=%fused_computation.9 | custom fusion | bytes 1579008 | tf_op jit(solution)/shard_map/jit(_take)/gather | solution.py:124
  239.8 3.4 %collective-permute-start.9 = (f32[512,128]{1,0:T(8,128)}, f32[512,128]{1,0:T(8,128)}, u32[]{:S(2)}, u32[]{:S(2)}) collective-permute-start(f32[512,128]{1,0:T(8,128)} %slice_subtract_fusion.1), channel_id=1, source_target_pairs={{0,128},{4,132},{8,136},{12,140},{16,144},{20,148},{24,152},{28,15... | collective-permute-start | bytes 786440 | tf_op jit(solution)/shard_map/ppermute | solution.py:12
  249.7 3.0 collective-permute-start.10
  255.2 3.7 %gather_fusion.11 = f32[1536,128]{1,0:T(8,128)} fusion(f32[2048,128]{1,0:T(8,128)S(1)} %pad_maximum_fusion.5, s32[2048]{0:T(1024)S(1)} %pad_clamp_fusion.1), kind=kCustom, calls=%fused_computation.11 | custom fusion | bytes 1579008 | tf_op jit(solution)/shard_map/jit(_take)/gather | solution.py:124
  258.9 13.2 %all-gather.23.cloned.1.call-done = f32[1,1,1024,512]{3,2,1,0:T(8,128)} async-done(((f32[1,1,256,512]{3,2,1,0:T(8,128)}), f32[1,1,1024,512]{3,2,1,0:T(8,128)}) %all-gather.23.cloned.1.call-update) | async-done | bytes 2097168 | tf_op jit(solution)/shard_map/all_gather | solution.py:84
  274.8 4.6 %collective-permute-start.11 = (f32[512,128]{1,0:T(8,128)}, f32[512,128]{1,0:T(8,128)}, u32[]{:S(2)}, u32[]{:S(2)}) collective-permute-start(f32[512,128]{1,0:T(8,128)} %slice_subtract_fusion), channel_id=1, source_target_pairs={{0,256},{4,260},{8,264},{12,268},{16,272},{20,276},{24,280},{28,28... | collective-permute-start | bytes 786440 | tf_op jit(solution)/shard_map/ppermute | solution.py:12
  285.6 3.4 %collective-permute-start.12 = (f32[512,128]{1,0:T(8,128)}, f32[512,128]{1,0:T(8,128)S(1)}, u32[]{:S(2)}, u32[]{:S(2)}) collective-permute-start(f32[512,128]{1,0:T(8,128)} %collective-permute-done.11), channel_id=1, source_target_pairs={{0,4},{4,0},{8,12},{12,8},{16,20},{20,16},{24,28},{28,24},{32,36},... | collective-permute-start | bytes 786440 | tf_op jit(solution)/shard_map/ppermute | solution.py:12
  291.6 3.1 %gather_fusion.13 = f32[1280,128]{1,0:T(8,128)} fusion(f32[2048,128]{1,0:T(8,128)S(1)} %pad_maximum_fusion.6, s32[2048]{0:T(1024)S(1)} %pad_clamp_fusion), kind=kCustom, calls=%fused_computation.13 | custom fusion | bytes 1315840 | tf_op jit(solution)/shard_map/jit(_take)/gather | solution.py:124
  (164 shorter events, 76.6 us)
Async XLA Ops:
  7.2 111.0 %all-gather.13.cloned.1.call-start = ((), (), s32[]{:S(2)}) async-start(), calls=%async_computation.5 | async-start | bytes 2621440 | tf_op jit(solution)/shard_map/all_gather | solution.py:84
  10.7 2.8 copy-start.5
  10.7 125.7 %all-gather.15.cloned.1.call-start = ((), (), s32[]{:S(2)}) async-start(), calls=%async_computation.6 | async-start | bytes 2621440 | tf_op jit(solution)/shard_map/all_gather | solution.py:84
  11.5 150.9 %all-gather.17.cloned.1.call-start = ((), (), s32[]{:S(2)}) async-start(), calls=%async_computation.7 | async-start | bytes 2621440 | tf_op jit(solution)/shard_map/all_gather | solution.py:84
  12.2 184.9 %all-gather.19.cloned.1.call-start = ((), (), s32[]{:S(2)}) async-start(), calls=%async_computation.8 | async-start | bytes 2621440 | tf_op jit(solution)/shard_map/all_gather | solution.py:84
  12.8 224.3 %all-gather.21.cloned.1.call-start = ((), (), s32[]{:S(2)}) async-start(), calls=%async_computation.9 | async-start | bytes 2621440 | tf_op jit(solution)/shard_map/all_gather | solution.py:84
  13.6 23.2 %copy-start.9 = (s32[1,32]{1,0:T(1,128)S(1)}, s32[1,32]{1,0:T(1,128)}, u32[]{:S(2)}) copy-start(s32[1,32]{1,0:T(1,128)} %param.11) | copy-start | bytes 388
  13.6 23.3 %copy-start.7 = (s32[1,7,2,1024]{3,2,1,0:T(2,128)S(1)}, s32[1,7,2,1024]{3,2,1,0:T(2,128)}, u32[]{:S(2)}) copy-start(s32[1,7,2,1024]{3,2,1,0:T(2,128)} %param.12) | copy-start | bytes 172036
  14.1 23.1 %copy-start.4 = (f32[1,32,4096]{2,1,0:T(8,128)S(1)}, f32[1,32,4096]{2,1,0:T(8,128)}, u32[]{:S(2)}) copy-start(f32[1,32,4096]{2,1,0:T(8,128)} %param.9) | copy-start | bytes 1572868
  15.6 58.9 %all-to-all-start = ((f32[1,128,1280]{2,0,1:T(1,128)}), f32[1,128,1280]{2,0,1:T(1,128)S(1)}, u32[]{:S(2)}, u32[]{:S(2)}) async-start(f32[1,128,1280]{2,0,1:T(1,128)} %pad_maximum_fusion.7), calls=%async_computation | async-start | bytes 1310720 | tf_op jit(solution)/shard_map/all_to_all | solution.py:40
  36.1 235.9 %all-gather.23.cloned.1.call-start = ((), (), s32[]{:S(2)}) async-start(), calls=%async_computation.10 | async-start | bytes 2621440 | tf_op jit(solution)/shard_map/all_gather | solution.py:84
  78.1 18.9 %all-to-all-start.1 = ((f32[4,256,128]{2,1,0:T(8,128)}), f32[4,256,128]{2,1,0:T(8,128)S(1)}, u32[]{:S(2)}, u32[]{:S(2)}) async-start(f32[4,256,128]{2,1,0:T(8,128)} %bitcast.11), calls=%async_computation.1 | async-start | bytes 1048576 | tf_op jit(solution)/shard_map/all_to_all | solution.py:25
  97.9 10.4 %all-to-all-start.2 = ((f32[4,256,128]{2,1,0:T(8,128)}), f32[4,256,128]{2,1,0:T(8,128)S(1)}, u32[]{:S(2)}, u32[]{:S(2)}) async-start(f32[4,256,128]{2,1,0:T(8,128)} %broadcast_in_dim.87), calls=%async_computation.2 | async-start | bytes 1048576 | tf_op jit(solution)/shard_map/all_to_all | solution.py:30
  108.3 7.1 %collective-permute-start = (f32[1024,128]{1,0:T(8,128)S(1)}, f32[1024,128]{1,0:T(8,128)S(1)}, u32[]{:S(2)}, u32[]{:S(2)}) collective-permute-start(f32[1024,128]{1,0:T(8,128)S(1)} %bitcast.136), channel_id=1, source_target_pairs={{0,4},{4,0},{8,12},{12,8},{16,20},{20,16},{24,28},{28,24},{32,36},... | collective-permute-start | bytes 1572872 | tf_op jit(solution)/shard_map/ppermute | solution.py:12
  120.0 13.8 %copy-start = (f32[512,128]{1,0:T(8,128)}, f32[512,128]{1,0:T(8,128)S(1)}, u32[]{:S(2)}) copy-start(f32[512,128]{1,0:T(8,128)S(1)} %slice_subtract_fusion.5) | copy-start | bytes 786436
  120.0 9.7 %collective-permute-start.1 = (f32[512,128]{1,0:T(8,128)S(1)}, f32[512,128]{1,0:T(8,128)S(1)}, u32[]{:S(2)}, u32[]{:S(2)}) collective-permute-start(f32[512,128]{1,0:T(8,128)S(1)} %slice_subtract_fusion.5), channel_id=1, source_target_pairs={{0,8},{4,12},{8,0},{12,4},{16,24},{20,28},{24,16},{28,20},{32,40},... | collective-permute-start | bytes 786440 | tf_op jit(solution)/shard_map/ppermute | solution.py:12
  129.7 4.0 %collective-permute-start.2 = (f32[512,128]{1,0:T(8,128)S(1)}, f32[512,128]{1,0:T(8,128)S(1)}, u32[]{:S(2)}, u32[]{:S(2)}) collective-permute-start(f32[512,128]{1,0:T(8,128)S(1)} %collective-permute-done.1), channel_id=1, source_target_pairs={{0,4},{4,0},{8,12},{12,8},{16,20},{20,16},{24,28},{28,24},{32,36},... | collective-permute-start | bytes 786440 | tf_op jit(solution)/shard_map/ppermute | solution.py:12
  138.3 24.1 %copy-start.2 = (f32[512,128]{1,0:T(8,128)}, f32[512,128]{1,0:T(8,128)S(1)}, u32[]{:S(2)}) copy-start(f32[512,128]{1,0:T(8,128)S(1)} %slice_subtract_fusion.4) | copy-start | bytes 786436
  138.3 16.1 %collective-permute-start.3 = (f32[512,128]{1,0:T(8,128)S(1)}, f32[512,128]{1,0:T(8,128)}, u32[]{:S(2)}, u32[]{:S(2)}) collective-permute-start(f32[512,128]{1,0:T(8,128)S(1)} %slice_subtract_fusion.4), channel_id=1, source_target_pairs={{0,16},{4,20},{8,24},{12,28},{16,0},{20,4},{24,8},{28,12},{32,48},... | collective-permute-start | bytes 786440 | tf_op jit(solution)/shard_map/ppermute | solution.py:12
  154.3 4.4 %collective-permute-start.4 = (f32[512,128]{1,0:T(8,128)}, f32[512,128]{1,0:T(8,128)S(1)}, u32[]{:S(2)}, u32[]{:S(2)}) collective-permute-start(f32[512,128]{1,0:T(8,128)} %collective-permute-done.3), channel_id=1, source_target_pairs={{0,4},{4,0},{8,12},{12,8},{16,20},{20,16},{24,28},{28,24},{32,36},... | collective-permute-start | bytes 786440 | tf_op jit(solution)/shard_map/ppermute | solution.py:12
  164.3 12.4 %collective-permute-start.5 = (f32[128,128]{1,0:T(8,128)S(1)}, f32[128,128]{1,0:T(8,128)S(1)}, u32[]{:S(2)}, u32[]{:S(2)}) collective-permute-start(f32[128,128]{1,0:T(8,128)S(1)} %constant_dynamic-slice_fusion.1), channel_id=1, source_target_pairs={{0,32},{4,36},{8,40},{12,44},{16,48},{20,52},{24,56},{28,60},{32,0... | collective-permute-start | bytes 196616 | tf_op jit(solution)/shard_map/ppermute | solution.py:12
  177.4 10.1 %all-to-all-start.3 = ((f32[4,128,128]{2,1,0:T(8,128)}), f32[4,128,128]{2,1,0:T(8,128)}, u32[]{:S(2)}, u32[]{:S(2)}) async-start(f32[4,128,128]{2,1,0:T(8,128)} %broadcast_in_dim.93), calls=%async_computation.3 | async-start | bytes 524288 | tf_op jit(solution)/shard_map/all_to_all | solution.py:100
  187.6 4.9 %collective-permute-start.6 = (f32[512,128]{1,0:T(8,128)}, f32[512,128]{1,0:T(8,128)S(1)}, u32[]{:S(2)}, u32[]{:S(2)}) collective-permute-start(f32[512,128]{1,0:T(8,128)} %bitcast.34), channel_id=1, source_target_pairs={{0,4},{4,0},{8,12},{12,8},{16,20},{20,16},{24,28},{28,24},{32,36},... | collective-permute-start | bytes 786440 | tf_op jit(solution)/shard_map/ppermute | solution.py:12
  199.2 13.8 %collective-permute-start.7 = (f32[128,128]{1,0:T(8,128)S(1)}, f32[128,128]{1,0:T(8,128)S(1)}, u32[]{:S(2)}, u32[]{:S(2)}) collective-permute-start(f32[128,128]{1,0:T(8,128)S(1)} %constant_dynamic-slice_fusion), channel_id=1, source_target_pairs={{0,64},{4,68},{8,72},{12,76},{16,80},{20,84},{24,88},{28,92},{32,9... | collective-permute-start | bytes 196616 | tf_op jit(solution)/shard_map/ppermute | solution.py:12
  213.8 12.2 %all-to-all-start.4 = ((f32[4,128,128]{2,1,0:T(8,128)}), f32[4,128,128]{2,1,0:T(8,128)S(1)}, u32[]{:S(2)}, u32[]{:S(2)}) async-start(f32[4,128,128]{2,1,0:T(8,128)} %broadcast_in_dim.96), calls=%async_computation.4 | async-start | bytes 524288 | tf_op jit(solution)/shard_map/all_to_all | solution.py:100
  226.0 5.3 %copy-start.3 = (f32[4,128,128]{2,1,0:T(8,128)}, f32[4,128,128]{2,1,0:T(8,128)S(1)}, u32[]{:S(2)}) copy-start(f32[4,128,128]{2,1,0:T(8,128)S(1)} %all-to-all-done.4) | copy-start | bytes 786436
  226.0 6.4 %collective-permute-start.8 = (f32[512,128]{1,0:T(8,128)S(1)}, f32[512,128]{1,0:T(8,128)S(1)}, u32[]{:S(2)}, u32[]{:S(2)}) collective-permute-start(f32[512,128]{1,0:T(8,128)S(1)} %bitcast.138), channel_id=1, source_target_pairs={{0,4},{4,0},{8,12},{12,8},{16,20},{20,16},{24,28},{28,24},{32,36},... | collective-permute-start | bytes 786440 | tf_op jit(solution)/shard_map/ppermute | solution.py:12
  239.8 9.9 %collective-permute-start.9 = (f32[512,128]{1,0:T(8,128)}, f32[512,128]{1,0:T(8,128)}, u32[]{:S(2)}, u32[]{:S(2)}) collective-permute-start(f32[512,128]{1,0:T(8,128)} %slice_subtract_fusion.1), channel_id=1, source_target_pairs={{0,128},{4,132},{8,136},{12,140},{16,144},{20,148},{24,152},{28,15... | collective-permute-start | bytes 786440 | tf_op jit(solution)/shard_map/ppermute | solution.py:12
  249.7 4.4 %collective-permute-start.10 = (f32[512,128]{1,0:T(8,128)}, f32[512,128]{1,0:T(8,128)S(1)}, u32[]{:S(2)}, u32[]{:S(2)}) collective-permute-start(f32[512,128]{1,0:T(8,128)} %collective-permute-done.9), channel_id=1, source_target_pairs={{0,4},{4,0},{8,12},{12,8},{16,20},{20,16},{24,28},{28,24},{32,36},... | collective-permute-start | bytes 786440 | tf_op jit(solution)/shard_map/ppermute | solution.py:12
  274.8 10.9 %collective-permute-start.11 = (f32[512,128]{1,0:T(8,128)}, f32[512,128]{1,0:T(8,128)}, u32[]{:S(2)}, u32[]{:S(2)}) collective-permute-start(f32[512,128]{1,0:T(8,128)} %slice_subtract_fusion), channel_id=1, source_target_pairs={{0,256},{4,260},{8,264},{12,268},{16,272},{20,276},{24,280},{28,28... | collective-permute-start | bytes 786440 | tf_op jit(solution)/shard_map/ppermute | solution.py:12
  285.6 4.8 %collective-permute-start.12 = (f32[512,128]{1,0:T(8,128)}, f32[512,128]{1,0:T(8,128)S(1)}, u32[]{:S(2)}, u32[]{:S(2)}) collective-permute-start(f32[512,128]{1,0:T(8,128)} %collective-permute-done.11), channel_id=1, source_target_pairs={{0,4},{4,0},{8,12},{12,8},{16,20},{20,16},{24,28},{28,24},{32,36},... | collective-permute-start | bytes 786440 | tf_op jit(solution)/shard_map/ppermute | solution.py:12
  291.5 3.1 %copy-start.1 = (f32[512,128]{1,0:T(8,128)S(1)}, f32[512,128]{1,0:T(8,128)}, u32[]{:S(2)}) copy-start(f32[512,128]{1,0:T(8,128)} %copy-done) | copy-start | bytes 786436
  (2 other events, 3.4 us)
Sparse Core Ops, SparseCore 0:
  10.9 43.7 all-gather.12
  56.8 44.1 all-gather.14
  103.1 41.5 all-gather.16
  146.6 38.5 all-gather.18
  187.2 44.2 all-gather.20
  233.4 38.5 all-gather.22

commit v10 on v8

--- a/solution.py
+++ b/solution.py
@@ -21,13 +21,12 @@
 def case_allreduce(value, position):
     groups = lax.axis_size("case")
     quarter = value.shape[0] // groups
-    chunks = value.reshape(groups, quarter, value.shape[1])
-    received = lax.all_to_all(chunks, "case", split_axis=0, concat_axis=0)
-    mine = received[0]
+    copies = jnp.broadcast_to(value[None], (groups,) + value.shape)
+    received = lax.all_to_all(copies, "case", split_axis=0, concat_axis=0)
+    full = received[0]
     for source in range(1, groups):
-        mine = mine + received[source]
-    copies = jnp.broadcast_to(mine[None], chunks.shape)
-    full = lax.all_to_all(copies, "case", split_axis=0, concat_axis=0).reshape(value.shape)
+        full = full + received[source]
+    mine = lax.dynamic_slice_in_dim(full, position * quarter, quarter, 0)
     return mine, full
 
 

time: 300 us -> 315 us (1.050)
  waiting for transfers between devices: 127 us -> 131 us
  starting transfers between devices: 74 us -> 77.8 us
  local copies, waits for them, and re-layouts: 39.5 us -> 42.8 us
    all_to_all x2 -> x1, waiting for transfers between devices: 21.8 us -> 34.4 us  [case_allreduce(): received = lax.all_to_all(copies, 'case', split_axis=0, concat_axis=0)]
    ppermute x13, waiting for transfers between devices: 65.2 us -> 57.5 us  [from_partner(): return lax.ppermute(value, axis, pairs)]
    ppermute x13, starting transfers between devices: 45.7 us -> 53 us  [from_partner(): return lax.ppermute(value, axis, pairs)]
    all_to_all x2 -> x1, starting transfers between devices: 7.48 us -> 4.01 us  [case_allreduce(): received = lax.all_to_all(copies, 'case', split_axis=0, concat_axis=0)]
  transfers between devices with their start and end apart: 22 -> 21, of which waited for: 17 -> 15; matrix products, arithmetic and copies ran while one was open for 23% -> 25% of each run, Pallas kernels for 0% -> 0%
where the time goes in v10:
time: 315 us; the launch traced here: 314 us
  waiting for transfers between devices  131 us (42%)
  starting transfers between devices  77.8 us (25%)
  local copies, waits for them, and re-layouts  42.8 us (14%)
  matrix products  31.1 us (10%)
  other arithmetic  15.5 us (5%)
  between operations  15.2 us (5%)
    ppermute x13, waiting for transfers between devices, from_partner(): return lax.ppermute(value, axis, pairs)  57.5 us
    ppermute x13, starting transfers between devices, from_partner(): return lax.ppermute(value, axis, pairs)  53 us
    all_to_all x1, waiting for transfers between devices, on_device(): lax.all_to_all(joined, 'sub', split_axis=1, concat_axis=0, tiled=True)  36.5 us
    all_to_all x1, waiting for transfers between devices, case_allreduce(): received = lax.all_to_all(copies, 'case', split_axis=0, concat_axis=0)  34.4 us
    dot_general x13, matrix products, rows_of(): return kept - jnp.dot(part, shared, precision=lax.Precision.HIGH)  29.5 us
    gather x7, local copies, waits for them, and re-layouts, on_device(): jnp.take(stacked, jnp.concatenate([left_index(maps[0, :shared_rows]), rig...  24.4 us
    all_to_all x1, starting transfers between devices, on_device(): lax.all_to_all(joined, 'sub', split_axis=1, concat_axis=0, tiled=True)  20.6 us
    gather x6, local copies, waits for them, and re-layouts, rows_of(): kept = jnp.take(stacked, index, axis=0, mode='clip')  9.86 us
  transfers between devices with their start and end apart: 21, of which 15 were waited for; matrix products, arithmetic and copies ran while one was open for 25% of the time, Pallas kernels for 0%

profile of v10, /device:TPU:1, one launch (start us, length us, event | category | flops | bytes accessed | tf_op | source)
XLA Modules:
  0.0 313.9 jit_solution(1155119729442884515)
XLA Ops:
  7.2 3.5 %fusion.88 = (f32[1,1,256,512]{3,2,1,0:T(8,128)}, f32[1,1,256,512]{3,2,1,0:T(8,128)}, f32[1,1,256,512]{3,2,1,0:T(8,128)}, f32[1,1,256,512]{3,2,1,0:T(8,128)}, f3...) fusion(f32[1,7,256,512]{3,2,1,0:T(8,128)} %param.13), kind=kLoop, calls=%fused_computation.221 | loop fusion | bytes 6291456 | tf_op jit(solution)/shard_map/slice | solution.py:83
  15.6 20.6 %all-to-all-start = ((f32[1,128,1280]{2,0,1:T(1,128)}), f32[1,128,1280]{2,0,1:T(1,128)S(1)}, u32[]{:S(2)}, u32[]{:S(2)}) async-start(f32[1,128,1280]{2,0,1:T(1,128)} %pad_maximum_fusion.7), calls=%async_computation | async-start | bytes 1310720 | tf_op jit(solution)/shard_map/all_to_all | solution.py:39
  37.9 36.5 %all-to-all-done = f32[1,128,1280]{2,0,1:T(1,128)S(1)} async-done(((f32[1,128,1280]{2,0,1:T(1,128)}), f32[1,128,1280]{2,0,1:T(1,128)S(1)}, u32[]{:S(2)}, u32[]{:S(2)}) %all-to-all-start) | async-done | bytes 655392 | tf_op jit(solution)/shard_map/all_to_all | solution.py:39
  78.8 4.0 %all-to-all-start.1 = ((f32[4,1024,128]{2,1,0:T(8,128)}), f32[4,1024,128]{2,1,0:T(8,128)S(1)}, u32[]{:S(2)}, u32[]{:S(2)}) async-start(f32[4,1024,128]{2,1,0:T(8,128)} %broadcast_in_dim.72), calls=%async_computation.1 | async-start | bytes 4194304 | tf_op jit(solution)/shard_map/all_to_all | solution.py:25
  83.0 34.4 %all-to-all-done.1 = f32[4,1024,128]{2,1,0:T(8,128)S(1)} async-done(((f32[4,1024,128]{2,1,0:T(8,128)}), f32[4,1024,128]{2,1,0:T(8,128)S(1)}, u32[]{:S(2)}, u32[]{:S(2)}) %all-to-all-start.1) | async-done | bytes 2097184 | tf_op jit(solution)/shard_map/all_to_all | solution.py:25
  117.4 3.0 collective-permute-start
  122.1 3.7 %gather_fusion.1 = f32[1536,128]{1,0:T(8,128)} fusion(f32[2048,128]{1,0:T(8,128)S(1)} %pad_maximum_fusion, s32[2048]{0:T(1024)S(1)} %pad_clamp_fusion.6), kind=kCustom, calls=%fused_computation.1 | custom fusion | bytes 1579008 | tf_op jit(solution)/shard_map/jit(_take)/gather | solution.py:115
  127.8 3.2 %collective-permute-start.1 = (f32[512,128]{1,0:T(8,128)S(1)}, f32[512,128]{1,0:T(8,128)}, u32[]{:S(2)}, u32[]{:S(2)}) collective-permute-start(f32[512,128]{1,0:T(8,128)S(1)} %slice_subtract_fusion.5), channel_id=1, source_target_pairs={{0,8},{4,12},{8,0},{12,4},{16,24},{20,28},{24,16},{28,20},{32,40},... | collective-permute-start | bytes 786440 | tf_op jit(solution)/shard_map/ppermute | solution.py:12
  137.3 3.1 collective-permute-start.2
  142.8 3.7 %gather_fusion.3 = f32[1536,128]{1,0:T(8,128)} fusion(f32[2048,128]{1,0:T(8,128)S(1)} %pad_maximum_fusion.1, s32[2048]{0:T(1024)S(1)} %pad_clamp_fusion.5), kind=kCustom, calls=%fused_computation.3 | custom fusion | bytes 1579008 | tf_op jit(solution)/shard_map/jit(_take)/gather | solution.py:115
  146.5 2.7 slice_subtract_fusion.4
  149.2 4.2 %collective-permute-start.3 = (f32[512,128]{1,0:T(8,128)}, f32[512,128]{1,0:T(8,128)}, u32[]{:S(2)}, u32[]{:S(2)}) collective-permute-start(f32[512,128]{1,0:T(8,128)} %slice_subtract_fusion.4), channel_id=1, source_target_pairs={{0,16},{4,20},{8,24},{12,28},{16,0},{20,4},{24,8},{28,12},{32,48},... | collective-permute-start | bytes 786440 | tf_op jit(solution)/shard_map/ppermute | solution.py:12
  158.0 7.5 %collective-permute-done.3 = f32[512,128]{1,0:T(8,128)} collective-permute-done((f32[512,128]{1,0:T(8,128)}, f32[512,128]{1,0:T(8,128)}, u32[]{:S(2)}, u32[]{:S(2)}) %collective-permute-start.3) | collective-permute-done | bytes 262176 | tf_op jit(solution)/shard_map/ppermute | solution.py:12
  165.5 3.3 %collective-permute-start.4 = (f32[512,128]{1,0:T(8,128)}, f32[512,128]{1,0:T(8,128)S(1)}, u32[]{:S(2)}, u32[]{:S(2)}) collective-permute-start(f32[512,128]{1,0:T(8,128)} %collective-permute-done.3), channel_id=1, source_target_pairs={{0,4},{4,0},{8,12},{12,8},{16,20},{20,16},{24,28},{28,24},{32,36},... | collective-permute-start | bytes 786440 | tf_op jit(solution)/shard_map/ppermute | solution.py:12
  171.0 3.7 %gather_fusion.5 = f32[1536,128]{1,0:T(8,128)} fusion(f32[2048,128]{1,0:T(8,128)S(1)} %pad_maximum_fusion.2, s32[2048]{0:T(1024)S(1)} %pad_clamp_fusion.4), kind=kCustom, calls=%fused_computation.5 | custom fusion | bytes 1579008 | tf_op jit(solution)/shard_map/jit(_take)/gather | solution.py:115
  174.7 2.8 slice_subtract_fusion.3
  177.5 7.3 %collective-permute-start.5 = (f32[512,128]{1,0:T(8,128)}, f32[512,128]{1,0:T(8,128)}, u32[]{:S(2)}, u32[]{:S(2)}) collective-permute-start(f32[512,128]{1,0:T(8,128)} %slice_subtract_fusion.3), channel_id=1, source_target_pairs={{0,32},{4,36},{8,40},{12,44},{16,48},{20,52},{24,56},{28,60},{32,0... | collective-permute-start | bytes 786440 | tf_op jit(solution)/shard_map/ppermute | solution.py:12
  190.2 17.5 %collective-permute-done.5 = f32[512,128]{1,0:T(8,128)} collective-permute-done((f32[512,128]{1,0:T(8,128)}, f32[512,128]{1,0:T(8,128)}, u32[]{:S(2)}, u32[]{:S(2)}) %collective-permute-start.5) | collective-permute-done | bytes 262176 | tf_op jit(solution)/shard_map/ppermute | solution.py:12
  212.8 3.7 %gather_fusion.7 = f32[1536,128]{1,0:T(8,128)} fusion(f32[2048,128]{1,0:T(8,128)S(1)} %pad_maximum_fusion.3, s32[2048]{0:T(1024)S(1)} %pad_clamp_fusion.3), kind=kCustom, calls=%fused_computation.7 | custom fusion | bytes 1579008 | tf_op jit(solution)/shard_map/jit(_take)/gather | solution.py:115
  216.5 2.8 slice_subtract_fusion.2
  219.3 10.9 %collective-permute-start.7 = (f32[512,128]{1,0:T(8,128)}, f32[512,128]{1,0:T(8,128)}, u32[]{:S(2)}, u32[]{:S(2)}) collective-permute-start(f32[512,128]{1,0:T(8,128)} %slice_subtract_fusion.2), channel_id=1, source_target_pairs={{0,64},{4,68},{8,72},{12,76},{16,80},{20,84},{24,88},{28,92},{32,9... | collective-permute-start | bytes 786440 | tf_op jit(solution)/shard_map/ppermute | solution.py:12
  234.8 17.8 %collective-permute-done.7 = f32[512,128]{1,0:T(8,128)} collective-permute-done((f32[512,128]{1,0:T(8,128)}, f32[512,128]{1,0:T(8,128)}, u32[]{:S(2)}, u32[]{:S(2)}) %collective-permute-start.7) | collective-permute-done | bytes 262176 | tf_op jit(solution)/shard_map/ppermute | solution.py:12
  252.7 2.4 collective-permute-start.8
  257.5 3.7 %gather_fusion.9 = f32[1536,128]{1,0:T(8,128)} fusion(f32[2048,128]{1,0:T(8,128)S(1)} %pad_maximum_fusion.4, s32[2048]{0:T(1024)S(1)} %pad_clamp_fusion.2), kind=kCustom, calls=%fused_computation.9 | custom fusion | bytes 1579008 | tf_op jit(solution)/shard_map/jit(_take)/gather | solution.py:115
  261.2 2.7 slice_subtract_fusion.1
  263.9 3.1 collective-permute-start.9
  273.7 3.1 collective-permute-start.10
  279.2 3.7 %gather_fusion.11 = f32[1536,128]{1,0:T(8,128)} fusion(f32[2048,128]{1,0:T(8,128)S(1)} %pad_maximum_fusion.5, s32[2048]{0:T(1024)S(1)} %pad_clamp_fusion.1), kind=kCustom, calls=%fused_computation.11 | custom fusion | bytes 1579008 | tf_op jit(solution)/shard_map/jit(_take)/gather | solution.py:115
  282.9 2.7 slice_subtract_fusion
  285.6 4.0 %collective-permute-start.11 = (f32[512,128]{1,0:T(8,128)}, f32[512,128]{1,0:T(8,128)}, u32[]{:S(2)}, u32[]{:S(2)}) collective-permute-start(f32[512,128]{1,0:T(8,128)} %slice_subtract_fusion), channel_id=1, source_target_pairs={{0,256},{4,260},{8,264},{12,268},{16,272},{20,276},{24,280},{28,28... | collective-permute-start | bytes 786440 | tf_op jit(solution)/shard_map/ppermute | solution.py:12
  294.3 2.5 collective-permute-done.11
  296.8 3.1 collective-permute-start.12
  (165 shorter events, 67.9 us)
Async XLA Ops:
  7.2 118.6 %all-gather.13.cloned.1.call-start = ((), (), s32[]{:S(2)}) async-start(), calls=%async_computation.2 | async-start | bytes 2621440 | tf_op jit(solution)/shard_map/all_gather | solution.py:83
  10.7 2.7 copy-start.11
  10.7 2.8 copy-start.10
  10.7 135.8 %all-gather.15.cloned.1.call-start = ((), (), s32[]{:S(2)}) async-start(), calls=%async_computation.3 | async-start | bytes 2621440 | tf_op jit(solution)/shard_map/all_gather | solution.py:83
  11.5 163.2 %all-gather.17.cloned.1.call-start = ((), (), s32[]{:S(2)}) async-start(), calls=%async_computation.4 | async-start | bytes 2621440 | tf_op jit(solution)/shard_map/all_gather | solution.py:83
  12.2 204.3 %all-gather.19.cloned.1.call-start = ((), (), s32[]{:S(2)}) async-start(), calls=%async_computation.5 | async-start | bytes 2621440 | tf_op jit(solution)/shard_map/all_gather | solution.py:83
  12.8 248.4 %all-gather.21.cloned.1.call-start = ((), (), s32[]{:S(2)}) async-start(), calls=%async_computation.6 | async-start | bytes 2621440 | tf_op jit(solution)/shard_map/all_gather | solution.py:83
  13.6 23.2 %copy-start.14 = (s32[1,32]{1,0:T(1,128)S(1)}, s32[1,32]{1,0:T(1,128)}, u32[]{:S(2)}) copy-start(s32[1,32]{1,0:T(1,128)} %param.11) | copy-start | bytes 388
  13.6 23.3 %copy-start.12 = (s32[1,7,2,1024]{3,2,1,0:T(2,128)S(1)}, s32[1,7,2,1024]{3,2,1,0:T(2,128)}, u32[]{:S(2)}) copy-start(s32[1,7,2,1024]{3,2,1,0:T(2,128)} %param.12) | copy-start | bytes 172036
  13.6 23.5 %copy-start.9 = (f32[1,32,4096]{2,1,0:T(8,128)S(1)}, f32[1,32,4096]{2,1,0:T(8,128)}, u32[]{:S(2)}) copy-start(f32[1,32,4096]{2,1,0:T(8,128)} %param.9) | copy-start | bytes 1572868
  15.6 58.9 %all-to-all-start = ((f32[1,128,1280]{2,0,1:T(1,128)}), f32[1,128,1280]{2,0,1:T(1,128)S(1)}, u32[]{:S(2)}, u32[]{:S(2)}) async-start(f32[1,128,1280]{2,0,1:T(1,128)} %pad_maximum_fusion.7), calls=%async_computation | async-start | bytes 1310720 | tf_op jit(solution)/shard_map/all_to_all | solution.py:39
  36.1 246.7 %all-gather.23.cloned.1.call-start = ((), (), s32[]{:S(2)}) async-start(), calls=%async_computation.7 | async-start | bytes 2621440 | tf_op jit(solution)/shard_map/all_gather | solution.py:83
  78.8 38.6 %all-to-all-start.1 = ((f32[4,1024,128]{2,1,0:T(8,128)}), f32[4,1024,128]{2,1,0:T(8,128)S(1)}, u32[]{:S(2)}, u32[]{:S(2)}) async-start(f32[4,1024,128]{2,1,0:T(8,128)} %broadcast_in_dim.72), calls=%async_computation.1 | async-start | bytes 4194304 | tf_op jit(solution)/shard_map/all_to_all | solution.py:25
  117.4 4.5 %collective-permute-start = (f32[1024,128]{1,0:T(8,128)S(1)}, f32[1024,128]{1,0:T(8,128)S(1)}, u32[]{:S(2)}, u32[]{:S(2)}) collective-permute-start(f32[1024,128]{1,0:T(8,128)S(1)} %fusion.99), channel_id=1, source_target_pairs={{0,4},{4,0},{8,12},{12,8},{16,20},{20,16},{24,28},{28,24},{32,36},... | collective-permute-start | bytes 1572872 | tf_op jit(solution)/shard_map/ppermute | solution.py:12
  127.7 7.8 %copy-start.7 = (f32[512,128]{1,0:T(8,128)}, f32[512,128]{1,0:T(8,128)S(1)}, u32[]{:S(2)}) copy-start(f32[512,128]{1,0:T(8,128)S(1)} %slice_subtract_fusion.5) | copy-start | bytes 786436
  127.8 9.5 %collective-permute-start.1 = (f32[512,128]{1,0:T(8,128)S(1)}, f32[512,128]{1,0:T(8,128)}, u32[]{:S(2)}, u32[]{:S(2)}) collective-permute-start(f32[512,128]{1,0:T(8,128)S(1)} %slice_subtract_fusion.5), channel_id=1, source_target_pairs={{0,8},{4,12},{8,0},{12,4},{16,24},{20,28},{24,16},{28,20},{32,40},... | collective-permute-start | bytes 786440 | tf_op jit(solution)/shard_map/ppermute | solution.py:12
  137.3 4.5 %collective-permute-start.2 = (f32[512,128]{1,0:T(8,128)}, f32[512,128]{1,0:T(8,128)S(1)}, u32[]{:S(2)}, u32[]{:S(2)}) collective-permute-start(f32[512,128]{1,0:T(8,128)} %collective-permute-done.1), channel_id=1, source_target_pairs={{0,4},{4,0},{8,12},{12,8},{16,20},{20,16},{24,28},{28,24},{32,36},... | collective-permute-start | bytes 786440 | tf_op jit(solution)/shard_map/ppermute | solution.py:12
  149.2 16.2 %collective-permute-start.3 = (f32[512,128]{1,0:T(8,128)}, f32[512,128]{1,0:T(8,128)}, u32[]{:S(2)}, u32[]{:S(2)}) collective-permute-start(f32[512,128]{1,0:T(8,128)} %slice_subtract_fusion.4), channel_id=1, source_target_pairs={{0,16},{4,20},{8,24},{12,28},{16,0},{20,4},{24,8},{28,12},{32,48},... | collective-permute-start | bytes 786440 | tf_op jit(solution)/shard_map/ppermute | solution.py:12
  158.0 11.9 %copy-start = (f32[512,128]{1,0:T(8,128)}, f32[512,128]{1,0:T(8,128)S(1)}, u32[]{:S(2)}) copy-start(f32[512,128]{1,0:T(8,128)S(1)} %sub.101) | copy-start | bytes 786436
  165.5 4.5 %collective-permute-start.4 = (f32[512,128]{1,0:T(8,128)}, f32[512,128]{1,0:T(8,128)S(1)}, u32[]{:S(2)}, u32[]{:S(2)}) collective-permute-start(f32[512,128]{1,0:T(8,128)} %collective-permute-done.3), channel_id=1, source_target_pairs={{0,4},{4,0},{8,12},{12,8},{16,20},{20,16},{24,28},{28,24},{32,36},... | collective-permute-start | bytes 786440 | tf_op jit(solution)/shard_map/ppermute | solution.py:12
  177.5 30.2 %collective-permute-start.5 = (f32[512,128]{1,0:T(8,128)}, f32[512,128]{1,0:T(8,128)}, u32[]{:S(2)}, u32[]{:S(2)}) collective-permute-start(f32[512,128]{1,0:T(8,128)} %slice_subtract_fusion.3), channel_id=1, source_target_pairs={{0,32},{4,36},{8,40},{12,44},{16,48},{20,52},{24,56},{28,60},{32,0... | collective-permute-start | bytes 786440 | tf_op jit(solution)/shard_map/ppermute | solution.py:12
  207.7 3.8 %collective-permute-start.6 = (f32[512,128]{1,0:T(8,128)}, f32[512,128]{1,0:T(8,128)}, u32[]{:S(2)}, u32[]{:S(2)}) collective-permute-start(f32[512,128]{1,0:T(8,128)} %collective-permute-done.5), channel_id=1, source_target_pairs={{0,4},{4,0},{8,12},{12,8},{16,20},{20,16},{24,28},{28,24},{32,36},... | collective-permute-start | bytes 786440 | tf_op jit(solution)/shard_map/ppermute | solution.py:12
  219.3 33.4 %collective-permute-start.7 = (f32[512,128]{1,0:T(8,128)}, f32[512,128]{1,0:T(8,128)}, u32[]{:S(2)}, u32[]{:S(2)}) collective-permute-start(f32[512,128]{1,0:T(8,128)} %slice_subtract_fusion.2), channel_id=1, source_target_pairs={{0,64},{4,68},{8,72},{12,76},{16,80},{20,84},{24,88},{28,92},{32,9... | collective-permute-start | bytes 786440 | tf_op jit(solution)/shard_map/ppermute | solution.py:12
  234.8 21.6 %copy-start.3 = (f32[512,128]{1,0:T(8,128)}, f32[512,128]{1,0:T(8,128)S(1)}, u32[]{:S(2)}) copy-start(f32[512,128]{1,0:T(8,128)S(1)} %sub.107) | copy-start | bytes 786436
  252.7 3.7 %collective-permute-start.8 = (f32[512,128]{1,0:T(8,128)}, f32[512,128]{1,0:T(8,128)S(1)}, u32[]{:S(2)}, u32[]{:S(2)}) collective-permute-start(f32[512,128]{1,0:T(8,128)} %collective-permute-done.7), channel_id=1, source_target_pairs={{0,4},{4,0},{8,12},{12,8},{16,20},{20,16},{24,28},{28,24},{32,36},... | collective-permute-start | bytes 786440 | tf_op jit(solution)/shard_map/ppermute | solution.py:12
  263.9 9.7 %collective-permute-start.9 = (f32[512,128]{1,0:T(8,128)}, f32[512,128]{1,0:T(8,128)}, u32[]{:S(2)}, u32[]{:S(2)}) collective-permute-start(f32[512,128]{1,0:T(8,128)} %slice_subtract_fusion.1), channel_id=1, source_target_pairs={{0,128},{4,132},{8,136},{12,140},{16,144},{20,148},{24,152},{28,15... | collective-permute-start | bytes 786440 | tf_op jit(solution)/shard_map/ppermute | solution.py:12
  271.6 6.5 %copy-start.5 = (f32[512,128]{1,0:T(8,128)}, f32[512,128]{1,0:T(8,128)S(1)}, u32[]{:S(2)}) copy-start(f32[512,128]{1,0:T(8,128)S(1)} %sub.110) | copy-start | bytes 786436
  273.7 4.4 %collective-permute-start.10 = (f32[512,128]{1,0:T(8,128)}, f32[512,128]{1,0:T(8,128)S(1)}, u32[]{:S(2)}, u32[]{:S(2)}) collective-permute-start(f32[512,128]{1,0:T(8,128)} %collective-permute-done.9), channel_id=1, source_target_pairs={{0,4},{4,0},{8,12},{12,8},{16,20},{20,16},{24,28},{28,24},{32,36},... | collective-permute-start | bytes 786440 | tf_op jit(solution)/shard_map/ppermute | solution.py:12
  285.6 11.2 %collective-permute-start.11 = (f32[512,128]{1,0:T(8,128)}, f32[512,128]{1,0:T(8,128)}, u32[]{:S(2)}, u32[]{:S(2)}) collective-permute-start(f32[512,128]{1,0:T(8,128)} %slice_subtract_fusion), channel_id=1, source_target_pairs={{0,256},{4,260},{8,264},{12,268},{16,272},{20,276},{24,280},{28,28... | collective-permute-start | bytes 786440 | tf_op jit(solution)/shard_map/ppermute | solution.py:12
  296.8 4.5 %collective-permute-start.12 = (f32[512,128]{1,0:T(8,128)}, f32[512,128]{1,0:T(8,128)S(1)}, u32[]{:S(2)}, u32[]{:S(2)}) collective-permute-start(f32[512,128]{1,0:T(8,128)} %collective-permute-done.11), channel_id=1, source_target_pairs={{0,4},{4,0},{8,12},{12,8},{16,20},{20,16},{24,28},{28,24},{32,36},... | collective-permute-start | bytes 786440 | tf_op jit(solution)/shard_map/ppermute | solution.py:12
  302.4 2.4 copy-start.1
  302.4 2.4 copy-start.2
  (4 other events, 7.9 us)
Sparse Core Ops, SparseCore 0:
  10.9 43.7 all-gather.12
  56.8 46.0 all-gather.14
  104.9 51.5 all-gather.16
  158.5 38.5 all-gather.18
  199.1 38.5 all-gather.20
  239.7 38.5 all-gather.22

commit v11 on v8

--- a/solution.py
+++ b/solution.py
@@ -38,6 +38,8 @@
     quarter = load_boundary.shape[2]
     joined = jnp.concatenate([load_interior, load_boundary], axis=2)
     joined = lax.all_to_all(joined, "sub", split_axis=1, concat_axis=0, tiled=True)
+    early = 2
+    joined, later_maps = lax.optimization_barrier((joined, merge_maps[0, early:]))
     interior = jnp.transpose(joined[:, 0, :local_rows])
     boundary = jnp.transpose(joined[:, 0, local_rows:])
     num_cases = interior.shape[1]
@@ -81,7 +83,8 @@
         if last:
             matrix = merge_maps[0, level - 1]
         else:
-            matrix = lax.all_gather(merge_maps[0, level - 1], "case", axis=0, tiled=True)
+            source = merge_maps[0, level - 1] if level <= early else later_maps[level - 1 - early]
+            matrix = lax.all_gather(source, "case", axis=0, tiled=True)
         shared_rows = matrix.shape[1]
         upper = slot // half % 2 == 1
         if level == 1:

time: 300 us -> 299 us (level)
  local copies, waits for them, and re-layouts: 39.5 us -> 42.7 us
    ppermute x13, waiting for transfers between devices: 65.2 us -> 69.6 us  [from_partner(): return lax.ppermute(value, axis, pairs)]
  transfers between devices with their start and end apart: 22 -> 22, of which waited for: 17 -> 16; matrix products, arithmetic and copies ran while one was open for 23% -> 23% of each run, Pallas kernels for 0% -> 0%
where the time goes in v11:
time: 299 us; the launch traced here: 297 us
  waiting for transfers between devices  128 us (43%)
  starting transfers between devices  72.7 us (24%)
  local copies, waits for them, and re-layouts  42.7 us (14%)
  matrix products  27.9 us (9%)
  between operations  15.3 us (5%)
  other arithmetic  11 us (4%)
    ppermute x13, waiting for transfers between devices, from_partner(): return lax.ppermute(value, axis, pairs)  69.6 us
    ppermute x13, starting transfers between devices, from_partner(): return lax.ppermute(value, axis, pairs)  44 us
    all_to_all x1, waiting for transfers between devices, on_device(): lax.all_to_all(joined, 'sub', split_axis=1, concat_axis=0, tiled=True)  35.6 us
    dot_general x13, matrix products, rows_of(): return kept - jnp.dot(part, shared, precision=lax.Precision.HIGH)  26.4 us
    gather x7, local copies, waits for them, and re-layouts, on_device(): jnp.take(stacked, jnp.concatenate([left_index(maps[0, :shared_rows]), rig...  23.1 us
    all_to_all x1, starting transfers between devices, on_device(): lax.all_to_all(joined, 'sub', split_axis=1, concat_axis=0, tiled=True)  21 us
    all_to_all x1, waiting for transfers between devices, case_allreduce(): received = lax.all_to_all(chunks, 'case', split_axis=0, concat_axis=0)  14.9 us
    gather x6, local copies, waits for them, and re-layouts, rows_of(): kept = jnp.take(stacked, index, axis=0, mode='clip')  8.04 us
  transfers between devices with their start and end apart: 22, of which 16 were waited for; matrix products, arithmetic and copies ran while one was open for 23% of the time, Pallas kernels for 0%

profile of v11, /device:TPU:1, one launch (start us, length us, event | category | flops | bytes accessed | tf_op | source)
XLA Modules:
  0.0 297.5 jit_solution(10076678910849663275)
XLA Ops:
  12.5 21.0 %all-to-all-start = ((f32[1,128,1280]{2,0,1:T(1,128)}), f32[1,128,1280]{2,0,1:T(1,128)}, u32[]{:S(2)}, u32[]{:S(2)}) async-start(f32[1,128,1280]{2,0,1:T(1,128)} %pad_maximum_fusion.7), calls=%async_computation | async-start | bytes 1310720 | tf_op jit(solution)/shard_map/all_to_all | solution.py:40
  35.9 35.6 %all-to-all-done = f32[1,128,1280]{2,0,1:T(1,128)} async-done(((f32[1,128,1280]{2,0,1:T(1,128)}), f32[1,128,1280]{2,0,1:T(1,128)}, u32[]{:S(2)}, u32[]{:S(2)}) %all-to-all-start) | async-done | bytes 655392 | tf_op jit(solution)/shard_map/all_to_all | solution.py:40
  79.9 4.0 %all-to-all-start.1 = ((f32[4,256,128]{2,1,0:T(8,128)}), f32[4,256,128]{2,1,0:T(8,128)S(1)}, u32[]{:S(2)}, u32[]{:S(2)}) async-start(f32[4,256,128]{2,1,0:T(8,128)} %bitcast.12), calls=%async_computation.1 | async-start | bytes 1048576 | tf_op jit(solution)/shard_map/all_to_all | solution.py:25
  83.9 14.9 %all-to-all-done.1 = f32[4,256,128]{2,1,0:T(8,128)S(1)} async-done(((f32[4,256,128]{2,1,0:T(8,128)}), f32[4,256,128]{2,1,0:T(8,128)S(1)}, u32[]{:S(2)}, u32[]{:S(2)}) %all-to-all-start.1) | async-done | bytes 524320 | tf_op jit(solution)/shard_map/all_to_all | solution.py:25
  99.7 3.5 %all-to-all-start.2 = ((f32[4,256,128]{2,1,0:T(8,128)}), f32[4,256,128]{2,1,0:T(8,128)S(1)}, u32[]{:S(2)}, u32[]{:S(2)}) async-start(f32[4,256,128]{2,1,0:T(8,128)} %broadcast_in_dim.75), calls=%async_computation.2 | async-start | bytes 1048576 | tf_op jit(solution)/shard_map/all_to_all | solution.py:30
  103.2 7.0 %all-to-all-done.2 = f32[4,256,128]{2,1,0:T(8,128)S(1)} async-done(((f32[4,256,128]{2,1,0:T(8,128)}), f32[4,256,128]{2,1,0:T(8,128)S(1)}, u32[]{:S(2)}, u32[]{:S(2)}) %all-to-all-start.2) | async-done | bytes 524320 | tf_op jit(solution)/shard_map/all_to_all | solution.py:30
  110.3 5.2 %collective-permute-start = (f32[1024,128]{1,0:T(8,128)S(1)}, f32[1024,128]{1,0:T(8,128)S(1)}, u32[]{:S(2)}, u32[]{:S(2)}) collective-permute-start(f32[1024,128]{1,0:T(8,128)S(1)} %bitcast.134), channel_id=1, source_target_pairs={{0,4},{4,0},{8,12},{12,8},{16,20},{20,16},{24,28},{28,24},{32,36},... | collective-permute-start | bytes 1572872 | tf_op jit(solution)/shard_map/ppermute | solution.py:12
  117.1 2.6 gather_fusion.1
  121.5 2.9 collective-permute-start.1
  127.4 3.6 %collective-permute-done.1 = f32[512,128]{1,0:T(8,128)S(1)} collective-permute-done((f32[512,128]{1,0:T(8,128)S(1)}, f32[512,128]{1,0:T(8,128)S(1)}, u32[]{:S(2)}, u32[]{:S(2)}) %collective-permute-start.1) | collective-permute-done | bytes 262176 | tf_op jit(solution)/shard_map/ppermute | solution.py:12
  131.0 3.0 %collective-permute-start.2 = (f32[512,128]{1,0:T(8,128)S(1)}, f32[512,128]{1,0:T(8,128)S(1)}, u32[]{:S(2)}, u32[]{:S(2)}) collective-permute-start(f32[512,128]{1,0:T(8,128)S(1)} %collective-permute-done.1), channel_id=1, source_target_pairs={{0,4},{4,0},{8,12},{12,8},{16,20},{20,16},{24,28},{28,24},{32,36},... | collective-permute-start | bytes 786440 | tf_op jit(solution)/shard_map/ppermute | solution.py:12
  135.2 2.6 gather_fusion.3
  139.7 3.3 %collective-permute-start.3 = (f32[512,128]{1,0:T(8,128)S(1)}, f32[512,128]{1,0:T(8,128)}, u32[]{:S(2)}, u32[]{:S(2)}) collective-permute-start(f32[512,128]{1,0:T(8,128)S(1)} %slice_subtract_fusion.4), channel_id=1, source_target_pairs={{0,16},{4,20},{8,24},{12,28},{16,0},{20,4},{24,8},{28,12},{32,48},... | collective-permute-start | bytes 786440 | tf_op jit(solution)/shard_map/ppermute | solution.py:12
  147.4 8.4 %collective-permute-done.3 = f32[512,128]{1,0:T(8,128)} collective-permute-done((f32[512,128]{1,0:T(8,128)S(1)}, f32[512,128]{1,0:T(8,128)}, u32[]{:S(2)}, u32[]{:S(2)}) %collective-permute-start.3) | collective-permute-done | bytes 262176 | tf_op jit(solution)/shard_map/ppermute | solution.py:12
  155.8 3.2 %collective-permute-start.4 = (f32[512,128]{1,0:T(8,128)}, f32[512,128]{1,0:T(8,128)S(1)}, u32[]{:S(2)}, u32[]{:S(2)}) collective-permute-start(f32[512,128]{1,0:T(8,128)} %collective-permute-done.3), channel_id=1, source_target_pairs={{0,4},{4,0},{8,12},{12,8},{16,20},{20,16},{24,28},{28,24},{32,36},... | collective-permute-start | bytes 786440 | tf_op jit(solution)/shard_map/ppermute | solution.py:12
  161.2 3.7 %gather_fusion.5 = f32[1536,128]{1,0:T(8,128)} fusion(f32[2048,128]{1,0:T(8,128)S(1)} %pad_maximum_fusion.2, s32[2048]{0:T(1024)S(1)} %pad_clamp_fusion.4), kind=kCustom, calls=%fused_computation.5 | custom fusion | bytes 1579008 | tf_op jit(solution)/shard_map/jit(_take)/gather | solution.py:119
  166.9 3.4 %collective-permute-start.5 = (f32[512,128]{1,0:T(8,128)S(1)}, f32[512,128]{1,0:T(8,128)S(1)}, u32[]{:S(2)}, u32[]{:S(2)}) collective-permute-start(f32[512,128]{1,0:T(8,128)S(1)} %slice_subtract_fusion.3), channel_id=1, source_target_pairs={{0,32},{4,36},{8,40},{12,44},{16,48},{20,52},{24,56},{28,60},{32,0... | collective-permute-start | bytes 786440 | tf_op jit(solution)/shard_map/ppermute | solution.py:12
  173.5 23.1 %collective-permute-done.5 = f32[512,128]{1,0:T(8,128)S(1)} collective-permute-done((f32[512,128]{1,0:T(8,128)S(1)}, f32[512,128]{1,0:T(8,128)S(1)}, u32[]{:S(2)}, u32[]{:S(2)}) %collective-permute-start.5) | collective-permute-done | bytes 262176 | tf_op jit(solution)/shard_map/ppermute | solution.py:12
  196.6 2.4 collective-permute-start.6
  200.2 3.7 %gather_fusion.7 = f32[1536,128]{1,0:T(8,128)} fusion(f32[2048,128]{1,0:T(8,128)S(1)} %pad_maximum_fusion.3, s32[2048]{0:T(1024)S(1)} %pad_clamp_fusion.3), kind=kCustom, calls=%fused_computation.7 | custom fusion | bytes 1579008 | tf_op jit(solution)/shard_map/jit(_take)/gather | solution.py:119
  206.0 5.2 %collective-permute-start.7 = (f32[512,128]{1,0:T(8,128)S(1)}, f32[512,128]{1,0:T(8,128)}, u32[]{:S(2)}, u32[]{:S(2)}) collective-permute-start(f32[512,128]{1,0:T(8,128)S(1)} %slice_subtract_fusion.2), channel_id=1, source_target_pairs={{0,64},{4,68},{8,72},{12,76},{16,80},{20,84},{24,88},{28,92},{32,9... | collective-permute-start | bytes 786440 | tf_op jit(solution)/shard_map/ppermute | solution.py:12
  214.4 21.7 %collective-permute-done.7 = f32[512,128]{1,0:T(8,128)} collective-permute-done((f32[512,128]{1,0:T(8,128)S(1)}, f32[512,128]{1,0:T(8,128)}, u32[]{:S(2)}, u32[]{:S(2)}) %collective-permute-start.7) | collective-permute-done | bytes 262176 | tf_op jit(solution)/shard_map/ppermute | solution.py:12
  236.1 2.4 collective-permute-start.8
  240.9 3.7 %gather_fusion.9 = f32[1536,128]{1,0:T(8,128)} fusion(f32[2048,128]{1,0:T(8,128)S(1)} %pad_maximum_fusion.4, s32[2048]{0:T(1024)S(1)} %pad_clamp_fusion.2), kind=kCustom, calls=%fused_computation.9 | custom fusion | bytes 1579008 | tf_op jit(solution)/shard_map/jit(_take)/gather | solution.py:119
  253.6 2.6 collective-permute-done.9
  256.2 3.1 %collective-permute-start.10 = (f32[512,128]{1,0:T(8,128)}, f32[512,128]{1,0:T(8,128)S(1)}, u32[]{:S(2)}, u32[]{:S(2)}) collective-permute-start(f32[512,128]{1,0:T(8,128)} %collective-permute-done.9), channel_id=1, source_target_pairs={{0,4},{4,0},{8,12},{12,8},{16,20},{20,16},{24,28},{28,24},{32,36},... | collective-permute-start | bytes 786440 | tf_op jit(solution)/shard_map/ppermute | solution.py:12
  261.7 3.7 %gather_fusion.11 = f32[1536,128]{1,0:T(8,128)} fusion(f32[2048,128]{1,0:T(8,128)S(1)} %pad_maximum_fusion.5, s32[2048]{0:T(1024)S(1)} %pad_clamp_fusion.1), kind=kCustom, calls=%fused_computation.11 | custom fusion | bytes 1579008 | tf_op jit(solution)/shard_map/jit(_take)/gather | solution.py:119
  265.4 2.7 slice_subtract_fusion
  268.1 4.4 %collective-permute-start.11 = (f32[512,128]{1,0:T(8,128)}, f32[512,128]{1,0:T(8,128)}, u32[]{:S(2)}, u32[]{:S(2)}) collective-permute-start(f32[512,128]{1,0:T(8,128)} %slice_subtract_fusion), channel_id=1, source_target_pairs={{0,256},{4,260},{8,264},{12,268},{16,272},{20,276},{24,280},{28,28... | collective-permute-start | bytes 786440 | tf_op jit(solution)/shard_map/ppermute | solution.py:12
  279.2 3.2 %collective-permute-start.12 = (f32[512,128]{1,0:T(8,128)}, f32[512,128]{1,0:T(8,128)}, u32[]{:S(2)}, u32[]{:S(2)}) collective-permute-start(f32[512,128]{1,0:T(8,128)} %collective-permute-done.11), channel_id=1, source_target_pairs={{0,4},{4,0},{8,12},{12,8},{16,20},{20,16},{24,28},{28,24},{32,36},... | collective-permute-start | bytes 786440 | tf_op jit(solution)/shard_map/ppermute | solution.py:12
  285.1 3.1 %gather_fusion.13 = f32[1280,128]{1,0:T(8,128)} fusion(f32[2048,128]{1,0:T(8,128)S(1)} %pad_maximum_fusion.6, s32[2048]{0:T(1024)S(1)} %pad_clamp_fusion), kind=kCustom, calls=%fused_computation.13 | custom fusion | bytes 1315840 | tf_op jit(solution)/shard_map/jit(_take)/gather | solution.py:119
  288.3 2.4 fusion.54
  (160 shorter events, 66.9 us)
Async XLA Ops:
  7.2 3.2 %copy-start.7 = (f32[1,128,256]{2,1,0:T(8,128)S(1)}, f32[1,128,256]{2,1,0:T(8,128)}, u32[]{:S(2)}) copy-start(f32[1,128,256]{2,1,0:T(8,128)} %param.8) | copy-start | bytes 393220
  7.2 3.3 %copy-start.6 = (f32[1,128,1024]{2,1,0:T(8,128)S(1)}, f32[1,128,1024]{2,1,0:T(8,128)}, u32[]{:S(2)}) copy-start(f32[1,128,1024]{2,1,0:T(8,128)} %param.7) | copy-start | bytes 1572868
  7.2 112.5 %all-gather.13.cloned.1.call-start = ((), (), s32[]{:S(2)}) async-start(), calls=%async_computation.3 | async-start | bytes 2621440 | tf_op jit(solution)/shard_map/all_gather | solution.py:87
  9.6 128.3 %all-gather.15.cloned.1.call-start = ((), (), s32[]{:S(2)}) async-start(), calls=%async_computation.4 | async-start | bytes 2621440 | tf_op jit(solution)/shard_map/all_gather | solution.py:87
  10.3 23.3 %copy-start.10 = (s32[1,32]{1,0:T(1,128)S(1)}, s32[1,32]{1,0:T(1,128)}, u32[]{:S(2)}) copy-start(s32[1,32]{1,0:T(1,128)} %param.11) | copy-start | bytes 388
  10.3 23.3 %copy-start.8 = (s32[1,7,2,1024]{3,2,1,0:T(2,128)S(1)}, s32[1,7,2,1024]{3,2,1,0:T(2,128)}, u32[]{:S(2)}) copy-start(s32[1,7,2,1024]{3,2,1,0:T(2,128)} %param.12) | copy-start | bytes 172036
  12.5 59.0 %all-to-all-start = ((f32[1,128,1280]{2,0,1:T(1,128)}), f32[1,128,1280]{2,0,1:T(1,128)}, u32[]{:S(2)}, u32[]{:S(2)}) async-start(f32[1,128,1280]{2,0,1:T(1,128)} %pad_maximum_fusion.7), calls=%async_computation | async-start | bytes 1310720 | tf_op jit(solution)/shard_map/all_to_all | solution.py:40
  33.5 131.4 %all-gather.17.cloned.1.call-start = ((), (), s32[]{:S(2)}) async-start(), calls=%async_computation.5 | async-start | bytes 2621440 | tf_op jit(solution)/shard_map/all_gather | solution.py:87
  74.3 129.6 %all-gather.19.cloned.1.call-start = ((), (), s32[]{:S(2)}) async-start(), calls=%async_computation.6 | async-start | bytes 2621440 | tf_op jit(solution)/shard_map/all_gather | solution.py:87
  79.9 18.9 %all-to-all-start.1 = ((f32[4,256,128]{2,1,0:T(8,128)}), f32[4,256,128]{2,1,0:T(8,128)S(1)}, u32[]{:S(2)}, u32[]{:S(2)}) async-start(f32[4,256,128]{2,1,0:T(8,128)} %bitcast.12), calls=%async_computation.1 | async-start | bytes 1048576 | tf_op jit(solution)/shard_map/all_to_all | solution.py:25
  99.7 10.6 %all-to-all-start.2 = ((f32[4,256,128]{2,1,0:T(8,128)}), f32[4,256,128]{2,1,0:T(8,128)S(1)}, u32[]{:S(2)}, u32[]{:S(2)}) async-start(f32[4,256,128]{2,1,0:T(8,128)} %broadcast_in_dim.75), calls=%async_computation.2 | async-start | bytes 1048576 | tf_op jit(solution)/shard_map/all_to_all | solution.py:30
  103.2 141.4 %all-gather.21.cloned.1.call-start = ((), (), s32[]{:S(2)}) async-start(), calls=%async_computation.7 | async-start | bytes 2621440 | tf_op jit(solution)/shard_map/all_gather | solution.py:87
  110.3 6.7 %collective-permute-start = (f32[1024,128]{1,0:T(8,128)S(1)}, f32[1024,128]{1,0:T(8,128)S(1)}, u32[]{:S(2)}, u32[]{:S(2)}) collective-permute-start(f32[1024,128]{1,0:T(8,128)S(1)} %bitcast.134), channel_id=1, source_target_pairs={{0,4},{4,0},{8,12},{12,8},{16,20},{20,16},{24,28},{28,24},{32,36},... | collective-permute-start | bytes 1572872 | tf_op jit(solution)/shard_map/ppermute | solution.py:12
  115.5 149.9 %all-gather.23.cloned.1.call-start = ((), (), s32[]{:S(2)}) async-start(), calls=%async_computation.8 | async-start | bytes 2621440 | tf_op jit(solution)/shard_map/all_gather | solution.py:87
  121.5 9.5 %collective-permute-start.1 = (f32[512,128]{1,0:T(8,128)S(1)}, f32[512,128]{1,0:T(8,128)S(1)}, u32[]{:S(2)}, u32[]{:S(2)}) collective-permute-start(f32[512,128]{1,0:T(8,128)S(1)} %slice_subtract_fusion.5), channel_id=1, source_target_pairs={{0,8},{4,12},{8,0},{12,4},{16,24},{20,28},{24,16},{28,20},{32,40},... | collective-permute-start | bytes 786440 | tf_op jit(solution)/shard_map/ppermute | solution.py:12
  131.0 4.1 %collective-permute-start.2 = (f32[512,128]{1,0:T(8,128)S(1)}, f32[512,128]{1,0:T(8,128)S(1)}, u32[]{:S(2)}, u32[]{:S(2)}) collective-permute-start(f32[512,128]{1,0:T(8,128)S(1)} %collective-permute-done.1), channel_id=1, source_target_pairs={{0,4},{4,0},{8,12},{12,8},{16,20},{20,16},{24,28},{28,24},{32,36},... | collective-permute-start | bytes 786440 | tf_op jit(solution)/shard_map/ppermute | solution.py:12
  139.7 20.5 %copy-start = (f32[512,128]{1,0:T(8,128)}, f32[512,128]{1,0:T(8,128)S(1)}, u32[]{:S(2)}) copy-start(f32[512,128]{1,0:T(8,128)S(1)} %slice_subtract_fusion.4) | copy-start | bytes 786436
  139.7 16.1 %collective-permute-start.3 = (f32[512,128]{1,0:T(8,128)S(1)}, f32[512,128]{1,0:T(8,128)}, u32[]{:S(2)}, u32[]{:S(2)}) collective-permute-start(f32[512,128]{1,0:T(8,128)S(1)} %slice_subtract_fusion.4), channel_id=1, source_target_pairs={{0,16},{4,20},{8,24},{12,28},{16,0},{20,4},{24,8},{28,12},{32,48},... | collective-permute-start | bytes 786440 | tf_op jit(solution)/shard_map/ppermute | solution.py:12
  155.8 4.4 %collective-permute-start.4 = (f32[512,128]{1,0:T(8,128)}, f32[512,128]{1,0:T(8,128)S(1)}, u32[]{:S(2)}, u32[]{:S(2)}) collective-permute-start(f32[512,128]{1,0:T(8,128)} %collective-permute-done.3), channel_id=1, source_target_pairs={{0,4},{4,0},{8,12},{12,8},{16,20},{20,16},{24,28},{28,24},{32,36},... | collective-permute-start | bytes 786440 | tf_op jit(solution)/shard_map/ppermute | solution.py:12
  166.9 33.2 %copy-start.2 = (f32[512,128]{1,0:T(8,128)}, f32[512,128]{1,0:T(8,128)S(1)}, u32[]{:S(2)}) copy-start(f32[512,128]{1,0:T(8,128)S(1)} %slice_subtract_fusion.3) | copy-start | bytes 786436
  166.9 29.6 %collective-permute-start.5 = (f32[512,128]{1,0:T(8,128)S(1)}, f32[512,128]{1,0:T(8,128)S(1)}, u32[]{:S(2)}, u32[]{:S(2)}) collective-permute-start(f32[512,128]{1,0:T(8,128)S(1)} %slice_subtract_fusion.3), channel_id=1, source_target_pairs={{0,32},{4,36},{8,40},{12,44},{16,48},{20,52},{24,56},{28,60},{32,0... | collective-permute-start | bytes 786440 | tf_op jit(solution)/shard_map/ppermute | solution.py:12
  196.6 3.5 %collective-permute-start.6 = (f32[512,128]{1,0:T(8,128)S(1)}, f32[512,128]{1,0:T(8,128)S(1)}, u32[]{:S(2)}, u32[]{:S(2)}) collective-permute-start(f32[512,128]{1,0:T(8,128)S(1)} %collective-permute-done.5), channel_id=1, source_target_pairs={{0,4},{4,0},{8,12},{12,8},{16,20},{20,16},{24,28},{28,24},{32,36},... | collective-permute-start | bytes 786440 | tf_op jit(solution)/shard_map/ppermute | solution.py:12
  206.0 33.8 %copy-start.4 = (f32[512,128]{1,0:T(8,128)}, f32[512,128]{1,0:T(8,128)S(1)}, u32[]{:S(2)}) copy-start(f32[512,128]{1,0:T(8,128)S(1)} %slice_subtract_fusion.2) | copy-start | bytes 786436
  206.0 30.1 %collective-permute-start.7 = (f32[512,128]{1,0:T(8,128)S(1)}, f32[512,128]{1,0:T(8,128)}, u32[]{:S(2)}, u32[]{:S(2)}) collective-permute-start(f32[512,128]{1,0:T(8,128)S(1)} %slice_subtract_fusion.2), channel_id=1, source_target_pairs={{0,64},{4,68},{8,72},{12,76},{16,80},{20,84},{24,88},{28,92},{32,9... | collective-permute-start | bytes 786440 | tf_op jit(solution)/shard_map/ppermute | solution.py:12
  236.1 3.7 %collective-permute-start.8 = (f32[512,128]{1,0:T(8,128)}, f32[512,128]{1,0:T(8,128)S(1)}, u32[]{:S(2)}, u32[]{:S(2)}) collective-permute-start(f32[512,128]{1,0:T(8,128)} %collective-permute-done.7), channel_id=1, source_target_pairs={{0,4},{4,0},{8,12},{12,8},{16,20},{20,16},{24,28},{28,24},{32,36},... | collective-permute-start | bytes 786440 | tf_op jit(solution)/shard_map/ppermute | solution.py:12
  246.7 14.0 %copy-start.5 = (f32[512,128]{1,0:T(8,128)}, f32[512,128]{1,0:T(8,128)S(1)}, u32[]{:S(2)}) copy-start(f32[512,128]{1,0:T(8,128)S(1)} %slice_subtract_fusion.1) | copy-start | bytes 786436
  246.7 9.5 %collective-permute-start.9 = (f32[512,128]{1,0:T(8,128)S(1)}, f32[512,128]{1,0:T(8,128)}, u32[]{:S(2)}, u32[]{:S(2)}) collective-permute-start(f32[512,128]{1,0:T(8,128)S(1)} %slice_subtract_fusion.1), channel_id=1, source_target_pairs={{0,128},{4,132},{8,136},{12,140},{16,144},{20,148},{24,152},{28,15... | collective-permute-start | bytes 786440 | tf_op jit(solution)/shard_map/ppermute | solution.py:12
  256.2 4.5 %collective-permute-start.10 = (f32[512,128]{1,0:T(8,128)}, f32[512,128]{1,0:T(8,128)S(1)}, u32[]{:S(2)}, u32[]{:S(2)}) collective-permute-start(f32[512,128]{1,0:T(8,128)} %collective-permute-done.9), channel_id=1, source_target_pairs={{0,4},{4,0},{8,12},{12,8},{16,20},{20,16},{24,28},{28,24},{32,36},... | collective-permute-start | bytes 786440 | tf_op jit(solution)/shard_map/ppermute | solution.py:12
  268.1 11.1 %collective-permute-start.11 = (f32[512,128]{1,0:T(8,128)}, f32[512,128]{1,0:T(8,128)}, u32[]{:S(2)}, u32[]{:S(2)}) collective-permute-start(f32[512,128]{1,0:T(8,128)} %slice_subtract_fusion), channel_id=1, source_target_pairs={{0,256},{4,260},{8,264},{12,268},{16,272},{20,276},{24,280},{28,28... | collective-permute-start | bytes 786440 | tf_op jit(solution)/shard_map/ppermute | solution.py:12
  279.2 4.7 %collective-permute-start.12 = (f32[512,128]{1,0:T(8,128)}, f32[512,128]{1,0:T(8,128)}, u32[]{:S(2)}, u32[]{:S(2)}) collective-permute-start(f32[512,128]{1,0:T(8,128)} %collective-permute-done.11), channel_id=1, source_target_pairs={{0,4},{4,0},{8,12},{12,8},{16,20},{20,16},{24,28},{28,24},{32,36},... | collective-permute-start | bytes 786440 | tf_op jit(solution)/shard_map/ppermute | solution.py:12
  285.1 3.2 %copy-start.1 = (f32[512,128]{1,0:T(8,128)S(1)}, f32[512,128]{1,0:T(8,128)}, u32[]{:S(2)}) copy-start(f32[512,128]{1,0:T(8,128)} %copy-done) | copy-start | bytes 786436
  285.1 3.1 %copy-start.3 = (f32[512,128]{1,0:T(8,128)S(1)}, f32[512,128]{1,0:T(8,128)}, u32[]{:S(2)}) copy-start(f32[512,128]{1,0:T(8,128)} %copy-done.2) | copy-start | bytes 786436
  (1 other events, 0.7 us)
Sparse Core Ops, SparseCore 0:
  10.1 43.7 all-gather.12
  56.0 43.7 all-gather.14
  101.9 41.5 all-gather.16
  145.4 38.5 all-gather.18
  186.0 38.5 all-gather.20
  226.6 38.5 all-gather.22

commit v12 on v11

--- a/solution.py
+++ b/solution.py
@@ -18,14 +18,15 @@
     return lax.ppermute(value, axis, pairs)
 
 
-def case_allreduce(value, position):
+def case_allreduce(value, boundary):
     groups = lax.axis_size("case")
     quarter = value.shape[0] // groups
     chunks = value.reshape(groups, quarter, value.shape[1])
     received = lax.all_to_all(chunks, "case", split_axis=0, concat_axis=0)
-    mine = received[0]
+    summed = received[0]
     for source in range(1, groups):
-        mine = mine + received[source]
+        summed = summed + received[source]
+    mine = boundary - summed
     copies = jnp.broadcast_to(mine[None], chunks.shape)
     full = lax.all_to_all(copies, "case", split_axis=0, concat_axis=0).reshape(value.shape)
     return mine, full
@@ -64,11 +65,7 @@
         precision=lax.Precision.HIGH,
     )
     partial_value = partial_value.reshape(full_rows, num_cases)
-    embedded = lax.dynamic_update_slice(
-        jnp.zeros((full_rows, num_cases), jnp.float32), boundary, (position * quarter, 0)
-    )
-    contribution = embedded - partial_value
-    leaf_share, current = case_allreduce(contribution, position)
+    leaf_share, current = case_allreduce(partial_value, boundary)
     slot = lax.axis_index("sub")
     levels = lax.axis_size("sub").bit_length() - 1
     nodes = jnp.zeros((quarter, num_cases), jnp.float32)

time: 299 us -> 298 us (level)
  waiting for transfers between devices: 128 us -> 131 us
  transfers between devices with their start and end apart: 22 -> 22, of which waited for: 16 -> 17; matrix products, arithmetic and copies ran while one was open for 23% -> 22% of each run, Pallas kernels for 0% -> 0%
where the time goes in v12:
time: 298 us; the launch traced here: 297 us
  waiting for transfers between devices  131 us (44%)
  starting transfers between devices  73.5 us (25%)
  local copies, waits for them, and re-layouts  41.6 us (14%)
  matrix products  27.7 us (9%)
  between operations  15.3 us (5%)
  other arithmetic  8.35 us (3%)
    ppermute x13, waiting for transfers between devices, from_partner(): return lax.ppermute(value, axis, pairs)  71.2 us
    ppermute x13, starting transfers between devices, from_partner(): return lax.ppermute(value, axis, pairs)  44.8 us
    all_to_all x1, waiting for transfers between devices, on_device(): lax.all_to_all(joined, 'sub', split_axis=1, concat_axis=0, tiled=True)  35.7 us
    dot_general x13, matrix products, rows_of(): return kept - jnp.dot(part, shared, precision=lax.Precision.HIGH)  26.1 us
    gather x7, local copies, waits for them, and re-layouts, on_device(): jnp.take(stacked, jnp.concatenate([left_index(maps[0, :shared_rows]), rig...  21.9 us
    all_to_all x1, starting transfers between devices, on_device(): lax.all_to_all(joined, 'sub', split_axis=1, concat_axis=0, tiled=True)  21 us
    all_to_all x1, waiting for transfers between devices, case_allreduce(): received = lax.all_to_all(chunks, 'case', split_axis=0, concat_axis=0)  14.9 us
    gather x6, local copies, waits for them, and re-layouts, rows_of(): kept = jnp.take(stacked, index, axis=0, mode='clip')  7.42 us
  transfers between devices with their start and end apart: 22, of which 17 were waited for; matrix products, arithmetic and copies ran while one was open for 22% of the time, Pallas kernels for 0%

profile of v12, /device:TPU:1, one launch (start us, length us, event | category | flops | bytes accessed | tf_op | source)
XLA Modules:
  0.0 297.0 jit_solution(14690298742240735321)
XLA Ops:
  12.5 21.0 %all-to-all-start = ((f32[1,128,1280]{2,0,1:T(1,128)}), f32[1,128,1280]{2,0,1:T(1,128)}, u32[]{:S(2)}, u32[]{:S(2)}) async-start(f32[1,128,1280]{2,0,1:T(1,128)} %pad_maximum_fusion.7), calls=%async_computation | async-start | bytes 1310720 | tf_op jit(solution)/shard_map/all_to_all | solution.py:41
  35.8 35.7 %all-to-all-done = f32[1,128,1280]{2,0,1:T(1,128)} async-done(((f32[1,128,1280]{2,0,1:T(1,128)}), f32[1,128,1280]{2,0,1:T(1,128)}, u32[]{:S(2)}, u32[]{:S(2)}) %all-to-all-start) | async-done | bytes 655392 | tf_op jit(solution)/shard_map/all_to_all | solution.py:41
  79.6 4.0 %all-to-all-start.1 = ((f32[4,256,128]{2,1,0:T(8,128)}), f32[4,256,128]{2,1,0:T(8,128)S(1)}, u32[]{:S(2)}, u32[]{:S(2)}) async-start(f32[4,256,128]{2,1,0:T(8,128)} %reshape_reshape.3), calls=%async_computation.1 | async-start | bytes 1048576 | tf_op jit(solution)/shard_map/all_to_all | solution.py:25
  83.6 14.9 %all-to-all-done.1 = f32[4,256,128]{2,1,0:T(8,128)S(1)} async-done(((f32[4,256,128]{2,1,0:T(8,128)}), f32[4,256,128]{2,1,0:T(8,128)S(1)}, u32[]{:S(2)}, u32[]{:S(2)}) %all-to-all-start.1) | async-done | bytes 524320 | tf_op jit(solution)/shard_map/all_to_all | solution.py:25
  99.4 3.5 %all-to-all-start.2 = ((f32[4,256,128]{2,1,0:T(8,128)}), f32[4,256,128]{2,1,0:T(8,128)S(1)}, u32[]{:S(2)}, u32[]{:S(2)}) async-start(f32[4,256,128]{2,1,0:T(8,128)} %broadcast_in_dim.71), calls=%async_computation.2 | async-start | bytes 1048576 | tf_op jit(solution)/shard_map/all_to_all | solution.py:31
  103.0 6.9 %all-to-all-done.2 = f32[4,256,128]{2,1,0:T(8,128)S(1)} async-done(((f32[4,256,128]{2,1,0:T(8,128)}), f32[4,256,128]{2,1,0:T(8,128)S(1)}, u32[]{:S(2)}, u32[]{:S(2)}) %all-to-all-start.2) | async-done | bytes 524320 | tf_op jit(solution)/shard_map/all_to_all | solution.py:31
  109.8 5.4 %collective-permute-start = (f32[1024,128]{1,0:T(8,128)S(1)}, f32[1024,128]{1,0:T(8,128)S(1)}, u32[]{:S(2)}, u32[]{:S(2)}) collective-permute-start(f32[1024,128]{1,0:T(8,128)S(1)} %bitcast.136), channel_id=1, source_target_pairs={{0,4},{4,0},{8,12},{12,8},{16,20},{20,16},{24,28},{28,24},{32,36},... | collective-permute-start | bytes 1572872 | tf_op jit(solution)/shard_map/ppermute | solution.py:12
  116.8 2.6 gather_fusion.1
  121.3 3.1 %collective-permute-start.1 = (f32[512,128]{1,0:T(8,128)S(1)}, f32[512,128]{1,0:T(8,128)S(1)}, u32[]{:S(2)}, u32[]{:S(2)}) collective-permute-start(f32[512,128]{1,0:T(8,128)S(1)} %slice_subtract_fusion.5), channel_id=1, source_target_pairs={{0,8},{4,12},{8,0},{12,4},{16,24},{20,28},{24,16},{28,20},{32,40},... | collective-permute-start | bytes 786440 | tf_op jit(solution)/shard_map/ppermute | solution.py:12
  127.3 3.4 %collective-permute-done.1 = f32[512,128]{1,0:T(8,128)S(1)} collective-permute-done((f32[512,128]{1,0:T(8,128)S(1)}, f32[512,128]{1,0:T(8,128)S(1)}, u32[]{:S(2)}, u32[]{:S(2)}) %collective-permute-start.1) | collective-permute-done | bytes 262176 | tf_op jit(solution)/shard_map/ppermute | solution.py:12
  130.8 3.0 %collective-permute-start.2 = (f32[512,128]{1,0:T(8,128)S(1)}, f32[512,128]{1,0:T(8,128)S(1)}, u32[]{:S(2)}, u32[]{:S(2)}) collective-permute-start(f32[512,128]{1,0:T(8,128)S(1)} %collective-permute-done.1), channel_id=1, source_target_pairs={{0,4},{4,0},{8,12},{12,8},{16,20},{20,16},{24,28},{28,24},{32,36},... | collective-permute-start | bytes 786440 | tf_op jit(solution)/shard_map/ppermute | solution.py:12
  135.0 2.6 gather_fusion.3
  139.5 3.3 %collective-permute-start.3 = (f32[512,128]{1,0:T(8,128)S(1)}, f32[512,128]{1,0:T(8,128)S(1)}, u32[]{:S(2)}, u32[]{:S(2)}) collective-permute-start(f32[512,128]{1,0:T(8,128)S(1)} %slice_subtract_fusion.4), channel_id=1, source_target_pairs={{0,16},{4,20},{8,24},{12,28},{16,0},{20,4},{24,8},{28,12},{32,48},... | collective-permute-start | bytes 786440 | tf_op jit(solution)/shard_map/ppermute | solution.py:12
  145.7 9.8 %collective-permute-done.3 = f32[512,128]{1,0:T(8,128)S(1)} collective-permute-done((f32[512,128]{1,0:T(8,128)S(1)}, f32[512,128]{1,0:T(8,128)S(1)}, u32[]{:S(2)}, u32[]{:S(2)}) %collective-permute-start.3) | collective-permute-done | bytes 262176 | tf_op jit(solution)/shard_map/ppermute | solution.py:12
  155.4 3.3 %collective-permute-start.4 = (f32[512,128]{1,0:T(8,128)S(1)}, f32[512,128]{1,0:T(8,128)S(1)}, u32[]{:S(2)}, u32[]{:S(2)}) collective-permute-start(f32[512,128]{1,0:T(8,128)S(1)} %collective-permute-done.3), channel_id=1, source_target_pairs={{0,4},{4,0},{8,12},{12,8},{16,20},{20,16},{24,28},{28,24},{32,36},... | collective-permute-start | bytes 786440 | tf_op jit(solution)/shard_map/ppermute | solution.py:12
  159.7 2.6 gather_fusion.5
  164.2 3.3 %collective-permute-start.5 = (f32[512,128]{1,0:T(8,128)S(1)}, f32[512,128]{1,0:T(8,128)}, u32[]{:S(2)}, u32[]{:S(2)}) collective-permute-start(f32[512,128]{1,0:T(8,128)S(1)} %slice_subtract_fusion.3), channel_id=1, source_target_pairs={{0,32},{4,36},{8,40},{12,44},{16,48},{20,52},{24,56},{28,60},{32,0... | collective-permute-start | bytes 786440 | tf_op jit(solution)/shard_map/ppermute | solution.py:12
  170.5 23.4 %collective-permute-done.5 = f32[512,128]{1,0:T(8,128)} collective-permute-done((f32[512,128]{1,0:T(8,128)S(1)}, f32[512,128]{1,0:T(8,128)}, u32[]{:S(2)}, u32[]{:S(2)}) %collective-permute-start.5) | collective-permute-done | bytes 262176 | tf_op jit(solution)/shard_map/ppermute | solution.py:12
  193.9 2.4 collective-permute-start.6
  198.7 3.7 %gather_fusion.7 = f32[1536,128]{1,0:T(8,128)} fusion(f32[2048,128]{1,0:T(8,128)S(1)} %pad_maximum_fusion.3, s32[2048]{0:T(1024)S(1)} %pad_clamp_fusion.3), kind=kCustom, calls=%fused_computation.7 | custom fusion | bytes 1579008 | tf_op jit(solution)/shard_map/jit(_take)/gather | solution.py:116
  204.5 5.4 %collective-permute-start.7 = (f32[512,128]{1,0:T(8,128)S(1)}, f32[512,128]{1,0:T(8,128)}, u32[]{:S(2)}, u32[]{:S(2)}) collective-permute-start(f32[512,128]{1,0:T(8,128)S(1)} %slice_subtract_fusion.2), channel_id=1, source_target_pairs={{0,64},{4,68},{8,72},{12,76},{16,80},{20,84},{24,88},{28,92},{32,9... | collective-permute-start | bytes 786440 | tf_op jit(solution)/shard_map/ppermute | solution.py:12
  213.0 21.6 %collective-permute-done.7 = f32[512,128]{1,0:T(8,128)} collective-permute-done((f32[512,128]{1,0:T(8,128)S(1)}, f32[512,128]{1,0:T(8,128)}, u32[]{:S(2)}, u32[]{:S(2)}) %collective-permute-start.7) | collective-permute-done | bytes 262176 | tf_op jit(solution)/shard_map/ppermute | solution.py:12
  234.6 2.4 collective-permute-start.8
  239.3 3.7 %gather_fusion.9 = f32[1536,128]{1,0:T(8,128)} fusion(f32[2048,128]{1,0:T(8,128)S(1)} %pad_maximum_fusion.4, s32[2048]{0:T(1024)S(1)} %pad_clamp_fusion.2), kind=kCustom, calls=%fused_computation.9 | custom fusion | bytes 1579008 | tf_op jit(solution)/shard_map/jit(_take)/gather | solution.py:116
  252.0 2.7 collective-permute-done.9
  254.7 3.0 %collective-permute-start.10 = (f32[512,128]{1,0:T(8,128)}, f32[512,128]{1,0:T(8,128)S(1)}, u32[]{:S(2)}, u32[]{:S(2)}) collective-permute-start(f32[512,128]{1,0:T(8,128)} %collective-permute-done.9), channel_id=1, source_target_pairs={{0,4},{4,0},{8,12},{12,8},{16,20},{20,16},{24,28},{28,24},{32,36},... | collective-permute-start | bytes 786440 | tf_op jit(solution)/shard_map/ppermute | solution.py:12
  260.2 3.7 %gather_fusion.11 = f32[1536,128]{1,0:T(8,128)} fusion(f32[2048,128]{1,0:T(8,128)S(1)} %pad_maximum_fusion.5, s32[2048]{0:T(1024)S(1)} %pad_clamp_fusion.1), kind=kCustom, calls=%fused_computation.11 | custom fusion | bytes 1579008 | tf_op jit(solution)/shard_map/jit(_take)/gather | solution.py:116
  265.0 2.7 slice_subtract_fusion
  267.7 4.6 %collective-permute-start.11 = (f32[512,128]{1,0:T(8,128)}, f32[512,128]{1,0:T(8,128)}, u32[]{:S(2)}, u32[]{:S(2)}) collective-permute-start(f32[512,128]{1,0:T(8,128)} %slice_subtract_fusion), channel_id=1, source_target_pairs={{0,256},{4,260},{8,264},{12,268},{16,272},{20,276},{24,280},{28,28... | collective-permute-start | bytes 786440 | tf_op jit(solution)/shard_map/ppermute | solution.py:12
  278.6 3.4 %collective-permute-start.12 = (f32[512,128]{1,0:T(8,128)}, f32[512,128]{1,0:T(8,128)}, u32[]{:S(2)}, u32[]{:S(2)}) collective-permute-start(f32[512,128]{1,0:T(8,128)} %collective-permute-done.11), channel_id=1, source_target_pairs={{0,4},{4,0},{8,12},{12,8},{16,20},{20,16},{24,28},{28,24},{32,36},... | collective-permute-start | bytes 786440 | tf_op jit(solution)/shard_map/ppermute | solution.py:12
  284.7 3.1 %gather_fusion.13 = f32[1280,128]{1,0:T(8,128)} fusion(f32[2048,128]{1,0:T(8,128)S(1)} %pad_maximum_fusion.6, s32[2048]{0:T(1024)S(1)} %pad_clamp_fusion), kind=kCustom, calls=%fused_computation.13 | custom fusion | bytes 1315840 | tf_op jit(solution)/shard_map/jit(_take)/gather | solution.py:116
  287.8 2.4 fusion.54
  (150 shorter events, 65.4 us)
Async XLA Ops:
  7.2 3.2 %copy-start.2 = (f32[1,128,1024]{2,1,0:T(8,128)S(1)}, f32[1,128,1024]{2,1,0:T(8,128)}, u32[]{:S(2)}) copy-start(f32[1,128,1024]{2,1,0:T(8,128)} %param.7) | copy-start | bytes 1572868
  7.2 3.7 %copy-start.4 = (f32[1,128,256]{2,1,0:T(8,128)S(1)}, f32[1,128,256]{2,1,0:T(8,128)}, u32[]{:S(2)}) copy-start(f32[1,128,256]{2,1,0:T(8,128)} %param.8) | copy-start | bytes 393220
  7.2 112.3 %all-gather.13.cloned.1.call-start = ((), (), s32[]{:S(2)}) async-start(), calls=%async_computation.3 | async-start | bytes 2621440 | tf_op jit(solution)/shard_map/all_gather | solution.py:84
  9.6 128.0 %all-gather.15.cloned.1.call-start = ((), (), s32[]{:S(2)}) async-start(), calls=%async_computation.4 | async-start | bytes 2621440 | tf_op jit(solution)/shard_map/all_gather | solution.py:84
  10.3 23.2 %copy-start.7 = (s32[1,32]{1,0:T(1,128)S(1)}, s32[1,32]{1,0:T(1,128)}, u32[]{:S(2)}) copy-start(s32[1,32]{1,0:T(1,128)} %param.11) | copy-start | bytes 388
  10.4 23.2 %copy-start.5 = (s32[1,7,2,1024]{3,2,1,0:T(2,128)S(1)}, s32[1,7,2,1024]{3,2,1,0:T(2,128)}, u32[]{:S(2)}) copy-start(s32[1,7,2,1024]{3,2,1,0:T(2,128)} %param.12) | copy-start | bytes 172036
  12.5 59.0 %all-to-all-start = ((f32[1,128,1280]{2,0,1:T(1,128)}), f32[1,128,1280]{2,0,1:T(1,128)}, u32[]{:S(2)}, u32[]{:S(2)}) async-start(f32[1,128,1280]{2,0,1:T(1,128)} %pad_maximum_fusion.7), calls=%async_computation | async-start | bytes 1310720 | tf_op jit(solution)/shard_map/all_to_all | solution.py:41
  33.4 128.9 %all-gather.17.cloned.1.call-start = ((), (), s32[]{:S(2)}) async-start(), calls=%async_computation.5 | async-start | bytes 2621440 | tf_op jit(solution)/shard_map/all_gather | solution.py:84
  74.2 128.2 %all-gather.19.cloned.1.call-start = ((), (), s32[]{:S(2)}) async-start(), calls=%async_computation.6 | async-start | bytes 2621440 | tf_op jit(solution)/shard_map/all_gather | solution.py:84
  77.2 0.7 copy-start.6
  79.6 18.9 %all-to-all-start.1 = ((f32[4,256,128]{2,1,0:T(8,128)}), f32[4,256,128]{2,1,0:T(8,128)S(1)}, u32[]{:S(2)}, u32[]{:S(2)}) async-start(f32[4,256,128]{2,1,0:T(8,128)} %reshape_reshape.3), calls=%async_computation.1 | async-start | bytes 1048576 | tf_op jit(solution)/shard_map/all_to_all | solution.py:25
  98.6 18.2 %copy-start.3 = (f32[256,128]{1,0:T(8,128)}, f32[256,128]{1,0:T(8,128)S(1)}, u32[]{:S(2)}) copy-start(f32[256,128]{1,0:T(8,128)S(1)} %fusion.61) | copy-start | bytes 393220
  99.4 10.4 %all-to-all-start.2 = ((f32[4,256,128]{2,1,0:T(8,128)}), f32[4,256,128]{2,1,0:T(8,128)S(1)}, u32[]{:S(2)}, u32[]{:S(2)}) async-start(f32[4,256,128]{2,1,0:T(8,128)} %broadcast_in_dim.71), calls=%async_computation.2 | async-start | bytes 1048576 | tf_op jit(solution)/shard_map/all_to_all | solution.py:31
  102.9 140.1 %all-gather.21.cloned.1.call-start = ((), (), s32[]{:S(2)}) async-start(), calls=%async_computation.7 | async-start | bytes 2621440 | tf_op jit(solution)/shard_map/all_gather | solution.py:84
  109.8 6.9 %collective-permute-start = (f32[1024,128]{1,0:T(8,128)S(1)}, f32[1024,128]{1,0:T(8,128)S(1)}, u32[]{:S(2)}, u32[]{:S(2)}) collective-permute-start(f32[1024,128]{1,0:T(8,128)S(1)} %bitcast.136), channel_id=1, source_target_pairs={{0,4},{4,0},{8,12},{12,8},{16,20},{20,16},{24,28},{28,24},{32,36},... | collective-permute-start | bytes 1572872 | tf_op jit(solution)/shard_map/ppermute | solution.py:12
  115.3 149.7 %all-gather.23.cloned.1.call-start = ((), (), s32[]{:S(2)}) async-start(), calls=%async_computation.8 | async-start | bytes 2621440 | tf_op jit(solution)/shard_map/all_gather | solution.py:84
  121.3 9.5 %collective-permute-start.1 = (f32[512,128]{1,0:T(8,128)S(1)}, f32[512,128]{1,0:T(8,128)S(1)}, u32[]{:S(2)}, u32[]{:S(2)}) collective-permute-start(f32[512,128]{1,0:T(8,128)S(1)} %slice_subtract_fusion.5), channel_id=1, source_target_pairs={{0,8},{4,12},{8,0},{12,4},{16,24},{20,28},{24,16},{28,20},{32,40},... | collective-permute-start | bytes 786440 | tf_op jit(solution)/shard_map/ppermute | solution.py:12
  130.8 4.1 %collective-permute-start.2 = (f32[512,128]{1,0:T(8,128)S(1)}, f32[512,128]{1,0:T(8,128)S(1)}, u32[]{:S(2)}, u32[]{:S(2)}) collective-permute-start(f32[512,128]{1,0:T(8,128)S(1)} %collective-permute-done.1), channel_id=1, source_target_pairs={{0,4},{4,0},{8,12},{12,8},{16,20},{20,16},{24,28},{28,24},{32,36},... | collective-permute-start | bytes 786440 | tf_op jit(solution)/shard_map/ppermute | solution.py:12
  139.5 15.9 %collective-permute-start.3 = (f32[512,128]{1,0:T(8,128)S(1)}, f32[512,128]{1,0:T(8,128)S(1)}, u32[]{:S(2)}, u32[]{:S(2)}) collective-permute-start(f32[512,128]{1,0:T(8,128)S(1)} %slice_subtract_fusion.4), channel_id=1, source_target_pairs={{0,16},{4,20},{8,24},{12,28},{16,0},{20,4},{24,8},{28,12},{32,48},... | collective-permute-start | bytes 786440 | tf_op jit(solution)/shard_map/ppermute | solution.py:12
  155.4 4.2 %collective-permute-start.4 = (f32[512,128]{1,0:T(8,128)S(1)}, f32[512,128]{1,0:T(8,128)S(1)}, u32[]{:S(2)}, u32[]{:S(2)}) collective-permute-start(f32[512,128]{1,0:T(8,128)S(1)} %collective-permute-done.3), channel_id=1, source_target_pairs={{0,4},{4,0},{8,12},{12,8},{16,20},{20,16},{24,28},{28,24},{32,36},... | collective-permute-start | bytes 786440 | tf_op jit(solution)/shard_map/ppermute | solution.py:12
  164.2 29.7 %collective-permute-start.5 = (f32[512,128]{1,0:T(8,128)S(1)}, f32[512,128]{1,0:T(8,128)}, u32[]{:S(2)}, u32[]{:S(2)}) collective-permute-start(f32[512,128]{1,0:T(8,128)S(1)} %slice_subtract_fusion.3), channel_id=1, source_target_pairs={{0,32},{4,36},{8,40},{12,44},{16,48},{20,52},{24,56},{28,60},{32,0... | collective-permute-start | bytes 786440 | tf_op jit(solution)/shard_map/ppermute | solution.py:12
  193.9 3.7 %collective-permute-start.6 = (f32[512,128]{1,0:T(8,128)}, f32[512,128]{1,0:T(8,128)S(1)}, u32[]{:S(2)}, u32[]{:S(2)}) collective-permute-start(f32[512,128]{1,0:T(8,128)} %collective-permute-done.5), channel_id=1, source_target_pairs={{0,4},{4,0},{8,12},{12,8},{16,20},{20,16},{24,28},{28,24},{32,36},... | collective-permute-start | bytes 786440 | tf_op jit(solution)/shard_map/ppermute | solution.py:12
  204.5 33.8 %copy-start = (f32[512,128]{1,0:T(8,128)}, f32[512,128]{1,0:T(8,128)S(1)}, u32[]{:S(2)}) copy-start(f32[512,128]{1,0:T(8,128)S(1)} %slice_subtract_fusion.2) | copy-start | bytes 786436
  204.5 30.1 %collective-permute-start.7 = (f32[512,128]{1,0:T(8,128)S(1)}, f32[512,128]{1,0:T(8,128)}, u32[]{:S(2)}, u32[]{:S(2)}) collective-permute-start(f32[512,128]{1,0:T(8,128)S(1)} %slice_subtract_fusion.2), channel_id=1, source_target_pairs={{0,64},{4,68},{8,72},{12,76},{16,80},{20,84},{24,88},{28,92},{32,9... | collective-permute-start | bytes 786440 | tf_op jit(solution)/shard_map/ppermute | solution.py:12
  234.6 3.7 %collective-permute-start.8 = (f32[512,128]{1,0:T(8,128)}, f32[512,128]{1,0:T(8,128)S(1)}, u32[]{:S(2)}, u32[]{:S(2)}) collective-permute-start(f32[512,128]{1,0:T(8,128)} %collective-permute-done.7), channel_id=1, source_target_pairs={{0,4},{4,0},{8,12},{12,8},{16,20},{20,16},{24,28},{28,24},{32,36},... | collective-permute-start | bytes 786440 | tf_op jit(solution)/shard_map/ppermute | solution.py:12
  245.2 14.0 %copy-start.1 = (f32[512,128]{1,0:T(8,128)}, f32[512,128]{1,0:T(8,128)S(1)}, u32[]{:S(2)}) copy-start(f32[512,128]{1,0:T(8,128)S(1)} %slice_subtract_fusion.1) | copy-start | bytes 786436
  245.2 9.6 %collective-permute-start.9 = (f32[512,128]{1,0:T(8,128)S(1)}, f32[512,128]{1,0:T(8,128)}, u32[]{:S(2)}, u32[]{:S(2)}) collective-permute-start(f32[512,128]{1,0:T(8,128)S(1)} %slice_subtract_fusion.1), channel_id=1, source_target_pairs={{0,128},{4,132},{8,136},{12,140},{16,144},{20,148},{24,152},{28,15... | collective-permute-start | bytes 786440 | tf_op jit(solution)/shard_map/ppermute | solution.py:12
  254.7 4.4 %collective-permute-start.10 = (f32[512,128]{1,0:T(8,128)}, f32[512,128]{1,0:T(8,128)S(1)}, u32[]{:S(2)}, u32[]{:S(2)}) collective-permute-start(f32[512,128]{1,0:T(8,128)} %collective-permute-done.9), channel_id=1, source_target_pairs={{0,4},{4,0},{8,12},{12,8},{16,20},{20,16},{24,28},{28,24},{32,36},... | collective-permute-start | bytes 786440 | tf_op jit(solution)/shard_map/ppermute | solution.py:12
  267.7 10.9 %collective-permute-start.11 = (f32[512,128]{1,0:T(8,128)}, f32[512,128]{1,0:T(8,128)}, u32[]{:S(2)}, u32[]{:S(2)}) collective-permute-start(f32[512,128]{1,0:T(8,128)} %slice_subtract_fusion), channel_id=1, source_target_pairs={{0,256},{4,260},{8,264},{12,268},{16,272},{20,276},{24,280},{28,28... | collective-permute-start | bytes 786440 | tf_op jit(solution)/shard_map/ppermute | solution.py:12
  278.6 4.9 %collective-permute-start.12 = (f32[512,128]{1,0:T(8,128)}, f32[512,128]{1,0:T(8,128)}, u32[]{:S(2)}, u32[]{:S(2)}) collective-permute-start(f32[512,128]{1,0:T(8,128)} %collective-permute-done.11), channel_id=1, source_target_pairs={{0,4},{4,0},{8,12},{12,8},{16,20},{20,16},{24,28},{28,24},{32,36},... | collective-permute-start | bytes 786440 | tf_op jit(solution)/shard_map/ppermute | solution.py:12
Sparse Core Ops, SparseCore 0:
  10.1 43.7 all-gather.12
  56.0 43.8 all-gather.14
  102.0 41.1 all-gather.16
  145.2 38.5 all-gather.18
  185.8 38.5 all-gather.20
  226.3 38.5 all-gather.22

commit v13 on v12

--- a/solution.py
+++ b/solution.py
@@ -39,7 +39,7 @@
     quarter = load_boundary.shape[2]
     joined = jnp.concatenate([load_interior, load_boundary], axis=2)
     joined = lax.all_to_all(joined, "sub", split_axis=1, concat_axis=0, tiled=True)
-    early = 2
+    early = 1
     joined, later_maps = lax.optimization_barrier((joined, merge_maps[0, early:]))
     interior = jnp.transpose(joined[:, 0, :local_rows])
     boundary = jnp.transpose(joined[:, 0, local_rows:])

time: 298 us -> 308 us (1.034)
  local copies, waits for them, and re-layouts: 41.6 us -> 46.5 us
  starting transfers between devices: 73.5 us -> 77.8 us
    ppermute x13, waiting for transfers between devices: 71.2 us -> 64.9 us  [from_partner(): return lax.ppermute(value, axis, pairs)]
    ppermute x13, starting transfers between devices: 44.8 us -> 49.1 us  [from_partner(): return lax.ppermute(value, axis, pairs)]
  transfers between devices with their start and end apart: 22 -> 22, of which waited for: 17 -> 17; matrix products, arithmetic and copies ran while one was open for 22% -> 24% of each run, Pallas kernels for 0% -> 0%
where the time goes in v13:
time: 308 us; the launch traced here: 306 us
  waiting for transfers between devices  128 us (42%)
  starting transfers between devices  77.8 us (25%)
  local copies, waits for them, and re-layouts  46.5 us (15%)
  matrix products  27.4 us (9%)
  between operations  15.3 us (5%)
  other arithmetic  11.4 us (4%)
    ppermute x13, waiting for transfers between devices, from_partner(): return lax.ppermute(value, axis, pairs)  64.9 us
    ppermute x13, starting transfers between devices, from_partner(): return lax.ppermute(value, axis, pairs)  49.1 us
    all_to_all x1, waiting for transfers between devices, on_device(): lax.all_to_all(joined, 'sub', split_axis=1, concat_axis=0, tiled=True)  35.6 us
    dot_general x13, matrix products, rows_of(): return kept - jnp.dot(part, shared, precision=lax.Precision.HIGH)  25.8 us
    gather x7, local copies, waits for them, and re-layouts, on_device(): jnp.take(stacked, jnp.concatenate([left_index(maps[0, :shared_rows]), rig...  22 us
    all_to_all x1, starting transfers between devices, on_device(): lax.all_to_all(joined, 'sub', split_axis=1, concat_axis=0, tiled=True)  21 us
    all_to_all x1, waiting for transfers between devices, case_allreduce(): received = lax.all_to_all(chunks, 'case', split_axis=0, concat_axis=0)  14.9 us
    gather x6, local copies, waits for them, and re-layouts, rows_of(): kept = jnp.take(stacked, index, axis=0, mode='clip')  8.67 us
  transfers between devices with their start and end apart: 22, of which 17 were waited for; matrix products, arithmetic and copies ran while one was open for 24% of the time, Pallas kernels for 0%

profile of v13, /device:TPU:1, one launch (start us, length us, event | category | flops | bytes accessed | tf_op | source)
XLA Modules:
  0.0 306.2 jit_solution(1369397679103349521)
XLA Ops:
  12.3 21.0 %all-to-all-start = ((f32[1,128,1280]{2,0,1:T(1,128)}), f32[1,128,1280]{2,0,1:T(1,128)}, u32[]{:S(2)}, u32[]{:S(2)}) async-start(f32[1,128,1280]{2,0,1:T(1,128)} %pad_maximum_fusion.7), calls=%async_computation | async-start | bytes 1310720 | tf_op jit(solution)/shard_map/all_to_all | solution.py:41
  35.7 35.6 %all-to-all-done = f32[1,128,1280]{2,0,1:T(1,128)} async-done(((f32[1,128,1280]{2,0,1:T(1,128)}), f32[1,128,1280]{2,0,1:T(1,128)}, u32[]{:S(2)}, u32[]{:S(2)}) %all-to-all-start) | async-done | bytes 655392 | tf_op jit(solution)/shard_map/all_to_all | solution.py:41
  83.4 4.0 %all-to-all-start.1 = ((f32[4,256,128]{2,1,0:T(8,128)}), f32[4,256,128]{2,1,0:T(8,128)S(1)}, u32[]{:S(2)}, u32[]{:S(2)}) async-start(f32[4,256,128]{2,1,0:T(8,128)} %reshape_reshape.3), calls=%async_computation.1 | async-start | bytes 1048576 | tf_op jit(solution)/shard_map/all_to_all | solution.py:25
  87.5 14.9 %all-to-all-done.1 = f32[4,256,128]{2,1,0:T(8,128)S(1)} async-done(((f32[4,256,128]{2,1,0:T(8,128)}), f32[4,256,128]{2,1,0:T(8,128)S(1)}, u32[]{:S(2)}, u32[]{:S(2)}) %all-to-all-start.1) | async-done | bytes 524320 | tf_op jit(solution)/shard_map/all_to_all | solution.py:25
  103.2 3.5 %all-to-all-start.2 = ((f32[4,256,128]{2,1,0:T(8,128)}), f32[4,256,128]{2,1,0:T(8,128)S(1)}, u32[]{:S(2)}, u32[]{:S(2)}) async-start(f32[4,256,128]{2,1,0:T(8,128)} %broadcast_in_dim.71), calls=%async_computation.2 | async-start | bytes 1048576 | tf_op jit(solution)/shard_map/all_to_all | solution.py:31
  106.8 8.0 %all-to-all-done.2 = f32[4,256,128]{2,1,0:T(8,128)S(1)} async-done(((f32[4,256,128]{2,1,0:T(8,128)}), f32[4,256,128]{2,1,0:T(8,128)S(1)}, u32[]{:S(2)}, u32[]{:S(2)}) %all-to-all-start.2) | async-done | bytes 524320 | tf_op jit(solution)/shard_map/all_to_all | solution.py:31
  114.8 5.0 %collective-permute-start = (f32[1024,128]{1,0:T(8,128)S(1)}, f32[1024,128]{1,0:T(8,128)S(1)}, u32[]{:S(2)}, u32[]{:S(2)}) collective-permute-start(f32[1024,128]{1,0:T(8,128)S(1)} %bitcast.136), channel_id=1, source_target_pairs={{0,4},{4,0},{8,12},{12,8},{16,20},{20,16},{24,28},{28,24},{32,36},... | collective-permute-start | bytes 1572872 | tf_op jit(solution)/shard_map/ppermute | solution.py:12
  121.3 2.6 gather_fusion.1
  125.8 3.2 %collective-permute-start.1 = (f32[512,128]{1,0:T(8,128)S(1)}, f32[512,128]{1,0:T(8,128)S(1)}, u32[]{:S(2)}, u32[]{:S(2)}) collective-permute-start(f32[512,128]{1,0:T(8,128)S(1)} %slice_subtract_fusion.5), channel_id=1, source_target_pairs={{0,8},{4,12},{8,0},{12,4},{16,24},{20,28},{24,16},{28,20},{32,40},... | collective-permute-start | bytes 786440 | tf_op jit(solution)/shard_map/ppermute | solution.py:12
  131.9 3.3 %collective-permute-done.1 = f32[512,128]{1,0:T(8,128)S(1)} collective-permute-done((f32[512,128]{1,0:T(8,128)S(1)}, f32[512,128]{1,0:T(8,128)S(1)}, u32[]{:S(2)}, u32[]{:S(2)}) %collective-permute-start.1) | collective-permute-done | bytes 262176 | tf_op jit(solution)/shard_map/ppermute | solution.py:12
  135.3 3.0 collective-permute-start.2
  139.5 2.6 gather_fusion.3
  144.0 4.2 %collective-permute-start.3 = (f32[512,128]{1,0:T(8,128)S(1)}, f32[512,128]{1,0:T(8,128)S(1)}, u32[]{:S(2)}, u32[]{:S(2)}) collective-permute-start(f32[512,128]{1,0:T(8,128)S(1)} %slice_subtract_fusion.4), channel_id=1, source_target_pairs={{0,16},{4,20},{8,24},{12,28},{16,0},{20,4},{24,8},{28,12},{32,48},... | collective-permute-start | bytes 786440 | tf_op jit(solution)/shard_map/ppermute | solution.py:12
  151.1 8.8 %collective-permute-done.3 = f32[512,128]{1,0:T(8,128)S(1)} collective-permute-done((f32[512,128]{1,0:T(8,128)S(1)}, f32[512,128]{1,0:T(8,128)S(1)}, u32[]{:S(2)}, u32[]{:S(2)}) %collective-permute-start.3) | collective-permute-done | bytes 262176 | tf_op jit(solution)/shard_map/ppermute | solution.py:12
  159.9 3.3 %collective-permute-start.4 = (f32[512,128]{1,0:T(8,128)S(1)}, f32[512,128]{1,0:T(8,128)S(1)}, u32[]{:S(2)}, u32[]{:S(2)}) collective-permute-start(f32[512,128]{1,0:T(8,128)S(1)} %collective-permute-done.3), channel_id=1, source_target_pairs={{0,4},{4,0},{8,12},{12,8},{16,20},{20,16},{24,28},{28,24},{32,36},... | collective-permute-start | bytes 786440 | tf_op jit(solution)/shard_map/ppermute | solution.py:12
  164.2 2.6 gather_fusion.5
  168.7 5.2 %collective-permute-start.5 = (f32[512,128]{1,0:T(8,128)S(1)}, f32[512,128]{1,0:T(8,128)}, u32[]{:S(2)}, u32[]{:S(2)}) collective-permute-start(f32[512,128]{1,0:T(8,128)S(1)} %slice_subtract_fusion.3), channel_id=1, source_target_pairs={{0,32},{4,36},{8,40},{12,44},{16,48},{20,52},{24,56},{28,60},{32,0... | collective-permute-start | bytes 786440 | tf_op jit(solution)/shard_map/ppermute | solution.py:12
  178.4 20.3 %collective-permute-done.5 = f32[512,128]{1,0:T(8,128)} collective-permute-done((f32[512,128]{1,0:T(8,128)S(1)}, f32[512,128]{1,0:T(8,128)}, u32[]{:S(2)}, u32[]{:S(2)}) %collective-permute-start.5) | collective-permute-done | bytes 262176 | tf_op jit(solution)/shard_map/ppermute | solution.py:12
  203.4 3.7 %gather_fusion.7 = f32[1536,128]{1,0:T(8,128)} fusion(f32[2048,128]{1,0:T(8,128)S(1)} %pad_maximum_fusion.3, s32[2048]{0:T(1024)S(1)} %pad_clamp_fusion.3), kind=kCustom, calls=%fused_computation.7 | custom fusion | bytes 1579008 | tf_op jit(solution)/shard_map/jit(_take)/gather | solution.py:116
  209.2 7.0 %collective-permute-start.7 = (f32[512,128]{1,0:T(8,128)S(1)}, f32[512,128]{1,0:T(8,128)}, u32[]{:S(2)}, u32[]{:S(2)}) collective-permute-start(f32[512,128]{1,0:T(8,128)S(1)} %slice_subtract_fusion.2), channel_id=1, source_target_pairs={{0,64},{4,68},{8,72},{12,76},{16,80},{20,84},{24,88},{28,92},{32,9... | collective-permute-start | bytes 786440 | tf_op jit(solution)/shard_map/ppermute | solution.py:12
  220.9 20.4 %collective-permute-done.7 = f32[512,128]{1,0:T(8,128)} collective-permute-done((f32[512,128]{1,0:T(8,128)S(1)}, f32[512,128]{1,0:T(8,128)}, u32[]{:S(2)}, u32[]{:S(2)}) %collective-permute-start.7) | collective-permute-done | bytes 262176 | tf_op jit(solution)/shard_map/ppermute | solution.py:12
  246.0 3.7 %gather_fusion.9 = f32[1536,128]{1,0:T(8,128)} fusion(f32[2048,128]{1,0:T(8,128)S(1)} %pad_maximum_fusion.4, s32[2048]{0:T(1024)S(1)} %pad_clamp_fusion.2), kind=kCustom, calls=%fused_computation.9 | custom fusion | bytes 1579008 | tf_op jit(solution)/shard_map/jit(_take)/gather | solution.py:116
  251.7 2.4 collective-permute-start.9
  258.7 2.5 collective-permute-done.9
  261.2 3.1 %collective-permute-start.10 = (f32[512,128]{1,0:T(8,128)}, f32[512,128]{1,0:T(8,128)S(1)}, u32[]{:S(2)}, u32[]{:S(2)}) collective-permute-start(f32[512,128]{1,0:T(8,128)} %collective-permute-done.9), channel_id=1, source_target_pairs={{0,4},{4,0},{8,12},{12,8},{16,20},{20,16},{24,28},{28,24},{32,36},... | collective-permute-start | bytes 786440 | tf_op jit(solution)/shard_map/ppermute | solution.py:12
  266.7 3.7 %gather_fusion.11 = f32[1536,128]{1,0:T(8,128)} fusion(f32[2048,128]{1,0:T(8,128)S(1)} %pad_maximum_fusion.5, s32[2048]{0:T(1024)S(1)} %pad_clamp_fusion.1), kind=kCustom, calls=%fused_computation.11 | custom fusion | bytes 1579008 | tf_op jit(solution)/shard_map/jit(_take)/gather | solution.py:116
  270.4 3.8 %all-gather.23.cloned.1.call-done = f32[1,1024,512]{2,1,0:T(8,128)} async-done(((f32[1,256,512]{2,1,0:T(8,128)}), f32[1,1024,512]{2,1,0:T(8,128)}) %all-gather.23.cloned.1.call-update) | async-done | bytes 2097168 | tf_op jit(solution)/shard_map/all_gather | solution.py:84
  274.1 2.7 slice_subtract_fusion
  276.9 4.6 %collective-permute-start.11 = (f32[512,128]{1,0:T(8,128)}, f32[512,128]{1,0:T(8,128)}, u32[]{:S(2)}, u32[]{:S(2)}) collective-permute-start(f32[512,128]{1,0:T(8,128)} %slice_subtract_fusion), channel_id=1, source_target_pairs={{0,256},{4,260},{8,264},{12,268},{16,272},{20,276},{24,280},{28,28... | collective-permute-start | bytes 786440 | tf_op jit(solution)/shard_map/ppermute | solution.py:12
  287.7 3.4 %collective-permute-start.12 = (f32[512,128]{1,0:T(8,128)}, f32[512,128]{1,0:T(8,128)}, u32[]{:S(2)}, u32[]{:S(2)}) collective-permute-start(f32[512,128]{1,0:T(8,128)} %collective-permute-done.11), channel_id=1, source_target_pairs={{0,4},{4,0},{8,12},{12,8},{16,20},{20,16},{24,28},{28,24},{32,36},... | collective-permute-start | bytes 786440 | tf_op jit(solution)/shard_map/ppermute | solution.py:12
  293.9 3.1 %gather_fusion.13 = f32[1280,128]{1,0:T(8,128)} fusion(f32[2048,128]{1,0:T(8,128)S(1)} %pad_maximum_fusion.6, s32[2048]{0:T(1024)S(1)} %pad_clamp_fusion), kind=kCustom, calls=%fused_computation.13 | custom fusion | bytes 1315840 | tf_op jit(solution)/shard_map/jit(_take)/gather | solution.py:116
  297.0 2.4 fusion.54
  (162 shorter events, 73.5 us)
Async XLA Ops:
  7.2 116.8 %all-gather.13.cloned.1.call-start = ((), (), s32[]{:S(2)}) async-start(), calls=%async_computation.3 | async-start | bytes 2621440 | tf_op jit(solution)/shard_map/all_gather | solution.py:84
  12.3 59.0 %all-to-all-start = ((f32[1,128,1280]{2,0,1:T(1,128)}), f32[1,128,1280]{2,0,1:T(1,128)}, u32[]{:S(2)}, u32[]{:S(2)}) async-start(f32[1,128,1280]{2,0,1:T(1,128)} %pad_maximum_fusion.7), calls=%async_computation | async-start | bytes 1310720 | tf_op jit(solution)/shard_map/all_to_all | solution.py:41
  33.3 108.8 %all-gather.15.cloned.1.call-start = ((), (), s32[]{:S(2)}) async-start(), calls=%async_computation.4 | async-start | bytes 2621440 | tf_op jit(solution)/shard_map/all_gather | solution.py:84
  74.9 5.4 %copy-start = (f32[1,128,1280]{1,2,0:T(8,128)S(1)}, f32[1,128,1280]{1,2,0:T(8,128)}, u32[]{:S(2)}) copy-start(f32[1,128,1280]{1,2,0:T(8,128)} %copy.20) | copy-start | bytes 1966084
  74.9 91.9 %all-gather.17.cloned.1.call-start = ((), (), s32[]{:S(2)}) async-start(), calls=%async_computation.5 | async-start | bytes 2621440 | tf_op jit(solution)/shard_map/all_gather | solution.py:84
  75.7 131.5 %all-gather.19.cloned.1.call-start = ((), (), s32[]{:S(2)}) async-start(), calls=%async_computation.6 | async-start | bytes 2621440 | tf_op jit(solution)/shard_map/all_gather | solution.py:84
  83.4 18.9 %all-to-all-start.1 = ((f32[4,256,128]{2,1,0:T(8,128)}), f32[4,256,128]{2,1,0:T(8,128)S(1)}, u32[]{:S(2)}, u32[]{:S(2)}) async-start(f32[4,256,128]{2,1,0:T(8,128)} %reshape_reshape.3), calls=%async_computation.1 | async-start | bytes 1048576 | tf_op jit(solution)/shard_map/all_to_all | solution.py:25
  102.4 18.9 %copy-start.3 = (f32[256,128]{1,0:T(8,128)}, f32[256,128]{1,0:T(8,128)S(1)}, u32[]{:S(2)}) copy-start(f32[256,128]{1,0:T(8,128)S(1)} %fusion.61) | copy-start | bytes 393220
  103.2 11.5 %all-to-all-start.2 = ((f32[4,256,128]{2,1,0:T(8,128)}), f32[4,256,128]{2,1,0:T(8,128)S(1)}, u32[]{:S(2)}, u32[]{:S(2)}) async-start(f32[4,256,128]{2,1,0:T(8,128)} %broadcast_in_dim.71), calls=%async_computation.2 | async-start | bytes 1048576 | tf_op jit(solution)/shard_map/all_to_all | solution.py:31
  106.7 143.0 %all-gather.21.cloned.1.call-start = ((), (), s32[]{:S(2)}) async-start(), calls=%async_computation.7 | async-start | bytes 2621440 | tf_op jit(solution)/shard_map/all_gather | solution.py:84
  114.8 6.5 %collective-permute-start = (f32[1024,128]{1,0:T(8,128)S(1)}, f32[1024,128]{1,0:T(8,128)S(1)}, u32[]{:S(2)}, u32[]{:S(2)}) collective-permute-start(f32[1024,128]{1,0:T(8,128)S(1)} %bitcast.136), channel_id=1, source_target_pairs={{0,4},{4,0},{8,12},{12,8},{16,20},{20,16},{24,28},{28,24},{32,36},... | collective-permute-start | bytes 1572872 | tf_op jit(solution)/shard_map/ppermute | solution.py:12
  120.4 153.8 %all-gather.23.cloned.1.call-start = ((), (), s32[]{:S(2)}) async-start(), calls=%async_computation.8 | async-start | bytes 2621440 | tf_op jit(solution)/shard_map/all_gather | solution.py:84
  125.8 9.5 %collective-permute-start.1 = (f32[512,128]{1,0:T(8,128)S(1)}, f32[512,128]{1,0:T(8,128)S(1)}, u32[]{:S(2)}, u32[]{:S(2)}) collective-permute-start(f32[512,128]{1,0:T(8,128)S(1)} %slice_subtract_fusion.5), channel_id=1, source_target_pairs={{0,8},{4,12},{8,0},{12,4},{16,24},{20,28},{24,16},{28,20},{32,40},... | collective-permute-start | bytes 786440 | tf_op jit(solution)/shard_map/ppermute | solution.py:12
  135.3 4.2 %collective-permute-start.2 = (f32[512,128]{1,0:T(8,128)S(1)}, f32[512,128]{1,0:T(8,128)S(1)}, u32[]{:S(2)}, u32[]{:S(2)}) collective-permute-start(f32[512,128]{1,0:T(8,128)S(1)} %collective-permute-done.1), channel_id=1, source_target_pairs={{0,4},{4,0},{8,12},{12,8},{16,20},{20,16},{24,28},{28,24},{32,36},... | collective-permute-start | bytes 786440 | tf_op jit(solution)/shard_map/ppermute | solution.py:12
  139.5 8.6 %copy-start.10 = (s32[512]{0:T(512)S(1)}, s32[512]{0:T(512)}, u32[]{:S(2)}) copy-start(s32[512]{0:T(512)} %get-tuple-element.68) | copy-start | bytes 6148
  144.0 15.9 %collective-permute-start.3 = (f32[512,128]{1,0:T(8,128)S(1)}, f32[512,128]{1,0:T(8,128)S(1)}, u32[]{:S(2)}, u32[]{:S(2)}) collective-permute-start(f32[512,128]{1,0:T(8,128)S(1)} %slice_subtract_fusion.4), channel_id=1, source_target_pairs={{0,16},{4,20},{8,24},{12,28},{16,0},{20,4},{24,8},{28,12},{32,48},... | collective-permute-start | bytes 786440 | tf_op jit(solution)/shard_map/ppermute | solution.py:12
  148.2 15.0 %copy-start.7 = (s32[1,512]{1,0:T(1,128)S(1)}, s32[1,512]{1,0:T(1,128)}, u32[]{:S(2)}) copy-start(s32[1,512]{1,0:T(1,128)} %get-tuple-element.36) | copy-start | bytes 6148
  148.2 15.0 %copy-start.8 = (s32[1,512]{1,0:T(1,128)S(1)}, s32[1,512]{1,0:T(1,128)}, u32[]{:S(2)}) copy-start(s32[1,512]{1,0:T(1,128)} %get-tuple-element.39) | copy-start | bytes 6148
  159.9 4.3 %collective-permute-start.4 = (f32[512,128]{1,0:T(8,128)S(1)}, f32[512,128]{1,0:T(8,128)S(1)}, u32[]{:S(2)}, u32[]{:S(2)}) collective-permute-start(f32[512,128]{1,0:T(8,128)S(1)} %collective-permute-done.3), channel_id=1, source_target_pairs={{0,4},{4,0},{8,12},{12,8},{16,20},{20,16},{24,28},{28,24},{32,36},... | collective-permute-start | bytes 786440 | tf_op jit(solution)/shard_map/ppermute | solution.py:12
  164.2 9.7 %copy-start.9 = (s32[512]{0:T(512)S(1)}, s32[512]{0:T(512)}, u32[]{:S(2)}) copy-start(s32[512]{0:T(512)} %get-tuple-element.66) | copy-start | bytes 6148
  168.7 30.0 %collective-permute-start.5 = (f32[512,128]{1,0:T(8,128)S(1)}, f32[512,128]{1,0:T(8,128)}, u32[]{:S(2)}, u32[]{:S(2)}) collective-permute-start(f32[512,128]{1,0:T(8,128)S(1)} %slice_subtract_fusion.3), channel_id=1, source_target_pairs={{0,32},{4,36},{8,40},{12,44},{16,48},{20,52},{24,56},{28,60},{32,0... | collective-permute-start | bytes 786440 | tf_op jit(solution)/shard_map/ppermute | solution.py:12
  173.9 27.1 %copy-start.11 = (s32[512]{0:T(512)S(1)}, s32[512]{0:T(512)}, u32[]{:S(2)}) copy-start(s32[512]{0:T(512)} %get-tuple-element.64) | copy-start | bytes 6148
  198.7 3.7 %collective-permute-start.6 = (f32[512,128]{1,0:T(8,128)}, f32[512,128]{1,0:T(8,128)S(1)}, u32[]{:S(2)}, u32[]{:S(2)}) collective-permute-start(f32[512,128]{1,0:T(8,128)} %collective-permute-done.5), channel_id=1, source_target_pairs={{0,4},{4,0},{8,12},{12,8},{16,20},{20,16},{24,28},{28,24},{32,36},... | collective-permute-start | bytes 786440 | tf_op jit(solution)/shard_map/ppermute | solution.py:12
  203.4 12.8 %copy-start.6 = (s32[1024]{0:T(1024)S(1)}, s32[1024]{0:T(1024)}, u32[]{:S(2)}) copy-start(s32[1024]{0:T(1024)} %get-tuple-element.77) | copy-start | bytes 12292
  209.2 40.5 %copy-start.1 = (f32[512,128]{1,0:T(8,128)}, f32[512,128]{1,0:T(8,128)S(1)}, u32[]{:S(2)}) copy-start(f32[512,128]{1,0:T(8,128)S(1)} %slice_subtract_fusion.2) | copy-start | bytes 786436
  209.2 32.1 %collective-permute-start.7 = (f32[512,128]{1,0:T(8,128)S(1)}, f32[512,128]{1,0:T(8,128)}, u32[]{:S(2)}, u32[]{:S(2)}) collective-permute-start(f32[512,128]{1,0:T(8,128)S(1)} %slice_subtract_fusion.2), channel_id=1, source_target_pairs={{0,64},{4,68},{8,72},{12,76},{16,80},{20,84},{24,88},{28,92},{32,9... | collective-permute-start | bytes 786440 | tf_op jit(solution)/shard_map/ppermute | solution.py:12
  241.2 3.7 %collective-permute-start.8 = (f32[512,128]{1,0:T(8,128)}, f32[512,128]{1,0:T(8,128)S(1)}, u32[]{:S(2)}, u32[]{:S(2)}) collective-permute-start(f32[512,128]{1,0:T(8,128)} %collective-permute-done.7), channel_id=1, source_target_pairs={{0,4},{4,0},{8,12},{12,8},{16,20},{20,16},{24,28},{28,24},{32,36},... | collective-permute-start | bytes 786440 | tf_op jit(solution)/shard_map/ppermute | solution.py:12
  251.7 18.7 %copy-start.2 = (f32[512,128]{1,0:T(8,128)}, f32[512,128]{1,0:T(8,128)S(1)}, u32[]{:S(2)}) copy-start(f32[512,128]{1,0:T(8,128)S(1)} %slice_subtract_fusion.1) | copy-start | bytes 786436
  251.7 9.5 %collective-permute-start.9 = (f32[512,128]{1,0:T(8,128)S(1)}, f32[512,128]{1,0:T(8,128)}, u32[]{:S(2)}, u32[]{:S(2)}) collective-permute-start(f32[512,128]{1,0:T(8,128)S(1)} %slice_subtract_fusion.1), channel_id=1, source_target_pairs={{0,128},{4,132},{8,136},{12,140},{16,144},{20,148},{24,152},{28,15... | collective-permute-start | bytes 786440 | tf_op jit(solution)/shard_map/ppermute | solution.py:12
  261.2 4.5 %collective-permute-start.10 = (f32[512,128]{1,0:T(8,128)}, f32[512,128]{1,0:T(8,128)S(1)}, u32[]{:S(2)}, u32[]{:S(2)}) collective-permute-start(f32[512,128]{1,0:T(8,128)} %collective-permute-done.9), channel_id=1, source_target_pairs={{0,4},{4,0},{8,12},{12,8},{16,20},{20,16},{24,28},{28,24},{32,36},... | collective-permute-start | bytes 786440 | tf_op jit(solution)/shard_map/ppermute | solution.py:12
  276.9 10.9 %collective-permute-start.11 = (f32[512,128]{1,0:T(8,128)}, f32[512,128]{1,0:T(8,128)}, u32[]{:S(2)}, u32[]{:S(2)}) collective-permute-start(f32[512,128]{1,0:T(8,128)} %slice_subtract_fusion), channel_id=1, source_target_pairs={{0,256},{4,260},{8,264},{12,268},{16,272},{20,276},{24,280},{28,28... | collective-permute-start | bytes 786440 | tf_op jit(solution)/shard_map/ppermute | solution.py:12
  287.7 4.9 %collective-permute-start.12 = (f32[512,128]{1,0:T(8,128)}, f32[512,128]{1,0:T(8,128)}, u32[]{:S(2)}, u32[]{:S(2)}) collective-permute-start(f32[512,128]{1,0:T(8,128)} %collective-permute-done.11), channel_id=1, source_target_pairs={{0,4},{4,0},{8,12},{12,8},{16,20},{20,16},{24,28},{28,24},{32,36},... | collective-permute-start | bytes 786440 | tf_op jit(solution)/shard_map/ppermute | solution.py:12
  (4 other events, 7.7 us)
Sparse Core Ops, SparseCore 0:
  10.1 43.7 all-gather.12
  75.0 36.8 all-gather.14
  114.0 38.3 all-gather.16
  154.3 38.5 all-gather.18
  194.9 38.5 all-gather.20
  235.5 38.5 all-gather.22

commit v14 on v12

--- a/solution.py
+++ b/solution.py
@@ -52,7 +52,10 @@
     position = lax.axis_index("case")
     local_cols = block_cols[0] - position * (local_rows // block_size)
     pieces = jnp.take(
-        interior.reshape(local_rows // block_size, block_size, num_cases), local_cols, axis=0
+        interior.reshape(local_rows // block_size, block_size, num_cases),
+        local_cols,
+        axis=0,
+        mode="clip",
     )
     products = jnp.einsum("krc,kcn->krn", blocks, pieces, precision=lax.Precision.HIGH)
     row_blocks = full_rows // block_size

time: 298 us -> 298 us (level)
  no operation moved by 1% of the time
where the time goes in v14:
time: 298 us; the launch traced here: 297 us
  waiting for transfers between devices  131 us (44%)
  starting transfers between devices  73.6 us (25%)
  local copies, waits for them, and re-layouts  41.7 us (14%)
  matrix products  27.6 us (9%)
  between operations  15.3 us (5%)
  other arithmetic  8.33 us (3%)
    ppermute x13, waiting for transfers between devices, from_partner(): return lax.ppermute(value, axis, pairs)  71.1 us
    ppermute x13, starting transfers between devices, from_partner(): return lax.ppermute(value, axis, pairs)  44.9 us
    all_to_all x1, waiting for transfers between devices, on_device(): lax.all_to_all(joined, 'sub', split_axis=1, concat_axis=0, tiled=True)  35.7 us
    dot_general x13, matrix products, rows_of(): return kept - jnp.dot(part, shared, precision=lax.Precision.HIGH)  26.1 us
    gather x7, local copies, waits for them, and re-layouts, on_device(): jnp.take(stacked, jnp.concatenate([left_index(maps[0, :shared_rows]), rig...  21.9 us
    all_to_all x1, starting transfers between devices, on_device(): lax.all_to_all(joined, 'sub', split_axis=1, concat_axis=0, tiled=True)  21 us
    all_to_all x1, waiting for transfers between devices, case_allreduce(): received = lax.all_to_all(chunks, 'case', split_axis=0, concat_axis=0)  14.9 us
    gather x6, local copies, waits for them, and re-layouts, rows_of(): kept = jnp.take(stacked, index, axis=0, mode='clip')  7.42 us
  transfers between devices with their start and end apart: 22, of which 17 were waited for; matrix products, arithmetic and copies ran while one was open for 22% of the time, Pallas kernels for 0%

profile of v14, /device:TPU:1, one launch (start us, length us, event | category | flops | bytes accessed | tf_op | source)
XLA Modules:
  0.0 297.0 jit_solution(4772075536726515069)
XLA Ops:
  12.5 21.0 %all-to-all-start = ((f32[1,128,1280]{2,0,1:T(1,128)}), f32[1,128,1280]{2,0,1:T(1,128)}, u32[]{:S(2)}, u32[]{:S(2)}) async-start(f32[1,128,1280]{2,0,1:T(1,128)} %pad_maximum_fusion.7), calls=%async_computation | async-start | bytes 1310720 | tf_op jit(solution)/shard_map/all_to_all | solution.py:41
  35.8 35.7 %all-to-all-done = f32[1,128,1280]{2,0,1:T(1,128)} async-done(((f32[1,128,1280]{2,0,1:T(1,128)}), f32[1,128,1280]{2,0,1:T(1,128)}, u32[]{:S(2)}, u32[]{:S(2)}) %all-to-all-start) | async-done | bytes 655392 | tf_op jit(solution)/shard_map/all_to_all | solution.py:41
  79.6 4.0 %all-to-all-start.1 = ((f32[4,256,128]{2,1,0:T(8,128)}), f32[4,256,128]{2,1,0:T(8,128)S(1)}, u32[]{:S(2)}, u32[]{:S(2)}) async-start(f32[4,256,128]{2,1,0:T(8,128)} %reshape_reshape.3), calls=%async_computation.1 | async-start | bytes 1048576 | tf_op jit(solution)/shard_map/all_to_all | solution.py:25
  83.6 14.9 %all-to-all-done.1 = f32[4,256,128]{2,1,0:T(8,128)S(1)} async-done(((f32[4,256,128]{2,1,0:T(8,128)}), f32[4,256,128]{2,1,0:T(8,128)S(1)}, u32[]{:S(2)}, u32[]{:S(2)}) %all-to-all-start.1) | async-done | bytes 524320 | tf_op jit(solution)/shard_map/all_to_all | solution.py:25
  99.4 3.5 %all-to-all-start.2 = ((f32[4,256,128]{2,1,0:T(8,128)}), f32[4,256,128]{2,1,0:T(8,128)S(1)}, u32[]{:S(2)}, u32[]{:S(2)}) async-start(f32[4,256,128]{2,1,0:T(8,128)} %broadcast_in_dim.61), calls=%async_computation.2 | async-start | bytes 1048576 | tf_op jit(solution)/shard_map/all_to_all | solution.py:31
  102.9 6.9 %all-to-all-done.2 = f32[4,256,128]{2,1,0:T(8,128)S(1)} async-done(((f32[4,256,128]{2,1,0:T(8,128)}), f32[4,256,128]{2,1,0:T(8,128)S(1)}, u32[]{:S(2)}, u32[]{:S(2)}) %all-to-all-start.2) | async-done | bytes 524320 | tf_op jit(solution)/shard_map/all_to_all | solution.py:31
  109.8 5.4 %collective-permute-start = (f32[1024,128]{1,0:T(8,128)S(1)}, f32[1024,128]{1,0:T(8,128)S(1)}, u32[]{:S(2)}, u32[]{:S(2)}) collective-permute-start(f32[1024,128]{1,0:T(8,128)S(1)} %bitcast.133), channel_id=1, source_target_pairs={{0,4},{4,0},{8,12},{12,8},{16,20},{20,16},{24,28},{28,24},{32,36},... | collective-permute-start | bytes 1572872 | tf_op jit(solution)/shard_map/ppermute | solution.py:12
  116.8 2.6 gather_fusion.1
  121.2 3.2 %collective-permute-start.1 = (f32[512,128]{1,0:T(8,128)S(1)}, f32[512,128]{1,0:T(8,128)S(1)}, u32[]{:S(2)}, u32[]{:S(2)}) collective-permute-start(f32[512,128]{1,0:T(8,128)S(1)} %slice_subtract_fusion.5), channel_id=1, source_target_pairs={{0,8},{4,12},{8,0},{12,4},{16,24},{20,28},{24,16},{28,20},{32,40},... | collective-permute-start | bytes 786440 | tf_op jit(solution)/shard_map/ppermute | solution.py:12
  127.3 3.4 %collective-permute-done.1 = f32[512,128]{1,0:T(8,128)S(1)} collective-permute-done((f32[512,128]{1,0:T(8,128)S(1)}, f32[512,128]{1,0:T(8,128)S(1)}, u32[]{:S(2)}, u32[]{:S(2)}) %collective-permute-start.1) | collective-permute-done | bytes 262176 | tf_op jit(solution)/shard_map/ppermute | solution.py:12
  130.7 3.0 %collective-permute-start.2 = (f32[512,128]{1,0:T(8,128)S(1)}, f32[512,128]{1,0:T(8,128)S(1)}, u32[]{:S(2)}, u32[]{:S(2)}) collective-permute-start(f32[512,128]{1,0:T(8,128)S(1)} %collective-permute-done.1), channel_id=1, source_target_pairs={{0,4},{4,0},{8,12},{12,8},{16,20},{20,16},{24,28},{28,24},{32,36},... | collective-permute-start | bytes 786440 | tf_op jit(solution)/shard_map/ppermute | solution.py:12
  134.9 2.6 gather_fusion.3
  139.4 3.3 %collective-permute-start.3 = (f32[512,128]{1,0:T(8,128)S(1)}, f32[512,128]{1,0:T(8,128)S(1)}, u32[]{:S(2)}, u32[]{:S(2)}) collective-permute-start(f32[512,128]{1,0:T(8,128)S(1)} %slice_subtract_fusion.4), channel_id=1, source_target_pairs={{0,16},{4,20},{8,24},{12,28},{16,0},{20,4},{24,8},{28,12},{32,48},... | collective-permute-start | bytes 786440 | tf_op jit(solution)/shard_map/ppermute | solution.py:12
  145.6 9.7 %collective-permute-done.3 = f32[512,128]{1,0:T(8,128)S(1)} collective-permute-done((f32[512,128]{1,0:T(8,128)S(1)}, f32[512,128]{1,0:T(8,128)S(1)}, u32[]{:S(2)}, u32[]{:S(2)}) %collective-permute-start.3) | collective-permute-done | bytes 262176 | tf_op jit(solution)/shard_map/ppermute | solution.py:12
  155.4 3.3 %collective-permute-start.4 = (f32[512,128]{1,0:T(8,128)S(1)}, f32[512,128]{1,0:T(8,128)S(1)}, u32[]{:S(2)}, u32[]{:S(2)}) collective-permute-start(f32[512,128]{1,0:T(8,128)S(1)} %collective-permute-done.3), channel_id=1, source_target_pairs={{0,4},{4,0},{8,12},{12,8},{16,20},{20,16},{24,28},{28,24},{32,36},... | collective-permute-start | bytes 786440 | tf_op jit(solution)/shard_map/ppermute | solution.py:12
  159.7 2.6 gather_fusion.5
  164.2 3.3 %collective-permute-start.5 = (f32[512,128]{1,0:T(8,128)S(1)}, f32[512,128]{1,0:T(8,128)}, u32[]{:S(2)}, u32[]{:S(2)}) collective-permute-start(f32[512,128]{1,0:T(8,128)S(1)} %slice_subtract_fusion.3), channel_id=1, source_target_pairs={{0,32},{4,36},{8,40},{12,44},{16,48},{20,52},{24,56},{28,60},{32,0... | collective-permute-start | bytes 786440 | tf_op jit(solution)/shard_map/ppermute | solution.py:12
  170.5 23.4 %collective-permute-done.5 = f32[512,128]{1,0:T(8,128)} collective-permute-done((f32[512,128]{1,0:T(8,128)S(1)}, f32[512,128]{1,0:T(8,128)}, u32[]{:S(2)}, u32[]{:S(2)}) %collective-permute-start.5) | collective-permute-done | bytes 262176 | tf_op jit(solution)/shard_map/ppermute | solution.py:12
  193.9 2.4 collective-permute-start.6
  198.6 3.7 %gather_fusion.7 = f32[1536,128]{1,0:T(8,128)} fusion(f32[2048,128]{1,0:T(8,128)S(1)} %pad_maximum_fusion.3, s32[2048]{0:T(1024)S(1)} %pad_clamp_fusion.3), kind=kCustom, calls=%fused_computation.7 | custom fusion | bytes 1579008 | tf_op jit(solution)/shard_map/jit(_take)/gather | solution.py:119
  204.4 5.4 %collective-permute-start.7 = (f32[512,128]{1,0:T(8,128)S(1)}, f32[512,128]{1,0:T(8,128)}, u32[]{:S(2)}, u32[]{:S(2)}) collective-permute-start(f32[512,128]{1,0:T(8,128)S(1)} %slice_subtract_fusion.2), channel_id=1, source_target_pairs={{0,64},{4,68},{8,72},{12,76},{16,80},{20,84},{24,88},{28,92},{32,9... | collective-permute-start | bytes 786440 | tf_op jit(solution)/shard_map/ppermute | solution.py:12
  212.9 21.6 %collective-permute-done.7 = f32[512,128]{1,0:T(8,128)} collective-permute-done((f32[512,128]{1,0:T(8,128)S(1)}, f32[512,128]{1,0:T(8,128)}, u32[]{:S(2)}, u32[]{:S(2)}) %collective-permute-start.7) | collective-permute-done | bytes 262176 | tf_op jit(solution)/shard_map/ppermute | solution.py:12
  234.5 2.4 collective-permute-start.8
  239.3 3.7 %gather_fusion.9 = f32[1536,128]{1,0:T(8,128)} fusion(f32[2048,128]{1,0:T(8,128)S(1)} %pad_maximum_fusion.4, s32[2048]{0:T(1024)S(1)} %pad_clamp_fusion.2), kind=kCustom, calls=%fused_computation.9 | custom fusion | bytes 1579008 | tf_op jit(solution)/shard_map/jit(_take)/gather | solution.py:119
  252.0 2.7 collective-permute-done.9
  254.7 3.0 %collective-permute-start.10 = (f32[512,128]{1,0:T(8,128)}, f32[512,128]{1,0:T(8,128)S(1)}, u32[]{:S(2)}, u32[]{:S(2)}) collective-permute-start(f32[512,128]{1,0:T(8,128)} %collective-permute-done.9), channel_id=1, source_target_pairs={{0,4},{4,0},{8,12},{12,8},{16,20},{20,16},{24,28},{28,24},{32,36},... | collective-permute-start | bytes 786440 | tf_op jit(solution)/shard_map/ppermute | solution.py:12
  260.1 3.7 %gather_fusion.11 = f32[1536,128]{1,0:T(8,128)} fusion(f32[2048,128]{1,0:T(8,128)S(1)} %pad_maximum_fusion.5, s32[2048]{0:T(1024)S(1)} %pad_clamp_fusion.1), kind=kCustom, calls=%fused_computation.11 | custom fusion | bytes 1579008 | tf_op jit(solution)/shard_map/jit(_take)/gather | solution.py:119
  264.9 2.7 slice_subtract_fusion
  267.6 4.6 %collective-permute-start.11 = (f32[512,128]{1,0:T(8,128)}, f32[512,128]{1,0:T(8,128)}, u32[]{:S(2)}, u32[]{:S(2)}) collective-permute-start(f32[512,128]{1,0:T(8,128)} %slice_subtract_fusion), channel_id=1, source_target_pairs={{0,256},{4,260},{8,264},{12,268},{16,272},{20,276},{24,280},{28,28... | collective-permute-start | bytes 786440 | tf_op jit(solution)/shard_map/ppermute | solution.py:12
  278.5 3.4 %collective-permute-start.12 = (f32[512,128]{1,0:T(8,128)}, f32[512,128]{1,0:T(8,128)}, u32[]{:S(2)}, u32[]{:S(2)}) collective-permute-start(f32[512,128]{1,0:T(8,128)} %collective-permute-done.11), channel_id=1, source_target_pairs={{0,4},{4,0},{8,12},{12,8},{16,20},{20,16},{24,28},{28,24},{32,36},... | collective-permute-start | bytes 786440 | tf_op jit(solution)/shard_map/ppermute | solution.py:12
  284.6 3.1 %gather_fusion.13 = f32[1280,128]{1,0:T(8,128)} fusion(f32[2048,128]{1,0:T(8,128)S(1)} %pad_maximum_fusion.6, s32[2048]{0:T(1024)S(1)} %pad_clamp_fusion), kind=kCustom, calls=%fused_computation.13 | custom fusion | bytes 1315840 | tf_op jit(solution)/shard_map/jit(_take)/gather | solution.py:119
  287.8 2.4 fusion.50
  (149 shorter events, 65.3 us)
Async XLA Ops:
  7.2 3.2 %copy-start.2 = (f32[1,128,1024]{2,1,0:T(8,128)S(1)}, f32[1,128,1024]{2,1,0:T(8,128)}, u32[]{:S(2)}) copy-start(f32[1,128,1024]{2,1,0:T(8,128)} %param.7) | copy-start | bytes 1572868
  7.2 3.7 %copy-start.4 = (f32[1,128,256]{2,1,0:T(8,128)S(1)}, f32[1,128,256]{2,1,0:T(8,128)}, u32[]{:S(2)}) copy-start(f32[1,128,256]{2,1,0:T(8,128)} %param.8) | copy-start | bytes 393220
  7.2 112.2 %all-gather.13.cloned.1.call-start = ((), (), s32[]{:S(2)}) async-start(), calls=%async_computation.3 | async-start | bytes 2621440 | tf_op jit(solution)/shard_map/all_gather | solution.py:87
  9.6 128.0 %all-gather.15.cloned.1.call-start = ((), (), s32[]{:S(2)}) async-start(), calls=%async_computation.4 | async-start | bytes 2621440 | tf_op jit(solution)/shard_map/all_gather | solution.py:87
  10.3 23.2 %copy-start.7 = (s32[1,32]{1,0:T(1,128)S(1)}, s32[1,32]{1,0:T(1,128)}, u32[]{:S(2)}) copy-start(s32[1,32]{1,0:T(1,128)} %param.11) | copy-start | bytes 388
  10.4 23.2 %copy-start.5 = (s32[1,7,2,1024]{3,2,1,0:T(2,128)S(1)}, s32[1,7,2,1024]{3,2,1,0:T(2,128)}, u32[]{:S(2)}) copy-start(s32[1,7,2,1024]{3,2,1,0:T(2,128)} %param.12) | copy-start | bytes 172036
  12.5 59.0 %all-to-all-start = ((f32[1,128,1280]{2,0,1:T(1,128)}), f32[1,128,1280]{2,0,1:T(1,128)}, u32[]{:S(2)}, u32[]{:S(2)}) async-start(f32[1,128,1280]{2,0,1:T(1,128)} %pad_maximum_fusion.7), calls=%async_computation | async-start | bytes 1310720 | tf_op jit(solution)/shard_map/all_to_all | solution.py:41
  33.4 128.8 %all-gather.17.cloned.1.call-start = ((), (), s32[]{:S(2)}) async-start(), calls=%async_computation.5 | async-start | bytes 2621440 | tf_op jit(solution)/shard_map/all_gather | solution.py:87
  74.2 128.1 %all-gather.19.cloned.1.call-start = ((), (), s32[]{:S(2)}) async-start(), calls=%async_computation.6 | async-start | bytes 2621440 | tf_op jit(solution)/shard_map/all_gather | solution.py:87
  77.2 0.7 copy-start.6
  79.6 18.9 %all-to-all-start.1 = ((f32[4,256,128]{2,1,0:T(8,128)}), f32[4,256,128]{2,1,0:T(8,128)S(1)}, u32[]{:S(2)}, u32[]{:S(2)}) async-start(f32[4,256,128]{2,1,0:T(8,128)} %reshape_reshape.3), calls=%async_computation.1 | async-start | bytes 1048576 | tf_op jit(solution)/shard_map/all_to_all | solution.py:25
  98.5 18.2 %copy-start.3 = (f32[256,128]{1,0:T(8,128)}, f32[256,128]{1,0:T(8,128)S(1)}, u32[]{:S(2)}) copy-start(f32[256,128]{1,0:T(8,128)S(1)} %fusion.57) | copy-start | bytes 393220
  99.4 10.4 %all-to-all-start.2 = ((f32[4,256,128]{2,1,0:T(8,128)}), f32[4,256,128]{2,1,0:T(8,128)S(1)}, u32[]{:S(2)}, u32[]{:S(2)}) async-start(f32[4,256,128]{2,1,0:T(8,128)} %broadcast_in_dim.61), calls=%async_computation.2 | async-start | bytes 1048576 | tf_op jit(solution)/shard_map/all_to_all | solution.py:31
  102.9 140.1 %all-gather.21.cloned.1.call-start = ((), (), s32[]{:S(2)}) async-start(), calls=%async_computation.7 | async-start | bytes 2621440 | tf_op jit(solution)/shard_map/all_gather | solution.py:87
  109.8 6.9 %collective-permute-start = (f32[1024,128]{1,0:T(8,128)S(1)}, f32[1024,128]{1,0:T(8,128)S(1)}, u32[]{:S(2)}, u32[]{:S(2)}) collective-permute-start(f32[1024,128]{1,0:T(8,128)S(1)} %bitcast.133), channel_id=1, source_target_pairs={{0,4},{4,0},{8,12},{12,8},{16,20},{20,16},{24,28},{28,24},{32,36},... | collective-permute-start | bytes 1572872 | tf_op jit(solution)/shard_map/ppermute | solution.py:12
  115.2 149.7 %all-gather.23.cloned.1.call-start = ((), (), s32[]{:S(2)}) async-start(), calls=%async_computation.8 | async-start | bytes 2621440 | tf_op jit(solution)/shard_map/all_gather | solution.py:87
  121.2 9.5 %collective-permute-start.1 = (f32[512,128]{1,0:T(8,128)S(1)}, f32[512,128]{1,0:T(8,128)S(1)}, u32[]{:S(2)}, u32[]{:S(2)}) collective-permute-start(f32[512,128]{1,0:T(8,128)S(1)} %slice_subtract_fusion.5), channel_id=1, source_target_pairs={{0,8},{4,12},{8,0},{12,4},{16,24},{20,28},{24,16},{28,20},{32,40},... | collective-permute-start | bytes 786440 | tf_op jit(solution)/shard_map/ppermute | solution.py:12
  130.7 4.1 %collective-permute-start.2 = (f32[512,128]{1,0:T(8,128)S(1)}, f32[512,128]{1,0:T(8,128)S(1)}, u32[]{:S(2)}, u32[]{:S(2)}) collective-permute-start(f32[512,128]{1,0:T(8,128)S(1)} %collective-permute-done.1), channel_id=1, source_target_pairs={{0,4},{4,0},{8,12},{12,8},{16,20},{20,16},{24,28},{28,24},{32,36},... | collective-permute-start | bytes 786440 | tf_op jit(solution)/shard_map/ppermute | solution.py:12
  139.4 15.9 %collective-permute-start.3 = (f32[512,128]{1,0:T(8,128)S(1)}, f32[512,128]{1,0:T(8,128)S(1)}, u32[]{:S(2)}, u32[]{:S(2)}) collective-permute-start(f32[512,128]{1,0:T(8,128)S(1)} %slice_subtract_fusion.4), channel_id=1, source_target_pairs={{0,16},{4,20},{8,24},{12,28},{16,0},{20,4},{24,8},{28,12},{32,48},... | collective-permute-start | bytes 786440 | tf_op jit(solution)/shard_map/ppermute | solution.py:12
  155.4 4.2 %collective-permute-start.4 = (f32[512,128]{1,0:T(8,128)S(1)}, f32[512,128]{1,0:T(8,128)S(1)}, u32[]{:S(2)}, u32[]{:S(2)}) collective-permute-start(f32[512,128]{1,0:T(8,128)S(1)} %collective-permute-done.3), channel_id=1, source_target_pairs={{0,4},{4,0},{8,12},{12,8},{16,20},{20,16},{24,28},{28,24},{32,36},... | collective-permute-start | bytes 786440 | tf_op jit(solution)/shard_map/ppermute | solution.py:12
  164.2 29.7 %collective-permute-start.5 = (f32[512,128]{1,0:T(8,128)S(1)}, f32[512,128]{1,0:T(8,128)}, u32[]{:S(2)}, u32[]{:S(2)}) collective-permute-start(f32[512,128]{1,0:T(8,128)S(1)} %slice_subtract_fusion.3), channel_id=1, source_target_pairs={{0,32},{4,36},{8,40},{12,44},{16,48},{20,52},{24,56},{28,60},{32,0... | collective-permute-start | bytes 786440 | tf_op jit(solution)/shard_map/ppermute | solution.py:12
  193.9 3.7 %collective-permute-start.6 = (f32[512,128]{1,0:T(8,128)}, f32[512,128]{1,0:T(8,128)S(1)}, u32[]{:S(2)}, u32[]{:S(2)}) collective-permute-start(f32[512,128]{1,0:T(8,128)} %collective-permute-done.5), channel_id=1, source_target_pairs={{0,4},{4,0},{8,12},{12,8},{16,20},{20,16},{24,28},{28,24},{32,36},... | collective-permute-start | bytes 786440 | tf_op jit(solution)/shard_map/ppermute | solution.py:12
  204.4 33.8 %copy-start = (f32[512,128]{1,0:T(8,128)}, f32[512,128]{1,0:T(8,128)S(1)}, u32[]{:S(2)}) copy-start(f32[512,128]{1,0:T(8,128)S(1)} %slice_subtract_fusion.2) | copy-start | bytes 786436
  204.4 30.1 %collective-permute-start.7 = (f32[512,128]{1,0:T(8,128)S(1)}, f32[512,128]{1,0:T(8,128)}, u32[]{:S(2)}, u32[]{:S(2)}) collective-permute-start(f32[512,128]{1,0:T(8,128)S(1)} %slice_subtract_fusion.2), channel_id=1, source_target_pairs={{0,64},{4,68},{8,72},{12,76},{16,80},{20,84},{24,88},{28,92},{32,9... | collective-permute-start | bytes 786440 | tf_op jit(solution)/shard_map/ppermute | solution.py:12
  234.5 3.7 %collective-permute-start.8 = (f32[512,128]{1,0:T(8,128)}, f32[512,128]{1,0:T(8,128)S(1)}, u32[]{:S(2)}, u32[]{:S(2)}) collective-permute-start(f32[512,128]{1,0:T(8,128)} %collective-permute-done.7), channel_id=1, source_target_pairs={{0,4},{4,0},{8,12},{12,8},{16,20},{20,16},{24,28},{28,24},{32,36},... | collective-permute-start | bytes 786440 | tf_op jit(solution)/shard_map/ppermute | solution.py:12
  245.1 14.0 %copy-start.1 = (f32[512,128]{1,0:T(8,128)}, f32[512,128]{1,0:T(8,128)S(1)}, u32[]{:S(2)}) copy-start(f32[512,128]{1,0:T(8,128)S(1)} %slice_subtract_fusion.1) | copy-start | bytes 786436
  245.1 9.6 %collective-permute-start.9 = (f32[512,128]{1,0:T(8,128)S(1)}, f32[512,128]{1,0:T(8,128)}, u32[]{:S(2)}, u32[]{:S(2)}) collective-permute-start(f32[512,128]{1,0:T(8,128)S(1)} %slice_subtract_fusion.1), channel_id=1, source_target_pairs={{0,128},{4,132},{8,136},{12,140},{16,144},{20,148},{24,152},{28,15... | collective-permute-start | bytes 786440 | tf_op jit(solution)/shard_map/ppermute | solution.py:12
  254.7 4.4 %collective-permute-start.10 = (f32[512,128]{1,0:T(8,128)}, f32[512,128]{1,0:T(8,128)S(1)}, u32[]{:S(2)}, u32[]{:S(2)}) collective-permute-start(f32[512,128]{1,0:T(8,128)} %collective-permute-done.9), channel_id=1, source_target_pairs={{0,4},{4,0},{8,12},{12,8},{16,20},{20,16},{24,28},{28,24},{32,36},... | collective-permute-start | bytes 786440 | tf_op jit(solution)/shard_map/ppermute | solution.py:12
  267.6 10.9 %collective-permute-start.11 = (f32[512,128]{1,0:T(8,128)}, f32[512,128]{1,0:T(8,128)}, u32[]{:S(2)}, u32[]{:S(2)}) collective-permute-start(f32[512,128]{1,0:T(8,128)} %slice_subtract_fusion), channel_id=1, source_target_pairs={{0,256},{4,260},{8,264},{12,268},{16,272},{20,276},{24,280},{28,28... | collective-permute-start | bytes 786440 | tf_op jit(solution)/shard_map/ppermute | solution.py:12
  278.5 4.9 %collective-permute-start.12 = (f32[512,128]{1,0:T(8,128)}, f32[512,128]{1,0:T(8,128)}, u32[]{:S(2)}, u32[]{:S(2)}) collective-permute-start(f32[512,128]{1,0:T(8,128)} %collective-permute-done.11), channel_id=1, source_target_pairs={{0,4},{4,0},{8,12},{12,8},{16,20},{20,16},{24,28},{28,24},{32,36},... | collective-permute-start | bytes 786440 | tf_op jit(solution)/shard_map/ppermute | solution.py:12
Sparse Core Ops, SparseCore 0:
  10.1 43.7 all-gather.12
  56.0 43.8 all-gather.14
  102.0 41.0 all-gather.16
  145.1 38.5 all-gather.18
  185.7 38.5 all-gather.20
  226.3 38.5 all-gather.22
